TPU v7x, 32 devices: a whole 2x2x4 slice. The times are simulated.
32 devices in a mesh: stn: 16 (over z, y, core), blk: 2 (over x).
Axes of the slice: x: 2, y: 2, z: 4, core: 2. Of those that a mesh axis runs over, the one named last changes fastest.
Arguments:
- samples: int32 [2, 512, 65536], P(None, 'stn', 'blk'), may hold values from -128 to 127, as said below
- fir_taps: float32 [8, 1024], replicated, may hold values from -2 to 2
- station_order: int32 [512], replicated, may hold values from 0 to 511, each once
Outputs:
- coherence: bfloat16 [2, 1024, 512, 512], P(None, 'stn', 'blk')
Inputs may be any that keep to these rules, and one draw needn't show every extreme that they name: `samples`: quantized voltages, real parts in row 0 and imaginary parts in row 1 of the leading dimension. `station_order`: each station number appears exactly once.
All inputs are finite; a program needn't handle non-finite values.
Results may differ from a plain program's by a relative error of at most 0.0033.
Values may be sent and summed in bfloat16 or wider, within the bound.
No kernel may reach another device: no remote copies, remote signals or barrier semaphores. Data moves between devices by JAX's collectives and lax.ppermute only.
A program may use at most 128 MiB of HBM per device.

v0:
```python
import math

import jax
import ml_dtypes
import numpy as np
import jax.numpy as jnp
from jax import lax
from jax.experimental import pallas as pl
from jax.sharding import PartitionSpec as P

epsilon = 1e-06


def passed_along(value, axis, steps):
    count = lax.axis_size(axis)
    initial, last = (max(0, -steps), min(count, count - steps))
    return lax.ppermute(value, axis, [(source, source + steps) for source in range(initial, last)])


def chunk_count(local_channels):
    for count in (4, 2):
        if local_channels % count == 0:
            return count
    return 1


def dft_weights(channels, groups, chunks):
    local = channels // groups
    width = local // chunks
    chunk = np.arange(chunks).reshape(chunks, 1, 1, 1)
    group = np.arange(groups).reshape(1, groups, 1, 1)
    inner = np.arange(width).reshape(1, 1, width, 1)
    column = np.arange(channels).reshape(1, 1, 1, channels)
    row = group * local + chunk * width + inner
    phase_index = (row * column % channels).astype(np.float32)
    angle = phase_index * np.float32(2.0 * math.pi / channels)
    cosine = np.cos(angle).astype(ml_dtypes.bfloat16)
    sine = np.sin(angle).astype(ml_dtypes.bfloat16)
    table = np.concatenate([cosine, sine], axis=3)
    return jnp.asarray(table.reshape(chunks, groups * width, 2 * channels))


def fir_kernel(taps_ref, halo_ref, frames_ref, out_ref):
    tap_count = taps_ref.shape[0]
    spectra = frames_ref.shape[2]
    channels = frames_ref.shape[3]
    filtered = []
    for part in range(2):
        extended = jnp.concatenate(
            [halo_ref[part, 0].astype(jnp.float32), frames_ref[part, 0].astype(jnp.float32)], axis=0
        )
        total = taps_ref[0:1, :] * extended[0:spectra]
        for tap_index in range(1, tap_count):
            total = total + taps_ref[tap_index : tap_index + 1, :] * extended[tap_index : tap_index + spectra]
        filtered.append(total.astype(jnp.bfloat16))
    out_ref[0, 0, :, 0:channels] = filtered[0]
    out_ref[0, 0, :, channels:] = filtered[1]
    out_ref[1, 0, :, 0:channels] = filtered[1]
    out_ref[1, 0, :, channels:] = -filtered[0]


def filter_frames(fir_taps, earlier, frames):
    tap_count, channels = fir_taps.shape
    _, stations_local, spectra, _ = frames.shape
    return pl.pallas_call(
        fir_kernel,
        grid=(stations_local,),
        in_specs=[
            pl.BlockSpec((tap_count, channels), lambda a: (0, 0)),
            pl.BlockSpec((2, 1, tap_count - 1, channels), lambda a: (0, a, 0, 0)),
            pl.BlockSpec((2, 1, spectra, channels), lambda a: (0, a, 0, 0)),
        ],
        out_specs=pl.BlockSpec((2, 1, spectra, 2 * channels), lambda a: (0, a, 0, 0)),
        out_shape=jax.ShapeDtypeStruct((2, stations_local, spectra, 2 * channels), jnp.bfloat16),
    )(fir_taps, earlier, frames)


def correlate_kernel(rows_ref, cols_ref, *refs):
    out_ref = refs[-1]
    row_count = out_ref.shape[2]
    left = rows_ref[0]
    right = cols_ref[0]
    product = jnp.dot(left, right, preferred_element_type=jnp.float32)
    right = right.astype(jnp.float32)
    rows = left[0:row_count].astype(jnp.float32)
    column_power = jnp.sum(right * right, axis=0, keepdims=True)
    row_power = jnp.sum(rows * rows, axis=1, keepdims=True)
    scale_row = lax.rsqrt(row_power + epsilon)
    scale_column = lax.rsqrt(column_power + epsilon)
    out_ref[0, 0] = (product[0:row_count] * scale_row * scale_column).astype(out_ref.dtype)
    out_ref[1, 0] = (product[row_count:] * scale_row * scale_column).astype(out_ref.dtype)


def correlate_chunk(left, right, previous, offset, local_channels):
    width, double_rows, depth = left.shape
    row_count = double_rows // 2
    stations = right.shape[2]
    in_specs = [
        pl.BlockSpec((1, double_rows, depth), lambda k: (k, 0, 0)),
        pl.BlockSpec((1, depth, stations), lambda k: (k, 0, 0)),
    ]
    operands = [left, right]
    aliases = {}
    if previous is not None:
        in_specs.append(pl.BlockSpec(memory_space=pl.ANY))
        operands.append(previous)
        aliases = {2: 0}
    return pl.pallas_call(
        correlate_kernel,
        grid=(width,),
        in_specs=in_specs,
        out_specs=pl.BlockSpec((2, 1, row_count, stations), lambda k: (0, offset + k, 0, 0)),
        out_shape=jax.ShapeDtypeStruct((2, local_channels, row_count, stations), jnp.bfloat16),
        input_output_aliases=aliases,
    )(*operands)


def per_device(samples, fir_taps, station_order):
    tap_count = fir_taps.shape[0]
    channels = fir_taps.shape[1]
    stations_local = samples.shape[1]
    spectra_local = samples.shape[2] // channels
    stations = station_order.shape[0]
    groups = lax.axis_size("stn")
    blocks = lax.axis_size("blk")
    local_channels = channels // groups
    row_count = stations // blocks
    chunks = chunk_count(local_channels)
    width = local_channels // chunks

    frames = samples.reshape(2, stations_local, spectra_local, channels)
    earlier = frames[:, :, spectra_local - (tap_count - 1) :, :].astype(jnp.bfloat16)
    earlier = passed_along(earlier, "blk", 1)
    filtered = filter_frames(fir_taps, earlier, frames)
    filtered = filtered.reshape(2 * stations_local * spectra_local, 2 * channels)

    weights = dft_weights(channels, groups, chunks)
    selector = (
        station_order[None, :] == jnp.arange(stations, dtype=jnp.int32)[:, None]
    ).astype(jnp.bfloat16)
    selector = selector.reshape(groups, stations_local, stations)
    row_start = lax.axis_index("blk") * row_count

    def correlate(chunk, gathered, result):
        gathered = gathered.reshape(width, 2, -1, stations)
        row_block = lax.dynamic_slice_in_dim(gathered, row_start, row_count, 3)
        direct = jnp.transpose(row_block, (0, 3, 1, 2))
        swapped = jnp.stack([direct[:, :, 1], -direct[:, :, 0]], axis=2)
        left = jnp.concatenate([direct, swapped], axis=1).reshape(width, 2 * row_count, -1)
        right = gathered.reshape(width, -1, stations)
        return correlate_chunk(left, right, result, chunk * width, local_channels)

    result = None
    pending = []
    for chunk in range(chunks):
        spectra = jnp.einsum(
            "kj,nj->kn", weights[chunk], filtered, preferred_element_type=jnp.float32
        ).astype(jnp.bfloat16)
        spectra = spectra.reshape(groups, width, 2 * stations_local * spectra_local)
        turned = lax.all_to_all(spectra, "stn", split_axis=0, concat_axis=0, tiled=True)
        turned = turned.reshape(groups, width, 2, stations_local, spectra_local)
        ordered = jnp.einsum(
            "gkias,gar->kisr", turned, selector, preferred_element_type=jnp.float32
        ).astype(jnp.bfloat16)
        ordered = ordered.reshape(width * 2, spectra_local, stations)
        if chunk >= 2:
            ordered, result = lax.optimization_barrier((ordered, result))
        pending.append(lax.all_gather(ordered, "blk", axis=1, tiled=True))
        if chunk >= 1:
            result = correlate(chunk - 1, pending[chunk - 1], result)
    result = correlate(chunks - 1, pending[chunks - 1], result)
    return result


def solution(mesh):
    placed = (P(None, "stn", "blk"), P(), P())
    return jax.shard_map(
        per_device,
        mesh=mesh,
        in_specs=placed,
        out_specs=P(None, "stn", "blk", None),
        check_vma=False,
    )
```

profile of v0, /device:TPU:14, one launch (start us, length us, event | category | flops | bytes accessed | tf_op | source)
XLA Modules:
  0.0 357.0 jit_solution(4302165144375906878)
XLA Ops:
  6.5 8.1 %copy.53 = s32[8,8,32,1024]{3,2,1,0:T(8,128)S(1)} copy(s32[8,8,32,1024]{3,1,2,0:T(8,128)} %bitcast.74) | data formatting | bytes 16777216
  14.7 3.4 copy-done
  18.1 0.3 slice_convert_fusion
  18.3 0.6 copy.30
  18.9 1.3 collective-permute-start
  20.2 22.7 %collective-permute-done = bf16[2,32,7,1024]{3,1,2,0:T(8,128)(2,1)S(1)} collective-permute-done((bf16[2,32,7,1024]{3,1,2,0:T(8,128)(2,1)S(1)}, bf16[2,32,7,1024]{3,1,2,0:T(8,128)(2,1)S(1)}, u32[]{:S(2)}, u32[]{:S(2)}) %collective-permute-start) | collective-permute-done | bytes 917536 | tf_op jit(solution)/shard_map/ppermute | solution.py:17
  42.9 1.5 copy.31.halo_ref
  44.5 24.9 %shard_map.46 = bf16[2,32,32,2048]{3,2,1,0:T(8,128)(2,1)} custom-call(f32[8,1024]{1,0:T(8,128)} %taps_ref.1, bf16[2,32,7,1024]{3,2,1,0:T(8,128)(2,1)} %copy.31.halo_ref, s32[2,32,32,1024]{3,2,1,0:T(8,128)} %bitcast.73), custom_call_target="tpu_custom_call" | custom-call | tf_op jit(solution)/shard_map/pallas_call | solution.py:65
  69.3 6.9 %convolution_convert_fusion = bf16[2048,256]{0,1:T(8,128)(2,1)} fusion(bf16[2048,2048]{1,0:T(8,128)(2,1)} %bitcast.75, bf16[256,2048]{1,0:T(8,128)(2,1)S(1)} %copy-done.5), kind=kOutput, calls=%fused_computation.8 | convolution fusion | flops 2148007936 | bytes 10485760 | tf_op jit(solution)/shard_map/kj,nj->kn/dot_general | solution.py:156
  76.2 6.2 %all-to-all-start.3 = ((bf16[16,16,2048]{2,1,0:T(8,128)(2,1)}), bf16[16,16,2048]{2,1,0:T(8,128)(2,1)S(1)}, u32[]{:S(2)}, u32[]{:S(2)}) async-start(bf16[16,16,2048]{2,1,0:T(8,128)(2,1)} %bitcast.21), calls=%async_computation.3 | async-start | bytes 2097152 | tf_op jit(solution)/shard_map/all_to_all | solution.py:160
  82.5 6.8 %convolution_convert_fusion.2 = bf16[2048,256]{0,1:T(8,128)(2,1)} fusion(bf16[2048,2048]{1,0:T(8,128)(2,1)} %bitcast.76, bf16[256,2048]{1,0:T(8,128)(2,1)S(1)} %copy-done.4), kind=kOutput, calls=%fused_computation.10 | convolution fusion | flops 2148007936 | bytes 10485760 | tf_op jit(solution)/shard_map/kj,nj->kn/dot_general | solution.py:156
  89.3 17.9 %all-to-all-done.3 = bf16[16,16,2048]{2,1,0:T(8,128)(2,1)S(1)} async-done(((bf16[16,16,2048]{2,1,0:T(8,128)(2,1)}), bf16[16,16,2048]{2,1,0:T(8,128)(2,1)S(1)}, u32[]{:S(2)}, u32[]{:S(2)}) %all-to-all-start.3) | async-done | bytes 1048608 | tf_op jit(solution)/shard_map/all_to_all | solution.py:160
  107.2 5.1 %all-to-all-start.1 = ((bf16[16,16,2048]{2,1,0:T(8,128)(2,1)}), bf16[16,16,2048]{2,1,0:T(8,128)(2,1)S(1)}, u32[]{:S(2)}, u32[]{:S(2)}) async-start(bf16[16,16,2048]{2,1,0:T(8,128)(2,1)} %bitcast.8), calls=%async_computation.1 | async-start | bytes 2097152 | tf_op jit(solution)/shard_map/all_to_all | solution.py:160
  112.3 6.7 %convolution_convert_fusion.3 = bf16[2048,256]{0,1:T(8,128)(2,1)} fusion(bf16[2048,2048]{1,0:T(8,128)(2,1)} %bitcast.77, bf16[256,2048]{1,0:T(8,128)(2,1)S(1)} %copy-done.3), kind=kOutput, calls=%fused_computation.11 | convolution fusion | flops 2148007936 | bytes 10485760 | tf_op jit(solution)/shard_map/kj,nj->kn/dot_general | solution.py:156
  119.0 18.0 %all-to-all-done.1 = bf16[16,16,2048]{2,1,0:T(8,128)(2,1)S(1)} async-done(((bf16[16,16,2048]{2,1,0:T(8,128)(2,1)}), bf16[16,16,2048]{2,1,0:T(8,128)(2,1)S(1)}, u32[]{:S(2)}, u32[]{:S(2)}) %all-to-all-start.1) | async-done | bytes 1048608 | tf_op jit(solution)/shard_map/all_to_all | solution.py:160
  137.0 5.1 %all-to-all-start = ((bf16[16,16,2048]{2,1,0:T(8,128)(2,1)}), bf16[16,16,2048]{2,1,0:T(8,128)(2,1)S(1)}, u32[]{:S(2)}, u32[]{:S(2)}) async-start(bf16[16,16,2048]{2,1,0:T(8,128)(2,1)} %bitcast.96), calls=%async_computation | async-start | bytes 2097152 | tf_op jit(solution)/shard_map/all_to_all | solution.py:160
  142.1 4.4 %reshape.88 = bf16[16,16,2,32,32]{4,3,2,1,0:T(8,128)(2,1)} reshape(bf16[16,16,2048]{2,1,0:T(8,128)(2,1)S(1)} %all-to-all-done.1) | data formatting | bytes 2097152 | tf_op jit(solution)/shard_map/reshape | solution.py:161
  146.5 3.6 %fusion.4 = bf16[16,2,32,512,1]{3,2,0,1,4:T(8,128)(2,1)S(1)} fusion(bf16[16,16,2,32,32]{4,3,2,1,0:T(8,128)(2,1)} %reshape.88, s32[16,32]{1,0:T(8,128)S(1)} %multiply_add_fusion, s32[512]{0:T(512)S(1)} %copy-done.1), kind=kOutput, calls=%fused_computation.4 | convolution fusion | flops 537133056 | bytes 2101248 | tf_op jit(solution)/shard_map/gkias,gar->kisr/dot_general | solution.py:162
  150.2 1.1 copy.68
  151.2 6.7 %convolution_convert_fusion.1 = bf16[2048,256]{0,1:T(8,128)(2,1)} fusion(bf16[2048,2048]{1,0:T(8,128)(2,1)} %bitcast.78, bf16[256,2048]{1,0:T(8,128)(2,1)S(1)} %copy-done.2), kind=kOutput, calls=%fused_computation.9 | convolution fusion | flops 2148007936 | bytes 10485760 | tf_op jit(solution)/shard_map/kj,nj->kn/dot_general | solution.py:156
  158.0 8.8 %all-to-all-done = bf16[16,16,2048]{2,1,0:T(8,128)(2,1)S(1)} async-done(((bf16[16,16,2048]{2,1,0:T(8,128)(2,1)}), bf16[16,16,2048]{2,1,0:T(8,128)(2,1)S(1)}, u32[]{:S(2)}, u32[]{:S(2)}) %all-to-all-start) | async-done | bytes 1048608 | tf_op jit(solution)/shard_map/all_to_all | solution.py:160
  166.8 5.1 %all-to-all-start.2 = ((bf16[16,16,2048]{2,1,0:T(8,128)(2,1)}), bf16[16,16,2048]{2,1,0:T(8,128)(2,1)S(1)}, u32[]{:S(2)}, u32[]{:S(2)}) async-start(bf16[16,16,2048]{2,1,0:T(8,128)(2,1)} %bitcast.95), calls=%async_computation.2 | async-start | bytes 2097152 | tf_op jit(solution)/shard_map/all_to_all | solution.py:160
  171.9 4.4 %reshape.96 = bf16[16,16,2,32,32]{4,3,2,1,0:T(8,128)(2,1)} reshape(bf16[16,16,2048]{2,1,0:T(8,128)(2,1)S(1)} %all-to-all-done.3) | data formatting | bytes 2097152 | tf_op jit(solution)/shard_map/reshape | solution.py:161
  176.3 3.6 fusion
  179.9 1.1 copy.66
  181.0 0.3 all-gather.9.cloned.1.call-start
  181.3 4.4 %reshape.85 = bf16[16,16,2,32,32]{4,3,2,1,0:T(8,128)(2,1)} reshape(bf16[16,16,2048]{2,1,0:T(8,128)(2,1)S(1)} %all-to-all-done) | data formatting | bytes 2097152 | tf_op jit(solution)/shard_map/reshape | solution.py:161
  185.6 3.6 fusion.6
  189.2 1.0 copy.69
  190.3 6.4 %all-to-all-done.2 = bf16[16,16,2048]{2,1,0:T(8,128)(2,1)S(1)} async-done(((bf16[16,16,2048]{2,1,0:T(8,128)(2,1)}), bf16[16,16,2048]{2,1,0:T(8,128)(2,1)S(1)}, u32[]{:S(2)}, u32[]{:S(2)}) %all-to-all-start.2) | async-done | bytes 1048608 | tf_op jit(solution)/shard_map/all_to_all | solution.py:160
  196.6 4.4 %reshape.93 = bf16[16,16,2,32,32]{4,3,2,1,0:T(8,128)(2,1)} reshape(bf16[16,16,2048]{2,1,0:T(8,128)(2,1)S(1)} %all-to-all-done.2) | data formatting | bytes 2097152 | tf_op jit(solution)/shard_map/reshape | solution.py:161
  201.0 3.6 fusion.2
  204.5 1.1 copy.67
  205.7 1.3 dynamic-slice_bitcast_fusion.3
  207.3 2.4 copy.37.rows_ref
  209.7 9.5 %all-gather.7.cloned.1.call-done = bf16[32,64,512]{2,1,0:T(8,128)(2,1)} async-done(((bf16[32,32,512]{2,1,0:T(8,128)(2,1)}), bf16[32,64,512]{2,1,0:T(8,128)(2,1)}) %all-gather.7.cloned.1.call-update) | async-done | bytes 2097168 | tf_op jit(solution)/shard_map/all_gather | solution.py:168
  219.2 1.3 dynamic-slice_bitcast_fusion.2
  220.8 2.4 copy.36.rows_ref
  223.2 13.0 %shard_map.47.refs_0_ = bf16[2,64,256,512]{3,2,1,0:T(8,128)(2,1)} custom-call(bf16[16,512,128]{2,1,0:T(8,128)(2,1)} %copy.36.rows_ref, bf16[16,128,512]{2,1,0:T(8,128)(2,1)} %bitcast.86), custom_call_target="tpu_custom_call" | custom-call | tf_op jit(solution)/shard_map/pallas_call | solution.py:108
  236.2 13.1 %shard_map.48.refs_0_ = bf16[2,64,256,512]{3,2,1,0:T(8,128)(2,1)} custom-call(bf16[16,512,128]{2,1,0:T(8,128)(2,1)} %copy.37.rows_ref, bf16[16,128,512]{2,1,0:T(8,128)(2,1)} %bitcast.84, bf16[2,64,256,512]{3,2,1,0:T(8,128)(2,1)} %shard_map.47.refs_0_), custom_call_target="tpu_custom_call", output_to_operand_aliasing={{}: (2, {})} | custom-call | tf_op jit(solution)/shard_map/pallas_call | solution.py:108
  249.4 0.5 all-gather.11.cloned.1.call-update
  249.9 32.7 %all-gather.9.cloned.1.call-done = bf16[32,64,512]{2,1,0:T(8,128)(2,1)} async-done(((bf16[32,32,512]{2,1,0:T(8,128)(2,1)}), bf16[32,64,512]{2,1,0:T(8,128)(2,1)}) %all-gather.9.cloned.1.call-update) | async-done | bytes 2097168 | tf_op jit(solution)/shard_map/all_gather | solution.py:168
  282.6 34.6 %all-gather.11.cloned.1.call-done = bf16[32,64,512]{2,1,0:T(8,128)(2,1)} async-done(((bf16[32,32,512]{2,1,0:T(8,128)(2,1)}), bf16[32,64,512]{2,1,0:T(8,128)(2,1)}) %all-gather.11.cloned.1.call-update) | async-done | bytes 2097168 | tf_op jit(solution)/shard_map/all_gather | solution.py:168
  317.1 1.7 dynamic-slice_bitcast_fusion
  319.1 2.4 copy.38.rows_ref
  321.9 2.4 copy.39.rows_ref
  324.3 13.1 %shard_map.49.refs_0_ = bf16[2,64,256,512]{3,2,1,0:T(8,128)(2,1)} custom-call(bf16[16,512,128]{2,1,0:T(8,128)(2,1)} %copy.38.rows_ref, bf16[16,128,512]{2,1,0:T(8,128)(2,1)} %bitcast.90, bf16[2,64,256,512]{3,2,1,0:T(8,128)(2,1)} %shard_map.48.refs_0_), custom_call_target="tpu_custom_call", output_to_operand_aliasing={{}: (2, {})} | custom-call | tf_op jit(solution)/shard_map/pallas_call | solution.py:108
  337.3 13.1 %shard_map.50 = bf16[2,64,256,512]{3,2,1,0:T(8,128)(2,1)} custom-call(bf16[16,512,128]{2,1,0:T(8,128)(2,1)} %copy.39.rows_ref, bf16[16,128,512]{2,1,0:T(8,128)(2,1)} %bitcast.88, bf16[2,64,256,512]{3,2,1,0:T(8,128)(2,1)} %shard_map.49.refs_0_), custom_call_target="tpu_custom_call", output_to_operand_aliasing={{}: (2, {})} | custom-call | tf_op jit(solution)/shard_map/pallas_call | solution.py:108
  (27 shorter events, 1.2 us)
Async XLA Ops:
  14.7 3.4 copy-start
  18.9 24.0 %collective-permute-start = (bf16[2,32,7,1024]{3,1,2,0:T(8,128)(2,1)S(1)}, bf16[2,32,7,1024]{3,1,2,0:T(8,128)(2,1)S(1)}, u32[]{:S(2)}, u32[]{:S(2)}) collective-permute-start(bf16[2,32,7,1024]{3,1,2,0:T(8,128)(2,1)S(1)} %copy.30), channel_id=1, source_target_pairs={{0,1},{2,3},{4,5},{6,7},{8,9},{10,11},{12,13},{14,15},{16,17},{18,... | collective-permute-start | bytes 2752520 | tf_op jit(solution)/shard_map/ppermute | solution.py:17
  44.5 24.9 %copy-start.5 = (bf16[256,2048]{1,0:T(8,128)(2,1)S(1)}, bf16[256,2048]{1,0:T(8,128)(2,1)}, u32[]{:S(2)}) copy-start(bf16[256,2048]{1,0:T(8,128)(2,1)} %constant.22) | copy-start | bytes 3145732
  69.3 13.1 %copy-start.4 = (bf16[256,2048]{1,0:T(8,128)(2,1)S(1)}, bf16[256,2048]{1,0:T(8,128)(2,1)}, u32[]{:S(2)}) copy-start(bf16[256,2048]{1,0:T(8,128)(2,1)} %constant.18) | copy-start | bytes 3145732
  76.2 31.0 %all-to-all-start.3 = ((bf16[16,16,2048]{2,1,0:T(8,128)(2,1)}), bf16[16,16,2048]{2,1,0:T(8,128)(2,1)S(1)}, u32[]{:S(2)}, u32[]{:S(2)}) async-start(bf16[16,16,2048]{2,1,0:T(8,128)(2,1)} %bitcast.21), calls=%async_computation.3 | async-start | bytes 2097152 | tf_op jit(solution)/shard_map/all_to_all | solution.py:160
  82.4 29.8 %copy-start.3 = (bf16[256,2048]{1,0:T(8,128)(2,1)S(1)}, bf16[256,2048]{1,0:T(8,128)(2,1)}, u32[]{:S(2)}) copy-start(bf16[256,2048]{1,0:T(8,128)(2,1)} %constant.16) | copy-start | bytes 3145732
  107.2 29.8 %all-to-all-start.1 = ((bf16[16,16,2048]{2,1,0:T(8,128)(2,1)}), bf16[16,16,2048]{2,1,0:T(8,128)(2,1)S(1)}, u32[]{:S(2)}, u32[]{:S(2)}) async-start(bf16[16,16,2048]{2,1,0:T(8,128)(2,1)} %bitcast.8), calls=%async_computation.1 | async-start | bytes 2097152 | tf_op jit(solution)/shard_map/all_to_all | solution.py:160
  119.0 27.5 %copy-start.1 = (s32[512]{0:T(512)S(1)}, s32[512]{0:T(512)}, u32[]{:S(2)}) copy-start(s32[512]{0:T(512)} %param.6) | copy-start | bytes 6148
  137.0 29.8 %all-to-all-start = ((bf16[16,16,2048]{2,1,0:T(8,128)(2,1)}), bf16[16,16,2048]{2,1,0:T(8,128)(2,1)S(1)}, u32[]{:S(2)}, u32[]{:S(2)}) async-start(bf16[16,16,2048]{2,1,0:T(8,128)(2,1)} %bitcast.96), calls=%async_computation | async-start | bytes 2097152 | tf_op jit(solution)/shard_map/all_to_all | solution.py:160
  142.1 63.6 %all-gather.5.cloned.1.call-start = ((), (), s32[]{:S(2)}) async-start(), calls=%async_computation.4 | async-start | bytes 3145728 | tf_op jit(solution)/shard_map/all_gather | solution.py:168
  146.5 4.7 %copy-start.2 = (bf16[256,2048]{1,0:T(8,128)(2,1)S(1)}, bf16[256,2048]{1,0:T(8,128)(2,1)}, u32[]{:S(2)}) copy-start(bf16[256,2048]{1,0:T(8,128)(2,1)} %constant.20) | copy-start | bytes 3145732
  166.8 29.8 %all-to-all-start.2 = ((bf16[16,16,2048]{2,1,0:T(8,128)(2,1)}), bf16[16,16,2048]{2,1,0:T(8,128)(2,1)S(1)}, u32[]{:S(2)}, u32[]{:S(2)}) async-start(bf16[16,16,2048]{2,1,0:T(8,128)(2,1)} %bitcast.95), calls=%async_computation.2 | async-start | bytes 2097152 | tf_op jit(solution)/shard_map/all_to_all | solution.py:160
  171.9 47.3 %all-gather.7.cloned.1.call-start = ((), (), s32[]{:S(2)}) async-start(), calls=%async_computation.5 | async-start | bytes 3145728 | tf_op jit(solution)/shard_map/all_gather | solution.py:168
  181.0 101.6 %all-gather.9.cloned.1.call-start = ((), (), s32[]{:S(2)}) async-start(), calls=%async_computation.6 | async-start | bytes 3145728 | tf_op jit(solution)/shard_map/all_gather | solution.py:168
  249.3 67.8 %all-gather.11.cloned.1.call-start = ((), (), s32[]{:S(2)}) async-start(), calls=%async_computation.7 | async-start | bytes 3145728 | tf_op jit(solution)/shard_map/all_gather | solution.py:168
Sparse Core Ops, SparseCore 0:
  151.4 33.0 all-gather.4
  186.0 33.1 all-gather.6
  249.4 33.1 all-gather.8
  284.0 33.1 all-gather.10
where the time goes:
time: 362 us; the launch traced here: 357 us
  waiting for transfers between devices  151 us (42%)
  Pallas kernels  77.2 us (21%)
  local copies, waits for them, and re-layouts  49.5 us (14%)
  matrix products  41.5 us (11%)
  starting transfers between devices  23.2 us (6%)
  between operations  13.3 us (4%)
    all_gather x4, waiting for transfers between devices, per_device(): pending.append(lax.all_gather(ordered, 'blk', axis=1, tiled=True))  76.7 us
    pallas_call x4, Pallas kernels, correlate_chunk(): pl.pallas_call(correlate_kernel, grid=(width,), in_specs=in_specs, out_sp...  52.3 us
    all_to_all x4, waiting for transfers between devices, per_device(): lax.all_to_all(spectra, 'stn', split_axis=0, concat_axis=0, tiled=True)  51.1 us
    dot_general x4, matrix products, per_device(): jnp.einsum('kj,nj->kn', weights[chunk], filtered, preferred_element_type=...  27.2 us
    pallas_call x1, Pallas kernels, filter_frames(): pl.pallas_call(fir_kernel, grid=(stations_local,), in_specs=[pl.BlockSpec...  24.9 us
    ppermute x1, waiting for transfers between devices, passed_along(): lax.ppermute(value, axis, [(source, source + steps) for source in range(i...  22.7 us
    all_to_all x4, starting transfers between devices, per_device(): lax.all_to_all(spectra, 'stn', split_axis=0, concat_axis=0, tiled=True)  21.5 us
    reshape x4, local copies, waits for them, and re-layouts, per_device(): turned = turned.reshape(groups, width, 2, stations_local, spectra_local)  17.5 us
  transfers between devices with their start and end apart: 9, of which 8 were waited for; matrix products, arithmetic and copies ran while one was open for 17% of the time, Pallas kernels for 0%

commit v1 on v0

--- a/solution.py
+++ b/solution.py
@@ -15,6 +15,15 @@
     count = lax.axis_size(axis)
     initial, last = (max(0, -steps), min(count, count - steps))
     return lax.ppermute(value, axis, [(source, source + steps) for source in range(initial, last)])
+
+
+def gathered_along(value, axis, dimension):
+    count = lax.axis_size(axis)
+    parts = [value]
+    for shift in range(1, count):
+        pairs = [(source, (source + shift) % count) for source in range(count)]
+        parts.append(lax.ppermute(value, axis, pairs))
+    return jnp.concatenate(parts, axis=dimension)
 
 
 def chunk_count(local_channels):
@@ -163,9 +172,7 @@
             "gkias,gar->kisr", turned, selector, preferred_element_type=jnp.float32
         ).astype(jnp.bfloat16)
         ordered = ordered.reshape(width * 2, spectra_local, stations)
-        if chunk >= 2:
-            ordered, result = lax.optimization_barrier((ordered, result))
-        pending.append(lax.all_gather(ordered, "blk", axis=1, tiled=True))
+        pending.append(gathered_along(ordered, "blk", 1))
         if chunk >= 1:
             result = correlate(chunk - 1, pending[chunk - 1], result)
     result = correlate(chunks - 1, pending[chunks - 1], result)

time: 362 us -> 350 us (0.967)
  waiting for transfers between devices: 151 us -> 122 us
  other arithmetic: 1.31 us -> 27.9 us
  between operations: 13.3 us -> 0.15 us
  starting transfers between devices: 23.2 us -> 27 us
    all_gather x4 -> x0, waiting for transfers between devices: 76.7 us -> none  [per_device(): pending.append(lax.all_gather(ordered, 'blk', axis=1, tiled=True))]
    ppermute x0 -> x4, waiting for transfers between devices: none -> 46.1 us  [gathered_along(): parts.append(lax.ppermute(value, axis, pairs))]
    concatenate x0 -> x4, other arithmetic: none -> 11.4 us  [gathered_along(): return jnp.concatenate(parts, axis=dimension)]
    concatenate x4, other arithmetic: 0.74 us -> 8.5 us  [correlate(): jnp.concatenate([direct, swapped], axis=1).reshape(width, 2 * row_count, -1)]
    reshape x4, local copies, waits for them, and re-layouts: 9.65 us -> 15.7 us  [correlate(): jnp.concatenate([direct, swapped], axis=1).reshape(width, 2 * row_count, -1)]
    transpose x0 -> x2, other arithmetic: none -> 5.05 us  [correlate(): direct = jnp.transpose(row_block, (0, 3, 1, 2))]
    transpose x3 -> x0, local copies, waits for them, and re-layouts: 4.37 us -> none  [correlate(): direct = jnp.transpose(row_block, (0, 3, 1, 2))]
    ppermute x0 -> x4, starting transfers between devices: none -> 4.22 us  [gathered_along(): parts.append(lax.ppermute(value, axis, pairs))]
  transfers between devices with their start and end apart: 9 -> 9, of which waited for: 8 -> 7; matrix products, arithmetic and copies ran while one was open for 17% -> 21% of each run, Pallas kernels for 0% -> 0%
where the time goes in v1:
time: 350 us; the launch traced here: 346 us
  waiting for transfers between devices  122 us (35%)
  Pallas kernels  77.2 us (22%)
  local copies, waits for them, and re-layouts  49.7 us (14%)
  matrix products  41.7 us (12%)
  other arithmetic  27.9 us (8%)
  starting transfers between devices  27 us (8%)
    all_to_all x4, waiting for transfers between devices, per_device(): lax.all_to_all(spectra, 'stn', split_axis=0, concat_axis=0, tiled=True)  53.6 us
    pallas_call x4, Pallas kernels, correlate_chunk(): pl.pallas_call(correlate_kernel, grid=(width,), in_specs=in_specs, out_sp...  52.3 us
    ppermute x4, waiting for transfers between devices, gathered_along(): parts.append(lax.ppermute(value, axis, pairs))  46.1 us
    dot_general x4, matrix products, per_device(): jnp.einsum('kj,nj->kn', weights[chunk], filtered, preferred_element_type=...  27.5 us
    pallas_call x1, Pallas kernels, filter_frames(): pl.pallas_call(fir_kernel, grid=(stations_local,), in_specs=[pl.BlockSpec...  24.9 us
    ppermute x1, waiting for transfers between devices, passed_along(): lax.ppermute(value, axis, [(source, source + steps) for source in range(i...  22.7 us
    all_to_all x4, starting transfers between devices, per_device(): lax.all_to_all(spectra, 'stn', split_axis=0, concat_axis=0, tiled=True)  21.5 us
    reshape x4, local copies, waits for them, and re-layouts, per_device(): turned = turned.reshape(groups, width, 2, stations_local, spectra_local)  19 us
  transfers between devices with their start and end apart: 9, of which 7 were waited for; matrix products, arithmetic and copies ran while one was open for 21% of the time, Pallas kernels for 0%

profile of v1, /device:TPU:14, one launch (start us, length us, event | category | flops | bytes accessed | tf_op | source)
XLA Modules:
  0.0 346.0 jit_solution(6586512108544012865)
XLA Ops:
  0.0 8.1 %copy.57 = s32[8,8,32,1024]{3,2,1,0:T(8,128)S(1)} copy(s32[8,8,32,1024]{3,1,2,0:T(8,128)} %bitcast.87) | data formatting | bytes 16777216
  8.1 3.4 copy-done
  12.4 1.3 collective-permute-start
  13.7 22.7 %collective-permute-done = bf16[2,32,7,1024]{3,1,2,0:T(8,128)(2,1)S(1)} collective-permute-done((bf16[2,32,7,1024]{3,1,2,0:T(8,128)(2,1)S(1)}, bf16[2,32,7,1024]{3,1,2,0:T(8,128)(2,1)S(1)}, u32[]{:S(2)}, u32[]{:S(2)}) %collective-permute-start) | collective-permute-done | bytes 917536 | tf_op jit(solution)/shard_map/ppermute | solution.py:17
  36.4 1.6 copy.35.halo_ref
  37.9 24.9 %shard_map.46 = bf16[2,32,32,2048]{3,2,1,0:T(8,128)(2,1)} custom-call(f32[8,1024]{1,0:T(8,128)} %taps_ref.1, bf16[2,32,7,1024]{3,2,1,0:T(8,128)(2,1)} %copy.35.halo_ref, s32[2,32,32,1024]{3,2,1,0:T(8,128)} %bitcast.73), custom_call_target="tpu_custom_call" | custom-call | tf_op jit(solution)/shard_map/pallas_call | solution.py:74
  62.9 6.9 %convolution_convert_fusion.1 = bf16[2048,256]{0,1:T(8,128)(2,1)} fusion(bf16[2048,2048]{1,0:T(8,128)(2,1)} %bitcast.88, bf16[256,2048]{1,0:T(8,128)(2,1)S(1)} %copy-done.4), kind=kOutput, calls=%fused_computation.9 | convolution fusion | flops 2148007936 | bytes 10485760 | tf_op jit(solution)/shard_map/kj,nj->kn/dot_general | solution.py:165
  69.7 6.2 %all-to-all-start.2 = ((bf16[16,16,2048]{2,1,0:T(8,128)(2,1)}), bf16[16,16,2048]{2,1,0:T(8,128)(2,1)S(1)}, u32[]{:S(2)}, u32[]{:S(2)}) async-start(bf16[16,16,2048]{2,1,0:T(8,128)(2,1)} %bitcast.21), calls=%async_computation.2 | async-start | bytes 2097152 | tf_op jit(solution)/shard_map/all_to_all | solution.py:169
  76.0 6.8 %convolution_convert_fusion.2 = bf16[2048,256]{0,1:T(8,128)(2,1)} fusion(bf16[2048,2048]{1,0:T(8,128)(2,1)} %bitcast.89, bf16[256,2048]{1,0:T(8,128)(2,1)S(1)} %copy-done.3), kind=kOutput, calls=%fused_computation.10 | convolution fusion | flops 2148007936 | bytes 10485760 | tf_op jit(solution)/shard_map/kj,nj->kn/dot_general | solution.py:165
  82.8 17.9 %all-to-all-done.2 = bf16[16,16,2048]{2,1,0:T(8,128)(2,1)S(1)} async-done(((bf16[16,16,2048]{2,1,0:T(8,128)(2,1)}), bf16[16,16,2048]{2,1,0:T(8,128)(2,1)S(1)}, u32[]{:S(2)}, u32[]{:S(2)}) %all-to-all-start.2) | async-done | bytes 1048608 | tf_op jit(solution)/shard_map/all_to_all | solution.py:169
  100.7 5.1 %all-to-all-start.1 = ((bf16[16,16,2048]{2,1,0:T(8,128)(2,1)}), bf16[16,16,2048]{2,1,0:T(8,128)(2,1)S(1)}, u32[]{:S(2)}, u32[]{:S(2)}) async-start(bf16[16,16,2048]{2,1,0:T(8,128)(2,1)} %bitcast.12), calls=%async_computation.1 | async-start | bytes 2097152 | tf_op jit(solution)/shard_map/all_to_all | solution.py:169
  105.8 6.7 %convolution_convert_fusion.3 = bf16[2048,256]{0,1:T(8,128)(2,1)} fusion(bf16[2048,2048]{1,0:T(8,128)(2,1)} %bitcast.90, bf16[256,2048]{1,0:T(8,128)(2,1)S(1)} %copy-done.2), kind=kOutput, calls=%fused_computation.11 | convolution fusion | flops 2148007936 | bytes 10485760 | tf_op jit(solution)/shard_map/kj,nj->kn/dot_general | solution.py:165
  112.6 18.0 %all-to-all-done.1 = bf16[16,16,2048]{2,1,0:T(8,128)(2,1)S(1)} async-done(((bf16[16,16,2048]{2,1,0:T(8,128)(2,1)}), bf16[16,16,2048]{2,1,0:T(8,128)(2,1)S(1)}, u32[]{:S(2)}, u32[]{:S(2)}) %all-to-all-start.1) | async-done | bytes 1048608 | tf_op jit(solution)/shard_map/all_to_all | solution.py:169
  130.5 5.1 %all-to-all-start = ((bf16[16,16,2048]{2,1,0:T(8,128)(2,1)}), bf16[16,16,2048]{2,1,0:T(8,128)(2,1)S(1)}, u32[]{:S(2)}, u32[]{:S(2)}) async-start(bf16[16,16,2048]{2,1,0:T(8,128)(2,1)} %bitcast.97), calls=%async_computation | async-start | bytes 2097152 | tf_op jit(solution)/shard_map/all_to_all | solution.py:169
  135.6 7.0 %convolution_convert_fusion = bf16[2048,256]{0,1:T(8,128)(2,1)} fusion(bf16[2048,2048]{1,0:T(8,128)(2,1)} %bitcast.91, bf16[256,2048]{1,0:T(8,128)(2,1)} %constant.22), kind=kOutput, calls=%fused_computation.8 | convolution fusion | flops 2148007936 | bytes 10485760 | tf_op jit(solution)/shard_map/kj,nj->kn/dot_general | solution.py:165
  142.7 17.7 %all-to-all-done = bf16[16,16,2048]{2,1,0:T(8,128)(2,1)S(1)} async-done(((bf16[16,16,2048]{2,1,0:T(8,128)(2,1)}), bf16[16,16,2048]{2,1,0:T(8,128)(2,1)S(1)}, u32[]{:S(2)}, u32[]{:S(2)}) %all-to-all-start) | async-done | bytes 1048608 | tf_op jit(solution)/shard_map/all_to_all | solution.py:169
  160.3 5.1 %all-to-all-start.3 = ((bf16[16,16,2048]{2,1,0:T(8,128)(2,1)}), bf16[16,16,2048]{2,1,0:T(8,128)(2,1)}, u32[]{:S(2)}, u32[]{:S(2)}) async-start(bf16[16,16,2048]{2,1,0:T(8,128)(2,1)} %bitcast.96), calls=%async_computation.3 | async-start | bytes 2097152 | tf_op jit(solution)/shard_map/all_to_all | solution.py:169
  165.4 4.4 %reshape.89 = bf16[16,16,2,32,32]{4,3,2,1,0:T(8,128)(2,1)} reshape(bf16[16,16,2048]{2,1,0:T(8,128)(2,1)S(1)} %all-to-all-done) | data formatting | bytes 2097152 | tf_op jit(solution)/shard_map/reshape | solution.py:170
  169.8 3.6 %fusion.6 = bf16[16,2,32,512,1]{3,2,0,1,4:T(8,128)(2,1)S(1)} fusion(bf16[16,16,2,32,32]{4,3,2,1,0:T(8,128)(2,1)} %reshape.89, s32[16,32]{1,0:T(8,128)S(1)} %multiply_add_fusion, s32[512]{0:T(512)S(1)} %copy-done.1), kind=kOutput, calls=%fused_computation.6 | convolution fusion | flops 537133056 | bytes 2101248 | tf_op jit(solution)/shard_map/gkias,gar->kisr/dot_general | solution.py:171
  173.5 4.4 %reshape.93 = bf16[16,16,2,32,32]{4,3,2,1,0:T(8,128)(2,1)} reshape(bf16[16,16,2048]{2,1,0:T(8,128)(2,1)S(1)} %all-to-all-done.1) | data formatting | bytes 2097152 | tf_op jit(solution)/shard_map/reshape | solution.py:170
  177.9 3.6 %fusion.4 = bf16[16,2,32,512,1]{3,2,0,1,4:T(8,128)(2,1)S(1)} fusion(bf16[16,16,2,32,32]{4,3,2,1,0:T(8,128)(2,1)} %reshape.93, s32[16,32]{1,0:T(8,128)S(1)} %multiply_add_fusion, s32[512]{0:T(512)S(1)} %copy-done.1), kind=kOutput, calls=%fused_computation.4 | convolution fusion | flops 537133056 | bytes 2101248 | tf_op jit(solution)/shard_map/gkias,gar->kisr/dot_general | solution.py:171
  181.6 2.1 collective-permute-start.2
  183.6 4.4 %reshape.97 = bf16[16,16,2,32,32]{4,3,2,1,0:T(8,128)(2,1)} reshape(bf16[16,16,2048]{2,1,0:T(8,128)(2,1)S(1)} %all-to-all-done.2) | data formatting | bytes 2097152 | tf_op jit(solution)/shard_map/reshape | solution.py:170
  188.0 3.6 %fusion.2 = bf16[16,2,32,512,1]{3,2,0,1,4:T(8,128)(2,1)S(1)} fusion(bf16[16,16,2,32,32]{4,3,2,1,0:T(8,128)(2,1)} %reshape.97, s32[16,32]{1,0:T(8,128)S(1)} %multiply_add_fusion, s32[512]{0:T(512)S(1)} %copy-done.1), kind=kOutput, calls=%fused_computation.2 | convolution fusion | flops 537133056 | bytes 2101248 | tf_op jit(solution)/shard_map/gkias,gar->kisr/dot_general | solution.py:171
  191.7 5.9 %reshape.101 = bf16[16,16,2,32,32]{4,3,2,1,0:T(8,128)(2,1)} reshape(bf16[16,16,2048]{2,1,0:T(8,128)(2,1)} %all-to-all-done.3) | data formatting | bytes 2097152 | tf_op jit(solution)/shard_map/reshape | solution.py:170
  197.7 3.6 %fusion = bf16[16,2,32,512,1]{3,2,0,1,4:T(8,128)(2,1)S(1)} fusion(bf16[16,16,2,32,32]{4,3,2,1,0:T(8,128)(2,1)} %reshape.101, s32[16,32]{1,0:T(8,128)S(1)} %multiply_add_fusion, s32[512]{0:T(512)S(1)} %copy-done.1), kind=kOutput, calls=%fused_computation | convolution fusion | flops 537133056 | bytes 2101248 | tf_op jit(solution)/shard_map/gkias,gar->kisr/dot_general | solution.py:171
  202.3 2.0 collective-permute-start.4
  204.3 17.8 %collective-permute-done.2 = bf16[32,32,512]{2,1,0:T(8,128)(2,1)} collective-permute-done((bf16[32,32,512]{2,1,0:T(8,128)(2,1)S(1)}, bf16[32,32,512]{2,1,0:T(8,128)(2,1)}, u32[]{:S(2)}, u32[]{:S(2)}) %collective-permute-start.2) | collective-permute-done | bytes 1048608 | tf_op jit(solution)/shard_map/ppermute | solution.py:25
  222.1 2.4 fusion.13
  224.6 1.5 maximum_maximum_fusion.1
  226.1 3.9 %copy.42.rows_ref = bf16[16,512,128]{2,1,0:T(8,128)(2,1)} copy(bf16[16,512,128]{1,2,0:T(8,128)(2,1)} %bitcast.92) | data formatting | bytes 4194304 | tf_op jit(solution)/shard_map/reshape | solution.py:158
  231.3 2.7 maximum_maximum_fusion
  234.1 3.9 %copy.43.rows_ref = bf16[16,512,128]{2,1,0:T(8,128)(2,1)} copy(bf16[16,512,128]{1,2,0:T(8,128)(2,1)} %bitcast.93) | data formatting | bytes 4194304 | tf_op jit(solution)/shard_map/reshape | solution.py:158
  238.0 6.6 %collective-permute-done.3 = bf16[32,32,512]{2,1,0:T(8,128)(2,1)} collective-permute-done((bf16[32,32,512]{2,1,0:T(8,128)(2,1)S(1)}, bf16[32,32,512]{2,1,0:T(8,128)(2,1)}, u32[]{:S(2)}, u32[]{:S(2)}) %collective-permute-start.3) | collective-permute-done | bytes 1048608 | tf_op jit(solution)/shard_map/ppermute | solution.py:25
  244.6 21.7 %collective-permute-done.4 = bf16[32,32,512]{2,1,0:T(8,128)(2,1)} collective-permute-done((bf16[32,32,512]{2,1,0:T(8,128)(2,1)}, bf16[32,32,512]{2,1,0:T(8,128)(2,1)}, u32[]{:S(2)}, u32[]{:S(2)}) %collective-permute-start.4) | collective-permute-done | bytes 1048608 | tf_op jit(solution)/shard_map/ppermute | solution.py:25
  266.3 2.6 fusion.9
  268.9 1.5 maximum_maximum_fusion.3
  270.5 4.0 %copy.40.rows_ref = bf16[16,512,128]{2,1,0:T(8,128)(2,1)} copy(bf16[16,512,128]{1,2,0:T(8,128)(2,1)} %bitcast.94) | data formatting | bytes 4194304 | tf_op jit(solution)/shard_map/reshape | solution.py:158
  275.7 2.7 maximum_maximum_fusion.2
  278.4 3.9 %copy.41.rows_ref = bf16[16,512,128]{2,1,0:T(8,128)(2,1)} copy(bf16[16,512,128]{1,2,0:T(8,128)(2,1)} %bitcast.95) | data formatting | bytes 4194304 | tf_op jit(solution)/shard_map/reshape | solution.py:158
  282.4 3.2 pad_maximum_fusion.3
  285.5 13.0 %shard_map.47.refs_0_ = bf16[2,64,256,512]{3,2,1,0:T(8,128)(2,1)} custom-call(bf16[16,512,128]{2,1,0:T(8,128)(2,1)} %copy.40.rows_ref, bf16[16,128,512]{2,1,0:T(8,128)(2,1)} %bitcast.86), custom_call_target="tpu_custom_call" | custom-call | tf_op jit(solution)/shard_map/pallas_call | solution.py:117
  298.6 2.8 pad_maximum_fusion.2
  301.3 13.1 %shard_map.48.refs_0_ = bf16[2,64,256,512]{3,2,1,0:T(8,128)(2,1)} custom-call(bf16[16,512,128]{2,1,0:T(8,128)(2,1)} %copy.41.rows_ref, bf16[16,128,512]{2,1,0:T(8,128)(2,1)} %bitcast.83, bf16[2,64,256,512]{3,2,1,0:T(8,128)(2,1)} %shard_map.47.refs_0_), custom_call_target="tpu_custom_call", output_to_operand_aliasing={{}: (2, {})} | custom-call | tf_op jit(solution)/shard_map/pallas_call | solution.py:117
  314.4 2.8 pad_maximum_fusion.1
  317.2 13.1 %shard_map.49.refs_0_ = bf16[2,64,256,512]{3,2,1,0:T(8,128)(2,1)} custom-call(bf16[16,512,128]{2,1,0:T(8,128)(2,1)} %copy.42.rows_ref, bf16[16,128,512]{2,1,0:T(8,128)(2,1)} %bitcast.84, bf16[2,64,256,512]{3,2,1,0:T(8,128)(2,1)} %shard_map.48.refs_0_), custom_call_target="tpu_custom_call", output_to_operand_aliasing={{}: (2, {})} | custom-call | tf_op jit(solution)/shard_map/pallas_call | solution.py:117
  330.2 2.7 pad_maximum_fusion
  332.9 13.1 %shard_map.50 = bf16[2,64,256,512]{3,2,1,0:T(8,128)(2,1)} custom-call(bf16[16,512,128]{2,1,0:T(8,128)(2,1)} %copy.43.rows_ref, bf16[16,128,512]{2,1,0:T(8,128)(2,1)} %bitcast.85, bf16[2,64,256,512]{3,2,1,0:T(8,128)(2,1)} %shard_map.49.refs_0_), custom_call_target="tpu_custom_call", output_to_operand_aliasing={{}: (2, {})} | custom-call | tf_op jit(solution)/shard_map/pallas_call | solution.py:117
  (24 shorter events, 5.0 us)
Async XLA Ops:
  8.1 3.4 copy-start
  12.4 24.0 %collective-permute-start = (bf16[2,32,7,1024]{3,1,2,0:T(8,128)(2,1)S(1)}, bf16[2,32,7,1024]{3,1,2,0:T(8,128)(2,1)S(1)}, u32[]{:S(2)}, u32[]{:S(2)}) collective-permute-start(bf16[2,32,7,1024]{3,1,2,0:T(8,128)(2,1)S(1)} %copy.34), channel_id=1, source_target_pairs={{0,1},{2,3},{4,5},{6,7},{8,9},{10,11},{12,13},{14,15},{16,17},{18,... | collective-permute-start | bytes 2752520 | tf_op jit(solution)/shard_map/ppermute | solution.py:17
  37.9 24.9 %copy-start.4 = (bf16[256,2048]{1,0:T(8,128)(2,1)S(1)}, bf16[256,2048]{1,0:T(8,128)(2,1)}, u32[]{:S(2)}) copy-start(bf16[256,2048]{1,0:T(8,128)(2,1)} %constant.20) | copy-start | bytes 3145732
  62.9 13.1 %copy-start.3 = (bf16[256,2048]{1,0:T(8,128)(2,1)S(1)}, bf16[256,2048]{1,0:T(8,128)(2,1)}, u32[]{:S(2)}) copy-start(bf16[256,2048]{1,0:T(8,128)(2,1)} %constant.18) | copy-start | bytes 3145732
  69.7 31.0 %all-to-all-start.2 = ((bf16[16,16,2048]{2,1,0:T(8,128)(2,1)}), bf16[16,16,2048]{2,1,0:T(8,128)(2,1)S(1)}, u32[]{:S(2)}, u32[]{:S(2)}) async-start(bf16[16,16,2048]{2,1,0:T(8,128)(2,1)} %bitcast.21), calls=%async_computation.2 | async-start | bytes 2097152 | tf_op jit(solution)/shard_map/all_to_all | solution.py:169
  76.0 29.8 %copy-start.2 = (bf16[256,2048]{1,0:T(8,128)(2,1)S(1)}, bf16[256,2048]{1,0:T(8,128)(2,1)}, u32[]{:S(2)}) copy-start(bf16[256,2048]{1,0:T(8,128)(2,1)} %constant.16) | copy-start | bytes 3145732
  100.7 29.8 %all-to-all-start.1 = ((bf16[16,16,2048]{2,1,0:T(8,128)(2,1)}), bf16[16,16,2048]{2,1,0:T(8,128)(2,1)S(1)}, u32[]{:S(2)}, u32[]{:S(2)}) async-start(bf16[16,16,2048]{2,1,0:T(8,128)(2,1)} %bitcast.12), calls=%async_computation.1 | async-start | bytes 2097152 | tf_op jit(solution)/shard_map/all_to_all | solution.py:169
  130.5 29.8 %all-to-all-start = ((bf16[16,16,2048]{2,1,0:T(8,128)(2,1)}), bf16[16,16,2048]{2,1,0:T(8,128)(2,1)S(1)}, u32[]{:S(2)}, u32[]{:S(2)}) async-start(bf16[16,16,2048]{2,1,0:T(8,128)(2,1)} %bitcast.97), calls=%async_computation | async-start | bytes 2097152 | tf_op jit(solution)/shard_map/all_to_all | solution.py:169
  142.6 27.2 %copy-start.1 = (s32[512]{0:T(512)S(1)}, s32[512]{0:T(512)}, u32[]{:S(2)}) copy-start(s32[512]{0:T(512)} %param.6) | copy-start | bytes 6148
  160.3 31.4 %all-to-all-start.3 = ((bf16[16,16,2048]{2,1,0:T(8,128)(2,1)}), bf16[16,16,2048]{2,1,0:T(8,128)(2,1)}, u32[]{:S(2)}, u32[]{:S(2)}) async-start(bf16[16,16,2048]{2,1,0:T(8,128)(2,1)} %bitcast.96), calls=%async_computation.3 | async-start | bytes 2097152 | tf_op jit(solution)/shard_map/all_to_all | solution.py:169
  173.5 30.8 %collective-permute-start.1 = (bf16[32,32,512]{2,1,0:T(8,128)(2,1)S(1)}, bf16[32,32,512]{2,1,0:T(8,128)(2,1)}, u32[]{:S(2)}, u32[]{:S(2)}) collective-permute-start(bf16[32,32,512]{2,1,0:T(8,128)(2,1)S(1)} %bitcast.74), channel_id=1, source_target_pairs={{0,1},{1,0},{2,3},{3,2},{4,5},{5,4},{6,7},{7,6},{8,9},{9,8},{10,11... | collective-permute-start | bytes 3145736 | tf_op jit(solution)/shard_map/ppermute | solution.py:25
  181.6 40.5 %collective-permute-start.2 = (bf16[32,32,512]{2,1,0:T(8,128)(2,1)S(1)}, bf16[32,32,512]{2,1,0:T(8,128)(2,1)}, u32[]{:S(2)}, u32[]{:S(2)}) collective-permute-start(bf16[32,32,512]{2,1,0:T(8,128)(2,1)S(1)} %bitcast.77), channel_id=1, source_target_pairs={{0,1},{1,0},{2,3},{3,2},{4,5},{5,4},{6,7},{7,6},{8,9},{9,8},{10,11... | collective-permute-start | bytes 3145736 | tf_op jit(solution)/shard_map/ppermute | solution.py:25
  191.6 53.0 %collective-permute-start.3 = (bf16[32,32,512]{2,1,0:T(8,128)(2,1)S(1)}, bf16[32,32,512]{2,1,0:T(8,128)(2,1)}, u32[]{:S(2)}, u32[]{:S(2)}) collective-permute-start(bf16[32,32,512]{2,1,0:T(8,128)(2,1)S(1)} %bitcast.80), channel_id=1, source_target_pairs={{0,1},{1,0},{2,3},{3,2},{4,5},{5,4},{6,7},{7,6},{8,9},{9,8},{10,11... | collective-permute-start | bytes 3145736 | tf_op jit(solution)/shard_map/ppermute | solution.py:25
  202.3 64.0 %collective-permute-start.4 = (bf16[32,32,512]{2,1,0:T(8,128)(2,1)}, bf16[32,32,512]{2,1,0:T(8,128)(2,1)}, u32[]{:S(2)}, u32[]{:S(2)}) collective-permute-start(bf16[32,32,512]{2,1,0:T(8,128)(2,1)} %bitcast.31), channel_id=1, source_target_pairs={{0,1},{1,0},{2,3},{3,2},{4,5},{5,4},{6,7},{7,6},{8,9},{9,8},{10,11... | collective-permute-start | bytes 3145736 | tf_op jit(solution)/shard_map/ppermute | solution.py:25

commit v2 on v1

--- a/solution.py
+++ b/solution.py
@@ -81,6 +81,11 @@
         ],
         out_specs=pl.BlockSpec((2, 1, spectra, 2 * channels), lambda a: (0, a, 0, 0)),
         out_shape=jax.ShapeDtypeStruct((2, stations_local, spectra, 2 * channels), jnp.bfloat16),
+        cost_estimate=pl.CostEstimate(
+            flops=4 * tap_count * frames.size,
+            transcendentals=0,
+            bytes_accessed=4 * frames.size + 4 * frames.size,
+        ),
     )(fir_taps, earlier, frames)
 
 
@@ -121,6 +126,11 @@
         out_specs=pl.BlockSpec((2, 1, row_count, stations), lambda k: (0, offset + k, 0, 0)),
         out_shape=jax.ShapeDtypeStruct((2, local_channels, row_count, stations), jnp.bfloat16),
         input_output_aliases=aliases,
+        cost_estimate=pl.CostEstimate(
+            flops=2 * width * double_rows * depth * stations,
+            transcendentals=width * (row_count + stations),
+            bytes_accessed=2 * (left.size + right.size + width * double_rows * stations),
+        ),
     )(*operands)
 
 
@@ -172,7 +182,10 @@
             "gkias,gar->kisr", turned, selector, preferred_element_type=jnp.float32
         ).astype(jnp.bfloat16)
         ordered = ordered.reshape(width * 2, spectra_local, stations)
-        pending.append(gathered_along(ordered, "blk", 1))
+        if 2 * chunk < chunks:
+            pending.append(lax.all_gather(ordered, "blk", axis=1, tiled=True))
+        else:
+            pending.append(gathered_along(ordered, "blk", 1))
         if chunk >= 1:
             result = correlate(chunk - 1, pending[chunk - 1], result)
     result = correlate(chunks - 1, pending[chunks - 1], result)

time: 350 us -> 353 us (level)
  other arithmetic: 27.9 us -> 10.9 us
  between operations: 0.15 us -> 13.6 us
  waiting for transfers between devices: 122 us -> 133 us
    ppermute x4 -> x2, waiting for transfers between devices: 46.1 us -> 59.5 us  [gathered_along(): parts.append(lax.ppermute(value, axis, pairs))]
    concatenate x4 -> x2, other arithmetic: 11.4 us -> 5.51 us  [gathered_along(): return jnp.concatenate(parts, axis=dimension)]
    concatenate x4, other arithmetic: 8.5 us -> 3.39 us  [correlate(): jnp.concatenate([direct, swapped], axis=1).reshape(width, 2 * row_count, -1)]
    transpose x2 -> x1, other arithmetic: 5.05 us -> 1.41 us  [correlate(): direct = jnp.transpose(row_block, (0, 3, 1, 2))]
where the time goes in v2:
time: 353 us; the launch traced here: 350 us
  waiting for transfers between devices  133 us (38%)
  Pallas kernels  77.2 us (22%)
  local copies, waits for them, and re-layouts  47.9 us (14%)
  matrix products  41.7 us (12%)
  starting transfers between devices  25.2 us (7%)
  between operations  13.6 us (4%)
  other arithmetic  10.9 us (3%)
    ppermute x2, waiting for transfers between devices, gathered_along(): parts.append(lax.ppermute(value, axis, pairs))  59.5 us
    pallas_call x4, Pallas kernels, correlate_chunk(): pl.pallas_call(correlate_kernel, grid=(width,), in_specs=in_specs, out_sp...  52.3 us
    all_to_all x4, waiting for transfers between devices, per_device(): lax.all_to_all(spectra, 'stn', split_axis=0, concat_axis=0, tiled=True)  50.7 us
    dot_general x4, matrix products, per_device(): jnp.einsum('kj,nj->kn', weights[chunk], filtered, preferred_element_type=...  27.5 us
    pallas_call x1, Pallas kernels, filter_frames(): pl.pallas_call(fir_kernel, grid=(stations_local,), in_specs=[pl.BlockSpec...  24.9 us
    ppermute x1, waiting for transfers between devices, passed_along(): lax.ppermute(value, axis, [(source, source + steps) for source in range(i...  22.7 us
    all_to_all x4, starting transfers between devices, per_device(): lax.all_to_all(spectra, 'stn', split_axis=0, concat_axis=0, tiled=True)  21.5 us
    reshape x4, local copies, waits for them, and re-layouts, per_device(): turned = turned.reshape(groups, width, 2, stations_local, spectra_local)  17.5 us
  transfers between devices with their start and end apart: 9, of which 7 were waited for; matrix products, arithmetic and copies ran while one was open for 21% of the time, Pallas kernels for 0%

profile of v2, /device:TPU:14, one launch (start us, length us, event | category | flops | bytes accessed | tf_op | source)
XLA Modules:
  0.0 349.5 jit_solution(5994669412155100889)
XLA Ops:
  6.5 8.1 %copy.55 = s32[8,8,32,1024]{3,2,1,0:T(8,128)S(1)} copy(s32[8,8,32,1024]{3,1,2,0:T(8,128)} %bitcast.82) | data formatting | bytes 16777216
  14.7 3.4 copy-done
  18.1 0.3 slice_convert_fusion
  18.3 0.6 copy.32
  18.9 1.3 collective-permute-start
  20.2 22.7 %collective-permute-done = bf16[2,32,7,1024]{3,1,2,0:T(8,128)(2,1)S(1)} collective-permute-done((bf16[2,32,7,1024]{3,1,2,0:T(8,128)(2,1)S(1)}, bf16[2,32,7,1024]{3,1,2,0:T(8,128)(2,1)S(1)}, u32[]{:S(2)}, u32[]{:S(2)}) %collective-permute-start) | collective-permute-done | bytes 917536 | tf_op jit(solution)/shard_map/ppermute | solution.py:17
  42.9 1.6 copy.33.halo_ref
  44.5 24.9 %shard_map.46 = bf16[2,32,32,2048]{3,2,1,0:T(8,128)(2,1)} custom-call(f32[8,1024]{1,0:T(8,128)} %taps_ref.1, bf16[2,32,7,1024]{3,2,1,0:T(8,128)(2,1)} %copy.33.halo_ref, s32[2,32,32,1024]{3,2,1,0:T(8,128)} %bitcast.73), custom_call_target="tpu_custom_call" | custom-call | flops 67108864 | bytes 16777216 | tf_op jit(solution)/shard_map/pallas_call | solution.py:74
  69.4 6.9 %convolution_convert_fusion.1 = bf16[2048,256]{0,1:T(8,128)(2,1)} fusion(bf16[2048,2048]{1,0:T(8,128)(2,1)} %bitcast.83, bf16[256,2048]{1,0:T(8,128)(2,1)S(1)} %copy-done.4), kind=kOutput, calls=%fused_computation.9 | convolution fusion | flops 2148007936 | bytes 10485760 | tf_op jit(solution)/shard_map/kj,nj->kn/dot_general | solution.py:175
  76.3 6.2 %all-to-all-start.2 = ((bf16[16,16,2048]{2,1,0:T(8,128)(2,1)}), bf16[16,16,2048]{2,1,0:T(8,128)(2,1)S(1)}, u32[]{:S(2)}, u32[]{:S(2)}) async-start(bf16[16,16,2048]{2,1,0:T(8,128)(2,1)} %bitcast.21), calls=%async_computation.2 | async-start | bytes 2097152 | tf_op jit(solution)/shard_map/all_to_all | solution.py:179
  82.6 6.8 %convolution_convert_fusion.2 = bf16[2048,256]{0,1:T(8,128)(2,1)} fusion(bf16[2048,2048]{1,0:T(8,128)(2,1)} %bitcast.84, bf16[256,2048]{1,0:T(8,128)(2,1)S(1)} %copy-done.3), kind=kOutput, calls=%fused_computation.10 | convolution fusion | flops 2148007936 | bytes 10485760 | tf_op jit(solution)/shard_map/kj,nj->kn/dot_general | solution.py:175
  89.4 17.9 %all-to-all-done.2 = bf16[16,16,2048]{2,1,0:T(8,128)(2,1)S(1)} async-done(((bf16[16,16,2048]{2,1,0:T(8,128)(2,1)}), bf16[16,16,2048]{2,1,0:T(8,128)(2,1)S(1)}, u32[]{:S(2)}, u32[]{:S(2)}) %all-to-all-start.2) | async-done | bytes 1048608 | tf_op jit(solution)/shard_map/all_to_all | solution.py:179
  107.3 5.1 %all-to-all-start.1 = ((bf16[16,16,2048]{2,1,0:T(8,128)(2,1)}), bf16[16,16,2048]{2,1,0:T(8,128)(2,1)S(1)}, u32[]{:S(2)}, u32[]{:S(2)}) async-start(bf16[16,16,2048]{2,1,0:T(8,128)(2,1)} %bitcast.12), calls=%async_computation.1 | async-start | bytes 2097152 | tf_op jit(solution)/shard_map/all_to_all | solution.py:179
  112.4 6.8 %convolution_convert_fusion.3 = bf16[2048,256]{0,1:T(8,128)(2,1)} fusion(bf16[2048,2048]{1,0:T(8,128)(2,1)} %bitcast.85, bf16[256,2048]{1,0:T(8,128)(2,1)S(1)} %copy-done.2), kind=kOutput, calls=%fused_computation.11 | convolution fusion | flops 2148007936 | bytes 10485760 | tf_op jit(solution)/shard_map/kj,nj->kn/dot_general | solution.py:175
  119.2 17.9 %all-to-all-done.1 = bf16[16,16,2048]{2,1,0:T(8,128)(2,1)S(1)} async-done(((bf16[16,16,2048]{2,1,0:T(8,128)(2,1)}), bf16[16,16,2048]{2,1,0:T(8,128)(2,1)S(1)}, u32[]{:S(2)}, u32[]{:S(2)}) %all-to-all-start.1) | async-done | bytes 1048608 | tf_op jit(solution)/shard_map/all_to_all | solution.py:179
  137.1 5.1 %all-to-all-start = ((bf16[16,16,2048]{2,1,0:T(8,128)(2,1)}), bf16[16,16,2048]{2,1,0:T(8,128)(2,1)S(1)}, u32[]{:S(2)}, u32[]{:S(2)}) async-start(bf16[16,16,2048]{2,1,0:T(8,128)(2,1)} %bitcast.98), calls=%async_computation | async-start | bytes 2097152 | tf_op jit(solution)/shard_map/all_to_all | solution.py:179
  142.2 7.0 %convolution_convert_fusion = bf16[2048,256]{0,1:T(8,128)(2,1)} fusion(bf16[2048,2048]{1,0:T(8,128)(2,1)} %bitcast.86, bf16[256,2048]{1,0:T(8,128)(2,1)} %constant.22), kind=kOutput, calls=%fused_computation.8 | convolution fusion | flops 2148007936 | bytes 10485760 | tf_op jit(solution)/shard_map/kj,nj->kn/dot_general | solution.py:175
  149.2 4.4 %reshape.95 = bf16[16,16,2,32,32]{4,3,2,1,0:T(8,128)(2,1)} reshape(bf16[16,16,2048]{2,1,0:T(8,128)(2,1)S(1)} %all-to-all-done.2) | data formatting | bytes 2097152 | tf_op jit(solution)/shard_map/reshape | solution.py:180
  153.5 13.4 %all-to-all-done = bf16[16,16,2048]{2,1,0:T(8,128)(2,1)S(1)} async-done(((bf16[16,16,2048]{2,1,0:T(8,128)(2,1)}), bf16[16,16,2048]{2,1,0:T(8,128)(2,1)S(1)}, u32[]{:S(2)}, u32[]{:S(2)}) %all-to-all-start) | async-done | bytes 1048608 | tf_op jit(solution)/shard_map/all_to_all | solution.py:179
  166.9 5.1 %all-to-all-start.3 = ((bf16[16,16,2048]{2,1,0:T(8,128)(2,1)}), bf16[16,16,2048]{2,1,0:T(8,128)(2,1)S(1)}, u32[]{:S(2)}, u32[]{:S(2)}) async-start(bf16[16,16,2048]{2,1,0:T(8,128)(2,1)} %bitcast.97), calls=%async_computation.3 | async-start | bytes 2097152 | tf_op jit(solution)/shard_map/all_to_all | solution.py:179
  172.1 3.6 %fusion.2 = bf16[16,2,32,512,1]{3,2,0,1,4:T(8,128)(2,1)S(1)} fusion(bf16[16,16,2,32,32]{4,3,2,1,0:T(8,128)(2,1)} %reshape.95, s32[16,32]{1,0:T(8,128)S(1)} %multiply_add_fusion, s32[512]{0:T(512)S(1)} %copy-done.1), kind=kOutput, calls=%fused_computation.2 | convolution fusion | flops 537133056 | bytes 2101248 | tf_op jit(solution)/shard_map/gkias,gar->kisr/dot_general | solution.py:181
  175.6 1.1 copy.69
  176.8 0.3 all-gather.5.cloned.1.call-start
  177.0 4.4 %reshape.87 = bf16[16,16,2,32,32]{4,3,2,1,0:T(8,128)(2,1)} reshape(bf16[16,16,2048]{2,1,0:T(8,128)(2,1)S(1)} %all-to-all-done) | data formatting | bytes 2097152 | tf_op jit(solution)/shard_map/reshape | solution.py:180
  181.4 3.6 %fusion.6 = bf16[16,2,32,512,1]{3,2,0,1,4:T(8,128)(2,1)S(1)} fusion(bf16[16,16,2,32,32]{4,3,2,1,0:T(8,128)(2,1)} %reshape.87, s32[16,32]{1,0:T(8,128)S(1)} %multiply_add_fusion, s32[512]{0:T(512)S(1)} %copy-done.1), kind=kOutput, calls=%fused_computation.6 | convolution fusion | flops 537133056 | bytes 2101248 | tf_op jit(solution)/shard_map/gkias,gar->kisr/dot_general | solution.py:181
  185.1 4.4 %reshape.91 = bf16[16,16,2,32,32]{4,3,2,1,0:T(8,128)(2,1)} reshape(bf16[16,16,2048]{2,1,0:T(8,128)(2,1)S(1)} %all-to-all-done.1) | data formatting | bytes 2097152 | tf_op jit(solution)/shard_map/reshape | solution.py:180
  189.5 3.6 %fusion.4 = bf16[16,2,32,512,1]{3,2,0,1,4:T(8,128)(2,1)S(1)} fusion(bf16[16,16,2,32,32]{4,3,2,1,0:T(8,128)(2,1)} %reshape.91, s32[16,32]{1,0:T(8,128)S(1)} %multiply_add_fusion, s32[512]{0:T(512)S(1)} %copy-done.1), kind=kOutput, calls=%fused_computation.4 | convolution fusion | flops 537133056 | bytes 2101248 | tf_op jit(solution)/shard_map/gkias,gar->kisr/dot_general | solution.py:181
  193.2 2.1 collective-permute-start.2
  195.2 1.5 all-to-all-done.3
  196.7 4.4 %reshape.100 = bf16[16,16,2,32,32]{4,3,2,1,0:T(8,128)(2,1)} reshape(bf16[16,16,2048]{2,1,0:T(8,128)(2,1)S(1)} %all-to-all-done.3) | data formatting | bytes 2097152 | tf_op jit(solution)/shard_map/reshape | solution.py:180
  201.1 3.6 %fusion = bf16[16,2,32,512,1]{3,2,0,1,4:T(8,128)(2,1)S(1)} fusion(bf16[16,16,2,32,32]{4,3,2,1,0:T(8,128)(2,1)} %reshape.100, s32[16,32]{1,0:T(8,128)S(1)} %multiply_add_fusion, s32[512]{0:T(512)S(1)} %copy-done.1), kind=kOutput, calls=%fused_computation | convolution fusion | flops 537133056 | bytes 2101248 | tf_op jit(solution)/shard_map/gkias,gar->kisr/dot_general | solution.py:181
  204.7 1.1 copy.68
  205.8 26.8 %collective-permute-done.1 = bf16[32,32,512]{2,1,0:T(8,128)(2,1)} collective-permute-done((bf16[32,32,512]{2,1,0:T(8,128)(2,1)S(1)}, bf16[32,32,512]{2,1,0:T(8,128)(2,1)}, u32[]{:S(2)}, u32[]{:S(2)}) %collective-permute-start.1) | collective-permute-done | bytes 1048608 | tf_op jit(solution)/shard_map/ppermute | solution.py:25
  232.6 32.7 %collective-permute-done.2 = bf16[32,32,512]{2,1,0:T(8,128)(2,1)} collective-permute-done((bf16[32,32,512]{2,1,0:T(8,128)(2,1)S(1)}, bf16[32,32,512]{2,1,0:T(8,128)(2,1)}, u32[]{:S(2)}, u32[]{:S(2)}) %collective-permute-start.2) | collective-permute-done | bytes 1048608 | tf_op jit(solution)/shard_map/ppermute | solution.py:25
  265.3 1.4 fusion.9
  266.8 1.5 maximum_maximum_fusion.1
  268.3 4.0 %copy.40.rows_ref = bf16[16,512,128]{2,1,0:T(8,128)(2,1)} copy(bf16[16,512,128]{1,2,0:T(8,128)(2,1)} %bitcast.87) | data formatting | bytes 4194304 | tf_op jit(solution)/shard_map/reshape | solution.py:168
  272.4 1.5 maximum_maximum_fusion
  273.9 3.9 %copy.41.rows_ref = bf16[16,512,128]{2,1,0:T(8,128)(2,1)} copy(bf16[16,512,128]{1,2,0:T(8,128)(2,1)} %bitcast.88) | data formatting | bytes 4194304 | tf_op jit(solution)/shard_map/reshape | solution.py:168
  277.8 2.8 pad_maximum_fusion
  280.5 2.7 pad_maximum_fusion.1
  283.3 1.7 dynamic-slice_bitcast_fusion
  285.3 2.4 copy.38.rows_ref
  287.9 2.5 copy.39.rows_ref
  290.4 13.0 %shard_map.47.refs_0_ = bf16[2,64,256,512]{3,2,1,0:T(8,128)(2,1)} custom-call(bf16[16,512,128]{2,1,0:T(8,128)(2,1)} %copy.38.rows_ref, bf16[16,128,512]{2,1,0:T(8,128)(2,1)} %bitcast.94), custom_call_target="tpu_custom_call" | custom-call | flops 1073741824 | bytes 12582912 | tf_op jit(solution)/shard_map/pallas_call | solution.py:122
  303.4 13.1 %shard_map.48.refs_0_ = bf16[2,64,256,512]{3,2,1,0:T(8,128)(2,1)} custom-call(bf16[16,512,128]{2,1,0:T(8,128)(2,1)} %copy.39.rows_ref, bf16[16,128,512]{2,1,0:T(8,128)(2,1)} %bitcast.92, bf16[2,64,256,512]{3,2,1,0:T(8,128)(2,1)} %shard_map.47.refs_0_), custom_call_target="tpu_custom_call", output_to_operand_aliasing={{}: (2, {})} | custom-call | flops 1073741824 | bytes 12582912 | tf_op jit(solution)/shard_map/pallas_call | solution.py:122
  316.5 13.1 %shard_map.49.refs_0_ = bf16[2,64,256,512]{3,2,1,0:T(8,128)(2,1)} custom-call(bf16[16,512,128]{2,1,0:T(8,128)(2,1)} %copy.40.rows_ref, bf16[16,128,512]{2,1,0:T(8,128)(2,1)} %bitcast.81, bf16[2,64,256,512]{3,2,1,0:T(8,128)(2,1)} %shard_map.48.refs_0_), custom_call_target="tpu_custom_call", output_to_operand_aliasing={{}: (2, {})} | custom-call | flops 1073741824 | bytes 12582912 | tf_op jit(solution)/shard_map/pallas_call | solution.py:122
  329.6 13.1 %shard_map.50 = bf16[2,64,256,512]{3,2,1,0:T(8,128)(2,1)} custom-call(bf16[16,512,128]{2,1,0:T(8,128)(2,1)} %copy.41.rows_ref, bf16[16,128,512]{2,1,0:T(8,128)(2,1)} %bitcast.80, bf16[2,64,256,512]{3,2,1,0:T(8,128)(2,1)} %shard_map.49.refs_0_), custom_call_target="tpu_custom_call", output_to_operand_aliasing={{}: (2, {})} | custom-call | flops 1073741824 | bytes 12582912 | tf_op jit(solution)/shard_map/pallas_call | solution.py:122
  (24 shorter events, 1.0 us)
Async XLA Ops:
  14.7 3.4 copy-start
  18.9 24.0 %collective-permute-start = (bf16[2,32,7,1024]{3,1,2,0:T(8,128)(2,1)S(1)}, bf16[2,32,7,1024]{3,1,2,0:T(8,128)(2,1)S(1)}, u32[]{:S(2)}, u32[]{:S(2)}) collective-permute-start(bf16[2,32,7,1024]{3,1,2,0:T(8,128)(2,1)S(1)} %copy.32), channel_id=1, source_target_pairs={{0,1},{2,3},{4,5},{6,7},{8,9},{10,11},{12,13},{14,15},{16,17},{18,... | collective-permute-start | bytes 2752520 | tf_op jit(solution)/shard_map/ppermute | solution.py:17
  44.5 24.9 %copy-start.4 = (bf16[256,2048]{1,0:T(8,128)(2,1)S(1)}, bf16[256,2048]{1,0:T(8,128)(2,1)}, u32[]{:S(2)}) copy-start(bf16[256,2048]{1,0:T(8,128)(2,1)} %constant.20) | copy-start | bytes 3145732
  69.4 13.1 %copy-start.3 = (bf16[256,2048]{1,0:T(8,128)(2,1)S(1)}, bf16[256,2048]{1,0:T(8,128)(2,1)}, u32[]{:S(2)}) copy-start(bf16[256,2048]{1,0:T(8,128)(2,1)} %constant.18) | copy-start | bytes 3145732
  76.3 31.0 %all-to-all-start.2 = ((bf16[16,16,2048]{2,1,0:T(8,128)(2,1)}), bf16[16,16,2048]{2,1,0:T(8,128)(2,1)S(1)}, u32[]{:S(2)}, u32[]{:S(2)}) async-start(bf16[16,16,2048]{2,1,0:T(8,128)(2,1)} %bitcast.21), calls=%async_computation.2 | async-start | bytes 2097152 | tf_op jit(solution)/shard_map/all_to_all | solution.py:179
  82.6 29.8 %copy-start.2 = (bf16[256,2048]{1,0:T(8,128)(2,1)S(1)}, bf16[256,2048]{1,0:T(8,128)(2,1)}, u32[]{:S(2)}) copy-start(bf16[256,2048]{1,0:T(8,128)(2,1)} %constant.16) | copy-start | bytes 3145732
  107.3 29.8 %all-to-all-start.1 = ((bf16[16,16,2048]{2,1,0:T(8,128)(2,1)}), bf16[16,16,2048]{2,1,0:T(8,128)(2,1)S(1)}, u32[]{:S(2)}, u32[]{:S(2)}) async-start(bf16[16,16,2048]{2,1,0:T(8,128)(2,1)} %bitcast.12), calls=%async_computation.1 | async-start | bytes 2097152 | tf_op jit(solution)/shard_map/all_to_all | solution.py:179
  137.1 29.8 %all-to-all-start = ((bf16[16,16,2048]{2,1,0:T(8,128)(2,1)}), bf16[16,16,2048]{2,1,0:T(8,128)(2,1)S(1)}, u32[]{:S(2)}, u32[]{:S(2)}) async-start(bf16[16,16,2048]{2,1,0:T(8,128)(2,1)} %bitcast.98), calls=%async_computation | async-start | bytes 2097152 | tf_op jit(solution)/shard_map/all_to_all | solution.py:179
  149.2 22.9 %copy-start.1 = (s32[512]{0:T(512)S(1)}, s32[512]{0:T(512)}, u32[]{:S(2)}) copy-start(s32[512]{0:T(512)} %param.6) | copy-start | bytes 6148
  166.9 29.8 %all-to-all-start.3 = ((bf16[16,16,2048]{2,1,0:T(8,128)(2,1)}), bf16[16,16,2048]{2,1,0:T(8,128)(2,1)S(1)}, u32[]{:S(2)}, u32[]{:S(2)}) async-start(bf16[16,16,2048]{2,1,0:T(8,128)(2,1)} %bitcast.97), calls=%async_computation.3 | async-start | bytes 2097152 | tf_op jit(solution)/shard_map/all_to_all | solution.py:179
  172.0 111.3 %all-gather.3.cloned.1.call-start = ((), (), s32[]{:S(2)}) async-start(), calls=%async_computation.4 | async-start | bytes 3145728 | tf_op jit(solution)/shard_map/all_gather | solution.py:186
  176.8 106.5 %all-gather.5.cloned.1.call-start = ((), (), s32[]{:S(2)}) async-start(), calls=%async_computation.5 | async-start | bytes 3145728 | tf_op jit(solution)/shard_map/all_gather | solution.py:186
  185.1 47.6 %collective-permute-start.1 = (bf16[32,32,512]{2,1,0:T(8,128)(2,1)S(1)}, bf16[32,32,512]{2,1,0:T(8,128)(2,1)}, u32[]{:S(2)}, u32[]{:S(2)}) collective-permute-start(bf16[32,32,512]{2,1,0:T(8,128)(2,1)S(1)} %bitcast.74), channel_id=1, source_target_pairs={{0,1},{1,0},{2,3},{3,2},{4,5},{5,4},{6,7},{7,6},{8,9},{9,8},{10,11... | collective-permute-start | bytes 3145736 | tf_op jit(solution)/shard_map/ppermute | solution.py:25
  193.2 72.2 %collective-permute-start.2 = (bf16[32,32,512]{2,1,0:T(8,128)(2,1)S(1)}, bf16[32,32,512]{2,1,0:T(8,128)(2,1)}, u32[]{:S(2)}, u32[]{:S(2)}) collective-permute-start(bf16[32,32,512]{2,1,0:T(8,128)(2,1)S(1)} %bitcast.77), channel_id=1, source_target_pairs={{0,1},{1,0},{2,3},{3,2},{4,5},{5,4},{6,7},{7,6},{8,9},{9,8},{10,11... | collective-permute-start | bytes 3145736 | tf_op jit(solution)/shard_map/ppermute | solution.py:25
Sparse Core Ops, SparseCore 0:
  176.9 55.2 all-gather.2
  233.7 43.6 all-gather.4

commit v3 on v2

--- a/solution.py
+++ b/solution.py
@@ -172,8 +172,12 @@
     result = None
     pending = []
     for chunk in range(chunks):
+        source = filtered
+        if chunk >= 2:
+            result = correlate(chunk - 2, pending[chunk - 2], result)
+            source, result = lax.optimization_barrier((filtered, result))
         spectra = jnp.einsum(
-            "kj,nj->kn", weights[chunk], filtered, preferred_element_type=jnp.float32
+            "kj,nj->kn", weights[chunk], source, preferred_element_type=jnp.float32
         ).astype(jnp.bfloat16)
         spectra = spectra.reshape(groups, width, 2 * stations_local * spectra_local)
         turned = lax.all_to_all(spectra, "stn", split_axis=0, concat_axis=0, tiled=True)
@@ -182,13 +186,9 @@
             "gkias,gar->kisr", turned, selector, preferred_element_type=jnp.float32
         ).astype(jnp.bfloat16)
         ordered = ordered.reshape(width * 2, spectra_local, stations)
-        if 2 * chunk < chunks:
-            pending.append(lax.all_gather(ordered, "blk", axis=1, tiled=True))
-        else:
-            pending.append(gathered_along(ordered, "blk", 1))
-        if chunk >= 1:
-            result = correlate(chunk - 1, pending[chunk - 1], result)
-    result = correlate(chunks - 1, pending[chunks - 1], result)
+        pending.append(gathered_along(ordered, "blk", 1))
+    for chunk in range(max(0, chunks - 2), chunks):
+        result = correlate(chunk, pending[chunk], result)
     return result
 
 

time: 353 us -> 311 us (0.88)
  waiting for transfers between devices: 133 us -> 98.9 us
  between operations: 13.6 us -> 0.21 us
  other arithmetic: 10.9 us -> 16.8 us
    ppermute x2 -> x4, waiting for transfers between devices: 59.5 us -> 25.6 us  [gathered_along(): parts.append(lax.ppermute(value, axis, pairs))]
    concatenate x2 -> x4, other arithmetic: 5.51 us -> 7.22 us  [gathered_along(): return jnp.concatenate(parts, axis=dimension)]
    unnamed x11 -> x21, local copies, waits for them, and re-layouts: 11.5 us -> 11.5 us
  transfers between devices with their start and end apart: 9 -> 9, of which waited for: 7 -> 6; matrix products, arithmetic and copies ran while one was open for 21% -> 22% of each run, Pallas kernels for 0% -> 9%
where the time goes in v3:
time: 311 us; the launch traced here: 308 us
  waiting for transfers between devices  98.9 us (32%)
  Pallas kernels  77.5 us (25%)
  local copies, waits for them, and re-layouts  47.2 us (15%)
  matrix products  41.4 us (13%)
  starting transfers between devices  26 us (8%)
  other arithmetic  16.8 us (5%)
    pallas_call x4, Pallas kernels, correlate_chunk(): pl.pallas_call(correlate_kernel, grid=(width,), in_specs=in_specs, out_sp...  52.5 us
    all_to_all x4, waiting for transfers between devices, per_device(): lax.all_to_all(spectra, 'stn', split_axis=0, concat_axis=0, tiled=True)  50.6 us
    dot_general x4, matrix products, per_device(): jnp.einsum('kj,nj->kn', weights[chunk], source, preferred_element_type=jn...  27.2 us
    ppermute x4, waiting for transfers between devices, gathered_along(): parts.append(lax.ppermute(value, axis, pairs))  25.6 us
    pallas_call x1, Pallas kernels, filter_frames(): pl.pallas_call(fir_kernel, grid=(stations_local,), in_specs=[pl.BlockSpec...  24.9 us
    all_to_all x4, starting transfers between devices, per_device(): lax.all_to_all(spectra, 'stn', split_axis=0, concat_axis=0, tiled=True)  23.4 us
    ppermute x1, waiting for transfers between devices, passed_along(): lax.ppermute(value, axis, [(source, source + steps) for source in range(i...  22.7 us
    reshape x4, local copies, waits for them, and re-layouts, per_device(): turned = turned.reshape(groups, width, 2, stations_local, spectra_local)  17.5 us
  transfers between devices with their start and end apart: 9, of which 6 were waited for; matrix products, arithmetic and copies ran while one was open for 22% of the time, Pallas kernels for 9%

profile of v3, /device:TPU:14, one launch (start us, length us, event | category | flops | bytes accessed | tf_op | source)
XLA Modules:
  0.0 308.0 jit_solution(4367611026721511945)
XLA Ops:
  0.0 8.1 %copy.57 = s32[8,8,32,1024]{3,2,1,0:T(8,128)S(1)} copy(s32[8,8,32,1024]{3,1,2,0:T(8,128)} %bitcast.90) | data formatting | bytes 16777216
  8.1 3.4 %copy-done = s32[8,8,32,1024]{3,2,1,0:T(8,128)} copy-done((s32[8,8,32,1024]{3,2,1,0:T(8,128)}, s32[8,8,32,1024]{3,2,1,0:T(8,128)S(1)}, u32[]{:S(2)}) %copy-start) | copy-done | bytes 8388632
  11.8 0.6 copy.34
  12.4 1.3 collective-permute-start
  13.7 22.7 %collective-permute-done = bf16[2,32,7,1024]{3,1,2,0:T(8,128)(2,1)S(1)} collective-permute-done((bf16[2,32,7,1024]{3,1,2,0:T(8,128)(2,1)S(1)}, bf16[2,32,7,1024]{3,1,2,0:T(8,128)(2,1)S(1)}, u32[]{:S(2)}, u32[]{:S(2)}) %collective-permute-start) | collective-permute-done | bytes 917536 | tf_op jit(solution)/shard_map/ppermute | solution.py:17
  36.4 1.6 copy.35.halo_ref
  38.0 24.9 %shard_map.46 = bf16[2,32,32,2048]{3,2,1,0:T(8,128)(2,1)} custom-call(f32[8,1024]{1,0:T(8,128)} %taps_ref.1, bf16[2,32,7,1024]{3,2,1,0:T(8,128)(2,1)} %copy.35.halo_ref, s32[2,32,32,1024]{3,2,1,0:T(8,128)} %bitcast.73), custom_call_target="tpu_custom_call" | custom-call | flops 67108864 | bytes 16777216 | tf_op jit(solution)/shard_map/pallas_call | solution.py:74
  62.9 6.8 %convolution_convert_fusion.2 = bf16[2048,256]{0,1:T(8,128)(2,1)} fusion(bf16[2048,2048]{1,0:T(8,128)(2,1)} %bitcast.91, bf16[256,2048]{1,0:T(8,128)(2,1)S(1)} %copy-done.9), kind=kOutput, calls=%fused_computation.10 | convolution fusion | flops 2148007936 | bytes 10485760 | tf_op jit(solution)/shard_map/kj,nj->kn/dot_general | solution.py:179
  69.7 6.2 %all-to-all-start.1 = ((bf16[16,16,2048]{2,1,0:T(8,128)(2,1)}), bf16[16,16,2048]{2,1,0:T(8,128)(2,1)S(1)}, u32[]{:S(2)}, u32[]{:S(2)}) async-start(bf16[16,16,2048]{2,1,0:T(8,128)(2,1)} %bitcast.12), calls=%async_computation.1 | async-start | bytes 2097152 | tf_op jit(solution)/shard_map/all_to_all | solution.py:183
  75.9 6.8 %convolution_convert_fusion.3 = bf16[2048,256]{0,1:T(8,128)(2,1)} fusion(bf16[2048,2048]{1,0:T(8,128)(2,1)} %bitcast.92, bf16[256,2048]{1,0:T(8,128)(2,1)S(1)} %copy-done.8), kind=kOutput, calls=%fused_computation.11 | convolution fusion | flops 2148007936 | bytes 10485760 | tf_op jit(solution)/shard_map/kj,nj->kn/dot_general | solution.py:179
  82.8 17.9 %all-to-all-done.1 = bf16[16,16,2048]{2,1,0:T(8,128)(2,1)S(1)} async-done(((bf16[16,16,2048]{2,1,0:T(8,128)(2,1)}), bf16[16,16,2048]{2,1,0:T(8,128)(2,1)S(1)}, u32[]{:S(2)}, u32[]{:S(2)}) %all-to-all-start.1) | async-done | bytes 1048608 | tf_op jit(solution)/shard_map/all_to_all | solution.py:183
  100.7 5.1 %all-to-all-start = ((bf16[16,16,2048]{2,1,0:T(8,128)(2,1)}), bf16[16,16,2048]{2,1,0:T(8,128)(2,1)S(1)}, u32[]{:S(2)}, u32[]{:S(2)}) async-start(bf16[16,16,2048]{2,1,0:T(8,128)(2,1)} %bitcast.2), calls=%async_computation | async-start | bytes 2097152 | tf_op jit(solution)/shard_map/all_to_all | solution.py:183
  105.7 4.4 %reshape.93 = bf16[16,16,2,32,32]{4,3,2,1,0:T(8,128)(2,1)} reshape(bf16[16,16,2048]{2,1,0:T(8,128)(2,1)S(1)} %all-to-all-done.1) | data formatting | bytes 2097152 | tf_op jit(solution)/shard_map/reshape | solution.py:184
  110.1 3.6 %fusion.4 = bf16[16,2,32,512,1]{3,2,0,1,4:T(8,128)(2,1)S(1)} fusion(bf16[16,16,2,32,32]{4,3,2,1,0:T(8,128)(2,1)} %reshape.93, s32[16,32]{1,0:T(8,128)S(1)} %multiply_add_fusion, s32[512]{0:T(512)S(1)} %copy-done.5), kind=kOutput, calls=%fused_computation.4 | convolution fusion | flops 537133056 | bytes 2101248 | tf_op jit(solution)/shard_map/gkias,gar->kisr/dot_general | solution.py:185
  113.9 16.6 %all-to-all-done = bf16[16,16,2048]{2,1,0:T(8,128)(2,1)S(1)} async-done(((bf16[16,16,2048]{2,1,0:T(8,128)(2,1)}), bf16[16,16,2048]{2,1,0:T(8,128)(2,1)S(1)}, u32[]{:S(2)}, u32[]{:S(2)}) %all-to-all-start) | async-done | bytes 1048608 | tf_op jit(solution)/shard_map/all_to_all | solution.py:183
  130.5 4.4 %reshape.89 = bf16[16,16,2,32,32]{4,3,2,1,0:T(8,128)(2,1)} reshape(bf16[16,16,2048]{2,1,0:T(8,128)(2,1)S(1)} %all-to-all-done) | data formatting | bytes 2097152 | tf_op jit(solution)/shard_map/reshape | solution.py:184
  134.8 3.6 %fusion.6 = bf16[16,2,32,512,1]{3,2,0,1,4:T(8,128)(2,1)S(1)} fusion(bf16[16,16,2,32,32]{4,3,2,1,0:T(8,128)(2,1)} %reshape.89, s32[16,32]{1,0:T(8,128)S(1)} %multiply_add_fusion, s32[512]{0:T(512)S(1)} %copy-done.5), kind=kOutput, calls=%fused_computation.6 | convolution fusion | flops 537133056 | bytes 2101248 | tf_op jit(solution)/shard_map/gkias,gar->kisr/dot_general | solution.py:185
  138.6 0.5 collective-permute-done.2
  139.2 1.5 maximum_maximum_fusion.1
  140.7 3.9 %copy.38.rows_ref = bf16[16,512,128]{2,1,0:T(8,128)(2,1)} copy(bf16[16,512,128]{1,2,0:T(8,128)(2,1)} %bitcast.95) | data formatting | bytes 4194304 | tf_op jit(solution)/shard_map/reshape | solution.py:168
  144.7 1.5 pad_maximum_fusion.1
  146.2 13.1 %shard_map.47.refs_0_ = bf16[2,64,256,512]{3,2,1,0:T(8,128)(2,1)} custom-call(bf16[16,512,128]{2,1,0:T(8,128)(2,1)} %copy.38.rows_ref, bf16[16,128,512]{2,1,0:T(8,128)(2,1)} %bitcast.89), custom_call_target="tpu_custom_call" | custom-call | flops 1073741824 | bytes 12582912 | tf_op jit(solution)/shard_map/pallas_call | solution.py:122
  159.3 6.8 %convolution_convert_fusion = bf16[2048,256]{0,1:T(8,128)(2,1)} fusion(bf16[2048,2048]{1,0:T(8,128)(2,1)} %bitcast.93, bf16[256,2048]{1,0:T(8,128)(2,1)S(1)} %copy-done.7), kind=kOutput, calls=%fused_computation.8 | convolution fusion | flops 2148007936 | bytes 10485760 | tf_op jit(solution)/shard_map/kj,nj->kn/dot_general | solution.py:179
  166.1 6.0 %all-to-all-start.3 = ((bf16[16,16,2048]{2,1,0:T(8,128)(2,1)}), bf16[16,16,2048]{2,1,0:T(8,128)(2,1)S(1)}, u32[]{:S(2)}, u32[]{:S(2)}) async-start(bf16[16,16,2048]{2,1,0:T(8,128)(2,1)} %bitcast.29), calls=%async_computation.3 | async-start | bytes 2097152 | tf_op jit(solution)/shard_map/all_to_all | solution.py:183
  172.1 1.2 fusion.15
  173.4 1.5 maximum_maximum_fusion
  174.9 3.9 %copy.39.rows_ref = bf16[16,512,128]{2,1,0:T(8,128)(2,1)} copy(bf16[16,512,128]{1,2,0:T(8,128)(2,1)} %bitcast.96) | data formatting | bytes 4194304 | tf_op jit(solution)/shard_map/reshape | solution.py:168
  178.8 2.7 pad_maximum_fusion
  181.6 13.2 %shard_map.48.refs_0_ = bf16[2,64,256,512]{3,2,1,0:T(8,128)(2,1)} custom-call(bf16[16,512,128]{2,1,0:T(8,128)(2,1)} %copy.39.rows_ref, bf16[16,128,512]{2,1,0:T(8,128)(2,1)} %bitcast.86, bf16[2,64,256,512]{3,2,1,0:T(8,128)(2,1)} %shard_map.47.refs_0_), custom_call_target="tpu_custom_call", output_to_operand_aliasing={{}: (2, {})} | custom-call | flops 1073741824 | bytes 12582912 | tf_op jit(solution)/shard_map/pallas_call | solution.py:122
  194.7 6.8 %convolution_convert_fusion.1 = bf16[2048,256]{0,1:T(8,128)(2,1)} fusion(bf16[2048,2048]{1,0:T(8,128)(2,1)} %bitcast.94, bf16[256,2048]{1,0:T(8,128)(2,1)S(1)} %copy-done.6), kind=kOutput, calls=%fused_computation.9 | convolution fusion | flops 2148007936 | bytes 10485760 | tf_op jit(solution)/shard_map/kj,nj->kn/dot_general | solution.py:179
  201.5 6.0 %all-to-all-start.2 = ((bf16[16,16,2048]{2,1,0:T(8,128)(2,1)}), bf16[16,16,2048]{2,1,0:T(8,128)(2,1)S(1)}, u32[]{:S(2)}, u32[]{:S(2)}) async-start(bf16[16,16,2048]{2,1,0:T(8,128)(2,1)} %bitcast.21), calls=%async_computation.2 | async-start | bytes 2097152 | tf_op jit(solution)/shard_map/all_to_all | solution.py:183
  207.6 4.4 %reshape.101 = bf16[16,16,2,32,32]{4,3,2,1,0:T(8,128)(2,1)} reshape(bf16[16,16,2048]{2,1,0:T(8,128)(2,1)S(1)} %all-to-all-done.3) | data formatting | bytes 2097152 | tf_op jit(solution)/shard_map/reshape | solution.py:184
  212.0 3.6 %fusion = bf16[16,2,32,512,1]{3,2,0,1,4:T(8,128)(2,1)S(1)} fusion(bf16[16,16,2,32,32]{4,3,2,1,0:T(8,128)(2,1)} %reshape.101, s32[16,32]{1,0:T(8,128)S(1)} %multiply_add_fusion, s32[512]{0:T(512)S(1)} %copy-done.5), kind=kOutput, calls=%fused_computation | convolution fusion | flops 537133056 | bytes 2101248 | tf_op jit(solution)/shard_map/gkias,gar->kisr/dot_general | solution.py:185
  215.6 0.6 collective-permute-start.4
  216.2 16.1 %all-to-all-done.2 = bf16[16,16,2048]{2,1,0:T(8,128)(2,1)S(1)} async-done(((bf16[16,16,2048]{2,1,0:T(8,128)(2,1)}), bf16[16,16,2048]{2,1,0:T(8,128)(2,1)S(1)}, u32[]{:S(2)}, u32[]{:S(2)}) %all-to-all-start.2) | async-done | bytes 1048608 | tf_op jit(solution)/shard_map/all_to_all | solution.py:183
  232.3 4.4 %reshape.97 = bf16[16,16,2,32,32]{4,3,2,1,0:T(8,128)(2,1)} reshape(bf16[16,16,2048]{2,1,0:T(8,128)(2,1)S(1)} %all-to-all-done.2) | data formatting | bytes 2097152 | tf_op jit(solution)/shard_map/reshape | solution.py:184
  236.7 3.6 %fusion.2 = bf16[16,2,32,512,1]{3,2,0,1,4:T(8,128)(2,1)S(1)} fusion(bf16[16,16,2,32,32]{4,3,2,1,0:T(8,128)(2,1)} %reshape.97, s32[16,32]{1,0:T(8,128)S(1)} %multiply_add_fusion, s32[512]{0:T(512)S(1)} %copy-done.5), kind=kOutput, calls=%fused_computation.2 | convolution fusion | flops 537133056 | bytes 2101248 | tf_op jit(solution)/shard_map/gkias,gar->kisr/dot_general | solution.py:185
  240.3 0.6 collective-permute-start.3
  240.9 25.1 %collective-permute-done.3 = bf16[32,32,512]{2,1,0:T(8,128)(2,1)S(1)} collective-permute-done((bf16[32,32,512]{2,1,0:T(8,128)(2,1)S(1)}, bf16[32,32,512]{2,1,0:T(8,128)(2,1)S(1)}, u32[]{:S(2)}, u32[]{:S(2)}) %collective-permute-start.3) | collective-permute-done | bytes 1048608 | tf_op jit(solution)/shard_map/ppermute | solution.py:25
  266.1 1.6 fusion.9
  267.8 1.5 maximum_maximum_fusion.3
  269.3 3.9 %copy.42.rows_ref = bf16[16,512,128]{2,1,0:T(8,128)(2,1)} copy(bf16[16,512,128]{1,2,0:T(8,128)(2,1)} %bitcast.97) | data formatting | bytes 4194304 | tf_op jit(solution)/shard_map/reshape | solution.py:168
  273.3 1.5 maximum_maximum_fusion.2
  274.8 4.0 %copy.43.rows_ref = bf16[16,512,128]{2,1,0:T(8,128)(2,1)} copy(bf16[16,512,128]{1,2,0:T(8,128)(2,1)} %bitcast.98) | data formatting | bytes 4194304 | tf_op jit(solution)/shard_map/reshape | solution.py:168
  278.8 1.5 pad_maximum_fusion.3
  280.3 13.2 %shard_map.49.refs_0_ = bf16[2,64,256,512]{3,2,1,0:T(8,128)(2,1)} custom-call(bf16[16,512,128]{2,1,0:T(8,128)(2,1)} %copy.42.rows_ref, bf16[16,128,512]{2,1,0:T(8,128)(2,1)} %bitcast.87, bf16[2,64,256,512]{3,2,1,0:T(8,128)(2,1)} %shard_map.48.refs_0_), custom_call_target="tpu_custom_call", output_to_operand_aliasing={{}: (2, {})} | custom-call | flops 1073741824 | bytes 12582912 | tf_op jit(solution)/shard_map/pallas_call | solution.py:122
  293.5 1.5 pad_maximum_fusion.2
  295.0 13.1 %shard_map.50 = bf16[2,64,256,512]{3,2,1,0:T(8,128)(2,1)} custom-call(bf16[16,512,128]{2,1,0:T(8,128)(2,1)} %copy.43.rows_ref, bf16[16,128,512]{2,1,0:T(8,128)(2,1)} %bitcast.88, bf16[2,64,256,512]{3,2,1,0:T(8,128)(2,1)} %shard_map.49.refs_0_), custom_call_target="tpu_custom_call", output_to_operand_aliasing={{}: (2, {})} | custom-call | flops 1073741824 | bytes 12582912 | tf_op jit(solution)/shard_map/pallas_call | solution.py:122
  (35 shorter events, 1.1 us)
Async XLA Ops:
  8.1 3.4 %copy-start = (s32[8,8,32,1024]{3,2,1,0:T(8,128)}, s32[8,8,32,1024]{3,2,1,0:T(8,128)S(1)}, u32[]{:S(2)}) copy-start(s32[8,8,32,1024]{3,2,1,0:T(8,128)S(1)} %copy.57) | copy-start | bytes 25165828
  12.4 24.0 %collective-permute-start = (bf16[2,32,7,1024]{3,1,2,0:T(8,128)(2,1)S(1)}, bf16[2,32,7,1024]{3,1,2,0:T(8,128)(2,1)S(1)}, u32[]{:S(2)}, u32[]{:S(2)}) collective-permute-start(bf16[2,32,7,1024]{3,1,2,0:T(8,128)(2,1)S(1)} %copy.34), channel_id=1, source_target_pairs={{0,1},{2,3},{4,5},{6,7},{8,9},{10,11},{12,13},{14,15},{16,17},{18,... | collective-permute-start | bytes 2752520 | tf_op jit(solution)/shard_map/ppermute | solution.py:17
  38.0 24.9 %copy-start.9 = (bf16[256,2048]{1,0:T(8,128)(2,1)S(1)}, bf16[256,2048]{1,0:T(8,128)(2,1)}, u32[]{:S(2)}) copy-start(bf16[256,2048]{1,0:T(8,128)(2,1)} %constant.18) | copy-start | bytes 3145732
  62.9 13.0 %copy-start.8 = (bf16[256,2048]{1,0:T(8,128)(2,1)S(1)}, bf16[256,2048]{1,0:T(8,128)(2,1)}, u32[]{:S(2)}) copy-start(bf16[256,2048]{1,0:T(8,128)(2,1)} %constant.16) | copy-start | bytes 3145732
  69.7 31.0 %all-to-all-start.1 = ((bf16[16,16,2048]{2,1,0:T(8,128)(2,1)}), bf16[16,16,2048]{2,1,0:T(8,128)(2,1)S(1)}, u32[]{:S(2)}, u32[]{:S(2)}) async-start(bf16[16,16,2048]{2,1,0:T(8,128)(2,1)} %bitcast.12), calls=%async_computation.1 | async-start | bytes 2097152 | tf_op jit(solution)/shard_map/all_to_all | solution.py:183
  82.7 27.4 %copy-start.5 = (s32[512]{0:T(512)S(1)}, s32[512]{0:T(512)}, u32[]{:S(2)}) copy-start(s32[512]{0:T(512)} %param.6) | copy-start | bytes 6148
  100.7 29.8 %all-to-all-start = ((bf16[16,16,2048]{2,1,0:T(8,128)(2,1)}), bf16[16,16,2048]{2,1,0:T(8,128)(2,1)S(1)}, u32[]{:S(2)}, u32[]{:S(2)}) async-start(bf16[16,16,2048]{2,1,0:T(8,128)(2,1)} %bitcast.2), calls=%async_computation | async-start | bytes 2097152 | tf_op jit(solution)/shard_map/all_to_all | solution.py:183
  113.8 25.3 %collective-permute-start.2 = (bf16[32,32,512]{2,1,0:T(8,128)(2,1)S(1)}, bf16[32,32,512]{2,1,0:T(8,128)(2,1)S(1)}, u32[]{:S(2)}, u32[]{:S(2)}) collective-permute-start(bf16[32,32,512]{2,1,0:T(8,128)(2,1)S(1)} %bitcast.80), channel_id=1, source_target_pairs={{0,1},{1,0},{2,3},{3,2},{4,5},{5,4},{6,7},{7,6},{8,9},{9,8},{10,11... | collective-permute-start | bytes 3145736 | tf_op jit(solution)/shard_map/ppermute | solution.py:25
  138.5 33.6 %collective-permute-start.1 = (bf16[32,32,512]{2,1,0:T(8,128)(2,1)S(1)}, bf16[32,32,512]{2,1,0:T(8,128)(2,1)}, u32[]{:S(2)}, u32[]{:S(2)}) collective-permute-start(bf16[32,32,512]{2,1,0:T(8,128)(2,1)S(1)} %bitcast.83), channel_id=1, source_target_pairs={{0,1},{1,0},{2,3},{3,2},{4,5},{5,4},{6,7},{7,6},{8,9},{9,8},{10,11... | collective-permute-start | bytes 3145736 | tf_op jit(solution)/shard_map/ppermute | solution.py:25
  146.2 13.1 %copy-start.7 = (bf16[256,2048]{1,0:T(8,128)(2,1)S(1)}, bf16[256,2048]{1,0:T(8,128)(2,1)}, u32[]{:S(2)}) copy-start(bf16[256,2048]{1,0:T(8,128)(2,1)} %constant.22) | copy-start | bytes 3145732
  166.1 35.5 %all-to-all-start.3 = ((bf16[16,16,2048]{2,1,0:T(8,128)(2,1)}), bf16[16,16,2048]{2,1,0:T(8,128)(2,1)S(1)}, u32[]{:S(2)}, u32[]{:S(2)}) async-start(bf16[16,16,2048]{2,1,0:T(8,128)(2,1)} %bitcast.29), calls=%async_computation.3 | async-start | bytes 2097152 | tf_op jit(solution)/shard_map/all_to_all | solution.py:183
  181.6 13.2 %copy-start.6 = (bf16[256,2048]{1,0:T(8,128)(2,1)S(1)}, bf16[256,2048]{1,0:T(8,128)(2,1)}, u32[]{:S(2)}) copy-start(bf16[256,2048]{1,0:T(8,128)(2,1)} %constant.20) | copy-start | bytes 3145732
  201.5 30.8 %all-to-all-start.2 = ((bf16[16,16,2048]{2,1,0:T(8,128)(2,1)}), bf16[16,16,2048]{2,1,0:T(8,128)(2,1)S(1)}, u32[]{:S(2)}, u32[]{:S(2)}) async-start(bf16[16,16,2048]{2,1,0:T(8,128)(2,1)} %bitcast.21), calls=%async_computation.2 | async-start | bytes 2097152 | tf_op jit(solution)/shard_map/all_to_all | solution.py:183
  215.6 25.3 %collective-permute-start.4 = (bf16[32,32,512]{2,1,0:T(8,128)(2,1)S(1)}, bf16[32,32,512]{2,1,0:T(8,128)(2,1)S(1)}, u32[]{:S(2)}, u32[]{:S(2)}) collective-permute-start(bf16[32,32,512]{2,1,0:T(8,128)(2,1)S(1)} %bitcast.74), channel_id=1, source_target_pairs={{0,1},{1,0},{2,3},{3,2},{4,5},{5,4},{6,7},{7,6},{8,9},{9,8},{10,11... | collective-permute-start | bytes 3145736 | tf_op jit(solution)/shard_map/ppermute | solution.py:25
  240.3 25.7 %collective-permute-start.3 = (bf16[32,32,512]{2,1,0:T(8,128)(2,1)S(1)}, bf16[32,32,512]{2,1,0:T(8,128)(2,1)S(1)}, u32[]{:S(2)}, u32[]{:S(2)}) collective-permute-start(bf16[32,32,512]{2,1,0:T(8,128)(2,1)S(1)} %bitcast.77), channel_id=1, source_target_pairs={{0,1},{1,0},{2,3},{3,2},{4,5},{5,4},{6,7},{7,6},{8,9},{9,8},{10,11... | collective-permute-start | bytes 3145736 | tf_op jit(solution)/shard_map/ppermute | solution.py:25
  240.9 25.1 %copy-start.1 = (bf16[32,32,512]{2,1,0:T(8,128)(2,1)}, bf16[32,32,512]{2,1,0:T(8,128)(2,1)S(1)}, u32[]{:S(2)}) copy-start(bf16[32,32,512]{2,1,0:T(8,128)(2,1)S(1)} %collective-permute-done.4) | copy-start | bytes 3145732
  266.0 1.7 copy-start.3
  274.8 4.0 %copy-start.2 = (bf16[32,32,512]{2,1,0:T(8,128)(2,1)S(1)}, bf16[32,32,512]{2,1,0:T(8,128)(2,1)}, u32[]{:S(2)}) copy-start(bf16[32,32,512]{2,1,0:T(8,128)(2,1)} %copy-done.1) | copy-start | bytes 3145732
  280.3 13.2 %copy-start.4 = (bf16[32,32,512]{2,1,0:T(8,128)(2,1)S(1)}, bf16[32,32,512]{2,1,0:T(8,128)(2,1)}, u32[]{:S(2)}) copy-start(bf16[32,32,512]{2,1,0:T(8,128)(2,1)} %copy-done.3) | copy-start | bytes 3145732

commit v4 on v3

--- a/solution.py
+++ b/solution.py
@@ -49,69 +49,109 @@
     return jnp.asarray(table.reshape(chunks, groups * width, 2 * channels))
 
 
-def fir_kernel(taps_ref, halo_ref, frames_ref, out_ref):
-    tap_count = taps_ref.shape[0]
+def fir_rows(taps_ref, extended, count):
+    total = taps_ref[0:1, :] * extended[0:count]
+    for tap_index in range(1, taps_ref.shape[0]):
+        total = total + taps_ref[tap_index : tap_index + 1, :] * extended[tap_index : tap_index + count]
+    return total.astype(jnp.bfloat16)
+
+
+def fir_store(out_ref, filtered, channels):
+    out_ref[0, 0, :, 0:channels] = filtered[0]
+    out_ref[0, 0, :, channels:] = filtered[1]
+    out_ref[1, 0, :, 0:channels] = filtered[1]
+    out_ref[1, 0, :, channels:] = -filtered[0]
+
+
+def fir_kernel(taps_ref, frames_ref, out_ref):
+    halo = taps_ref.shape[0] - 1
     spectra = frames_ref.shape[2]
+    channels = frames_ref.shape[3]
+    filtered = []
+    for part in range(2):
+        frames = frames_ref[part, 0].astype(jnp.float32)
+        extended = jnp.concatenate([jnp.zeros((halo, channels), jnp.float32), frames], axis=0)
+        filtered.append(fir_rows(taps_ref, extended, spectra))
+    fir_store(out_ref, filtered, channels)
+
+
+def fir_edge_kernel(taps_ref, halo_ref, frames_ref, previous_ref, out_ref):
+    count = frames_ref.shape[2]
     channels = frames_ref.shape[3]
     filtered = []
     for part in range(2):
         extended = jnp.concatenate(
             [halo_ref[part, 0].astype(jnp.float32), frames_ref[part, 0].astype(jnp.float32)], axis=0
         )
-        total = taps_ref[0:1, :] * extended[0:spectra]
-        for tap_index in range(1, tap_count):
-            total = total + taps_ref[tap_index : tap_index + 1, :] * extended[tap_index : tap_index + spectra]
-        filtered.append(total.astype(jnp.bfloat16))
-    out_ref[0, 0, :, 0:channels] = filtered[0]
-    out_ref[0, 0, :, channels:] = filtered[1]
-    out_ref[1, 0, :, 0:channels] = filtered[1]
-    out_ref[1, 0, :, channels:] = -filtered[0]
+        filtered.append(fir_rows(taps_ref, extended, count))
+    fir_store(out_ref, filtered, channels)
 
 
 def filter_frames(fir_taps, earlier, frames):
     tap_count, channels = fir_taps.shape
     _, stations_local, spectra, _ = frames.shape
-    return pl.pallas_call(
+    out_shape = jax.ShapeDtypeStruct((2, stations_local, spectra, 2 * channels), jnp.bfloat16)
+    whole = pl.pallas_call(
         fir_kernel,
         grid=(stations_local,),
         in_specs=[
             pl.BlockSpec((tap_count, channels), lambda a: (0, 0)),
-            pl.BlockSpec((2, 1, tap_count - 1, channels), lambda a: (0, a, 0, 0)),
             pl.BlockSpec((2, 1, spectra, channels), lambda a: (0, a, 0, 0)),
         ],
         out_specs=pl.BlockSpec((2, 1, spectra, 2 * channels), lambda a: (0, a, 0, 0)),
-        out_shape=jax.ShapeDtypeStruct((2, stations_local, spectra, 2 * channels), jnp.bfloat16),
+        out_shape=out_shape,
         cost_estimate=pl.CostEstimate(
             flops=4 * tap_count * frames.size,
             transcendentals=0,
             bytes_accessed=4 * frames.size + 4 * frames.size,
         ),
-    )(fir_taps, earlier, frames)
+    )(fir_taps, frames)
+    edge = 8
+    return pl.pallas_call(
+        fir_edge_kernel,
+        grid=(stations_local,),
+        in_specs=[
+            pl.BlockSpec((tap_count, channels), lambda a: (0, 0)),
+            pl.BlockSpec((2, 1, tap_count - 1, channels), lambda a: (0, a, 0, 0)),
+            pl.BlockSpec((2, 1, edge, channels), lambda a: (0, a, 0, 0)),
+            pl.BlockSpec(memory_space=pl.ANY),
+        ],
+        out_specs=pl.BlockSpec((2, 1, edge, 2 * channels), lambda a: (0, a, 0, 0)),
+        out_shape=out_shape,
+        input_output_aliases={3: 0},
+        cost_estimate=pl.CostEstimate(
+            flops=4 * tap_count * edge * frames.size // spectra,
+            transcendentals=0,
+            bytes_accessed=8 * edge * frames.size // spectra,
+        ),
+    )(fir_taps, earlier, frames, whole)
 
 
 def correlate_kernel(rows_ref, cols_ref, *refs):
     out_ref = refs[-1]
     row_count = out_ref.shape[2]
-    left = rows_ref[0]
-    right = cols_ref[0]
-    product = jnp.dot(left, right, preferred_element_type=jnp.float32)
-    right = right.astype(jnp.float32)
-    rows = left[0:row_count].astype(jnp.float32)
-    column_power = jnp.sum(right * right, axis=0, keepdims=True)
-    row_power = jnp.sum(rows * rows, axis=1, keepdims=True)
-    scale_row = lax.rsqrt(row_power + epsilon)
-    scale_column = lax.rsqrt(column_power + epsilon)
-    out_ref[0, 0] = (product[0:row_count] * scale_row * scale_column).astype(out_ref.dtype)
-    out_ref[1, 0] = (product[row_count:] * scale_row * scale_column).astype(out_ref.dtype)
+    for index in range(out_ref.shape[1]):
+        left = rows_ref[index]
+        right = cols_ref[index]
+        product = jnp.dot(left, right, preferred_element_type=jnp.float32)
+        right = right.astype(jnp.float32)
+        rows = left[0:row_count].astype(jnp.float32)
+        column_power = jnp.sum(right * right, axis=0, keepdims=True)
+        row_power = jnp.sum(rows * rows, axis=1, keepdims=True)
+        scale_row = lax.rsqrt(row_power + epsilon)
+        scale_column = lax.rsqrt(column_power + epsilon)
+        out_ref[0, index] = (product[0:row_count] * scale_row * scale_column).astype(out_ref.dtype)
+        out_ref[1, index] = (product[row_count:] * scale_row * scale_column).astype(out_ref.dtype)
 
 
 def correlate_chunk(left, right, previous, offset, local_channels):
     width, double_rows, depth = left.shape
     row_count = double_rows // 2
     stations = right.shape[2]
+    step = 4 if width % 4 == 0 and offset % 4 == 0 else 1
     in_specs = [
-        pl.BlockSpec((1, double_rows, depth), lambda k: (k, 0, 0)),
-        pl.BlockSpec((1, depth, stations), lambda k: (k, 0, 0)),
+        pl.BlockSpec((step, double_rows, depth), lambda k: (k, 0, 0)),
+        pl.BlockSpec((step, depth, stations), lambda k: (k, 0, 0)),
     ]
     operands = [left, right]
     aliases = {}
@@ -121,9 +161,11 @@
         aliases = {2: 0}
     return pl.pallas_call(
         correlate_kernel,
-        grid=(width,),
+        grid=(width // step,),
         in_specs=in_specs,
-        out_specs=pl.BlockSpec((2, 1, row_count, stations), lambda k: (0, offset + k, 0, 0)),
+        out_specs=pl.BlockSpec(
+            (2, step, row_count, stations), lambda k: (0, offset // step + k, 0, 0)
+        ),
         out_shape=jax.ShapeDtypeStruct((2, local_channels, row_count, stations), jnp.bfloat16),
         input_output_aliases=aliases,
         cost_estimate=pl.CostEstimate(

time: 311 us -> 285 us (0.916)
  waiting for transfers between devices: 98.9 us -> 72.6 us
  Pallas kernels: 77.5 us -> 71.1 us
  starting transfers between devices: 26 us -> 31.5 us
    ppermute x1, waiting for transfers between devices: 22.7 us -> 0.01 us  [passed_along(): lax.ppermute(value, axis, [(source, source + steps) for source in range(i...]
    ppermute x4, starting transfers between devices: 1.36 us -> 8.53 us  [gathered_along(): parts.append(lax.ppermute(value, axis, pairs))]
    pallas_call x4 -> x5, Pallas kernels: 52.5 us -> 46.5 us  [the longest x4 28.4 us: correlate_chunk(): pl.pallas_call(correlate_kernel, grid=(width // step,), in_specs=in_specs...]
  transfers between devices with their start and end apart: 9 -> 9, of which waited for: 6 -> 5; matrix products, arithmetic and copies ran while one was open for 22% -> 25% of each run, Pallas kernels for 9% -> 14%
where the time goes in v4:
time: 285 us; the launch traced here: 281 us
  waiting for transfers between devices  72.6 us (25%)
  Pallas kernels  71.1 us (25%)
  local copies, waits for them, and re-layouts  47.2 us (17%)
  matrix products  41.4 us (15%)
  starting transfers between devices  31.5 us (11%)
  other arithmetic  16.8 us (6%)
    all_to_all x4, waiting for transfers between devices, per_device(): lax.all_to_all(spectra, 'stn', split_axis=0, concat_axis=0, tiled=True)  48.3 us
    pallas_call x4, Pallas kernels, correlate_chunk(): pl.pallas_call(correlate_kernel, grid=(width // step,), in_specs=in_specs...  28.4 us
    dot_general x4, matrix products, per_device(): jnp.einsum('kj,nj->kn', weights[chunk], source, preferred_element_type=jn...  27.2 us
    pallas_call x1, Pallas kernels, filter_frames(): pl.pallas_call(fir_kernel, grid=(stations_local,), in_specs=[pl.BlockSpec...  24.5 us
    ppermute x4, waiting for transfers between devices, gathered_along(): parts.append(lax.ppermute(value, axis, pairs))  24.2 us
    all_to_all x4, starting transfers between devices, per_device(): lax.all_to_all(spectra, 'stn', split_axis=0, concat_axis=0, tiled=True)  21.7 us
    pallas_call x1, Pallas kernels, filter_frames(): pl.pallas_call(fir_edge_kernel, grid=(stations_local,), in_specs=[pl.Bloc...  18.1 us
    reshape x4, local copies, waits for them, and re-layouts, per_device(): turned = turned.reshape(groups, width, 2, stations_local, spectra_local)  17.5 us
  transfers between devices with their start and end apart: 9, of which 5 were waited for; matrix products, arithmetic and copies ran while one was open for 25% of the time, Pallas kernels for 14%

profile of v4, /device:TPU:14, one launch (start us, length us, event | category | flops | bytes accessed | tf_op | source)
XLA Modules:
  0.0 280.8 jit_solution(13529309164128970840)
XLA Ops:
  0.0 8.1 %copy.58 = s32[8,8,32,1024]{3,2,1,0:T(8,128)S(1)} copy(s32[8,8,32,1024]{3,1,2,0:T(8,128)} %bitcast.95) | data formatting | bytes 16777216
  8.1 3.4 %copy-done = s32[8,8,32,1024]{3,2,1,0:T(8,128)} copy-done((s32[8,8,32,1024]{3,2,1,0:T(8,128)}, s32[8,8,32,1024]{3,2,1,0:T(8,128)S(1)}, u32[]{:S(2)}) %copy-start) | copy-done | bytes 8388632
  12.4 1.3 collective-permute-start
  13.7 24.5 %shard_map.46.previous_ref = bf16[2,32,32,2048]{3,2,1,0:T(8,128)(2,1)} custom-call(f32[8,1024]{1,0:T(8,128)} %taps_ref.3, s32[2,32,32,1024]{3,2,1,0:T(8,128)} %bitcast.73), custom_call_target="tpu_custom_call" | custom-call | flops 67108864 | bytes 16777216 | tf_op jit(solution)/shard_map/pallas_call | solution.py:94
  38.2 1.6 copy.36.halo_ref
  39.8 18.1 %shard_map.47 = bf16[2,32,32,2048]{3,2,1,0:T(8,128)(2,1)} custom-call(f32[8,1024]{1,0:T(8,128)} %taps_ref.3, bf16[2,32,7,1024]{3,2,1,0:T(8,128)(2,1)} %copy.36.halo_ref, s32[2,32,32,1024]{3,2,1,0:T(8,128)} %bitcast.74, bf16[2,32,32,2048]{3,2,1,0:T(8,128)(2,1)} %shard_map.46.previous_ref), custom_call_target="tpu_custom_call", output_to_operand_aliasing={{}: (3, {})} | custom-call | flops 16777216 | bytes 4194304 | tf_op jit(solution)/shard_map/pallas_call | solution.py:110
  57.9 6.8 %convolution_convert_fusion.2 = bf16[2048,256]{0,1:T(8,128)(2,1)} fusion(bf16[2048,2048]{1,0:T(8,128)(2,1)} %bitcast.75, bf16[256,2048]{1,0:T(8,128)(2,1)S(1)} %copy-done.9), kind=kOutput, calls=%fused_computation.10 | convolution fusion | flops 2148007936 | bytes 10485760 | tf_op jit(solution)/shard_map/kj,nj->kn/dot_general | solution.py:221
  64.7 6.2 %all-to-all-start.1 = ((bf16[16,16,2048]{2,1,0:T(8,128)(2,1)}), bf16[16,16,2048]{2,1,0:T(8,128)(2,1)S(1)}, u32[]{:S(2)}, u32[]{:S(2)}) async-start(bf16[16,16,2048]{2,1,0:T(8,128)(2,1)} %bitcast.12), calls=%async_computation.1 | async-start | bytes 2097152 | tf_op jit(solution)/shard_map/all_to_all | solution.py:225
  71.0 6.8 %convolution_convert_fusion.3 = bf16[2048,256]{0,1:T(8,128)(2,1)} fusion(bf16[2048,2048]{1,0:T(8,128)(2,1)} %bitcast.76, bf16[256,2048]{1,0:T(8,128)(2,1)S(1)} %copy-done.8), kind=kOutput, calls=%fused_computation.11 | convolution fusion | flops 2148007936 | bytes 10485760 | tf_op jit(solution)/shard_map/kj,nj->kn/dot_general | solution.py:221
  77.8 17.9 %all-to-all-done.1 = bf16[16,16,2048]{2,1,0:T(8,128)(2,1)S(1)} async-done(((bf16[16,16,2048]{2,1,0:T(8,128)(2,1)}), bf16[16,16,2048]{2,1,0:T(8,128)(2,1)S(1)}, u32[]{:S(2)}, u32[]{:S(2)}) %all-to-all-start.1) | async-done | bytes 1048608 | tf_op jit(solution)/shard_map/all_to_all | solution.py:225
  95.7 5.3 %all-to-all-start = ((bf16[16,16,2048]{2,1,0:T(8,128)(2,1)}), bf16[16,16,2048]{2,1,0:T(8,128)(2,1)S(1)}, u32[]{:S(2)}, u32[]{:S(2)}) async-start(bf16[16,16,2048]{2,1,0:T(8,128)(2,1)} %bitcast.2), calls=%async_computation | async-start | bytes 2097152 | tf_op jit(solution)/shard_map/all_to_all | solution.py:225
  101.0 4.4 %reshape.93 = bf16[16,16,2,32,32]{4,3,2,1,0:T(8,128)(2,1)} reshape(bf16[16,16,2048]{2,1,0:T(8,128)(2,1)S(1)} %all-to-all-done.1) | data formatting | bytes 2097152 | tf_op jit(solution)/shard_map/reshape | solution.py:226
  105.4 3.6 %fusion.4 = bf16[16,2,32,512,1]{3,2,0,1,4:T(8,128)(2,1)S(1)} fusion(bf16[16,16,2,32,32]{4,3,2,1,0:T(8,128)(2,1)} %reshape.93, s32[16,32]{1,0:T(8,128)S(1)} %multiply_add_fusion, s32[512]{0:T(512)S(1)} %copy-done.5), kind=kOutput, calls=%fused_computation.4 | convolution fusion | flops 537133056 | bytes 2101248 | tf_op jit(solution)/shard_map/gkias,gar->kisr/dot_general | solution.py:227
  109.0 2.8 collective-permute-start.2
  111.8 13.9 %all-to-all-done = bf16[16,16,2048]{2,1,0:T(8,128)(2,1)S(1)} async-done(((bf16[16,16,2048]{2,1,0:T(8,128)(2,1)}), bf16[16,16,2048]{2,1,0:T(8,128)(2,1)S(1)}, u32[]{:S(2)}, u32[]{:S(2)}) %all-to-all-start) | async-done | bytes 1048608 | tf_op jit(solution)/shard_map/all_to_all | solution.py:225
  125.7 4.4 %reshape.89 = bf16[16,16,2,32,32]{4,3,2,1,0:T(8,128)(2,1)} reshape(bf16[16,16,2048]{2,1,0:T(8,128)(2,1)S(1)} %all-to-all-done) | data formatting | bytes 2097152 | tf_op jit(solution)/shard_map/reshape | solution.py:226
  130.1 3.6 %fusion.6 = bf16[16,2,32,512,1]{3,2,0,1,4:T(8,128)(2,1)S(1)} fusion(bf16[16,16,2,32,32]{4,3,2,1,0:T(8,128)(2,1)} %reshape.89, s32[16,32]{1,0:T(8,128)S(1)} %multiply_add_fusion, s32[512]{0:T(512)S(1)} %copy-done.5), kind=kOutput, calls=%fused_computation.6 | convolution fusion | flops 537133056 | bytes 2101248 | tf_op jit(solution)/shard_map/gkias,gar->kisr/dot_general | solution.py:227
  133.7 2.8 collective-permute-start.1
  136.7 1.5 maximum_maximum_fusion.1
  138.2 3.9 %copy.39.rows_ref = bf16[16,512,128]{2,1,0:T(8,128)(2,1)} copy(bf16[16,512,128]{1,2,0:T(8,128)(2,1)} %bitcast.96) | data formatting | bytes 4194304 | tf_op jit(solution)/shard_map/reshape | solution.py:210
  142.1 1.5 pad_maximum_fusion.1
  143.6 7.1 %shard_map.48.refs_0_ = bf16[2,64,256,512]{3,2,1,0:T(8,128)(2,1)} custom-call(bf16[16,512,128]{2,1,0:T(8,128)(2,1)} %copy.39.rows_ref, bf16[16,128,512]{2,1,0:T(8,128)(2,1)} %bitcast.94), custom_call_target="tpu_custom_call" | custom-call | flops 1073741824 | bytes 12582912 | tf_op jit(solution)/shard_map/pallas_call | solution.py:162
  150.7 6.8 %convolution_convert_fusion = bf16[2048,256]{0,1:T(8,128)(2,1)} fusion(bf16[2048,2048]{1,0:T(8,128)(2,1)} %bitcast.77, bf16[256,2048]{1,0:T(8,128)(2,1)S(1)} %copy-done.7), kind=kOutput, calls=%fused_computation.8 | convolution fusion | flops 2148007936 | bytes 10485760 | tf_op jit(solution)/shard_map/kj,nj->kn/dot_general | solution.py:221
  157.5 5.1 %all-to-all-start.3 = ((bf16[16,16,2048]{2,1,0:T(8,128)(2,1)}), bf16[16,16,2048]{2,1,0:T(8,128)(2,1)S(1)}, u32[]{:S(2)}, u32[]{:S(2)}) async-start(bf16[16,16,2048]{2,1,0:T(8,128)(2,1)} %bitcast.29), calls=%async_computation.3 | async-start | bytes 2097152 | tf_op jit(solution)/shard_map/all_to_all | solution.py:225
  163.8 1.5 maximum_maximum_fusion
  165.3 3.9 %copy.40.rows_ref = bf16[16,512,128]{2,1,0:T(8,128)(2,1)} copy(bf16[16,512,128]{1,2,0:T(8,128)(2,1)} %bitcast.97) | data formatting | bytes 4194304 | tf_op jit(solution)/shard_map/reshape | solution.py:210
  169.3 2.7 pad_maximum_fusion
  172.0 7.1 %shard_map.49.refs_0_ = bf16[2,64,256,512]{3,2,1,0:T(8,128)(2,1)} custom-call(bf16[16,512,128]{2,1,0:T(8,128)(2,1)} %copy.40.rows_ref, bf16[16,128,512]{2,1,0:T(8,128)(2,1)} %bitcast.91, bf16[2,64,256,512]{3,2,1,0:T(8,128)(2,1)} %shard_map.48.refs_0_), custom_call_target="tpu_custom_call", output_to_operand_aliasing={{}: (2, {})} | custom-call | flops 1073741824 | bytes 12582912 | tf_op jit(solution)/shard_map/pallas_call | solution.py:162
  179.1 6.8 %convolution_convert_fusion.1 = bf16[2048,256]{0,1:T(8,128)(2,1)} fusion(bf16[2048,2048]{1,0:T(8,128)(2,1)} %bitcast.78, bf16[256,2048]{1,0:T(8,128)(2,1)S(1)} %copy-done.6), kind=kOutput, calls=%fused_computation.9 | convolution fusion | flops 2148007936 | bytes 10485760 | tf_op jit(solution)/shard_map/kj,nj->kn/dot_general | solution.py:221
  186.0 1.3 all-to-all-done.3
  187.3 5.1 %all-to-all-start.2 = ((bf16[16,16,2048]{2,1,0:T(8,128)(2,1)}), bf16[16,16,2048]{2,1,0:T(8,128)(2,1)S(1)}, u32[]{:S(2)}, u32[]{:S(2)}) async-start(bf16[16,16,2048]{2,1,0:T(8,128)(2,1)} %bitcast.21), calls=%async_computation.2 | async-start | bytes 2097152 | tf_op jit(solution)/shard_map/all_to_all | solution.py:225
  192.4 4.4 %reshape.101 = bf16[16,16,2,32,32]{4,3,2,1,0:T(8,128)(2,1)} reshape(bf16[16,16,2048]{2,1,0:T(8,128)(2,1)S(1)} %all-to-all-done.3) | data formatting | bytes 2097152 | tf_op jit(solution)/shard_map/reshape | solution.py:226
  196.8 3.6 %fusion = bf16[16,2,32,512,1]{3,2,0,1,4:T(8,128)(2,1)S(1)} fusion(bf16[16,16,2,32,32]{4,3,2,1,0:T(8,128)(2,1)} %reshape.101, s32[16,32]{1,0:T(8,128)S(1)} %multiply_add_fusion, s32[512]{0:T(512)S(1)} %copy-done.5), kind=kOutput, calls=%fused_computation | convolution fusion | flops 537133056 | bytes 2101248 | tf_op jit(solution)/shard_map/gkias,gar->kisr/dot_general | solution.py:227
  200.4 1.5 collective-permute-start.4
  201.9 15.2 %all-to-all-done.2 = bf16[16,16,2048]{2,1,0:T(8,128)(2,1)S(1)} async-done(((bf16[16,16,2048]{2,1,0:T(8,128)(2,1)}), bf16[16,16,2048]{2,1,0:T(8,128)(2,1)S(1)}, u32[]{:S(2)}, u32[]{:S(2)}) %all-to-all-start.2) | async-done | bytes 1048608 | tf_op jit(solution)/shard_map/all_to_all | solution.py:225
  217.1 4.4 %reshape.97 = bf16[16,16,2,32,32]{4,3,2,1,0:T(8,128)(2,1)} reshape(bf16[16,16,2048]{2,1,0:T(8,128)(2,1)S(1)} %all-to-all-done.2) | data formatting | bytes 2097152 | tf_op jit(solution)/shard_map/reshape | solution.py:226
  221.5 3.6 %fusion.2 = bf16[16,2,32,512,1]{3,2,0,1,4:T(8,128)(2,1)S(1)} fusion(bf16[16,16,2,32,32]{4,3,2,1,0:T(8,128)(2,1)} %reshape.97, s32[16,32]{1,0:T(8,128)S(1)} %multiply_add_fusion, s32[512]{0:T(512)S(1)} %copy-done.5), kind=kOutput, calls=%fused_computation.2 | convolution fusion | flops 537133056 | bytes 2101248 | tf_op jit(solution)/shard_map/gkias,gar->kisr/dot_general | solution.py:227
  225.1 1.5 collective-permute-start.3
  226.7 24.2 %collective-permute-done.3 = bf16[32,32,512]{2,1,0:T(8,128)(2,1)S(1)} collective-permute-done((bf16[32,32,512]{2,1,0:T(8,128)(2,1)S(1)}, bf16[32,32,512]{2,1,0:T(8,128)(2,1)S(1)}, u32[]{:S(2)}, u32[]{:S(2)}) %collective-permute-start.3) | collective-permute-done | bytes 1048608 | tf_op jit(solution)/shard_map/ppermute | solution.py:25
  250.9 1.6 fusion.9
  252.6 1.5 maximum_maximum_fusion.3
  254.1 3.9 %copy.43.rows_ref = bf16[16,512,128]{2,1,0:T(8,128)(2,1)} copy(bf16[16,512,128]{1,2,0:T(8,128)(2,1)} %bitcast.98) | data formatting | bytes 4194304 | tf_op jit(solution)/shard_map/reshape | solution.py:210
  258.1 1.5 maximum_maximum_fusion.2
  259.6 4.0 %copy.44.rows_ref = bf16[16,512,128]{2,1,0:T(8,128)(2,1)} copy(bf16[16,512,128]{1,2,0:T(8,128)(2,1)} %bitcast.99) | data formatting | bytes 4194304 | tf_op jit(solution)/shard_map/reshape | solution.py:210
  263.6 1.5 pad_maximum_fusion.3
  265.2 7.1 %shard_map.50.refs_0_ = bf16[2,64,256,512]{3,2,1,0:T(8,128)(2,1)} custom-call(bf16[16,512,128]{2,1,0:T(8,128)(2,1)} %copy.43.rows_ref, bf16[16,128,512]{2,1,0:T(8,128)(2,1)} %bitcast.92, bf16[2,64,256,512]{3,2,1,0:T(8,128)(2,1)} %shard_map.49.refs_0_), custom_call_target="tpu_custom_call", output_to_operand_aliasing={{}: (2, {})} | custom-call | flops 1073741824 | bytes 12582912 | tf_op jit(solution)/shard_map/pallas_call | solution.py:162
  272.3 1.5 pad_maximum_fusion.2
  273.7 7.0 %shard_map.51 = bf16[2,64,256,512]{3,2,1,0:T(8,128)(2,1)} custom-call(bf16[16,512,128]{2,1,0:T(8,128)(2,1)} %copy.44.rows_ref, bf16[16,128,512]{2,1,0:T(8,128)(2,1)} %bitcast.93, bf16[2,64,256,512]{3,2,1,0:T(8,128)(2,1)} %shard_map.50.refs_0_), custom_call_target="tpu_custom_call", output_to_operand_aliasing={{}: (2, {})} | custom-call | flops 1073741824 | bytes 12582912 | tf_op jit(solution)/shard_map/pallas_call | solution.py:162
  (36 shorter events, 2.7 us)
Async XLA Ops:
  8.1 3.4 %copy-start = (s32[8,8,32,1024]{3,2,1,0:T(8,128)}, s32[8,8,32,1024]{3,2,1,0:T(8,128)S(1)}, u32[]{:S(2)}) copy-start(s32[8,8,32,1024]{3,2,1,0:T(8,128)S(1)} %copy.58) | copy-start | bytes 25165828
  12.4 25.8 %collective-permute-start = (bf16[2,32,7,1024]{3,1,2,0:T(8,128)(2,1)S(1)}, bf16[2,32,7,1024]{3,1,2,0:T(8,128)(2,1)S(1)}, u32[]{:S(2)}, u32[]{:S(2)}) collective-permute-start(bf16[2,32,7,1024]{3,1,2,0:T(8,128)(2,1)S(1)} %copy.35), channel_id=1, source_target_pairs={{0,1},{2,3},{4,5},{6,7},{8,9},{10,11},{12,13},{14,15},{16,17},{18,... | collective-permute-start | bytes 2752520 | tf_op jit(solution)/shard_map/ppermute | solution.py:17
  39.8 18.1 %copy-start.9 = (bf16[256,2048]{1,0:T(8,128)(2,1)S(1)}, bf16[256,2048]{1,0:T(8,128)(2,1)}, u32[]{:S(2)}) copy-start(bf16[256,2048]{1,0:T(8,128)(2,1)} %constant.18) | copy-start | bytes 3145732
  57.9 13.0 %copy-start.8 = (bf16[256,2048]{1,0:T(8,128)(2,1)S(1)}, bf16[256,2048]{1,0:T(8,128)(2,1)}, u32[]{:S(2)}) copy-start(bf16[256,2048]{1,0:T(8,128)(2,1)} %constant.16) | copy-start | bytes 3145732
  64.7 31.0 %all-to-all-start.1 = ((bf16[16,16,2048]{2,1,0:T(8,128)(2,1)}), bf16[16,16,2048]{2,1,0:T(8,128)(2,1)S(1)}, u32[]{:S(2)}, u32[]{:S(2)}) async-start(bf16[16,16,2048]{2,1,0:T(8,128)(2,1)} %bitcast.12), calls=%async_computation.1 | async-start | bytes 2097152 | tf_op jit(solution)/shard_map/all_to_all | solution.py:225
  77.8 27.6 %copy-start.5 = (s32[512]{0:T(512)S(1)}, s32[512]{0:T(512)}, u32[]{:S(2)}) copy-start(s32[512]{0:T(512)} %param.6) | copy-start | bytes 6148
  95.7 30.0 %all-to-all-start = ((bf16[16,16,2048]{2,1,0:T(8,128)(2,1)}), bf16[16,16,2048]{2,1,0:T(8,128)(2,1)S(1)}, u32[]{:S(2)}, u32[]{:S(2)}) async-start(bf16[16,16,2048]{2,1,0:T(8,128)(2,1)} %bitcast.2), calls=%async_computation | async-start | bytes 2097152 | tf_op jit(solution)/shard_map/all_to_all | solution.py:225
  109.0 27.5 %collective-permute-start.2 = (bf16[32,32,512]{2,1,0:T(8,128)(2,1)S(1)}, bf16[32,32,512]{2,1,0:T(8,128)(2,1)S(1)}, u32[]{:S(2)}, u32[]{:S(2)}) collective-permute-start(bf16[32,32,512]{2,1,0:T(8,128)(2,1)S(1)} %bitcast.85), channel_id=1, source_target_pairs={{0,1},{1,0},{2,3},{3,2},{4,5},{5,4},{6,7},{7,6},{8,9},{9,8},{10,11... | collective-permute-start | bytes 3145736 | tf_op jit(solution)/shard_map/ppermute | solution.py:25
  133.7 28.9 %collective-permute-start.1 = (bf16[32,32,512]{2,1,0:T(8,128)(2,1)S(1)}, bf16[32,32,512]{2,1,0:T(8,128)(2,1)}, u32[]{:S(2)}, u32[]{:S(2)}) collective-permute-start(bf16[32,32,512]{2,1,0:T(8,128)(2,1)S(1)} %bitcast.88), channel_id=1, source_target_pairs={{0,1},{1,0},{2,3},{3,2},{4,5},{5,4},{6,7},{7,6},{8,9},{9,8},{10,11... | collective-permute-start | bytes 3145736 | tf_op jit(solution)/shard_map/ppermute | solution.py:25
  143.6 7.1 %copy-start.7 = (bf16[256,2048]{1,0:T(8,128)(2,1)S(1)}, bf16[256,2048]{1,0:T(8,128)(2,1)}, u32[]{:S(2)}) copy-start(bf16[256,2048]{1,0:T(8,128)(2,1)} %constant.22) | copy-start | bytes 3145732
  157.5 29.8 %all-to-all-start.3 = ((bf16[16,16,2048]{2,1,0:T(8,128)(2,1)}), bf16[16,16,2048]{2,1,0:T(8,128)(2,1)S(1)}, u32[]{:S(2)}, u32[]{:S(2)}) async-start(bf16[16,16,2048]{2,1,0:T(8,128)(2,1)} %bitcast.29), calls=%async_computation.3 | async-start | bytes 2097152 | tf_op jit(solution)/shard_map/all_to_all | solution.py:225
  172.0 7.1 %copy-start.6 = (bf16[256,2048]{1,0:T(8,128)(2,1)S(1)}, bf16[256,2048]{1,0:T(8,128)(2,1)}, u32[]{:S(2)}) copy-start(bf16[256,2048]{1,0:T(8,128)(2,1)} %constant.20) | copy-start | bytes 3145732
  187.3 29.8 %all-to-all-start.2 = ((bf16[16,16,2048]{2,1,0:T(8,128)(2,1)}), bf16[16,16,2048]{2,1,0:T(8,128)(2,1)S(1)}, u32[]{:S(2)}, u32[]{:S(2)}) async-start(bf16[16,16,2048]{2,1,0:T(8,128)(2,1)} %bitcast.21), calls=%async_computation.2 | async-start | bytes 2097152 | tf_op jit(solution)/shard_map/all_to_all | solution.py:225
  200.4 26.2 %collective-permute-start.4 = (bf16[32,32,512]{2,1,0:T(8,128)(2,1)S(1)}, bf16[32,32,512]{2,1,0:T(8,128)(2,1)S(1)}, u32[]{:S(2)}, u32[]{:S(2)}) collective-permute-start(bf16[32,32,512]{2,1,0:T(8,128)(2,1)S(1)} %bitcast.79), channel_id=1, source_target_pairs={{0,1},{1,0},{2,3},{3,2},{4,5},{5,4},{6,7},{7,6},{8,9},{9,8},{10,11... | collective-permute-start | bytes 3145736 | tf_op jit(solution)/shard_map/ppermute | solution.py:25
  225.1 25.7 %collective-permute-start.3 = (bf16[32,32,512]{2,1,0:T(8,128)(2,1)S(1)}, bf16[32,32,512]{2,1,0:T(8,128)(2,1)S(1)}, u32[]{:S(2)}, u32[]{:S(2)}) collective-permute-start(bf16[32,32,512]{2,1,0:T(8,128)(2,1)S(1)} %bitcast.82), channel_id=1, source_target_pairs={{0,1},{1,0},{2,3},{3,2},{4,5},{5,4},{6,7},{7,6},{8,9},{9,8},{10,11... | collective-permute-start | bytes 3145736 | tf_op jit(solution)/shard_map/ppermute | solution.py:25
  226.6 24.2 %copy-start.1 = (bf16[32,32,512]{2,1,0:T(8,128)(2,1)}, bf16[32,32,512]{2,1,0:T(8,128)(2,1)S(1)}, u32[]{:S(2)}) copy-start(bf16[32,32,512]{2,1,0:T(8,128)(2,1)S(1)} %collective-permute-done.4) | copy-start | bytes 3145732
  250.9 1.7 copy-start.3
  259.6 4.0 %copy-start.2 = (bf16[32,32,512]{2,1,0:T(8,128)(2,1)S(1)}, bf16[32,32,512]{2,1,0:T(8,128)(2,1)}, u32[]{:S(2)}) copy-start(bf16[32,32,512]{2,1,0:T(8,128)(2,1)} %copy-done.1) | copy-start | bytes 3145732
  265.2 7.1 %copy-start.4 = (bf16[32,32,512]{2,1,0:T(8,128)(2,1)S(1)}, bf16[32,32,512]{2,1,0:T(8,128)(2,1)}, u32[]{:S(2)}) copy-start(bf16[32,32,512]{2,1,0:T(8,128)(2,1)} %copy-done.3) | copy-start | bytes 3145732

commit v5 on v4

--- a/solution.py
+++ b/solution.py
@@ -6,6 +6,7 @@
 import jax.numpy as jnp
 from jax import lax
 from jax.experimental import pallas as pl
+from jax.experimental.pallas import tpu as pltpu
 from jax.sharding import PartitionSpec as P
 
 epsilon = 1e-06
@@ -56,67 +57,82 @@
     return total.astype(jnp.bfloat16)
 
 
-def fir_store(out_ref, filtered, channels):
-    out_ref[0, 0, :, 0:channels] = filtered[0]
-    out_ref[0, 0, :, channels:] = filtered[1]
-    out_ref[1, 0, :, 0:channels] = filtered[1]
-    out_ref[1, 0, :, channels:] = -filtered[0]
+def fir_store(out_ref, station, filtered, channels):
+    out_ref[0, station, :, 0:channels] = filtered[0]
+    out_ref[0, station, :, channels:] = filtered[1]
+    out_ref[1, station, :, 0:channels] = filtered[1]
+    out_ref[1, station, :, channels:] = -filtered[0]
 
 
 def fir_kernel(taps_ref, frames_ref, out_ref):
     halo = taps_ref.shape[0] - 1
     spectra = frames_ref.shape[2]
     channels = frames_ref.shape[3]
-    filtered = []
-    for part in range(2):
-        frames = frames_ref[part, 0].astype(jnp.float32)
-        extended = jnp.concatenate([jnp.zeros((halo, channels), jnp.float32), frames], axis=0)
-        filtered.append(fir_rows(taps_ref, extended, spectra))
-    fir_store(out_ref, filtered, channels)
+
+    def body(station, carry):
+        filtered = []
+        for part in range(2):
+            frames = frames_ref[part, station].astype(jnp.float32)
+            extended = jnp.concatenate([jnp.zeros((halo, channels), jnp.float32), frames], axis=0)
+            filtered.append(fir_rows(taps_ref, extended, spectra))
+        fir_store(out_ref, station, filtered, channels)
+        return carry
+
+    lax.fori_loop(0, frames_ref.shape[1], body, 0)
 
 
 def fir_edge_kernel(taps_ref, halo_ref, frames_ref, previous_ref, out_ref):
     count = frames_ref.shape[2]
     channels = frames_ref.shape[3]
-    filtered = []
-    for part in range(2):
-        extended = jnp.concatenate(
-            [halo_ref[part, 0].astype(jnp.float32), frames_ref[part, 0].astype(jnp.float32)], axis=0
-        )
-        filtered.append(fir_rows(taps_ref, extended, count))
-    fir_store(out_ref, filtered, channels)
+
+    def body(station, carry):
+        filtered = []
+        for part in range(2):
+            extended = jnp.concatenate(
+                [
+                    halo_ref[part, station].astype(jnp.float32),
+                    frames_ref[part, station].astype(jnp.float32),
+                ],
+                axis=0,
+            )
+            filtered.append(fir_rows(taps_ref, extended, count))
+        fir_store(out_ref, station, filtered, channels)
+        return carry
+
+    lax.fori_loop(0, frames_ref.shape[1], body, 0)
 
 
 def filter_frames(fir_taps, earlier, frames):
     tap_count, channels = fir_taps.shape
     _, stations_local, spectra, _ = frames.shape
     out_shape = jax.ShapeDtypeStruct((2, stations_local, spectra, 2 * channels), jnp.bfloat16)
+    group = 4 if stations_local % 4 == 0 else 1
     whole = pl.pallas_call(
         fir_kernel,
-        grid=(stations_local,),
+        grid=(stations_local // group,),
         in_specs=[
             pl.BlockSpec((tap_count, channels), lambda a: (0, 0)),
-            pl.BlockSpec((2, 1, spectra, channels), lambda a: (0, a, 0, 0)),
+            pl.BlockSpec((2, group, spectra, channels), lambda a: (0, a, 0, 0)),
         ],
-        out_specs=pl.BlockSpec((2, 1, spectra, 2 * channels), lambda a: (0, a, 0, 0)),
+        out_specs=pl.BlockSpec((2, group, spectra, 2 * channels), lambda a: (0, a, 0, 0)),
         out_shape=out_shape,
         cost_estimate=pl.CostEstimate(
             flops=4 * tap_count * frames.size,
             transcendentals=0,
-            bytes_accessed=4 * frames.size + 4 * frames.size,
+            bytes_accessed=2 * frames.size + 4 * frames.size,
         ),
     )(fir_taps, frames)
     edge = 8
     return pl.pallas_call(
         fir_edge_kernel,
-        grid=(stations_local,),
+        grid=(1,),
         in_specs=[
             pl.BlockSpec((tap_count, channels), lambda a: (0, 0)),
-            pl.BlockSpec((2, 1, tap_count - 1, channels), lambda a: (0, a, 0, 0)),
-            pl.BlockSpec((2, 1, edge, channels), lambda a: (0, a, 0, 0)),
+            pl.BlockSpec((2, stations_local, tap_count - 1, channels), lambda a: (0, 0, 0, 0)),
+            pl.BlockSpec((2, stations_local, edge, channels), lambda a: (0, 0, 0, 0)),
             pl.BlockSpec(memory_space=pl.ANY),
         ],
-        out_specs=pl.BlockSpec((2, 1, edge, 2 * channels), lambda a: (0, a, 0, 0)),
+        out_specs=pl.BlockSpec((2, stations_local, edge, 2 * channels), lambda a: (0, 0, 0, 0)),
         out_shape=out_shape,
         input_output_aliases={3: 0},
         cost_estimate=pl.CostEstimate(
@@ -176,6 +192,60 @@
     )(*operands)
 
 
+def correlate_rows_kernel(block_ref, rows_ref, cols_ref, *refs):
+    out_ref = refs[-1]
+    half = cols_ref.shape[1] // 2
+    contract_first = (((0,), (0,)), ((), ()))
+    for index in range(out_ref.shape[1]):
+        rows = rows_ref[index]
+        right = cols_ref[index]
+        swapped = jnp.concatenate([rows[half:], -rows[:half]], axis=0)
+        real_vis = lax.dot_general(rows, right, contract_first, preferred_element_type=jnp.float32)
+        imag_vis = lax.dot_general(swapped, right, contract_first, preferred_element_type=jnp.float32)
+        right = right.astype(jnp.float32)
+        rows = rows.astype(jnp.float32)
+        column_power = jnp.sum(right * right, axis=0, keepdims=True)
+        row_power = jnp.sum(jnp.transpose(rows * rows), axis=1, keepdims=True)
+        scale_row = lax.rsqrt(row_power + epsilon)
+        scale_column = lax.rsqrt(column_power + epsilon)
+        out_ref[0, index] = (real_vis * scale_row * scale_column).astype(out_ref.dtype)
+        out_ref[1, index] = (imag_vis * scale_row * scale_column).astype(out_ref.dtype)
+
+
+def correlate_rows_chunk(right, block, row_count, previous, offset, local_channels):
+    width, depth, stations = right.shape
+    step = 4 if width % 4 == 0 and offset % 4 == 0 else 1
+    in_specs = [
+        pl.BlockSpec((step, depth, row_count), lambda k, b: (k, 0, b[0])),
+        pl.BlockSpec((step, depth, stations), lambda k, b: (k, 0, 0)),
+    ]
+    operands = [block, right, right]
+    aliases = {}
+    if previous is not None:
+        in_specs.append(pl.BlockSpec(memory_space=pl.ANY))
+        operands.append(previous)
+        aliases = {3: 0}
+    grid_spec = pltpu.PrefetchScalarGridSpec(
+        num_scalar_prefetch=1,
+        grid=(width // step,),
+        in_specs=in_specs,
+        out_specs=pl.BlockSpec(
+            (2, step, row_count, stations), lambda k, b: (0, offset // step + k, 0, 0)
+        ),
+    )
+    return pl.pallas_call(
+        correlate_rows_kernel,
+        grid_spec=grid_spec,
+        out_shape=jax.ShapeDtypeStruct((2, local_channels, row_count, stations), jnp.bfloat16),
+        input_output_aliases=aliases,
+        cost_estimate=pl.CostEstimate(
+            flops=4 * width * row_count * depth * stations,
+            transcendentals=width * (row_count + stations),
+            bytes_accessed=2 * (right.size + width * depth * row_count + 2 * width * row_count * stations),
+        ),
+    )(*operands)
+
+
 def per_device(samples, fir_taps, station_order):
     tap_count = fir_taps.shape[0]
     channels = fir_taps.shape[1]
@@ -189,8 +259,8 @@
     chunks = chunk_count(local_channels)
     width = local_channels // chunks
 
-    frames = samples.reshape(2, stations_local, spectra_local, channels)
-    earlier = frames[:, :, spectra_local - (tap_count - 1) :, :].astype(jnp.bfloat16)
+    frames = samples.astype(jnp.bfloat16).reshape(2, stations_local, spectra_local, channels)
+    earlier = frames[:, :, spectra_local - (tap_count - 1) :, :]
     earlier = passed_along(earlier, "blk", 1)
     filtered = filter_frames(fir_taps, earlier, frames)
     filtered = filtered.reshape(2 * stations_local * spectra_local, 2 * channels)
@@ -202,7 +272,14 @@
     selector = selector.reshape(groups, stations_local, stations)
     row_start = lax.axis_index("blk") * row_count
 
+    block_index = jnp.reshape(lax.axis_index("blk"), (1,)).astype(jnp.int32)
+
     def correlate(chunk, gathered, result):
+        if row_count % 128 == 0:
+            right = gathered.reshape(width, -1, stations)
+            return correlate_rows_chunk(
+                right, block_index, row_count, result, chunk * width, local_channels
+            )
         gathered = gathered.reshape(width, 2, -1, stations)
         row_block = lax.dynamic_slice_in_dim(gathered, row_start, row_count, 3)
         direct = jnp.transpose(row_block, (0, 3, 1, 2))

time: 285 us -> 241 us (0.85)
  local copies, waits for them, and re-layouts: 47.2 us -> 24.7 us
  Pallas kernels: 71.1 us -> 51.1 us
  waiting for transfers between devices: 72.6 us -> 83.6 us
  starting transfers between devices: 31.5 us -> 24.9 us
  other arithmetic: 16.8 us -> 13.7 us
    pallas_call x6, Pallas kernels: 71.1 us -> 51.1 us  [the longest x4 29.9 us: correlate_rows_chunk(): pl.pallas_call(correlate_rows_kernel, grid_spec=grid_spec, out_shape=jax....]
    reshape x4 -> x0, local copies, waits for them, and re-layouts: 15.7 us -> none  [correlate(): jnp.concatenate([direct, swapped], axis=1).reshape(width, 2 * row_count, -1)]
    ppermute x1, waiting for transfers between devices: 0.01 us -> 8.37 us  [passed_along(): lax.ppermute(value, axis, [(source, source + steps) for source in range(i...]
    all_to_all x4, waiting for transfers between devices: 48.3 us -> 56.1 us  [per_device(): lax.all_to_all(spectra, 'stn', split_axis=0, concat_axis=0, tiled=True)]
    ppermute x4, starting transfers between devices: 8.53 us -> 1.21 us  [gathered_along(): parts.append(lax.ppermute(value, axis, pairs))]
    unnamed x21 -> x13, local copies, waits for them, and re-layouts: 11.5 us -> 4.5 us
    concatenate x4 -> x0, other arithmetic: 6.11 us -> none  [correlate(): jnp.concatenate([direct, swapped], axis=1).reshape(width, 2 * row_count, -1)]
    ppermute x4, waiting for transfers between devices: 24.2 us -> 19.1 us  [gathered_along(): parts.append(lax.ppermute(value, axis, pairs))]
  transfers between devices with their start and end apart: 9 -> 9, of which waited for: 5 -> 8; matrix products, arithmetic and copies ran while one was open for 25% -> 25% of each run, Pallas kernels for 14% -> 15%
where the time goes in v5:
time: 241 us; the launch traced here: 239 us
  waiting for transfers between devices  83.6 us (35%)
  Pallas kernels  51.1 us (21%)
  matrix products  41.3 us (17%)
  starting transfers between devices  24.9 us (10%)
  local copies, waits for them, and re-layouts  24.7 us (10%)
  other arithmetic  13.7 us (6%)
    all_to_all x4, waiting for transfers between devices, per_device(): lax.all_to_all(spectra, 'stn', split_axis=0, concat_axis=0, tiled=True)  56.1 us
    pallas_call x4, Pallas kernels, correlate_rows_chunk(): pl.pallas_call(correlate_rows_kernel, grid_spec=grid_spec, out_shape=jax....  29.9 us
    dot_general x4, matrix products, per_device(): jnp.einsum('kj,nj->kn', weights[chunk], source, preferred_element_type=jn...  27.1 us
    all_to_all x4, starting transfers between devices, per_device(): lax.all_to_all(spectra, 'stn', split_axis=0, concat_axis=0, tiled=True)  22.4 us
    ppermute x4, waiting for transfers between devices, gathered_along(): parts.append(lax.ppermute(value, axis, pairs))  19.1 us
    reshape x4, local copies, waits for them, and re-layouts, per_device(): turned = turned.reshape(groups, width, 2, stations_local, spectra_local)  17.6 us
    pallas_call x1, Pallas kernels, filter_frames(): pl.pallas_call(fir_kernel, grid=(stations_local // group,), in_specs=[pl....  14.3 us
    dot_general x4, matrix products, per_device(): jnp.einsum('gkias,gar->kisr', turned, selector, preferred_element_type=jn...  14.2 us
  transfers between devices with their start and end apart: 9, of which 8 were waited for; matrix products, arithmetic and copies ran while one was open for 25% of the time, Pallas kernels for 15%

profile of v5, /device:TPU:14, one launch (start us, length us, event | category | flops | bytes accessed | tf_op | source)
XLA Modules:
  0.0 239.5 jit_solution(2840682905778371916)
XLA Ops:
  0.0 3.8 %convert_element_type.40 = bf16[2,32,32768]{2,1,0:T(8,128)(2,1)S(1)} convert(s32[2,32,32768]{2,1,0:T(8,128)} %param.4) | non-fusion elementwise | flops 2097152 | bytes 12582912 | tf_op jit(solution)/shard_map/convert_element_type | solution.py:262
  3.8 2.5 %copy.38 = bf16[8,8,32,1024]{3,2,1,0:T(8,128)(2,1)S(1)} copy(bf16[8,8,32,1024]{3,1,2,0:T(8,128)(2,1)S(1)} %bitcast.72) | data formatting | bytes 8388608
  6.3 2.0 copy-done
  8.3 0.3 slice.20
  8.6 0.6 copy.19
  9.1 1.3 collective-permute-start
  10.4 14.3 %shard_map.46.previous_ref = bf16[2,32,32,2048]{3,2,1,0:T(8,128)(2,1)} custom-call(f32[8,1024]{1,0:T(8,128)} %taps_ref.3, bf16[2,32,32,1024]{3,2,1,0:T(8,128)(2,1)} %bitcast.58), custom_call_target="tpu_custom_call" | custom-call | flops 67108864 | bytes 12582912 | tf_op jit(solution)/shard_map/pallas_call | solution.py:110
  24.7 8.4 %collective-permute-done = bf16[2,32,7,1024]{3,1,2,0:T(8,128)(2,1)S(1)} collective-permute-done((bf16[2,32,7,1024]{3,1,2,0:T(8,128)(2,1)S(1)}, bf16[2,32,7,1024]{3,1,2,0:T(8,128)(2,1)S(1)}, u32[]{:S(2)}, u32[]{:S(2)}) %collective-permute-start) | collective-permute-done | bytes 917536 | tf_op jit(solution)/shard_map/ppermute | solution.py:18
  33.1 1.6 copy.20.halo_ref
  34.7 6.8 %shard_map.47 = bf16[2,32,32,2048]{3,2,1,0:T(8,128)(2,1)} custom-call(f32[8,1024]{1,0:T(8,128)} %taps_ref.3, bf16[2,32,7,1024]{3,2,1,0:T(8,128)(2,1)} %copy.20.halo_ref, bf16[2,32,32,1024]{3,2,1,0:T(8,128)(2,1)} %bitcast.59, bf16[2,32,32,2048]{3,2,1,0:T(8,128)(2,1)} %shard_map.46.previous_ref), custom_call_target="tpu_custom_call", output_to_operand_aliasing={{}: (3, {})} | custom-call | flops 16777216 | bytes 4194304 | tf_op jit(solution)/shard_map/pallas_call | solution.py:126
  41.5 6.8 %convolution_convert_fusion.2 = bf16[2048,256]{0,1:T(8,128)(2,1)} fusion(bf16[2048,2048]{1,0:T(8,128)(2,1)} %bitcast.60, bf16[256,2048]{1,0:T(8,128)(2,1)S(1)} %copy-done.5), kind=kOutput, calls=%fused_computation.10 | convolution fusion | flops 2148007936 | bytes 10485760 | tf_op jit(solution)/shard_map/kj,nj->kn/dot_general | solution.py:298
  48.3 6.2 %all-to-all-start.1 = ((bf16[16,16,2048]{2,1,0:T(8,128)(2,1)}), bf16[16,16,2048]{2,1,0:T(8,128)(2,1)S(1)}, u32[]{:S(2)}, u32[]{:S(2)}) async-start(bf16[16,16,2048]{2,1,0:T(8,128)(2,1)} %bitcast.10), calls=%async_computation.1 | async-start | bytes 2097152 | tf_op jit(solution)/shard_map/all_to_all | solution.py:302
  54.5 6.8 %convolution_convert_fusion.3 = bf16[2048,256]{0,1:T(8,128)(2,1)} fusion(bf16[2048,2048]{1,0:T(8,128)(2,1)} %bitcast.61, bf16[256,2048]{1,0:T(8,128)(2,1)S(1)} %copy-done.4), kind=kOutput, calls=%fused_computation.11 | convolution fusion | flops 2148007936 | bytes 10485760 | tf_op jit(solution)/shard_map/kj,nj->kn/dot_general | solution.py:298
  61.3 17.9 %all-to-all-done.1 = bf16[16,16,2048]{2,1,0:T(8,128)(2,1)S(1)} async-done(((bf16[16,16,2048]{2,1,0:T(8,128)(2,1)}), bf16[16,16,2048]{2,1,0:T(8,128)(2,1)S(1)}, u32[]{:S(2)}, u32[]{:S(2)}) %all-to-all-start.1) | async-done | bytes 1048608 | tf_op jit(solution)/shard_map/all_to_all | solution.py:302
  79.3 5.1 %all-to-all-start = ((bf16[16,16,2048]{2,1,0:T(8,128)(2,1)}), bf16[16,16,2048]{2,1,0:T(8,128)(2,1)S(1)}, u32[]{:S(2)}, u32[]{:S(2)}) async-start(bf16[16,16,2048]{2,1,0:T(8,128)(2,1)} %bitcast.3), calls=%async_computation | async-start | bytes 2097152 | tf_op jit(solution)/shard_map/all_to_all | solution.py:302
  84.4 4.4 %reshape.81 = bf16[16,16,2,32,32]{4,3,2,1,0:T(8,128)(2,1)} reshape(bf16[16,16,2048]{2,1,0:T(8,128)(2,1)S(1)} %all-to-all-done.1) | data formatting | bytes 2097152 | tf_op jit(solution)/shard_map/reshape | solution.py:303
  88.7 3.6 %fusion.4 = bf16[16,2,32,512,1]{3,2,0,1,4:T(8,128)(2,1)S(1)} fusion(bf16[16,16,2,32,32]{4,3,2,1,0:T(8,128)(2,1)} %reshape.81, s32[16,32]{1,0:T(8,128)S(1)} %multiply_add_fusion, s32[512]{0:T(512)S(1)} %copy-done.1), kind=kOutput, calls=%fused_computation.4 | convolution fusion | flops 537133056 | bytes 2101248 | tf_op jit(solution)/shard_map/gkias,gar->kisr/dot_general | solution.py:304
  92.3 0.1 copy.53
  92.4 0.1 collective-permute-start.2
  92.5 16.6 %all-to-all-done = bf16[16,16,2048]{2,1,0:T(8,128)(2,1)S(1)} async-done(((bf16[16,16,2048]{2,1,0:T(8,128)(2,1)}), bf16[16,16,2048]{2,1,0:T(8,128)(2,1)S(1)}, u32[]{:S(2)}, u32[]{:S(2)}) %all-to-all-start) | async-done | bytes 1048608 | tf_op jit(solution)/shard_map/all_to_all | solution.py:302
  109.1 4.4 %reshape.77 = bf16[16,16,2,32,32]{4,3,2,1,0:T(8,128)(2,1)} reshape(bf16[16,16,2048]{2,1,0:T(8,128)(2,1)S(1)} %all-to-all-done) | data formatting | bytes 2097152 | tf_op jit(solution)/shard_map/reshape | solution.py:303
  113.4 3.6 %fusion.6 = bf16[16,2,32,512,1]{3,2,0,1,4:T(8,128)(2,1)S(1)} fusion(bf16[16,16,2,32,32]{4,3,2,1,0:T(8,128)(2,1)} %reshape.77, s32[16,32]{1,0:T(8,128)S(1)} %multiply_add_fusion, s32[512]{0:T(512)S(1)} %copy-done.1), kind=kOutput, calls=%fused_computation.6 | convolution fusion | flops 537133056 | bytes 2101248 | tf_op jit(solution)/shard_map/gkias,gar->kisr/dot_general | solution.py:304
  117.0 0.1 copy.54
  117.2 0.6 collective-permute-done.2
  117.8 2.8 %pad_maximum_fusion.1 = bf16[32,64,512]{2,1,0:T(8,128)(2,1)} fusion(bf16[32,32,512]{2,1,0:T(8,128)(2,1)} %collective-permute-done.2, bf16[32,32,512]{2,1,0:T(8,128)(2,1)S(1)} %bitcast.74), kind=kLoop, calls=%fused_computation.13 | loop fusion | flops 4194304 | bytes 4194304 | tf_op jit(solution)/shard_map/concatenate | solution.py:27
  120.6 7.5 %shard_map.48.refs_0_ = bf16[2,64,256,512]{3,2,1,0:T(8,128)(2,1)} custom-call(s32[1]{0:T(128)} %bitcast.block_ref, bf16[16,128,512]{2,1,0:T(8,128)(2,1)} %bitcast.64, bf16[16,128,512]{2,1,0:T(8,128)(2,1)} %bitcast.65), custom_call_target="tpu_custom_call" | custom-call | flops 1073741824 | bytes 11534336 | tf_op jit(solution)/shard_map/pallas_call | solution.py:236
  128.1 6.7 %convolution_convert_fusion = bf16[2048,256]{0,1:T(8,128)(2,1)} fusion(bf16[2048,2048]{1,0:T(8,128)(2,1)} %bitcast.62, bf16[256,2048]{1,0:T(8,128)(2,1)S(1)} %copy-done.3), kind=kOutput, calls=%fused_computation.8 | convolution fusion | flops 2148007936 | bytes 10485760 | tf_op jit(solution)/shard_map/kj,nj->kn/dot_general | solution.py:298
  134.8 6.0 %all-to-all-start.3 = ((bf16[16,16,2048]{2,1,0:T(8,128)(2,1)}), bf16[16,16,2048]{2,1,0:T(8,128)(2,1)S(1)}, u32[]{:S(2)}, u32[]{:S(2)}) async-start(bf16[16,16,2048]{2,1,0:T(8,128)(2,1)} %bitcast.21), calls=%async_computation.3 | async-start | bytes 2097152 | tf_op jit(solution)/shard_map/all_to_all | solution.py:302
  140.8 2.2 collective-permute-done.1
  143.0 2.8 %pad_maximum_fusion = bf16[32,64,512]{2,1,0:T(8,128)(2,1)} fusion(bf16[32,32,512]{2,1,0:T(8,128)(2,1)} %collective-permute-done.1, bf16[32,32,512]{2,1,0:T(8,128)(2,1)S(1)} %bitcast.78), kind=kLoop, calls=%fused_computation.12 | loop fusion | flops 4194304 | bytes 4194304 | tf_op jit(solution)/shard_map/concatenate | solution.py:27
  145.8 7.5 %shard_map.49.refs_0_ = bf16[2,64,256,512]{3,2,1,0:T(8,128)(2,1)} custom-call(s32[1]{0:T(128)} %bitcast.block_ref, bf16[16,128,512]{2,1,0:T(8,128)(2,1)} %bitcast.68, bf16[16,128,512]{2,1,0:T(8,128)(2,1)} %bitcast.69, bf16[2,64,256,512]{3,2,1,0:T(8,128)(2,1)} %shard_map.48.refs_0_), custom_call_target="tpu_custom_call", output_to_operand_aliasing={{}: (3, {})} | custom-call | flops 1073741824 | bytes 11534336 | tf_op jit(solution)/shard_map/pallas_call | solution.py:236
  153.3 6.8 %convolution_convert_fusion.1 = bf16[2048,256]{0,1:T(8,128)(2,1)} fusion(bf16[2048,2048]{1,0:T(8,128)(2,1)} %bitcast.63, bf16[256,2048]{1,0:T(8,128)(2,1)S(1)} %copy-done.2), kind=kOutput, calls=%fused_computation.9 | convolution fusion | flops 2148007936 | bytes 10485760 | tf_op jit(solution)/shard_map/kj,nj->kn/dot_general | solution.py:298
  160.1 5.4 %all-to-all-done.3 = bf16[16,16,2048]{2,1,0:T(8,128)(2,1)S(1)} async-done(((bf16[16,16,2048]{2,1,0:T(8,128)(2,1)}), bf16[16,16,2048]{2,1,0:T(8,128)(2,1)S(1)}, u32[]{:S(2)}, u32[]{:S(2)}) %all-to-all-start.3) | async-done | bytes 1048608 | tf_op jit(solution)/shard_map/all_to_all | solution.py:302
  165.6 5.1 %all-to-all-start.2 = ((bf16[16,16,2048]{2,1,0:T(8,128)(2,1)}), bf16[16,16,2048]{2,1,0:T(8,128)(2,1)S(1)}, u32[]{:S(2)}, u32[]{:S(2)}) async-start(bf16[16,16,2048]{2,1,0:T(8,128)(2,1)} %bitcast.16), calls=%async_computation.2 | async-start | bytes 2097152 | tf_op jit(solution)/shard_map/all_to_all | solution.py:302
  170.7 4.4 %reshape.89 = bf16[16,16,2,32,32]{4,3,2,1,0:T(8,128)(2,1)} reshape(bf16[16,16,2048]{2,1,0:T(8,128)(2,1)S(1)} %all-to-all-done.3) | data formatting | bytes 2097152 | tf_op jit(solution)/shard_map/reshape | solution.py:303
  175.1 3.6 %fusion = bf16[16,2,32,512,1]{3,2,0,1,4:T(8,128)(2,1)S(1)} fusion(bf16[16,16,2,32,32]{4,3,2,1,0:T(8,128)(2,1)} %reshape.89, s32[16,32]{1,0:T(8,128)S(1)} %multiply_add_fusion, s32[512]{0:T(512)S(1)} %copy-done.1), kind=kOutput, calls=%fused_computation | convolution fusion | flops 537133056 | bytes 2101248 | tf_op jit(solution)/shard_map/gkias,gar->kisr/dot_general | solution.py:304
  178.6 0.1 copy.51
  178.7 0.5 collective-permute-start.4
  179.3 16.1 %all-to-all-done.2 = bf16[16,16,2048]{2,1,0:T(8,128)(2,1)S(1)} async-done(((bf16[16,16,2048]{2,1,0:T(8,128)(2,1)}), bf16[16,16,2048]{2,1,0:T(8,128)(2,1)S(1)}, u32[]{:S(2)}, u32[]{:S(2)}) %all-to-all-start.2) | async-done | bytes 1048608 | tf_op jit(solution)/shard_map/all_to_all | solution.py:302
  195.4 4.4 %reshape.85 = bf16[16,16,2,32,32]{4,3,2,1,0:T(8,128)(2,1)} reshape(bf16[16,16,2048]{2,1,0:T(8,128)(2,1)S(1)} %all-to-all-done.2) | data formatting | bytes 2097152 | tf_op jit(solution)/shard_map/reshape | solution.py:303
  199.8 3.6 %fusion.2 = bf16[16,2,32,512,1]{3,2,0,1,4:T(8,128)(2,1)S(1)} fusion(bf16[16,16,2,32,32]{4,3,2,1,0:T(8,128)(2,1)} %reshape.85, s32[16,32]{1,0:T(8,128)S(1)} %multiply_add_fusion, s32[512]{0:T(512)S(1)} %copy-done.1), kind=kOutput, calls=%fused_computation.2 | convolution fusion | flops 537133056 | bytes 2101248 | tf_op jit(solution)/shard_map/gkias,gar->kisr/dot_general | solution.py:304
  203.4 0.1 copy.52
  203.4 0.5 collective-permute-start.3
  204.0 1.5 pad_maximum_fusion.3
  205.5 7.4 %shard_map.50.refs_0_ = bf16[2,64,256,512]{3,2,1,0:T(8,128)(2,1)} custom-call(s32[1]{0:T(128)} %bitcast.block_ref, bf16[16,128,512]{2,1,0:T(8,128)(2,1)} %bitcast.70, bf16[16,128,512]{2,1,0:T(8,128)(2,1)} %bitcast.71, bf16[2,64,256,512]{3,2,1,0:T(8,128)(2,1)} %shard_map.49.refs_0_), custom_call_target="tpu_custom_call", output_to_operand_aliasing={{}: (3, {})} | custom-call | flops 1073741824 | bytes 11534336 | tf_op jit(solution)/shard_map/pallas_call | solution.py:236
  213.0 16.3 %collective-permute-done.3 = bf16[32,32,512]{2,1,0:T(8,128)(2,1)} collective-permute-done((bf16[32,32,512]{2,1,0:T(8,128)(2,1)S(1)}, bf16[32,32,512]{2,1,0:T(8,128)(2,1)}, u32[]{:S(2)}, u32[]{:S(2)}) %collective-permute-start.3) | collective-permute-done | bytes 1048608 | tf_op jit(solution)/shard_map/ppermute | solution.py:26
  229.3 2.7 %pad_maximum_fusion.2 = bf16[32,64,512]{2,1,0:T(8,128)(2,1)} fusion(bf16[32,32,512]{2,1,0:T(8,128)(2,1)} %collective-permute-done.3, bf16[32,32,512]{2,1,0:T(8,128)(2,1)S(1)} %bitcast.80), kind=kLoop, calls=%fused_computation.14 | loop fusion | flops 4194304 | bytes 4194304 | tf_op jit(solution)/shard_map/concatenate | solution.py:27
  232.0 7.5 %shard_map.51 = bf16[2,64,256,512]{3,2,1,0:T(8,128)(2,1)} custom-call(s32[1]{0:T(128)} %bitcast.block_ref, bf16[16,128,512]{2,1,0:T(8,128)(2,1)} %bitcast.66, bf16[16,128,512]{2,1,0:T(8,128)(2,1)} %bitcast.67, bf16[2,64,256,512]{3,2,1,0:T(8,128)(2,1)} %shard_map.50.refs_0_), custom_call_target="tpu_custom_call", output_to_operand_aliasing={{}: (3, {})} | custom-call | flops 1073741824 | bytes 11534336 | tf_op jit(solution)/shard_map/pallas_call | solution.py:236
  (14 shorter events, 0.1 us)
Async XLA Ops:
  6.3 2.0 copy-start
  9.1 24.0 %collective-permute-start = (bf16[2,32,7,1024]{3,1,2,0:T(8,128)(2,1)S(1)}, bf16[2,32,7,1024]{3,1,2,0:T(8,128)(2,1)S(1)}, u32[]{:S(2)}, u32[]{:S(2)}) collective-permute-start(bf16[2,32,7,1024]{3,1,2,0:T(8,128)(2,1)S(1)} %copy.19), channel_id=1, source_target_pairs={{0,1},{2,3},{4,5},{6,7},{8,9},{10,11},{12,13},{14,15},{16,17},{18,... | collective-permute-start | bytes 2752520 | tf_op jit(solution)/shard_map/ppermute | solution.py:18
  34.7 6.8 %copy-start.5 = (bf16[256,2048]{1,0:T(8,128)(2,1)S(1)}, bf16[256,2048]{1,0:T(8,128)(2,1)}, u32[]{:S(2)}) copy-start(bf16[256,2048]{1,0:T(8,128)(2,1)} %constant.12) | copy-start | bytes 3145732
  41.5 13.1 %copy-start.4 = (bf16[256,2048]{1,0:T(8,128)(2,1)S(1)}, bf16[256,2048]{1,0:T(8,128)(2,1)}, u32[]{:S(2)}) copy-start(bf16[256,2048]{1,0:T(8,128)(2,1)} %constant.10) | copy-start | bytes 3145732
  48.3 31.0 %all-to-all-start.1 = ((bf16[16,16,2048]{2,1,0:T(8,128)(2,1)}), bf16[16,16,2048]{2,1,0:T(8,128)(2,1)S(1)}, u32[]{:S(2)}, u32[]{:S(2)}) async-start(bf16[16,16,2048]{2,1,0:T(8,128)(2,1)} %bitcast.10), calls=%async_computation.1 | async-start | bytes 2097152 | tf_op jit(solution)/shard_map/all_to_all | solution.py:302
  61.3 27.4 %copy-start.1 = (s32[512]{0:T(512)S(1)}, s32[512]{0:T(512)}, u32[]{:S(2)}) copy-start(s32[512]{0:T(512)} %param.6) | copy-start | bytes 6148
  79.3 29.8 %all-to-all-start = ((bf16[16,16,2048]{2,1,0:T(8,128)(2,1)}), bf16[16,16,2048]{2,1,0:T(8,128)(2,1)S(1)}, u32[]{:S(2)}, u32[]{:S(2)}) async-start(bf16[16,16,2048]{2,1,0:T(8,128)(2,1)} %bitcast.3), calls=%async_computation | async-start | bytes 2097152 | tf_op jit(solution)/shard_map/all_to_all | solution.py:302
  92.4 25.4 %collective-permute-start.2 = (bf16[32,32,512]{2,1,0:T(8,128)(2,1)S(1)}, bf16[32,32,512]{2,1,0:T(8,128)(2,1)}, u32[]{:S(2)}, u32[]{:S(2)}) collective-permute-start(bf16[32,32,512]{2,1,0:T(8,128)(2,1)S(1)} %bitcast.73), channel_id=1, source_target_pairs={{0,1},{1,0},{2,3},{3,2},{4,5},{5,4},{6,7},{7,6},{8,9},{9,8},{10,11... | collective-permute-start | bytes 3145736 | tf_op jit(solution)/shard_map/ppermute | solution.py:26
  117.1 25.9 %collective-permute-start.1 = (bf16[32,32,512]{2,1,0:T(8,128)(2,1)S(1)}, bf16[32,32,512]{2,1,0:T(8,128)(2,1)}, u32[]{:S(2)}, u32[]{:S(2)}) collective-permute-start(bf16[32,32,512]{2,1,0:T(8,128)(2,1)S(1)} %bitcast.77), channel_id=1, source_target_pairs={{0,1},{1,0},{2,3},{3,2},{4,5},{5,4},{6,7},{7,6},{8,9},{9,8},{10,11... | collective-permute-start | bytes 3145736 | tf_op jit(solution)/shard_map/ppermute | solution.py:26
  120.6 7.5 %copy-start.3 = (bf16[256,2048]{1,0:T(8,128)(2,1)S(1)}, bf16[256,2048]{1,0:T(8,128)(2,1)}, u32[]{:S(2)}) copy-start(bf16[256,2048]{1,0:T(8,128)(2,1)} %constant.16) | copy-start | bytes 3145732
  134.8 30.7 %all-to-all-start.3 = ((bf16[16,16,2048]{2,1,0:T(8,128)(2,1)}), bf16[16,16,2048]{2,1,0:T(8,128)(2,1)S(1)}, u32[]{:S(2)}, u32[]{:S(2)}) async-start(bf16[16,16,2048]{2,1,0:T(8,128)(2,1)} %bitcast.21), calls=%async_computation.3 | async-start | bytes 2097152 | tf_op jit(solution)/shard_map/all_to_all | solution.py:302
  145.8 7.5 %copy-start.2 = (bf16[256,2048]{1,0:T(8,128)(2,1)S(1)}, bf16[256,2048]{1,0:T(8,128)(2,1)}, u32[]{:S(2)}) copy-start(bf16[256,2048]{1,0:T(8,128)(2,1)} %constant.14) | copy-start | bytes 3145732
  165.6 29.8 %all-to-all-start.2 = ((bf16[16,16,2048]{2,1,0:T(8,128)(2,1)}), bf16[16,16,2048]{2,1,0:T(8,128)(2,1)S(1)}, u32[]{:S(2)}, u32[]{:S(2)}) async-start(bf16[16,16,2048]{2,1,0:T(8,128)(2,1)} %bitcast.16), calls=%async_computation.2 | async-start | bytes 2097152 | tf_op jit(solution)/shard_map/all_to_all | solution.py:302
  178.7 25.3 %collective-permute-start.4 = (bf16[32,32,512]{2,1,0:T(8,128)(2,1)S(1)}, bf16[32,32,512]{2,1,0:T(8,128)(2,1)S(1)}, u32[]{:S(2)}, u32[]{:S(2)}) collective-permute-start(bf16[32,32,512]{2,1,0:T(8,128)(2,1)S(1)} %bitcast.75), channel_id=1, source_target_pairs={{0,1},{1,0},{2,3},{3,2},{4,5},{5,4},{6,7},{7,6},{8,9},{9,8},{10,11... | collective-permute-start | bytes 3145736 | tf_op jit(solution)/shard_map/ppermute | solution.py:26
  203.4 25.8 %collective-permute-start.3 = (bf16[32,32,512]{2,1,0:T(8,128)(2,1)S(1)}, bf16[32,32,512]{2,1,0:T(8,128)(2,1)}, u32[]{:S(2)}, u32[]{:S(2)}) collective-permute-start(bf16[32,32,512]{2,1,0:T(8,128)(2,1)S(1)} %bitcast.79), channel_id=1, source_target_pairs={{0,1},{1,0},{2,3},{3,2},{4,5},{5,4},{6,7},{7,6},{8,9},{9,8},{10,11... | collective-permute-start | bytes 3145736 | tf_op jit(solution)/shard_map/ppermute | solution.py:26

commit v6 on v5

--- a/solution.py
+++ b/solution.py
@@ -18,13 +18,13 @@
     return lax.ppermute(value, axis, [(source, source + steps) for source in range(initial, last)])
 
 
-def gathered_along(value, axis, dimension):
+def gathered_along(value, axis):
     count = lax.axis_size(axis)
     parts = [value]
     for shift in range(1, count):
         pairs = [(source, (source + shift) % count) for source in range(count)]
         parts.append(lax.ppermute(value, axis, pairs))
-    return jnp.concatenate(parts, axis=dimension)
+    return parts
 
 
 def chunk_count(local_channels):
@@ -123,16 +123,17 @@
         ),
     )(fir_taps, frames)
     edge = 8
+    edge_group = stations_local // 4 if stations_local % 4 == 0 else stations_local
     return pl.pallas_call(
         fir_edge_kernel,
-        grid=(1,),
+        grid=(stations_local // edge_group,),
         in_specs=[
             pl.BlockSpec((tap_count, channels), lambda a: (0, 0)),
-            pl.BlockSpec((2, stations_local, tap_count - 1, channels), lambda a: (0, 0, 0, 0)),
-            pl.BlockSpec((2, stations_local, edge, channels), lambda a: (0, 0, 0, 0)),
+            pl.BlockSpec((2, edge_group, tap_count - 1, channels), lambda a: (0, a, 0, 0)),
+            pl.BlockSpec((2, edge_group, edge, channels), lambda a: (0, a, 0, 0)),
             pl.BlockSpec(memory_space=pl.ANY),
         ],
-        out_specs=pl.BlockSpec((2, stations_local, edge, 2 * channels), lambda a: (0, 0, 0, 0)),
+        out_specs=pl.BlockSpec((2, edge_group, edge, 2 * channels), lambda a: (0, a, 0, 0)),
         out_shape=out_shape,
         input_output_aliases={3: 0},
         cost_estimate=pl.CostEstimate(
@@ -192,13 +193,20 @@
     )(*operands)
 
 
-def correlate_rows_kernel(block_ref, rows_ref, cols_ref, *refs):
+def correlate_rows_kernel(block_ref, *refs):
     out_ref = refs[-1]
-    half = cols_ref.shape[1] // 2
+    pieces = (len(refs) - 1) // 2
+    rows_refs = refs[0:pieces]
+    cols_refs = refs[pieces : 2 * pieces]
     contract_first = (((0,), (0,)), ((), ()))
     for index in range(out_ref.shape[1]):
-        rows = rows_ref[index]
-        right = cols_ref[index]
+        rows = jnp.concatenate(
+            [ref[index, part] for part in range(2) for ref in rows_refs], axis=0
+        )
+        right = jnp.concatenate(
+            [ref[index, part] for part in range(2) for ref in cols_refs], axis=0
+        )
+        half = rows.shape[0] // 2
         swapped = jnp.concatenate([rows[half:], -rows[:half]], axis=0)
         real_vis = lax.dot_general(rows, right, contract_first, preferred_element_type=jnp.float32)
         imag_vis = lax.dot_general(swapped, right, contract_first, preferred_element_type=jnp.float32)
@@ -212,19 +220,18 @@
         out_ref[1, index] = (imag_vis * scale_row * scale_column).astype(out_ref.dtype)
 
 
-def correlate_rows_chunk(right, block, row_count, previous, offset, local_channels):
-    width, depth, stations = right.shape
+def correlate_rows_chunk(parts, block, row_count, previous, offset, local_channels):
+    width, _, spectra, stations = parts[0].shape
     step = 4 if width % 4 == 0 and offset % 4 == 0 else 1
-    in_specs = [
-        pl.BlockSpec((step, depth, row_count), lambda k, b: (k, 0, b[0])),
-        pl.BlockSpec((step, depth, stations), lambda k, b: (k, 0, 0)),
-    ]
-    operands = [block, right, right]
+    rows_spec = pl.BlockSpec((step, 2, spectra, row_count), lambda k, b: (k, 0, 0, b[0]))
+    cols_spec = pl.BlockSpec((step, 2, spectra, stations), lambda k, b: (k, 0, 0, 0))
+    in_specs = [rows_spec] * len(parts) + [cols_spec] * len(parts)
+    operands = [block] + list(parts) + list(parts)
     aliases = {}
     if previous is not None:
         in_specs.append(pl.BlockSpec(memory_space=pl.ANY))
         operands.append(previous)
-        aliases = {3: 0}
+        aliases = {len(operands) - 1: 0}
     grid_spec = pltpu.PrefetchScalarGridSpec(
         num_scalar_prefetch=1,
         grid=(width // step,),
@@ -233,6 +240,7 @@
             (2, step, row_count, stations), lambda k, b: (0, offset // step + k, 0, 0)
         ),
     )
+    depth = 2 * spectra * len(parts)
     return pl.pallas_call(
         correlate_rows_kernel,
         grid_spec=grid_spec,
@@ -241,7 +249,8 @@
         cost_estimate=pl.CostEstimate(
             flops=4 * width * row_count * depth * stations,
             transcendentals=width * (row_count + stations),
-            bytes_accessed=2 * (right.size + width * depth * row_count + 2 * width * row_count * stations),
+            bytes_accessed=2 * width * depth * (stations + row_count)
+            + 4 * width * row_count * stations,
         ),
     )(*operands)
 
@@ -259,8 +268,9 @@
     chunks = chunk_count(local_channels)
     width = local_channels // chunks
 
+    earlier = samples[:, :, (spectra_local - (tap_count - 1)) * channels :].astype(jnp.bfloat16)
+    earlier = earlier.reshape(2, stations_local, tap_count - 1, channels)
     frames = samples.astype(jnp.bfloat16).reshape(2, stations_local, spectra_local, channels)
-    earlier = frames[:, :, spectra_local - (tap_count - 1) :, :]
     earlier = passed_along(earlier, "blk", 1)
     filtered = filter_frames(fir_taps, earlier, frames)
     filtered = filtered.reshape(2 * stations_local * spectra_local, 2 * channels)
@@ -274,13 +284,13 @@
 
     block_index = jnp.reshape(lax.axis_index("blk"), (1,)).astype(jnp.int32)
 
-    def correlate(chunk, gathered, result):
+    def correlate(chunk, parts, result):
+        parts = [part.reshape(width, 2, spectra_local, stations) for part in parts]
         if row_count % 128 == 0:
-            right = gathered.reshape(width, -1, stations)
             return correlate_rows_chunk(
-                right, block_index, row_count, result, chunk * width, local_channels
+                parts, block_index, row_count, result, chunk * width, local_channels
             )
-        gathered = gathered.reshape(width, 2, -1, stations)
+        gathered = jnp.concatenate(parts, axis=2)
         row_block = lax.dynamic_slice_in_dim(gathered, row_start, row_count, 3)
         direct = jnp.transpose(row_block, (0, 3, 1, 2))
         swapped = jnp.stack([direct[:, :, 1], -direct[:, :, 0]], axis=2)
@@ -305,7 +315,7 @@
             "gkias,gar->kisr", turned, selector, preferred_element_type=jnp.float32
         ).astype(jnp.bfloat16)
         ordered = ordered.reshape(width * 2, spectra_local, stations)
-        pending.append(gathered_along(ordered, "blk", 1))
+        pending.append(gathered_along(ordered, "blk"))
     for chunk in range(max(0, chunks - 2), chunks):
         result = correlate(chunk, pending[chunk], result)
     return result

time: 241 us -> 251 us (1.041)
  waiting for transfers between devices: 83.6 us -> 101 us
  other arithmetic: 13.7 us -> 3.8 us
    ppermute x4, waiting for transfers between devices: 19.1 us -> 46.2 us  [gathered_along(): parts.append(lax.ppermute(value, axis, pairs))]
    concatenate x4 -> x0, other arithmetic: 9.86 us -> none  [gathered_along(): return jnp.concatenate(parts, axis=dimension)]
    all_to_all x4, waiting for transfers between devices: 56.1 us -> 50.8 us  [per_device(): lax.all_to_all(spectra, 'stn', split_axis=0, concat_axis=0, tiled=True)]
    ppermute x1, waiting for transfers between devices: 8.37 us -> 3.87 us  [passed_along(): lax.ppermute(value, axis, [(source, source + steps) for source in range(i...]
    another operation x0 -> x1, other arithmetic: none -> 3.79 us
    convert_element_type x1 -> x0, other arithmetic: 3.79 us -> none  [per_device(): samples.astype(jnp.bfloat16)]
    unnamed x13 -> x23, local copies, waits for them, and re-layouts: 4.5 us -> 7.48 us
  transfers between devices with their start and end apart: 9 -> 9, of which waited for: 8 -> 8; matrix products, arithmetic and copies ran while one was open for 25% -> 20% of each run, Pallas kernels for 15% -> 12%
where the time goes in v6:
time: 251 us; the launch traced here: 249 us
  waiting for transfers between devices  101 us (40%)
  Pallas kernels  49.8 us (20%)
  matrix products  41.6 us (17%)
  local copies, waits for them, and re-layouts  27.1 us (11%)
  starting transfers between devices  25.8 us (10%)
  other arithmetic  3.8 us (2%)
    all_to_all x4, waiting for transfers between devices, per_device(): lax.all_to_all(spectra, 'stn', split_axis=0, concat_axis=0, tiled=True)  50.8 us
    ppermute x4, waiting for transfers between devices, gathered_along(): parts.append(lax.ppermute(value, axis, pairs))  46.2 us
    pallas_call x4, Pallas kernels, correlate_rows_chunk(): pl.pallas_call(correlate_rows_kernel, grid_spec=grid_spec, out_shape=jax....  29.4 us
    dot_general x4, matrix products, per_device(): jnp.einsum('kj,nj->kn', weights[chunk], source, preferred_element_type=jn...  27.4 us
    all_to_all x4, starting transfers between devices, per_device(): lax.all_to_all(spectra, 'stn', split_axis=0, concat_axis=0, tiled=True)  23.4 us
    reshape x4, local copies, waits for them, and re-layouts, per_device(): turned = turned.reshape(groups, width, 2, stations_local, spectra_local)  17.6 us
    pallas_call x1, Pallas kernels, filter_frames(): pl.pallas_call(fir_kernel, grid=(stations_local // group,), in_specs=[pl....  14.3 us
    dot_general x4, matrix products, per_device(): jnp.einsum('gkias,gar->kisr', turned, selector, preferred_element_type=jn...  14.2 us
  transfers between devices with their start and end apart: 9, of which 8 were waited for; matrix products, arithmetic and copies ran while one was open for 20% of the time, Pallas kernels for 12%

profile of v6, /device:TPU:14, one launch (start us, length us, event | category | flops | bytes accessed | tf_op | source)
XLA Modules:
  0.0 249.3 jit_solution(2422251038422725724)
XLA Ops:
  0.0 3.8 %convert.3 = bf16[2,32,32768]{2,1,0:T(8,128)(2,1)S(1)} convert(s32[2,32,32768]{2,1,0:T(8,128)} %param.4) | non-fusion elementwise | flops 2097152 | bytes 12582912 | tf_op jit(solution)/shard_map/convert
  3.8 0.1 slice.21
  3.9 0.1 copy.59
  4.0 1.3 collective-permute-start
  5.3 4.5 %copy.33 = bf16[8,8,32,1024]{3,2,1,0:T(8,128)(2,1)} copy(bf16[8,8,32,1024]{3,1,2,0:T(8,128)(2,1)S(1)} %bitcast.63) | data formatting | bytes 8388608
  9.7 14.3 %shard_map.46.previous_ref = bf16[2,32,32,2048]{3,2,1,0:T(8,128)(2,1)} custom-call(f32[8,1024]{1,0:T(8,128)} %taps_ref.3, bf16[2,32,32,1024]{3,2,1,0:T(8,128)(2,1)} %bitcast.57), custom_call_target="tpu_custom_call" | custom-call | flops 67108864 | bytes 12582912 | tf_op jit(solution)/shard_map/pallas_call | solution.py:110
  24.1 3.9 %collective-permute-done = bf16[2,32,7,1024]{3,1,2,0:T(8,128)(2,1)S(1)} collective-permute-done((bf16[2,32,7,1024]{3,1,2,0:T(8,128)(2,1)S(1)}, bf16[2,32,7,1024]{3,1,2,0:T(8,128)(2,1)S(1)}, u32[]{:S(2)}, u32[]{:S(2)}) %collective-permute-start) | collective-permute-done | bytes 917536 | tf_op jit(solution)/shard_map/ppermute | solution.py:18
  27.9 1.6 copy.14.halo_ref
  29.5 6.1 %shard_map.47 = bf16[2,32,32,2048]{3,2,1,0:T(8,128)(2,1)} custom-call(f32[8,1024]{1,0:T(8,128)} %taps_ref.3, bf16[2,32,7,1024]{3,2,1,0:T(8,128)(2,1)} %copy.14.halo_ref, bf16[2,32,32,1024]{3,2,1,0:T(8,128)(2,1)} %bitcast.58, bf16[2,32,32,2048]{3,2,1,0:T(8,128)(2,1)} %shard_map.46.previous_ref), custom_call_target="tpu_custom_call", output_to_operand_aliasing={{}: (3, {})} | custom-call | flops 16777216 | bytes 4194304 | tf_op jit(solution)/shard_map/pallas_call | solution.py:127
  35.7 6.8 %convolution_convert_fusion.2 = bf16[2048,256]{0,1:T(8,128)(2,1)} fusion(bf16[2048,2048]{1,0:T(8,128)(2,1)} %bitcast.59, bf16[256,2048]{1,0:T(8,128)(2,1)S(1)} %copy-done.10), kind=kOutput, calls=%fused_computation.10 | convolution fusion | flops 2148007936 | bytes 10485760 | tf_op jit(solution)/shard_map/kj,nj->kn/dot_general | solution.py:308
  42.5 6.2 %all-to-all-start.1 = ((bf16[16,16,2048]{2,1,0:T(8,128)(2,1)}), bf16[16,16,2048]{2,1,0:T(8,128)(2,1)S(1)}, u32[]{:S(2)}, u32[]{:S(2)}) async-start(bf16[16,16,2048]{2,1,0:T(8,128)(2,1)} %bitcast.10), calls=%async_computation.1 | async-start | bytes 2097152 | tf_op jit(solution)/shard_map/all_to_all | solution.py:312
  48.7 6.8 %convolution_convert_fusion.3 = bf16[2048,256]{0,1:T(8,128)(2,1)} fusion(bf16[2048,2048]{1,0:T(8,128)(2,1)} %bitcast.60, bf16[256,2048]{1,0:T(8,128)(2,1)S(1)} %copy-done.9), kind=kOutput, calls=%fused_computation.11 | convolution fusion | flops 2148007936 | bytes 10485760 | tf_op jit(solution)/shard_map/kj,nj->kn/dot_general | solution.py:308
  55.5 17.9 %all-to-all-done.1 = bf16[16,16,2048]{2,1,0:T(8,128)(2,1)S(1)} async-done(((bf16[16,16,2048]{2,1,0:T(8,128)(2,1)}), bf16[16,16,2048]{2,1,0:T(8,128)(2,1)S(1)}, u32[]{:S(2)}, u32[]{:S(2)}) %all-to-all-start.1) | async-done | bytes 1048608 | tf_op jit(solution)/shard_map/all_to_all | solution.py:312
  73.4 5.1 %all-to-all-start = ((bf16[16,16,2048]{2,1,0:T(8,128)(2,1)}), bf16[16,16,2048]{2,1,0:T(8,128)(2,1)S(1)}, u32[]{:S(2)}, u32[]{:S(2)}) async-start(bf16[16,16,2048]{2,1,0:T(8,128)(2,1)} %bitcast.3), calls=%async_computation | async-start | bytes 2097152 | tf_op jit(solution)/shard_map/all_to_all | solution.py:312
  78.5 4.4 %reshape.85 = bf16[16,16,2,32,32]{4,3,2,1,0:T(8,128)(2,1)} reshape(bf16[16,16,2048]{2,1,0:T(8,128)(2,1)S(1)} %all-to-all-done.1) | data formatting | bytes 2097152 | tf_op jit(solution)/shard_map/reshape | solution.py:313
  82.9 3.6 %fusion.11 = bf16[16,2,32,512]{3,2,0,1:T(8,128)(2,1)S(1)} fusion(bf16[16,16,2,32,32]{4,3,2,1,0:T(8,128)(2,1)} %reshape.85, s32[16,32]{1,0:T(8,128)S(1)} %multiply_add_fusion, s32[512]{0:T(512)S(1)} %copy-done.7), kind=kOutput, calls=%fused_computation.17 | convolution fusion | flops 537133056 | bytes 2101248 | tf_op jit(solution)/shard_map/gkias,gar->kisr/dot_general | solution.py:314
  86.5 0.1 copy.57.refs_0_.refs_2_
  86.6 0.1 collective-permute-start.2
  86.7 16.6 %all-to-all-done = bf16[16,16,2048]{2,1,0:T(8,128)(2,1)S(1)} async-done(((bf16[16,16,2048]{2,1,0:T(8,128)(2,1)}), bf16[16,16,2048]{2,1,0:T(8,128)(2,1)S(1)}, u32[]{:S(2)}, u32[]{:S(2)}) %all-to-all-start) | async-done | bytes 1048608 | tf_op jit(solution)/shard_map/all_to_all | solution.py:312
  103.2 4.5 %reshape.81 = bf16[16,16,2,32,32]{4,3,2,1,0:T(8,128)(2,1)} reshape(bf16[16,16,2048]{2,1,0:T(8,128)(2,1)S(1)} %all-to-all-done) | data formatting | bytes 2097152 | tf_op jit(solution)/shard_map/reshape | solution.py:313
  107.7 4.2 %collective-permute-done.2 = bf16[32,32,512]{2,1,0:T(8,128)(2,1)S(1)} collective-permute-done((bf16[32,32,512]{2,1,0:T(8,128)(2,1)S(1)}, bf16[32,32,512]{2,1,0:T(8,128)(2,1)S(1)}, u32[]{:S(2)}, u32[]{:S(2)}) %collective-permute-start.2) | collective-permute-done | bytes 1048608 | tf_op jit(solution)/shard_map/ppermute | solution.py:26
  111.9 1.0 copy-done.6
  112.9 7.4 %shard_map.48.refs_4_ = bf16[2,64,256,512]{3,2,1,0:T(8,128)(2,1)} custom-call(s32[1]{0:T(128)} %bitcast.block_ref, bf16[16,2,32,512]{3,2,1,0:T(8,128)(2,1)} %copy-done.3, bf16[16,2,32,512]{3,2,1,0:T(8,128)(2,1)} %bitcast.72, bf16[16,2,32,512]{3,2,1,0:T(8,128)(2,1)} %copy-done.3, bf16[16,2,32,512]{3,2,1,0:T(8,128)(2,1)} %bitcast.73), custom_call_target="tpu_custom_call" | custom-call | flops 1073741824 | bytes 11534336 | tf_op jit(solution)/shard_map/pallas_call | solution.py:244
  120.3 6.8 %convolution_convert_fusion = bf16[2048,256]{0,1:T(8,128)(2,1)} fusion(bf16[2048,2048]{1,0:T(8,128)(2,1)} %bitcast.61, bf16[256,2048]{1,0:T(8,128)(2,1)S(1)} %copy-done.8), kind=kOutput, calls=%fused_computation.8 | convolution fusion | flops 2148007936 | bytes 10485760 | tf_op jit(solution)/shard_map/kj,nj->kn/dot_general | solution.py:308
  127.1 6.0 %all-to-all-start.3 = ((bf16[16,16,2048]{2,1,0:T(8,128)(2,1)}), bf16[16,16,2048]{2,1,0:T(8,128)(2,1)S(1)}, u32[]{:S(2)}, u32[]{:S(2)}) async-start(bf16[16,16,2048]{2,1,0:T(8,128)(2,1)} %bitcast.21), calls=%async_computation.3 | async-start | bytes 2097152 | tf_op jit(solution)/shard_map/all_to_all | solution.py:312
  133.1 3.6 %fusion.8 = bf16[16,2,32,512]{3,2,0,1:T(8,128)(2,1)S(1)} fusion(bf16[16,16,2,32,32]{4,3,2,1,0:T(8,128)(2,1)} %reshape.81, s32[16,32]{1,0:T(8,128)S(1)} %multiply_add_fusion, s32[512]{0:T(512)S(1)} %copy-done.7), kind=kOutput, calls=%fused_computation.16 | convolution fusion | flops 537133056 | bytes 2101248 | tf_op jit(solution)/shard_map/gkias,gar->kisr/dot_general | solution.py:314
  136.6 0.1 copy.58.refs_0_.refs_2_
  136.8 0.4 collective-permute-start.1
  137.1 24.9 %collective-permute-done.1 = bf16[32,32,512]{2,1,0:T(8,128)(2,1)S(1)} collective-permute-done((bf16[32,32,512]{2,1,0:T(8,128)(2,1)S(1)}, bf16[32,32,512]{2,1,0:T(8,128)(2,1)S(1)}, u32[]{:S(2)}, u32[]{:S(2)}) %collective-permute-start.1) | collective-permute-done | bytes 1048608 | tf_op jit(solution)/shard_map/ppermute | solution.py:26
  162.0 1.0 copy-done.5
  163.0 7.3 %shard_map.49.refs_4_ = bf16[2,64,256,512]{3,2,1,0:T(8,128)(2,1)} custom-call(s32[1]{0:T(128)} %bitcast.block_ref, bf16[16,2,32,512]{3,2,1,0:T(8,128)(2,1)} %copy-done.2, bf16[16,2,32,512]{3,2,1,0:T(8,128)(2,1)} %bitcast.70, bf16[16,2,32,512]{3,2,1,0:T(8,128)(2,1)} %copy-done.2, bf16[16,2,32,512]{3,2,1,0:T(8,128)(2,1)} %bitcast.71, ...), custom_call_target="tpu_custom_call", output_to_operand_aliasing={{}: (5, {})} | custom-call | flops 1073741824 | bytes 11534336 | tf_op jit(solution)/shard_map/pallas_call | solution.py:244
  170.4 7.0 %convolution_convert_fusion.1 = bf16[2048,256]{0,1:T(8,128)(2,1)} fusion(bf16[2048,2048]{1,0:T(8,128)(2,1)} %bitcast.62, bf16[256,2048]{1,0:T(8,128)(2,1)} %constant.14), kind=kOutput, calls=%fused_computation.9 | convolution fusion | flops 2148007936 | bytes 10485760 | tf_op jit(solution)/shard_map/kj,nj->kn/dot_general | solution.py:308
  177.4 0.0 all-to-all-done.3
  177.4 6.0 %all-to-all-start.2 = ((bf16[16,16,2048]{2,1,0:T(8,128)(2,1)}), bf16[16,16,2048]{2,1,0:T(8,128)(2,1)S(1)}, u32[]{:S(2)}, u32[]{:S(2)}) async-start(bf16[16,16,2048]{2,1,0:T(8,128)(2,1)} %bitcast.16), calls=%async_computation.2 | async-start | bytes 2097152 | tf_op jit(solution)/shard_map/all_to_all | solution.py:312
  183.4 4.4 %reshape.93 = bf16[16,16,2,32,32]{4,3,2,1,0:T(8,128)(2,1)} reshape(bf16[16,16,2048]{2,1,0:T(8,128)(2,1)S(1)} %all-to-all-done.3) | data formatting | bytes 2097152 | tf_op jit(solution)/shard_map/reshape | solution.py:313
  187.8 3.6 %fusion.17 = bf16[16,2,32,512]{3,2,0,1:T(8,128)(2,1)S(1)} fusion(bf16[16,16,2,32,32]{4,3,2,1,0:T(8,128)(2,1)} %reshape.93, s32[16,32]{1,0:T(8,128)S(1)} %multiply_add_fusion, s32[512]{0:T(512)S(1)} %copy-done.7), kind=kOutput, calls=%fused_computation.19 | convolution fusion | flops 537133056 | bytes 2101248 | tf_op jit(solution)/shard_map/gkias,gar->kisr/dot_general | solution.py:314
  191.4 0.1 copy.55.refs_0_.refs_2_
  191.5 0.4 collective-permute-start.4
  191.8 16.3 %all-to-all-done.2 = bf16[16,16,2048]{2,1,0:T(8,128)(2,1)S(1)} async-done(((bf16[16,16,2048]{2,1,0:T(8,128)(2,1)}), bf16[16,16,2048]{2,1,0:T(8,128)(2,1)S(1)}, u32[]{:S(2)}, u32[]{:S(2)}) %all-to-all-start.2) | async-done | bytes 1048608 | tf_op jit(solution)/shard_map/all_to_all | solution.py:312
  208.1 4.4 %reshape.89 = bf16[16,16,2,32,32]{4,3,2,1,0:T(8,128)(2,1)} reshape(bf16[16,16,2048]{2,1,0:T(8,128)(2,1)S(1)} %all-to-all-done.2) | data formatting | bytes 2097152 | tf_op jit(solution)/shard_map/reshape | solution.py:313
  212.5 3.6 %fusion.14 = bf16[16,2,32,512]{3,2,0,1:T(8,128)(2,1)S(1)} fusion(bf16[16,16,2,32,32]{4,3,2,1,0:T(8,128)(2,1)} %reshape.89, s32[16,32]{1,0:T(8,128)S(1)} %multiply_add_fusion, s32[512]{0:T(512)S(1)} %copy-done.7), kind=kOutput, calls=%fused_computation.18 | convolution fusion | flops 537133056 | bytes 2101248 | tf_op jit(solution)/shard_map/gkias,gar->kisr/dot_general | solution.py:314
  216.1 0.1 copy.56.refs_0_.refs_2_
  216.2 0.4 collective-permute-start.3
  216.5 0.2 collective-permute-done.4
  216.7 1.0 copy-done.4
  217.7 7.3 %shard_map.50.refs_4_ = bf16[2,64,256,512]{3,2,1,0:T(8,128)(2,1)} custom-call(s32[1]{0:T(128)} %bitcast.block_ref, bf16[16,2,32,512]{3,2,1,0:T(8,128)(2,1)} %copy-done, bf16[16,2,32,512]{3,2,1,0:T(8,128)(2,1)} %bitcast.68, bf16[16,2,32,512]{3,2,1,0:T(8,128)(2,1)} %copy-done, bf16[16,2,32,512]{3,2,1,0:T(8,128)(2,1)} %bitcast.69, ...), custom_call_target="tpu_custom_call", output_to_operand_aliasing={{}: (5, {})} | custom-call | flops 1073741824 | bytes 11534336 | tf_op jit(solution)/shard_map/pallas_call | solution.py:244
  225.0 17.0 %collective-permute-done.3 = bf16[32,32,512]{2,1,0:T(8,128)(2,1)} collective-permute-done((bf16[32,32,512]{2,1,0:T(8,128)(2,1)S(1)}, bf16[32,32,512]{2,1,0:T(8,128)(2,1)}, u32[]{:S(2)}, u32[]{:S(2)}) %collective-permute-start.3) | collective-permute-done | bytes 1048608 | tf_op jit(solution)/shard_map/ppermute | solution.py:26
  242.0 7.3 %shard_map.51 = bf16[2,64,256,512]{3,2,1,0:T(8,128)(2,1)} custom-call(s32[1]{0:T(128)} %bitcast.block_ref, bf16[16,2,32,512]{3,2,1,0:T(8,128)(2,1)} %copy-done.1, bf16[16,2,32,512]{3,2,1,0:T(8,128)(2,1)} %bitcast.19.refs_1_.refs_3_, bf16[16,2,32,512]{3,2,1,0:T(8,128)(2,1)} %copy-done.1, ...), custom_call_target="tpu_custom_call", output_to_operand_aliasing={{}: (5, {})} | custom-call | flops 1073741824 | bytes 11534336 | tf_op jit(solution)/shard_map/pallas_call | solution.py:244
  (20 shorter events, 0.0 us)
Async XLA Ops:
  4.0 24.0 %collective-permute-start = (bf16[2,32,7,1024]{3,1,2,0:T(8,128)(2,1)S(1)}, bf16[2,32,7,1024]{3,1,2,0:T(8,128)(2,1)S(1)}, u32[]{:S(2)}, u32[]{:S(2)}) collective-permute-start(bf16[2,32,7,1024]{3,1,2,0:T(8,128)(2,1)S(1)} %bitcast.75), channel_id=1, source_target_pairs={{0,1},{2,3},{4,5},{6,7},{8,9},{10,11},{12,13},{14,15},{16,17},{18,... | collective-permute-start | bytes 2752520 | tf_op jit(solution)/shard_map/ppermute | solution.py:18
  29.5 6.1 %copy-start.10 = (bf16[256,2048]{1,0:T(8,128)(2,1)S(1)}, bf16[256,2048]{1,0:T(8,128)(2,1)}, u32[]{:S(2)}) copy-start(bf16[256,2048]{1,0:T(8,128)(2,1)} %constant.12) | copy-start | bytes 3145732
  35.6 13.1 %copy-start.9 = (bf16[256,2048]{1,0:T(8,128)(2,1)S(1)}, bf16[256,2048]{1,0:T(8,128)(2,1)}, u32[]{:S(2)}) copy-start(bf16[256,2048]{1,0:T(8,128)(2,1)} %constant.10) | copy-start | bytes 3145732
  42.5 31.0 %all-to-all-start.1 = ((bf16[16,16,2048]{2,1,0:T(8,128)(2,1)}), bf16[16,16,2048]{2,1,0:T(8,128)(2,1)S(1)}, u32[]{:S(2)}, u32[]{:S(2)}) async-start(bf16[16,16,2048]{2,1,0:T(8,128)(2,1)} %bitcast.10), calls=%async_computation.1 | async-start | bytes 2097152 | tf_op jit(solution)/shard_map/all_to_all | solution.py:312
  55.5 27.4 %copy-start.7 = (s32[512]{0:T(512)S(1)}, s32[512]{0:T(512)}, u32[]{:S(2)}) copy-start(s32[512]{0:T(512)} %param.6) | copy-start | bytes 6148
  73.4 29.8 %all-to-all-start = ((bf16[16,16,2048]{2,1,0:T(8,128)(2,1)}), bf16[16,16,2048]{2,1,0:T(8,128)(2,1)S(1)}, u32[]{:S(2)}, u32[]{:S(2)}) async-start(bf16[16,16,2048]{2,1,0:T(8,128)(2,1)} %bitcast.3), calls=%async_computation | async-start | bytes 2097152 | tf_op jit(solution)/shard_map/all_to_all | solution.py:312
  86.6 25.3 %copy-start.3 = (bf16[16,2,32,512]{3,2,1,0:T(8,128)(2,1)}, bf16[16,2,32,512]{3,2,1,0:T(8,128)(2,1)S(1)}, u32[]{:S(2)}) copy-start(bf16[16,2,32,512]{3,2,1,0:T(8,128)(2,1)S(1)} %copy.57.refs_0_.refs_2_) | copy-start | bytes 3145732
  86.6 25.3 %collective-permute-start.2 = (bf16[32,32,512]{2,1,0:T(8,128)(2,1)S(1)}, bf16[32,32,512]{2,1,0:T(8,128)(2,1)S(1)}, u32[]{:S(2)}, u32[]{:S(2)}) collective-permute-start(bf16[32,32,512]{2,1,0:T(8,128)(2,1)S(1)} %bitcast.67), channel_id=1, source_target_pairs={{0,1},{1,0},{2,3},{3,2},{4,5},{5,4},{6,7},{7,6},{8,9},{9,8},{10,11... | collective-permute-start | bytes 3145736 | tf_op jit(solution)/shard_map/ppermute | solution.py:26
  111.9 1.0 copy-start.6
  112.9 7.4 %copy-start.8 = (bf16[256,2048]{1,0:T(8,128)(2,1)S(1)}, bf16[256,2048]{1,0:T(8,128)(2,1)}, u32[]{:S(2)}) copy-start(bf16[256,2048]{1,0:T(8,128)(2,1)} %constant.16) | copy-start | bytes 3145732
  127.1 50.3 %all-to-all-start.3 = ((bf16[16,16,2048]{2,1,0:T(8,128)(2,1)}), bf16[16,16,2048]{2,1,0:T(8,128)(2,1)S(1)}, u32[]{:S(2)}, u32[]{:S(2)}) async-start(bf16[16,16,2048]{2,1,0:T(8,128)(2,1)} %bitcast.21), calls=%async_computation.3 | async-start | bytes 2097152 | tf_op jit(solution)/shard_map/all_to_all | solution.py:312
  136.7 25.3 %copy-start.2 = (bf16[16,2,32,512]{3,2,1,0:T(8,128)(2,1)}, bf16[16,2,32,512]{3,2,1,0:T(8,128)(2,1)S(1)}, u32[]{:S(2)}) copy-start(bf16[16,2,32,512]{3,2,1,0:T(8,128)(2,1)S(1)} %copy.58.refs_0_.refs_2_) | copy-start | bytes 3145732
  136.8 25.3 %collective-permute-start.1 = (bf16[32,32,512]{2,1,0:T(8,128)(2,1)S(1)}, bf16[32,32,512]{2,1,0:T(8,128)(2,1)S(1)}, u32[]{:S(2)}, u32[]{:S(2)}) collective-permute-start(bf16[32,32,512]{2,1,0:T(8,128)(2,1)S(1)} %bitcast.66), channel_id=1, source_target_pairs={{0,1},{1,0},{2,3},{3,2},{4,5},{5,4},{6,7},{7,6},{8,9},{9,8},{10,11... | collective-permute-start | bytes 3145736 | tf_op jit(solution)/shard_map/ppermute | solution.py:26
  162.0 1.0 copy-start.5
  177.4 30.7 %all-to-all-start.2 = ((bf16[16,16,2048]{2,1,0:T(8,128)(2,1)}), bf16[16,16,2048]{2,1,0:T(8,128)(2,1)S(1)}, u32[]{:S(2)}, u32[]{:S(2)}) async-start(bf16[16,16,2048]{2,1,0:T(8,128)(2,1)} %bitcast.16), calls=%async_computation.2 | async-start | bytes 2097152 | tf_op jit(solution)/shard_map/all_to_all | solution.py:312
  191.4 24.6 %copy-start = (bf16[16,2,32,512]{3,2,1,0:T(8,128)(2,1)}, bf16[16,2,32,512]{3,2,1,0:T(8,128)(2,1)S(1)}, u32[]{:S(2)}) copy-start(bf16[16,2,32,512]{3,2,1,0:T(8,128)(2,1)S(1)} %copy.55.refs_0_.refs_2_) | copy-start | bytes 3145732
  191.5 25.3 %collective-permute-start.4 = (bf16[32,32,512]{2,1,0:T(8,128)(2,1)S(1)}, bf16[32,32,512]{2,1,0:T(8,128)(2,1)S(1)}, u32[]{:S(2)}, u32[]{:S(2)}) collective-permute-start(bf16[32,32,512]{2,1,0:T(8,128)(2,1)S(1)} %bitcast.64), channel_id=1, source_target_pairs={{0,1},{1,0},{2,3},{3,2},{4,5},{5,4},{6,7},{7,6},{8,9},{9,8},{10,11... | collective-permute-start | bytes 3145736 | tf_op jit(solution)/shard_map/ppermute | solution.py:26
  216.2 8.9 %copy-start.1 = (bf16[16,2,32,512]{3,2,1,0:T(8,128)(2,1)}, bf16[16,2,32,512]{3,2,1,0:T(8,128)(2,1)S(1)}, u32[]{:S(2)}) copy-start(bf16[16,2,32,512]{3,2,1,0:T(8,128)(2,1)S(1)} %copy.56.refs_0_.refs_2_) | copy-start | bytes 3145732
  216.2 25.8 %collective-permute-start.3 = (bf16[32,32,512]{2,1,0:T(8,128)(2,1)S(1)}, bf16[32,32,512]{2,1,0:T(8,128)(2,1)}, u32[]{:S(2)}, u32[]{:S(2)}) collective-permute-start(bf16[32,32,512]{2,1,0:T(8,128)(2,1)S(1)} %bitcast.65), channel_id=1, source_target_pairs={{0,1},{1,0},{2,3},{3,2},{4,5},{5,4},{6,7},{7,6},{8,9},{9,8},{10,11... | collective-permute-start | bytes 3145736 | tf_op jit(solution)/shard_map/ppermute | solution.py:26
  216.7 1.0 copy-start.4

commit v7 on v6

--- a/solution.py
+++ b/solution.py
@@ -298,8 +298,16 @@
         right = gathered.reshape(width, -1, stations)
         return correlate_chunk(left, right, result, chunk * width, local_channels)
 
+    def reorder(turned):
+        turned = turned.reshape(groups, width, 2, stations_local, spectra_local)
+        ordered = jnp.einsum(
+            "gkias,gar->kisr", turned, selector, preferred_element_type=jnp.float32
+        ).astype(jnp.bfloat16)
+        return ordered.reshape(width * 2, spectra_local, stations)
+
     result = None
     pending = []
+    turned = None
     for chunk in range(chunks):
         source = filtered
         if chunk >= 2:
@@ -309,13 +317,12 @@
             "kj,nj->kn", weights[chunk], source, preferred_element_type=jnp.float32
         ).astype(jnp.bfloat16)
         spectra = spectra.reshape(groups, width, 2 * stations_local * spectra_local)
+        if chunk >= 1:
+            ordered = reorder(turned)
+            spectra, ordered = lax.optimization_barrier((spectra, ordered))
+            pending.append(gathered_along(ordered, "blk"))
         turned = lax.all_to_all(spectra, "stn", split_axis=0, concat_axis=0, tiled=True)
-        turned = turned.reshape(groups, width, 2, stations_local, spectra_local)
-        ordered = jnp.einsum(
-            "gkias,gar->kisr", turned, selector, preferred_element_type=jnp.float32
-        ).astype(jnp.bfloat16)
-        ordered = ordered.reshape(width * 2, spectra_local, stations)
-        pending.append(gathered_along(ordered, "blk"))
+    pending.append(gathered_along(reorder(turned), "blk"))
     for chunk in range(max(0, chunks - 2), chunks):
         result = correlate(chunk, pending[chunk], result)
     return result

time: 251 us -> 263 us (1.048)
  waiting for transfers between devices: 101 us -> 113 us
    ppermute x4, waiting for transfers between devices: 46.2 us -> 67.3 us  [gathered_along(): parts.append(lax.ppermute(value, axis, pairs))]
    all_to_all x4, waiting for transfers between devices: 50.8 us -> 42.3 us  [per_device(): lax.all_to_all(spectra, 'stn', split_axis=0, concat_axis=0, tiled=True)]
    unnamed x23 -> x21, local copies, waits for them, and re-layouts: 7.48 us -> 7.46 us
  transfers between devices with their start and end apart: 9 -> 9, of which waited for: 8 -> 6; matrix products, arithmetic and copies ran while one was open for 20% -> 13% of each run, Pallas kernels for 12% -> 14%
where the time goes in v7:
time: 263 us; the launch traced here: 262 us
  waiting for transfers between devices  113 us (43%)
  Pallas kernels  49.8 us (19%)
  matrix products  41.9 us (16%)
  local copies, waits for them, and re-layouts  27.1 us (10%)
  starting transfers between devices  25.8 us (10%)
  other arithmetic  3.8 us (1%)
    ppermute x4, waiting for transfers between devices, gathered_along(): parts.append(lax.ppermute(value, axis, pairs))  67.3 us
    all_to_all x4, waiting for transfers between devices, per_device(): lax.all_to_all(spectra, 'stn', split_axis=0, concat_axis=0, tiled=True)  42.3 us
    pallas_call x4, Pallas kernels, correlate_rows_chunk(): pl.pallas_call(correlate_rows_kernel, grid_spec=grid_spec, out_shape=jax....  29.3 us
    dot_general x4, matrix products, per_device(): jnp.einsum('kj,nj->kn', weights[chunk], source, preferred_element_type=jn...  27.6 us
    all_to_all x4, starting transfers between devices, per_device(): lax.all_to_all(spectra, 'stn', split_axis=0, concat_axis=0, tiled=True)  23.4 us
    reshape x4, local copies, waits for them, and re-layouts, reorder(): turned = turned.reshape(groups, width, 2, stations_local, spectra_local)  17.6 us
    pallas_call x1, Pallas kernels, filter_frames(): pl.pallas_call(fir_kernel, grid=(stations_local // group,), in_specs=[pl....  14.3 us
    dot_general x4, matrix products, reorder(): jnp.einsum('gkias,gar->kisr', turned, selector, preferred_element_type=jn...  14.2 us
  transfers between devices with their start and end apart: 9, of which 6 were waited for; matrix products, arithmetic and copies ran while one was open for 13% of the time, Pallas kernels for 14%

profile of v7, /device:TPU:14, one launch (start us, length us, event | category | flops | bytes accessed | tf_op | source)
XLA Modules:
  0.0 261.9 jit_solution(12429259485304736088)
XLA Ops:
  0.0 3.8 %convert.3 = bf16[2,32,32768]{2,1,0:T(8,128)(2,1)S(1)} convert(s32[2,32,32768]{2,1,0:T(8,128)} %param.4) | non-fusion elementwise | flops 2097152 | bytes 12582912 | tf_op jit(solution)/shard_map/convert
  3.8 0.1 slice.21
  3.9 0.1 copy.58
  4.0 1.3 collective-permute-start
  5.3 4.5 %copy.40 = bf16[8,8,32,1024]{3,2,1,0:T(8,128)(2,1)} copy(bf16[8,8,32,1024]{3,1,2,0:T(8,128)(2,1)S(1)} %bitcast.70) | data formatting | bytes 8388608
  9.7 14.3 %shard_map.46.previous_ref = bf16[2,32,32,2048]{3,2,1,0:T(8,128)(2,1)} custom-call(f32[8,1024]{1,0:T(8,128)} %taps_ref.3, bf16[2,32,32,1024]{3,2,1,0:T(8,128)(2,1)} %bitcast.64), custom_call_target="tpu_custom_call" | custom-call | flops 67108864 | bytes 12582912 | tf_op jit(solution)/shard_map/pallas_call | solution.py:110
  24.1 3.9 %collective-permute-done = bf16[2,32,7,1024]{3,1,2,0:T(8,128)(2,1)S(1)} collective-permute-done((bf16[2,32,7,1024]{3,1,2,0:T(8,128)(2,1)S(1)}, bf16[2,32,7,1024]{3,1,2,0:T(8,128)(2,1)S(1)}, u32[]{:S(2)}, u32[]{:S(2)}) %collective-permute-start) | collective-permute-done | bytes 917536 | tf_op jit(solution)/shard_map/ppermute | solution.py:18
  27.9 1.6 copy.21.halo_ref
  29.5 6.1 %shard_map.47 = bf16[2,32,32,2048]{3,2,1,0:T(8,128)(2,1)} custom-call(f32[8,1024]{1,0:T(8,128)} %taps_ref.3, bf16[2,32,7,1024]{3,2,1,0:T(8,128)(2,1)} %copy.21.halo_ref, bf16[2,32,32,1024]{3,2,1,0:T(8,128)(2,1)} %bitcast.65, bf16[2,32,32,2048]{3,2,1,0:T(8,128)(2,1)} %shard_map.46.previous_ref), custom_call_target="tpu_custom_call", output_to_operand_aliasing={{}: (3, {})} | custom-call | flops 16777216 | bytes 4194304 | tf_op jit(solution)/shard_map/pallas_call | solution.py:127
  35.7 6.8 %convolution_convert_fusion.2 = bf16[2048,256]{0,1:T(8,128)(2,1)} fusion(bf16[2048,2048]{1,0:T(8,128)(2,1)} %bitcast.66, bf16[256,2048]{1,0:T(8,128)(2,1)S(1)} %copy-done.9), kind=kOutput, calls=%fused_computation.10 | convolution fusion | flops 2148007936 | bytes 10485760 | tf_op jit(solution)/shard_map/kj,nj->kn/dot_general | solution.py:316
  42.5 6.2 %all-to-all-start = ((bf16[16,16,2048]{2,1,0:T(8,128)(2,1)}), bf16[16,16,2048]{2,1,0:T(8,128)(2,1)S(1)}, u32[]{:S(2)}, u32[]{:S(2)}) async-start(bf16[16,16,2048]{2,1,0:T(8,128)(2,1)} %bitcast.5), calls=%async_computation | async-start | bytes 2097152 | tf_op jit(solution)/shard_map/all_to_all | solution.py:324
  48.7 6.8 %convolution_convert_fusion.3 = bf16[2048,256]{0,1:T(8,128)(2,1)} fusion(bf16[2048,2048]{1,0:T(8,128)(2,1)} %bitcast.67, bf16[256,2048]{1,0:T(8,128)(2,1)S(1)} %copy-done.8), kind=kOutput, calls=%fused_computation.11 | convolution fusion | flops 2148007936 | bytes 10485760 | tf_op jit(solution)/shard_map/kj,nj->kn/dot_general | solution.py:316
  55.5 17.9 %all-to-all-done = bf16[16,16,2048]{2,1,0:T(8,128)(2,1)S(1)} async-done(((bf16[16,16,2048]{2,1,0:T(8,128)(2,1)}), bf16[16,16,2048]{2,1,0:T(8,128)(2,1)S(1)}, u32[]{:S(2)}, u32[]{:S(2)}) %all-to-all-start) | async-done | bytes 1048608 | tf_op jit(solution)/shard_map/all_to_all | solution.py:324
  73.4 4.4 %reshape.91 = bf16[16,16,2,32,32]{4,3,2,1,0:T(8,128)(2,1)} reshape(bf16[16,16,2048]{2,1,0:T(8,128)(2,1)S(1)} %all-to-all-done) | data formatting | bytes 2097152 | tf_op jit(solution)/shard_map/reshape | solution.py:302
  77.8 3.6 %fusion.6 = bf16[16,2,32,512,1]{3,2,0,1,4:T(8,128)(2,1)S(1)} fusion(bf16[16,16,2,32,32]{4,3,2,1,0:T(8,128)(2,1)} %reshape.91, s32[16,32]{1,0:T(8,128)S(1)} %multiply_add_fusion, s32[512]{0:T(512)S(1)} %copy-done.7), kind=kOutput, calls=%fused_computation.6 | convolution fusion | flops 537133056 | bytes 2101248 | tf_op jit(solution)/shard_map/gkias,gar->kisr/dot_general | solution.py:303
  81.4 0.1 copy.57
  81.5 5.1 %all-to-all-start.1 = ((bf16[16,16,2048]{2,1,0:T(8,128)(2,1)}), bf16[16,16,2048]{2,1,0:T(8,128)(2,1)S(1)}, u32[]{:S(2)}, u32[]{:S(2)}) async-start(bf16[16,16,2048]{2,1,0:T(8,128)(2,1)} %bitcast.3), calls=%async_computation.1 | async-start | bytes 2097152 | tf_op jit(solution)/shard_map/all_to_all | solution.py:324
  86.5 0.1 collective-permute-start.1
  86.6 25.2 %collective-permute-done.1 = bf16[32,32,512]{2,1,0:T(8,128)(2,1)S(1)} collective-permute-done((bf16[32,32,512]{2,1,0:T(8,128)(2,1)S(1)}, bf16[32,32,512]{2,1,0:T(8,128)(2,1)S(1)}, u32[]{:S(2)}, u32[]{:S(2)}) %collective-permute-start.1) | collective-permute-done | bytes 1048608 | tf_op jit(solution)/shard_map/ppermute | solution.py:26
  111.8 1.0 copy-done.6
  112.8 7.3 %shard_map.48.refs_4_ = bf16[2,64,256,512]{3,2,1,0:T(8,128)(2,1)} custom-call(s32[1]{0:T(128)} %bitcast.block_ref, bf16[16,2,32,512]{3,2,1,0:T(8,128)(2,1)} %bitcast.81, bf16[16,2,32,512]{3,2,1,0:T(8,128)(2,1)} %bitcast.87, bf16[16,2,32,512]{3,2,1,0:T(8,128)(2,1)} %bitcast.82, bf16[16,2,32,512]{3,2,1,0:T(8,128)(2,1)} %bitcast.88), custom_call_target="tpu_custom_call" | custom-call | flops 1073741824 | bytes 11534336 | tf_op jit(solution)/shard_map/pallas_call | solution.py:244
  120.1 7.0 %convolution_convert_fusion.1 = bf16[2048,256]{0,1:T(8,128)(2,1)} fusion(bf16[2048,2048]{1,0:T(8,128)(2,1)} %bitcast.68, bf16[256,2048]{1,0:T(8,128)(2,1)} %constant.14), kind=kOutput, calls=%fused_computation.9 | convolution fusion | flops 2148007936 | bytes 10485760 | tf_op jit(solution)/shard_map/kj,nj->kn/dot_general | solution.py:316
  127.1 0.0 all-to-all-done.1
  127.1 4.5 %reshape.96 = bf16[16,16,2,32,32]{4,3,2,1,0:T(8,128)(2,1)} reshape(bf16[16,16,2048]{2,1,0:T(8,128)(2,1)S(1)} %all-to-all-done.1) | data formatting | bytes 2097152 | tf_op jit(solution)/shard_map/reshape | solution.py:302
  131.6 3.6 %fusion.4 = bf16[16,2,32,512,1]{3,2,0,1,4:T(8,128)(2,1)S(1)} fusion(bf16[16,16,2,32,32]{4,3,2,1,0:T(8,128)(2,1)} %reshape.96, s32[16,32]{1,0:T(8,128)S(1)} %multiply_add_fusion, s32[512]{0:T(512)S(1)} %copy-done.7), kind=kOutput, calls=%fused_computation.4 | convolution fusion | flops 537133056 | bytes 2101248 | tf_op jit(solution)/shard_map/gkias,gar->kisr/dot_general | solution.py:303
  135.2 0.1 copy.56
  135.3 6.0 %all-to-all-start.2 = ((bf16[16,16,2048]{2,1,0:T(8,128)(2,1)}), bf16[16,16,2048]{2,1,0:T(8,128)(2,1)S(1)}, u32[]{:S(2)}, u32[]{:S(2)}) async-start(bf16[16,16,2048]{2,1,0:T(8,128)(2,1)} %bitcast.13), calls=%async_computation.2 | async-start | bytes 2097152 | tf_op jit(solution)/shard_map/all_to_all | solution.py:324
  141.3 0.3 collective-permute-start.2
  141.6 24.9 %collective-permute-done.2 = bf16[32,32,512]{2,1,0:T(8,128)(2,1)S(1)} collective-permute-done((bf16[32,32,512]{2,1,0:T(8,128)(2,1)S(1)}, bf16[32,32,512]{2,1,0:T(8,128)(2,1)S(1)}, u32[]{:S(2)}, u32[]{:S(2)}) %collective-permute-start.2) | collective-permute-done | bytes 1048608 | tf_op jit(solution)/shard_map/ppermute | solution.py:26
  166.5 1.0 copy-done.5
  167.5 7.3 %shard_map.49.refs_4_ = bf16[2,64,256,512]{3,2,1,0:T(8,128)(2,1)} custom-call(s32[1]{0:T(128)} %bitcast.block_ref, bf16[16,2,32,512]{3,2,1,0:T(8,128)(2,1)} %bitcast.78, bf16[16,2,32,512]{3,2,1,0:T(8,128)(2,1)} %bitcast.85, bf16[16,2,32,512]{3,2,1,0:T(8,128)(2,1)} %bitcast.79, bf16[16,2,32,512]{3,2,1,0:T(8,128)(2,1)} %bitcast.86, ...), custom_call_target="tpu_custom_call", output_to_operand_aliasing={{}: (5, {})} | custom-call | flops 1073741824 | bytes 11534336 | tf_op jit(solution)/shard_map/pallas_call | solution.py:244
  174.8 7.0 %convolution_convert_fusion = bf16[2048,256]{0,1:T(8,128)(2,1)} fusion(bf16[2048,2048]{1,0:T(8,128)(2,1)} %bitcast.69, bf16[256,2048]{1,0:T(8,128)(2,1)} %constant.16), kind=kOutput, calls=%fused_computation.8 | convolution fusion | flops 2148007936 | bytes 10485760 | tf_op jit(solution)/shard_map/kj,nj->kn/dot_general | solution.py:316
  181.9 0.0 all-to-all-done.2
  181.9 4.4 %reshape.101 = bf16[16,16,2,32,32]{4,3,2,1,0:T(8,128)(2,1)} reshape(bf16[16,16,2048]{2,1,0:T(8,128)(2,1)S(1)} %all-to-all-done.2) | data formatting | bytes 2097152 | tf_op jit(solution)/shard_map/reshape | solution.py:302
  186.2 3.6 %fusion.2 = bf16[16,2,32,512,1]{3,2,0,1,4:T(8,128)(2,1)S(1)} fusion(bf16[16,16,2,32,32]{4,3,2,1,0:T(8,128)(2,1)} %reshape.101, s32[16,32]{1,0:T(8,128)S(1)} %multiply_add_fusion, s32[512]{0:T(512)S(1)} %copy-done.7), kind=kOutput, calls=%fused_computation.2 | convolution fusion | flops 537133056 | bytes 2101248 | tf_op jit(solution)/shard_map/gkias,gar->kisr/dot_general | solution.py:303
  189.8 0.1 copy.55
  189.9 6.0 %all-to-all-start.3 = ((bf16[16,16,2048]{2,1,0:T(8,128)(2,1)}), bf16[16,16,2048]{2,1,0:T(8,128)(2,1)S(1)}, u32[]{:S(2)}, u32[]{:S(2)}) async-start(bf16[16,16,2048]{2,1,0:T(8,128)(2,1)} %bitcast.20), calls=%async_computation.3 | async-start | bytes 2097152 | tf_op jit(solution)/shard_map/all_to_all | solution.py:324
  195.9 0.4 collective-permute-start.4
  196.3 24.4 %all-to-all-done.3 = bf16[16,16,2048]{2,1,0:T(8,128)(2,1)S(1)} async-done(((bf16[16,16,2048]{2,1,0:T(8,128)(2,1)}), bf16[16,16,2048]{2,1,0:T(8,128)(2,1)S(1)}, u32[]{:S(2)}, u32[]{:S(2)}) %all-to-all-start.3) | async-done | bytes 1048608 | tf_op jit(solution)/shard_map/all_to_all | solution.py:324
  220.7 4.4 %reshape.103 = bf16[16,16,2,32,32]{4,3,2,1,0:T(8,128)(2,1)} reshape(bf16[16,16,2048]{2,1,0:T(8,128)(2,1)S(1)} %all-to-all-done.3) | data formatting | bytes 2097152 | tf_op jit(solution)/shard_map/reshape | solution.py:302
  225.1 3.6 %fusion = bf16[16,2,32,512,1]{3,2,0,1,4:T(8,128)(2,1)S(1)} fusion(bf16[16,16,2,32,32]{4,3,2,1,0:T(8,128)(2,1)} %reshape.103, s32[16,32]{1,0:T(8,128)S(1)} %multiply_add_fusion, s32[512]{0:T(512)S(1)} %copy-done.7), kind=kOutput, calls=%fused_computation | convolution fusion | flops 537133056 | bytes 2101248 | tf_op jit(solution)/shard_map/gkias,gar->kisr/dot_general | solution.py:303
  228.6 0.1 copy.54
  228.7 0.4 collective-permute-start.3
  229.1 0.0 collective-permute-done.4
  229.1 1.0 copy-done.4
  230.1 7.3 %shard_map.50.refs_4_ = bf16[2,64,256,512]{3,2,1,0:T(8,128)(2,1)} custom-call(s32[1]{0:T(128)} %bitcast.block_ref, bf16[16,2,32,512]{3,2,1,0:T(8,128)(2,1)} %bitcast.72, bf16[16,2,32,512]{3,2,1,0:T(8,128)(2,1)} %bitcast.83, bf16[16,2,32,512]{3,2,1,0:T(8,128)(2,1)} %bitcast.73, bf16[16,2,32,512]{3,2,1,0:T(8,128)(2,1)} %bitcast.84, ...), custom_call_target="tpu_custom_call", output_to_operand_aliasing={{}: (5, {})} | custom-call | flops 1073741824 | bytes 11534336 | tf_op jit(solution)/shard_map/pallas_call | solution.py:244
  237.4 17.2 %collective-permute-done.3 = bf16[32,32,512]{2,1,0:T(8,128)(2,1)} collective-permute-done((bf16[32,32,512]{2,1,0:T(8,128)(2,1)S(1)}, bf16[32,32,512]{2,1,0:T(8,128)(2,1)}, u32[]{:S(2)}, u32[]{:S(2)}) %collective-permute-start.3) | collective-permute-done | bytes 1048608 | tf_op jit(solution)/shard_map/ppermute | solution.py:26
  254.5 7.3 %shard_map.51 = bf16[2,64,256,512]{3,2,1,0:T(8,128)(2,1)} custom-call(s32[1]{0:T(128)} %bitcast.block_ref, bf16[16,2,32,512]{3,2,1,0:T(8,128)(2,1)} %bitcast.75, bf16[16,2,32,512]{3,2,1,0:T(8,128)(2,1)} %bitcast.25.refs_1_.refs_3_, bf16[16,2,32,512]{3,2,1,0:T(8,128)(2,1)} %bitcast.76, ...), custom_call_target="tpu_custom_call", output_to_operand_aliasing={{}: (5, {})} | custom-call | flops 1073741824 | bytes 11534336 | tf_op jit(solution)/shard_map/pallas_call | solution.py:244
  (18 shorter events, 0.0 us)
Async XLA Ops:
  4.0 24.0 %collective-permute-start = (bf16[2,32,7,1024]{3,1,2,0:T(8,128)(2,1)S(1)}, bf16[2,32,7,1024]{3,1,2,0:T(8,128)(2,1)S(1)}, u32[]{:S(2)}, u32[]{:S(2)}) collective-permute-start(bf16[2,32,7,1024]{3,1,2,0:T(8,128)(2,1)S(1)} %bitcast.90), channel_id=1, source_target_pairs={{0,1},{2,3},{4,5},{6,7},{8,9},{10,11},{12,13},{14,15},{16,17},{18,... | collective-permute-start | bytes 2752520 | tf_op jit(solution)/shard_map/ppermute | solution.py:18
  29.5 6.2 %copy-start.9 = (bf16[256,2048]{1,0:T(8,128)(2,1)S(1)}, bf16[256,2048]{1,0:T(8,128)(2,1)}, u32[]{:S(2)}) copy-start(bf16[256,2048]{1,0:T(8,128)(2,1)} %constant.12) | copy-start | bytes 3145732
  35.7 13.1 %copy-start.8 = (bf16[256,2048]{1,0:T(8,128)(2,1)S(1)}, bf16[256,2048]{1,0:T(8,128)(2,1)}, u32[]{:S(2)}) copy-start(bf16[256,2048]{1,0:T(8,128)(2,1)} %constant.10) | copy-start | bytes 3145732
  42.5 31.0 %all-to-all-start = ((bf16[16,16,2048]{2,1,0:T(8,128)(2,1)}), bf16[16,16,2048]{2,1,0:T(8,128)(2,1)S(1)}, u32[]{:S(2)}, u32[]{:S(2)}) async-start(bf16[16,16,2048]{2,1,0:T(8,128)(2,1)} %bitcast.5), calls=%async_computation | async-start | bytes 2097152 | tf_op jit(solution)/shard_map/all_to_all | solution.py:324
  55.5 22.3 %copy-start.7 = (s32[512]{0:T(512)S(1)}, s32[512]{0:T(512)}, u32[]{:S(2)}) copy-start(s32[512]{0:T(512)} %param.6) | copy-start | bytes 6148
  81.4 30.4 %copy-start.3 = (bf16[16,2,32,512,1]{3,2,1,0,4:T(8,128)(2,1)}, bf16[16,2,32,512,1]{3,2,1,0,4:T(8,128)(2,1)S(1)}, u32[]{:S(2)}) copy-start(bf16[16,2,32,512,1]{3,2,1,0,4:T(8,128)(2,1)S(1)} %copy.57) | copy-start | bytes 3145732
  81.5 45.7 %all-to-all-start.1 = ((bf16[16,16,2048]{2,1,0:T(8,128)(2,1)}), bf16[16,16,2048]{2,1,0:T(8,128)(2,1)S(1)}, u32[]{:S(2)}, u32[]{:S(2)}) async-start(bf16[16,16,2048]{2,1,0:T(8,128)(2,1)} %bitcast.3), calls=%async_computation.1 | async-start | bytes 2097152 | tf_op jit(solution)/shard_map/all_to_all | solution.py:324
  86.5 25.3 %collective-permute-start.1 = (bf16[32,32,512]{2,1,0:T(8,128)(2,1)S(1)}, bf16[32,32,512]{2,1,0:T(8,128)(2,1)S(1)}, u32[]{:S(2)}, u32[]{:S(2)}) collective-permute-start(bf16[32,32,512]{2,1,0:T(8,128)(2,1)S(1)} %bitcast.80), channel_id=1, source_target_pairs={{0,1},{1,0},{2,3},{3,2},{4,5},{5,4},{6,7},{7,6},{8,9},{9,8},{10,11... | collective-permute-start | bytes 3145736 | tf_op jit(solution)/shard_map/ppermute | solution.py:26
  111.8 1.0 copy-start.6
  135.3 31.3 %copy-start.2 = (bf16[16,2,32,512,1]{3,2,1,0,4:T(8,128)(2,1)}, bf16[16,2,32,512,1]{3,2,1,0,4:T(8,128)(2,1)S(1)}, u32[]{:S(2)}) copy-start(bf16[16,2,32,512,1]{3,2,1,0,4:T(8,128)(2,1)S(1)} %copy.56) | copy-start | bytes 3145732
  135.3 46.6 %all-to-all-start.2 = ((bf16[16,16,2048]{2,1,0:T(8,128)(2,1)}), bf16[16,16,2048]{2,1,0:T(8,128)(2,1)S(1)}, u32[]{:S(2)}, u32[]{:S(2)}) async-start(bf16[16,16,2048]{2,1,0:T(8,128)(2,1)} %bitcast.13), calls=%async_computation.2 | async-start | bytes 2097152 | tf_op jit(solution)/shard_map/all_to_all | solution.py:324
  141.3 25.2 %collective-permute-start.2 = (bf16[32,32,512]{2,1,0:T(8,128)(2,1)S(1)}, bf16[32,32,512]{2,1,0:T(8,128)(2,1)S(1)}, u32[]{:S(2)}, u32[]{:S(2)}) collective-permute-start(bf16[32,32,512]{2,1,0:T(8,128)(2,1)S(1)} %bitcast.77), channel_id=1, source_target_pairs={{0,1},{1,0},{2,3},{3,2},{4,5},{5,4},{6,7},{7,6},{8,9},{9,8},{10,11... | collective-permute-start | bytes 3145736 | tf_op jit(solution)/shard_map/ppermute | solution.py:26
  166.5 1.0 copy-start.5
  189.9 38.7 %copy-start = (bf16[16,2,32,512,1]{3,2,1,0,4:T(8,128)(2,1)}, bf16[16,2,32,512,1]{3,2,1,0,4:T(8,128)(2,1)S(1)}, u32[]{:S(2)}) copy-start(bf16[16,2,32,512,1]{3,2,1,0,4:T(8,128)(2,1)S(1)} %copy.55) | copy-start | bytes 3145732
  189.9 30.8 %all-to-all-start.3 = ((bf16[16,16,2048]{2,1,0:T(8,128)(2,1)}), bf16[16,16,2048]{2,1,0:T(8,128)(2,1)S(1)}, u32[]{:S(2)}, u32[]{:S(2)}) async-start(bf16[16,16,2048]{2,1,0:T(8,128)(2,1)} %bitcast.20), calls=%async_computation.3 | async-start | bytes 2097152 | tf_op jit(solution)/shard_map/all_to_all | solution.py:324
  195.9 33.1 %collective-permute-start.4 = (bf16[32,32,512]{2,1,0:T(8,128)(2,1)S(1)}, bf16[32,32,512]{2,1,0:T(8,128)(2,1)S(1)}, u32[]{:S(2)}, u32[]{:S(2)}) collective-permute-start(bf16[32,32,512]{2,1,0:T(8,128)(2,1)S(1)} %bitcast.71), channel_id=1, source_target_pairs={{0,1},{1,0},{2,3},{3,2},{4,5},{5,4},{6,7},{7,6},{8,9},{9,8},{10,11... | collective-permute-start | bytes 3145736 | tf_op jit(solution)/shard_map/ppermute | solution.py:26
  228.7 8.7 %copy-start.1 = (bf16[16,2,32,512,1]{3,2,1,0,4:T(8,128)(2,1)}, bf16[16,2,32,512,1]{3,2,1,0,4:T(8,128)(2,1)S(1)}, u32[]{:S(2)}) copy-start(bf16[16,2,32,512,1]{3,2,1,0,4:T(8,128)(2,1)S(1)} %copy.54) | copy-start | bytes 3145732
  228.7 25.8 %collective-permute-start.3 = (bf16[32,32,512]{2,1,0:T(8,128)(2,1)S(1)}, bf16[32,32,512]{2,1,0:T(8,128)(2,1)}, u32[]{:S(2)}, u32[]{:S(2)}) collective-permute-start(bf16[32,32,512]{2,1,0:T(8,128)(2,1)S(1)} %bitcast.74), channel_id=1, source_target_pairs={{0,1},{1,0},{2,3},{3,2},{4,5},{5,4},{6,7},{7,6},{8,9},{9,8},{10,11... | collective-permute-start | bytes 3145736 | tf_op jit(solution)/shard_map/ppermute | solution.py:26
  229.1 1.0 copy-start.4

commit v8 on v7

--- a/solution.py
+++ b/solution.py
@@ -307,24 +307,27 @@
 
     result = None
     pending = []
-    turned = None
+    reordered = []
     for chunk in range(chunks):
         source = filtered
         if chunk >= 2:
-            result = correlate(chunk - 2, pending[chunk - 2], result)
+            parts, following = lax.optimization_barrier((pending[chunk - 2], reordered[chunk - 1]))
+            pending.append(gathered_along(following, "blk"))
+            result = correlate(chunk - 2, parts, result)
             source, result = lax.optimization_barrier((filtered, result))
         spectra = jnp.einsum(
             "kj,nj->kn", weights[chunk], source, preferred_element_type=jnp.float32
         ).astype(jnp.bfloat16)
         spectra = spectra.reshape(groups, width, 2 * stations_local * spectra_local)
-        if chunk >= 1:
-            ordered = reorder(turned)
-            spectra, ordered = lax.optimization_barrier((spectra, ordered))
-            pending.append(gathered_along(ordered, "blk"))
         turned = lax.all_to_all(spectra, "stn", split_axis=0, concat_axis=0, tiled=True)
-    pending.append(gathered_along(reorder(turned), "blk"))
-    for chunk in range(max(0, chunks - 2), chunks):
-        result = correlate(chunk, pending[chunk], result)
+        reordered.append(reorder(turned))
+        if chunk == 0:
+            pending.append(gathered_along(reordered[0], "blk"))
+    if chunks >= 2:
+        parts, following = lax.optimization_barrier((pending[chunks - 2], reordered[chunks - 1]))
+        pending.append(gathered_along(following, "blk"))
+        result = correlate(chunks - 2, parts, result)
+    result = correlate(chunks - 1, pending[chunks - 1], result)
     return result
 
 

time: 263 us -> 254 us (0.966)
  waiting for transfers between devices: 113 us -> 105 us
    ppermute x4, waiting for transfers between devices: 67.3 us -> 18 us  [gathered_along(): parts.append(lax.ppermute(value, axis, pairs))]
    all_to_all x4, waiting for transfers between devices: 42.3 us -> 83.3 us  [per_device(): lax.all_to_all(spectra, 'stn', split_axis=0, concat_axis=0, tiled=True)]
    unnamed x21 -> x27, local copies, waits for them, and re-layouts: 7.46 us -> 8.11 us
  transfers between devices with their start and end apart: 9 -> 9, of which waited for: 6 -> 7; matrix products, arithmetic and copies ran while one was open for 13% -> 17% of each run, Pallas kernels for 14% -> 9%
where the time goes in v8:
time: 254 us; the launch traced here: 253 us
  waiting for transfers between devices  105 us (41%)
  Pallas kernels  49.9 us (20%)
  matrix products  41.3 us (16%)
  local copies, waits for them, and re-layouts  27.7 us (11%)
  starting transfers between devices  25.1 us (10%)
  other arithmetic  3.8 us (1%)
    all_to_all x4, waiting for transfers between devices, per_device(): lax.all_to_all(spectra, 'stn', split_axis=0, concat_axis=0, tiled=True)  83.3 us
    pallas_call x4, Pallas kernels, correlate_rows_chunk(): pl.pallas_call(correlate_rows_kernel, grid_spec=grid_spec, out_shape=jax....  29.5 us
    dot_general x4, matrix products, per_device(): jnp.einsum('kj,nj->kn', weights[chunk], source, preferred_element_type=jn...  27.1 us
    all_to_all x4, starting transfers between devices, per_device(): lax.all_to_all(spectra, 'stn', split_axis=0, concat_axis=0, tiled=True)  22.6 us
    ppermute x4, waiting for transfers between devices, gathered_along(): parts.append(lax.ppermute(value, axis, pairs))  18 us
    reshape x4, local copies, waits for them, and re-layouts, reorder(): turned = turned.reshape(groups, width, 2, stations_local, spectra_local)  17.6 us
    pallas_call x1, Pallas kernels, filter_frames(): pl.pallas_call(fir_kernel, grid=(stations_local // group,), in_specs=[pl....  14.3 us
    dot_general x4, matrix products, reorder(): jnp.einsum('gkias,gar->kisr', turned, selector, preferred_element_type=jn...  14.2 us
  transfers between devices with their start and end apart: 9, of which 7 were waited for; matrix products, arithmetic and copies ran while one was open for 17% of the time, Pallas kernels for 9%

profile of v8, /device:TPU:14, one launch (start us, length us, event | category | flops | bytes accessed | tf_op | source)
XLA Modules:
  0.0 253.2 jit_solution(11613511839971473109)
XLA Ops:
  0.0 3.8 %convert.3 = bf16[2,32,32768]{2,1,0:T(8,128)(2,1)S(1)} convert(s32[2,32,32768]{2,1,0:T(8,128)} %param.4) | non-fusion elementwise | flops 2097152 | bytes 12582912 | tf_op jit(solution)/shard_map/convert
  3.8 0.1 slice.21
  3.9 0.1 copy.57
  4.0 1.3 collective-permute-start
  5.3 4.5 %copy.39 = bf16[8,8,32,1024]{3,2,1,0:T(8,128)(2,1)} copy(bf16[8,8,32,1024]{3,1,2,0:T(8,128)(2,1)S(1)} %bitcast.71) | data formatting | bytes 8388608
  9.7 14.3 %shard_map.46.previous_ref = bf16[2,32,32,2048]{3,2,1,0:T(8,128)(2,1)} custom-call(f32[8,1024]{1,0:T(8,128)} %taps_ref.3, bf16[2,32,32,1024]{3,2,1,0:T(8,128)(2,1)} %bitcast.65), custom_call_target="tpu_custom_call" | custom-call | flops 67108864 | bytes 12582912 | tf_op jit(solution)/shard_map/pallas_call | solution.py:110
  24.1 3.9 %collective-permute-done = bf16[2,32,7,1024]{3,1,2,0:T(8,128)(2,1)S(1)} collective-permute-done((bf16[2,32,7,1024]{3,1,2,0:T(8,128)(2,1)S(1)}, bf16[2,32,7,1024]{3,1,2,0:T(8,128)(2,1)S(1)}, u32[]{:S(2)}, u32[]{:S(2)}) %collective-permute-start) | collective-permute-done | bytes 917536 | tf_op jit(solution)/shard_map/ppermute | solution.py:18
  27.9 1.6 copy.20.halo_ref
  29.5 6.1 %shard_map.47 = bf16[2,32,32,2048]{3,2,1,0:T(8,128)(2,1)} custom-call(f32[8,1024]{1,0:T(8,128)} %taps_ref.3, bf16[2,32,7,1024]{3,2,1,0:T(8,128)(2,1)} %copy.20.halo_ref, bf16[2,32,32,1024]{3,2,1,0:T(8,128)(2,1)} %bitcast.66, bf16[2,32,32,2048]{3,2,1,0:T(8,128)(2,1)} %shard_map.46.previous_ref), custom_call_target="tpu_custom_call", output_to_operand_aliasing={{}: (3, {})} | custom-call | flops 16777216 | bytes 4194304 | tf_op jit(solution)/shard_map/pallas_call | solution.py:127
  35.7 6.8 %convolution_convert_fusion.3 = bf16[2048,256]{0,1:T(8,128)(2,1)} fusion(bf16[2048,2048]{1,0:T(8,128)(2,1)} %bitcast.67, bf16[256,2048]{1,0:T(8,128)(2,1)S(1)} %copy-done.12), kind=kOutput, calls=%fused_computation.11 | convolution fusion | flops 2148007936 | bytes 10485760 | tf_op jit(solution)/shard_map/kj,nj->kn/dot_general | solution.py:318
  42.5 6.2 %all-to-all-start = ((bf16[16,16,2048]{2,1,0:T(8,128)(2,1)}), bf16[16,16,2048]{2,1,0:T(8,128)(2,1)S(1)}, u32[]{:S(2)}, u32[]{:S(2)}) async-start(bf16[16,16,2048]{2,1,0:T(8,128)(2,1)} %bitcast.3), calls=%async_computation | async-start | bytes 2097152 | tf_op jit(solution)/shard_map/all_to_all | solution.py:322
  48.7 6.7 %convolution_convert_fusion.2 = bf16[2048,256]{0,1:T(8,128)(2,1)} fusion(bf16[2048,2048]{1,0:T(8,128)(2,1)} %bitcast.68, bf16[256,2048]{1,0:T(8,128)(2,1)S(1)} %copy-done.11), kind=kOutput, calls=%fused_computation.10 | convolution fusion | flops 2148007936 | bytes 10485760 | tf_op jit(solution)/shard_map/kj,nj->kn/dot_general | solution.py:318
  55.5 18.0 %all-to-all-done = bf16[16,16,2048]{2,1,0:T(8,128)(2,1)S(1)} async-done(((bf16[16,16,2048]{2,1,0:T(8,128)(2,1)}), bf16[16,16,2048]{2,1,0:T(8,128)(2,1)S(1)}, u32[]{:S(2)}, u32[]{:S(2)}) %all-to-all-start) | async-done | bytes 1048608 | tf_op jit(solution)/shard_map/all_to_all | solution.py:322
  73.4 5.1 %all-to-all-start.1 = ((bf16[16,16,2048]{2,1,0:T(8,128)(2,1)}), bf16[16,16,2048]{2,1,0:T(8,128)(2,1)S(1)}, u32[]{:S(2)}, u32[]{:S(2)}) async-start(bf16[16,16,2048]{2,1,0:T(8,128)(2,1)} %bitcast.9), calls=%async_computation.1 | async-start | bytes 2097152 | tf_op jit(solution)/shard_map/all_to_all | solution.py:322
  78.5 4.4 %reshape.93 = bf16[16,16,2,32,32]{4,3,2,1,0:T(8,128)(2,1)} reshape(bf16[16,16,2048]{2,1,0:T(8,128)(2,1)S(1)} %all-to-all-done) | data formatting | bytes 2097152 | tf_op jit(solution)/shard_map/reshape | solution.py:302
  82.9 3.6 %fusion.6 = bf16[16,2,32,512,1]{3,2,0,1,4:T(8,128)(2,1)S(1)} fusion(bf16[16,16,2,32,32]{4,3,2,1,0:T(8,128)(2,1)} %reshape.93, s32[16,32]{1,0:T(8,128)S(1)} %multiply_add_fusion, s32[512]{0:T(512)S(1)} %copy-done.8), kind=kOutput, calls=%fused_computation.6 | convolution fusion | flops 537133056 | bytes 2101248 | tf_op jit(solution)/shard_map/gkias,gar->kisr/dot_general | solution.py:303
  86.5 0.1 copy.56
  86.6 0.1 collective-permute-start.1
  86.7 16.6 %all-to-all-done.1 = bf16[16,16,2048]{2,1,0:T(8,128)(2,1)S(1)} async-done(((bf16[16,16,2048]{2,1,0:T(8,128)(2,1)}), bf16[16,16,2048]{2,1,0:T(8,128)(2,1)S(1)}, u32[]{:S(2)}, u32[]{:S(2)}) %all-to-all-start.1) | async-done | bytes 1048608 | tf_op jit(solution)/shard_map/all_to_all | solution.py:322
  103.3 4.4 %reshape.96 = bf16[16,16,2,32,32]{4,3,2,1,0:T(8,128)(2,1)} reshape(bf16[16,16,2048]{2,1,0:T(8,128)(2,1)S(1)} %all-to-all-done.1) | data formatting | bytes 2097152 | tf_op jit(solution)/shard_map/reshape | solution.py:302
  107.6 3.6 %fusion.4 = bf16[16,2,32,512,1]{3,2,0,1,4:T(8,128)(2,1)S(1)} fusion(bf16[16,16,2,32,32]{4,3,2,1,0:T(8,128)(2,1)} %reshape.96, s32[16,32]{1,0:T(8,128)S(1)} %multiply_add_fusion, s32[512]{0:T(512)S(1)} %copy-done.8), kind=kOutput, calls=%fused_computation.4 | convolution fusion | flops 537133056 | bytes 2101248 | tf_op jit(solution)/shard_map/gkias,gar->kisr/dot_general | solution.py:303
  111.2 0.1 copy.55
  111.3 0.6 collective-permute-done.1
  111.8 1.0 copy-done.7
  112.8 7.4 %shard_map.48.refs_4_ = bf16[2,64,256,512]{3,2,1,0:T(8,128)(2,1)} custom-call(s32[1]{0:T(128)} %bitcast.block_ref, bf16[16,2,32,512]{3,2,1,0:T(8,128)(2,1)} %bitcast.82, bf16[16,2,32,512]{3,2,1,0:T(8,128)(2,1)} %bitcast.90, bf16[16,2,32,512]{3,2,1,0:T(8,128)(2,1)} %bitcast.83, bf16[16,2,32,512]{3,2,1,0:T(8,128)(2,1)} %bitcast.91), custom_call_target="tpu_custom_call" | custom-call | flops 1073741824 | bytes 11534336 | tf_op jit(solution)/shard_map/pallas_call | solution.py:244
  120.2 6.8 %convolution_convert_fusion.1 = bf16[2048,256]{0,1:T(8,128)(2,1)} fusion(bf16[2048,2048]{1,0:T(8,128)(2,1)} %bitcast.69, bf16[256,2048]{1,0:T(8,128)(2,1)S(1)} %copy-done.10), kind=kOutput, calls=%fused_computation.9 | convolution fusion | flops 2148007936 | bytes 10485760 | tf_op jit(solution)/shard_map/kj,nj->kn/dot_general | solution.py:318
  127.1 6.0 %all-to-all-start.2 = ((bf16[16,16,2048]{2,1,0:T(8,128)(2,1)}), bf16[16,16,2048]{2,1,0:T(8,128)(2,1)S(1)}, u32[]{:S(2)}, u32[]{:S(2)}) async-start(bf16[16,16,2048]{2,1,0:T(8,128)(2,1)} %bitcast.16), calls=%async_computation.2 | async-start | bytes 2097152 | tf_op jit(solution)/shard_map/all_to_all | solution.py:322
  133.1 0.4 collective-permute-start.2
  133.4 24.4 %all-to-all-done.2 = bf16[16,16,2048]{2,1,0:T(8,128)(2,1)S(1)} async-done(((bf16[16,16,2048]{2,1,0:T(8,128)(2,1)}), bf16[16,16,2048]{2,1,0:T(8,128)(2,1)S(1)}, u32[]{:S(2)}, u32[]{:S(2)}) %all-to-all-start.2) | async-done | bytes 1048608 | tf_op jit(solution)/shard_map/all_to_all | solution.py:322
  157.8 4.5 %reshape.101 = bf16[16,16,2,32,32]{4,3,2,1,0:T(8,128)(2,1)} reshape(bf16[16,16,2048]{2,1,0:T(8,128)(2,1)S(1)} %all-to-all-done.2) | data formatting | bytes 2097152 | tf_op jit(solution)/shard_map/reshape | solution.py:302
  162.3 3.6 %fusion.2 = bf16[16,2,32,512,1]{3,2,0,1,4:T(8,128)(2,1)S(1)} fusion(bf16[16,16,2,32,32]{4,3,2,1,0:T(8,128)(2,1)} %reshape.101, s32[16,32]{1,0:T(8,128)S(1)} %multiply_add_fusion, s32[512]{0:T(512)S(1)} %copy-done.8), kind=kOutput, calls=%fused_computation.2 | convolution fusion | flops 537133056 | bytes 2101248 | tf_op jit(solution)/shard_map/gkias,gar->kisr/dot_general | solution.py:303
  165.9 0.1 copy.54
  166.0 0.0 collective-permute-done.2
  166.0 1.0 copy-done.5
  167.0 7.4 %shard_map.49.refs_4_ = bf16[2,64,256,512]{3,2,1,0:T(8,128)(2,1)} custom-call(s32[1]{0:T(128)} %bitcast.block_ref, bf16[16,2,32,512]{3,2,1,0:T(8,128)(2,1)} %bitcast.76, bf16[16,2,32,512]{3,2,1,0:T(8,128)(2,1)} %bitcast.86, bf16[16,2,32,512]{3,2,1,0:T(8,128)(2,1)} %bitcast.77, bf16[16,2,32,512]{3,2,1,0:T(8,128)(2,1)} %bitcast.87, ...), custom_call_target="tpu_custom_call", output_to_operand_aliasing={{}: (5, {})} | custom-call | flops 1073741824 | bytes 11534336 | tf_op jit(solution)/shard_map/pallas_call | solution.py:244
  174.4 6.7 %convolution_convert_fusion = bf16[2048,256]{0,1:T(8,128)(2,1)} fusion(bf16[2048,2048]{1,0:T(8,128)(2,1)} %bitcast.70, bf16[256,2048]{1,0:T(8,128)(2,1)S(1)} %copy-done.9), kind=kOutput, calls=%fused_computation.8 | convolution fusion | flops 2148007936 | bytes 10485760 | tf_op jit(solution)/shard_map/kj,nj->kn/dot_general | solution.py:318
  181.1 5.3 %all-to-all-start.3 = ((bf16[16,16,2048]{2,1,0:T(8,128)(2,1)}), bf16[16,16,2048]{2,1,0:T(8,128)(2,1)S(1)}, u32[]{:S(2)}, u32[]{:S(2)}) async-start(bf16[16,16,2048]{2,1,0:T(8,128)(2,1)} %bitcast.22), calls=%async_computation.3 | async-start | bytes 2097152 | tf_op jit(solution)/shard_map/all_to_all | solution.py:322
  186.4 0.4 collective-permute-start.3
  186.8 24.4 %all-to-all-done.3 = bf16[16,16,2048]{2,1,0:T(8,128)(2,1)S(1)} async-done(((bf16[16,16,2048]{2,1,0:T(8,128)(2,1)}), bf16[16,16,2048]{2,1,0:T(8,128)(2,1)S(1)}, u32[]{:S(2)}, u32[]{:S(2)}) %all-to-all-start.3) | async-done | bytes 1048608 | tf_op jit(solution)/shard_map/all_to_all | solution.py:322
  211.2 4.4 %reshape.106 = bf16[16,16,2,32,32]{4,3,2,1,0:T(8,128)(2,1)} reshape(bf16[16,16,2048]{2,1,0:T(8,128)(2,1)S(1)} %all-to-all-done.3) | data formatting | bytes 2097152 | tf_op jit(solution)/shard_map/reshape | solution.py:302
  215.6 3.6 %fusion = bf16[16,2,32,512,1]{3,2,0,1,4:T(8,128)(2,1)S(1)} fusion(bf16[16,16,2,32,32]{4,3,2,1,0:T(8,128)(2,1)} %reshape.106, s32[16,32]{1,0:T(8,128)S(1)} %multiply_add_fusion, s32[512]{0:T(512)S(1)} %copy-done.8), kind=kOutput, calls=%fused_computation | convolution fusion | flops 537133056 | bytes 2101248 | tf_op jit(solution)/shard_map/gkias,gar->kisr/dot_general | solution.py:303
  219.1 0.1 copy.53
  219.2 0.4 collective-permute-start.4
  219.6 0.6 copy-done.4
  220.2 7.3 %shard_map.50.refs_4_ = bf16[2,64,256,512]{3,2,1,0:T(8,128)(2,1)} custom-call(s32[1]{0:T(128)} %bitcast.block_ref, bf16[16,2,32,512]{3,2,1,0:T(8,128)(2,1)} %bitcast.73, bf16[16,2,32,512]{3,2,1,0:T(8,128)(2,1)} %bitcast.84, bf16[16,2,32,512]{3,2,1,0:T(8,128)(2,1)} %bitcast.74, bf16[16,2,32,512]{3,2,1,0:T(8,128)(2,1)} %bitcast.85, ...), custom_call_target="tpu_custom_call", output_to_operand_aliasing={{}: (5, {})} | custom-call | flops 1073741824 | bytes 11534336 | tf_op jit(solution)/shard_map/pallas_call | solution.py:244
  227.5 17.4 %collective-permute-done.4 = bf16[32,32,512]{2,1,0:T(8,128)(2,1)S(1)} collective-permute-done((bf16[32,32,512]{2,1,0:T(8,128)(2,1)S(1)}, bf16[32,32,512]{2,1,0:T(8,128)(2,1)S(1)}, u32[]{:S(2)}, u32[]{:S(2)}) %collective-permute-start.4) | collective-permute-done | bytes 1048608 | tf_op jit(solution)/shard_map/ppermute | solution.py:26
  245.0 1.0 copy-done.6
  245.9 7.3 %shard_map.51 = bf16[2,64,256,512]{3,2,1,0:T(8,128)(2,1)} custom-call(s32[1]{0:T(128)} %bitcast.block_ref, bf16[16,2,32,512]{3,2,1,0:T(8,128)(2,1)} %bitcast.79, bf16[16,2,32,512]{3,2,1,0:T(8,128)(2,1)} %bitcast.88, bf16[16,2,32,512]{3,2,1,0:T(8,128)(2,1)} %bitcast.80, bf16[16,2,32,512]{3,2,1,0:T(8,128)(2,1)} %bitcast.89, ...), custom_call_target="tpu_custom_call", output_to_operand_aliasing={{}: (5, {})} | custom-call | flops 1073741824 | bytes 11534336 | tf_op jit(solution)/shard_map/pallas_call | solution.py:244
  (24 shorter events, 0.1 us)
Async XLA Ops:
  4.0 24.0 %collective-permute-start = (bf16[2,32,7,1024]{3,1,2,0:T(8,128)(2,1)S(1)}, bf16[2,32,7,1024]{3,1,2,0:T(8,128)(2,1)S(1)}, u32[]{:S(2)}, u32[]{:S(2)}) collective-permute-start(bf16[2,32,7,1024]{3,1,2,0:T(8,128)(2,1)S(1)} %bitcast.93), channel_id=1, source_target_pairs={{0,1},{2,3},{4,5},{6,7},{8,9},{10,11},{12,13},{14,15},{16,17},{18,... | collective-permute-start | bytes 2752520 | tf_op jit(solution)/shard_map/ppermute | solution.py:18
  29.5 6.1 %copy-start.12 = (bf16[256,2048]{1,0:T(8,128)(2,1)S(1)}, bf16[256,2048]{1,0:T(8,128)(2,1)}, u32[]{:S(2)}) copy-start(bf16[256,2048]{1,0:T(8,128)(2,1)} %constant.10) | copy-start | bytes 3145732
  35.7 13.0 %copy-start.11 = (bf16[256,2048]{1,0:T(8,128)(2,1)S(1)}, bf16[256,2048]{1,0:T(8,128)(2,1)}, u32[]{:S(2)}) copy-start(bf16[256,2048]{1,0:T(8,128)(2,1)} %constant.12) | copy-start | bytes 3145732
  42.5 31.0 %all-to-all-start = ((bf16[16,16,2048]{2,1,0:T(8,128)(2,1)}), bf16[16,16,2048]{2,1,0:T(8,128)(2,1)S(1)}, u32[]{:S(2)}, u32[]{:S(2)}) async-start(bf16[16,16,2048]{2,1,0:T(8,128)(2,1)} %bitcast.3), calls=%async_computation | async-start | bytes 2097152 | tf_op jit(solution)/shard_map/all_to_all | solution.py:322
  55.4 27.5 %copy-start.8 = (s32[512]{0:T(512)S(1)}, s32[512]{0:T(512)}, u32[]{:S(2)}) copy-start(s32[512]{0:T(512)} %param.6) | copy-start | bytes 6148
  73.4 29.8 %all-to-all-start.1 = ((bf16[16,16,2048]{2,1,0:T(8,128)(2,1)}), bf16[16,16,2048]{2,1,0:T(8,128)(2,1)S(1)}, u32[]{:S(2)}, u32[]{:S(2)}) async-start(bf16[16,16,2048]{2,1,0:T(8,128)(2,1)} %bitcast.9), calls=%async_computation.1 | async-start | bytes 2097152 | tf_op jit(solution)/shard_map/all_to_all | solution.py:322
  86.6 24.6 %copy-start.3 = (bf16[16,2,32,512,1]{3,2,1,0,4:T(8,128)(2,1)}, bf16[16,2,32,512,1]{3,2,1,0,4:T(8,128)(2,1)S(1)}, u32[]{:S(2)}) copy-start(bf16[16,2,32,512,1]{3,2,1,0,4:T(8,128)(2,1)S(1)} %copy.56) | copy-start | bytes 3145732
  86.6 25.3 %collective-permute-start.1 = (bf16[32,32,512]{2,1,0:T(8,128)(2,1)S(1)}, bf16[32,32,512]{2,1,0:T(8,128)(2,1)S(1)}, u32[]{:S(2)}, u32[]{:S(2)}) collective-permute-start(bf16[32,32,512]{2,1,0:T(8,128)(2,1)S(1)} %bitcast.81), channel_id=1, source_target_pairs={{0,1},{1,0},{2,3},{3,2},{4,5},{5,4},{6,7},{7,6},{8,9},{9,8},{10,11... | collective-permute-start | bytes 3145736 | tf_op jit(solution)/shard_map/ppermute | solution.py:26
  111.3 21.8 %copy-start.1 = (bf16[16,2,32,512,1]{3,2,1,0,4:T(8,128)(2,1)}, bf16[16,2,32,512,1]{3,2,1,0,4:T(8,128)(2,1)S(1)}, u32[]{:S(2)}) copy-start(bf16[16,2,32,512,1]{3,2,1,0,4:T(8,128)(2,1)S(1)} %copy.55) | copy-start | bytes 3145732
  111.8 1.0 copy-start.7
  112.8 7.4 %copy-start.10 = (bf16[256,2048]{1,0:T(8,128)(2,1)S(1)}, bf16[256,2048]{1,0:T(8,128)(2,1)}, u32[]{:S(2)}) copy-start(bf16[256,2048]{1,0:T(8,128)(2,1)} %constant.14) | copy-start | bytes 3145732
  127.1 30.7 %all-to-all-start.2 = ((bf16[16,16,2048]{2,1,0:T(8,128)(2,1)}), bf16[16,16,2048]{2,1,0:T(8,128)(2,1)S(1)}, u32[]{:S(2)}, u32[]{:S(2)}) async-start(bf16[16,16,2048]{2,1,0:T(8,128)(2,1)} %bitcast.16), calls=%async_computation.2 | async-start | bytes 2097152 | tf_op jit(solution)/shard_map/all_to_all | solution.py:322
  133.1 32.9 %collective-permute-start.2 = (bf16[32,32,512]{2,1,0:T(8,128)(2,1)S(1)}, bf16[32,32,512]{2,1,0:T(8,128)(2,1)S(1)}, u32[]{:S(2)}, u32[]{:S(2)}) collective-permute-start(bf16[32,32,512]{2,1,0:T(8,128)(2,1)S(1)} %bitcast.75), channel_id=1, source_target_pairs={{0,1},{1,0},{2,3},{3,2},{4,5},{5,4},{6,7},{7,6},{8,9},{9,8},{10,11... | collective-permute-start | bytes 3145736 | tf_op jit(solution)/shard_map/ppermute | solution.py:26
  166.0 20.5 %copy-start = (bf16[16,2,32,512,1]{3,2,1,0,4:T(8,128)(2,1)}, bf16[16,2,32,512,1]{3,2,1,0,4:T(8,128)(2,1)S(1)}, u32[]{:S(2)}) copy-start(bf16[16,2,32,512,1]{3,2,1,0,4:T(8,128)(2,1)S(1)} %copy.54) | copy-start | bytes 3145732
  166.0 1.0 copy-start.5
  167.0 7.4 %copy-start.9 = (bf16[256,2048]{1,0:T(8,128)(2,1)S(1)}, bf16[256,2048]{1,0:T(8,128)(2,1)}, u32[]{:S(2)}) copy-start(bf16[256,2048]{1,0:T(8,128)(2,1)} %constant.16) | copy-start | bytes 3145732
  181.1 30.0 %all-to-all-start.3 = ((bf16[16,16,2048]{2,1,0:T(8,128)(2,1)}), bf16[16,16,2048]{2,1,0:T(8,128)(2,1)S(1)}, u32[]{:S(2)}, u32[]{:S(2)}) async-start(bf16[16,16,2048]{2,1,0:T(8,128)(2,1)} %bitcast.22), calls=%async_computation.3 | async-start | bytes 2097152 | tf_op jit(solution)/shard_map/all_to_all | solution.py:322
  186.4 32.8 %collective-permute-start.3 = (bf16[32,32,512]{2,1,0:T(8,128)(2,1)S(1)}, bf16[32,32,512]{2,1,0:T(8,128)(2,1)S(1)}, u32[]{:S(2)}, u32[]{:S(2)}) collective-permute-start(bf16[32,32,512]{2,1,0:T(8,128)(2,1)S(1)} %bitcast.72), channel_id=1, source_target_pairs={{0,1},{1,0},{2,3},{3,2},{4,5},{5,4},{6,7},{7,6},{8,9},{9,8},{10,11... | collective-permute-start | bytes 3145736 | tf_op jit(solution)/shard_map/ppermute | solution.py:26
  219.2 8.3 %copy-start.2 = (bf16[16,2,32,512,1]{3,2,1,0,4:T(8,128)(2,1)}, bf16[16,2,32,512,1]{3,2,1,0,4:T(8,128)(2,1)S(1)}, u32[]{:S(2)}) copy-start(bf16[16,2,32,512,1]{3,2,1,0,4:T(8,128)(2,1)S(1)} %copy.53) | copy-start | bytes 3145732
  219.2 1.0 copy-start.4
  219.2 25.7 %collective-permute-start.4 = (bf16[32,32,512]{2,1,0:T(8,128)(2,1)S(1)}, bf16[32,32,512]{2,1,0:T(8,128)(2,1)S(1)}, u32[]{:S(2)}, u32[]{:S(2)}) collective-permute-start(bf16[32,32,512]{2,1,0:T(8,128)(2,1)S(1)} %bitcast.78), channel_id=1, source_target_pairs={{0,1},{1,0},{2,3},{3,2},{4,5},{5,4},{6,7},{7,6},{8,9},{9,8},{10,11... | collective-permute-start | bytes 3145736 | tf_op jit(solution)/shard_map/ppermute | solution.py:26
  244.9 1.0 copy-start.6

commit v9 on v5

--- a/solution.py
+++ b/solution.py
@@ -123,16 +123,17 @@
         ),
     )(fir_taps, frames)
     edge = 8
+    edge_group = stations_local // 4 if stations_local % 4 == 0 else stations_local
     return pl.pallas_call(
         fir_edge_kernel,
-        grid=(1,),
+        grid=(stations_local // edge_group,),
         in_specs=[
             pl.BlockSpec((tap_count, channels), lambda a: (0, 0)),
-            pl.BlockSpec((2, stations_local, tap_count - 1, channels), lambda a: (0, 0, 0, 0)),
-            pl.BlockSpec((2, stations_local, edge, channels), lambda a: (0, 0, 0, 0)),
+            pl.BlockSpec((2, edge_group, tap_count - 1, channels), lambda a: (0, a, 0, 0)),
+            pl.BlockSpec((2, edge_group, edge, channels), lambda a: (0, a, 0, 0)),
             pl.BlockSpec(memory_space=pl.ANY),
         ],
-        out_specs=pl.BlockSpec((2, stations_local, edge, 2 * channels), lambda a: (0, 0, 0, 0)),
+        out_specs=pl.BlockSpec((2, edge_group, edge, 2 * channels), lambda a: (0, a, 0, 0)),
         out_shape=out_shape,
         input_output_aliases={3: 0},
         cost_estimate=pl.CostEstimate(
@@ -259,8 +260,9 @@
     chunks = chunk_count(local_channels)
     width = local_channels // chunks
 
+    earlier = samples[:, :, (spectra_local - (tap_count - 1)) * channels :].astype(jnp.bfloat16)
+    earlier = earlier.reshape(2, stations_local, tap_count - 1, channels)
     frames = samples.astype(jnp.bfloat16).reshape(2, stations_local, spectra_local, channels)
-    earlier = frames[:, :, spectra_local - (tap_count - 1) :, :]
     earlier = passed_along(earlier, "blk", 1)
     filtered = filter_frames(fir_taps, earlier, frames)
     filtered = filtered.reshape(2 * stations_local * spectra_local, 2 * channels)

time: 241 us -> 235 us (0.975)
  waiting for transfers between devices: 83.6 us -> 79.1 us
    ppermute x1, waiting for transfers between devices: 8.37 us -> 3.92 us  [passed_along(): lax.ppermute(value, axis, [(source, source + steps) for source in range(i...]
    another operation x0 -> x1, other arithmetic: none -> 3.79 us
    convert_element_type x1 -> x0, other arithmetic: 3.79 us -> none  [per_device(): samples.astype(jnp.bfloat16)]
  transfers between devices with their start and end apart: 9 -> 9, of which waited for: 8 -> 8; matrix products, arithmetic and copies ran while one was open for 25% -> 27% of each run, Pallas kernels for 15% -> 16%
where the time goes in v9:
time: 235 us; the launch traced here: 234 us
  waiting for transfers between devices  79.1 us (34%)
  Pallas kernels  50.3 us (21%)
  matrix products  41.4 us (18%)
  starting transfers between devices  24.9 us (11%)
  local copies, waits for them, and re-layouts  24.1 us (10%)
  other arithmetic  13.6 us (6%)
    all_to_all x4, waiting for transfers between devices, per_device(): lax.all_to_all(spectra, 'stn', split_axis=0, concat_axis=0, tiled=True)  56.1 us
    pallas_call x4, Pallas kernels, correlate_rows_chunk(): pl.pallas_call(correlate_rows_kernel, grid_spec=grid_spec, out_shape=jax....  29.9 us
    dot_general x4, matrix products, per_device(): jnp.einsum('kj,nj->kn', weights[chunk], source, preferred_element_type=jn...  27.1 us
    all_to_all x4, starting transfers between devices, per_device(): lax.all_to_all(spectra, 'stn', split_axis=0, concat_axis=0, tiled=True)  22.4 us
    ppermute x4, waiting for transfers between devices, gathered_along(): parts.append(lax.ppermute(value, axis, pairs))  19.1 us
    reshape x4, local copies, waits for them, and re-layouts, per_device(): turned = turned.reshape(groups, width, 2, stations_local, spectra_local)  17.6 us
    pallas_call x1, Pallas kernels, filter_frames(): pl.pallas_call(fir_kernel, grid=(stations_local // group,), in_specs=[pl....  14.3 us
    dot_general x4, matrix products, per_device(): jnp.einsum('gkias,gar->kisr', turned, selector, preferred_element_type=jn...  14.2 us
  transfers between devices with their start and end apart: 9, of which 8 were waited for; matrix products, arithmetic and copies ran while one was open for 27% of the time, Pallas kernels for 16%

profile of v9, /device:TPU:14, one launch (start us, length us, event | category | flops | bytes accessed | tf_op | source)
XLA Modules:
  0.0 233.6 jit_solution(18015714493061800441)
XLA Ops:
  0.0 3.8 %convert.3 = bf16[2,32,32768]{2,1,0:T(8,128)(2,1)S(1)} convert(s32[2,32,32768]{2,1,0:T(8,128)} %param.4) | non-fusion elementwise | flops 2097152 | bytes 12582912 | tf_op jit(solution)/shard_map/convert
  3.8 0.1 slice.21
  3.9 0.1 copy.57
  4.0 1.3 collective-permute-start
  5.3 4.5 %copy.39 = bf16[8,8,32,1024]{3,2,1,0:T(8,128)(2,1)} copy(bf16[8,8,32,1024]{3,1,2,0:T(8,128)(2,1)S(1)} %bitcast.67) | data formatting | bytes 8388608
  9.7 14.3 %shard_map.46.previous_ref = bf16[2,32,32,2048]{3,2,1,0:T(8,128)(2,1)} custom-call(f32[8,1024]{1,0:T(8,128)} %taps_ref.3, bf16[2,32,32,1024]{3,2,1,0:T(8,128)(2,1)} %bitcast.61), custom_call_target="tpu_custom_call" | custom-call | flops 67108864 | bytes 12582912 | tf_op jit(solution)/shard_map/pallas_call | solution.py:110
  24.0 3.9 %collective-permute-done = bf16[2,32,7,1024]{3,1,2,0:T(8,128)(2,1)S(1)} collective-permute-done((bf16[2,32,7,1024]{3,1,2,0:T(8,128)(2,1)S(1)}, bf16[2,32,7,1024]{3,1,2,0:T(8,128)(2,1)S(1)}, u32[]{:S(2)}, u32[]{:S(2)}) %collective-permute-start) | collective-permute-done | bytes 917536 | tf_op jit(solution)/shard_map/ppermute | solution.py:18
  27.9 1.6 copy.20.halo_ref
  29.5 6.1 %shard_map.47 = bf16[2,32,32,2048]{3,2,1,0:T(8,128)(2,1)} custom-call(f32[8,1024]{1,0:T(8,128)} %taps_ref.3, bf16[2,32,7,1024]{3,2,1,0:T(8,128)(2,1)} %copy.20.halo_ref, bf16[2,32,32,1024]{3,2,1,0:T(8,128)(2,1)} %bitcast.62, bf16[2,32,32,2048]{3,2,1,0:T(8,128)(2,1)} %shard_map.46.previous_ref), custom_call_target="tpu_custom_call", output_to_operand_aliasing={{}: (3, {})} | custom-call | flops 16777216 | bytes 4194304 | tf_op jit(solution)/shard_map/pallas_call | solution.py:127
  35.6 6.8 %convolution_convert_fusion.2 = bf16[2048,256]{0,1:T(8,128)(2,1)} fusion(bf16[2048,2048]{1,0:T(8,128)(2,1)} %bitcast.63, bf16[256,2048]{1,0:T(8,128)(2,1)S(1)} %copy-done.4), kind=kOutput, calls=%fused_computation.10 | convolution fusion | flops 2148007936 | bytes 10485760 | tf_op jit(solution)/shard_map/kj,nj->kn/dot_general | solution.py:300
  42.4 6.2 %all-to-all-start.1 = ((bf16[16,16,2048]{2,1,0:T(8,128)(2,1)}), bf16[16,16,2048]{2,1,0:T(8,128)(2,1)S(1)}, u32[]{:S(2)}, u32[]{:S(2)}) async-start(bf16[16,16,2048]{2,1,0:T(8,128)(2,1)} %bitcast.10), calls=%async_computation.1 | async-start | bytes 2097152 | tf_op jit(solution)/shard_map/all_to_all | solution.py:304
  48.7 6.8 %convolution_convert_fusion.3 = bf16[2048,256]{0,1:T(8,128)(2,1)} fusion(bf16[2048,2048]{1,0:T(8,128)(2,1)} %bitcast.64, bf16[256,2048]{1,0:T(8,128)(2,1)S(1)} %copy-done.3), kind=kOutput, calls=%fused_computation.11 | convolution fusion | flops 2148007936 | bytes 10485760 | tf_op jit(solution)/shard_map/kj,nj->kn/dot_general | solution.py:300
  55.5 17.9 %all-to-all-done.1 = bf16[16,16,2048]{2,1,0:T(8,128)(2,1)S(1)} async-done(((bf16[16,16,2048]{2,1,0:T(8,128)(2,1)}), bf16[16,16,2048]{2,1,0:T(8,128)(2,1)S(1)}, u32[]{:S(2)}, u32[]{:S(2)}) %all-to-all-start.1) | async-done | bytes 1048608 | tf_op jit(solution)/shard_map/all_to_all | solution.py:304
  73.4 5.1 %all-to-all-start = ((bf16[16,16,2048]{2,1,0:T(8,128)(2,1)}), bf16[16,16,2048]{2,1,0:T(8,128)(2,1)S(1)}, u32[]{:S(2)}, u32[]{:S(2)}) async-start(bf16[16,16,2048]{2,1,0:T(8,128)(2,1)} %bitcast.3), calls=%async_computation | async-start | bytes 2097152 | tf_op jit(solution)/shard_map/all_to_all | solution.py:304
  78.5 4.4 %reshape.85 = bf16[16,16,2,32,32]{4,3,2,1,0:T(8,128)(2,1)} reshape(bf16[16,16,2048]{2,1,0:T(8,128)(2,1)S(1)} %all-to-all-done.1) | data formatting | bytes 2097152 | tf_op jit(solution)/shard_map/reshape | solution.py:305
  82.9 3.6 %fusion.4 = bf16[16,2,32,512,1]{3,2,0,1,4:T(8,128)(2,1)S(1)} fusion(bf16[16,16,2,32,32]{4,3,2,1,0:T(8,128)(2,1)} %reshape.85, s32[16,32]{1,0:T(8,128)S(1)} %multiply_add_fusion, s32[512]{0:T(512)S(1)} %copy-done), kind=kOutput, calls=%fused_computation.4 | convolution fusion | flops 537133056 | bytes 2101248 | tf_op jit(solution)/shard_map/gkias,gar->kisr/dot_general | solution.py:306
  86.4 0.1 copy.55
  86.5 0.1 collective-permute-start.2
  86.6 16.6 %all-to-all-done = bf16[16,16,2048]{2,1,0:T(8,128)(2,1)S(1)} async-done(((bf16[16,16,2048]{2,1,0:T(8,128)(2,1)}), bf16[16,16,2048]{2,1,0:T(8,128)(2,1)S(1)}, u32[]{:S(2)}, u32[]{:S(2)}) %all-to-all-start) | async-done | bytes 1048608 | tf_op jit(solution)/shard_map/all_to_all | solution.py:304
  103.2 4.4 %reshape.81 = bf16[16,16,2,32,32]{4,3,2,1,0:T(8,128)(2,1)} reshape(bf16[16,16,2048]{2,1,0:T(8,128)(2,1)S(1)} %all-to-all-done) | data formatting | bytes 2097152 | tf_op jit(solution)/shard_map/reshape | solution.py:305
  107.6 3.6 %fusion.6 = bf16[16,2,32,512,1]{3,2,0,1,4:T(8,128)(2,1)S(1)} fusion(bf16[16,16,2,32,32]{4,3,2,1,0:T(8,128)(2,1)} %reshape.81, s32[16,32]{1,0:T(8,128)S(1)} %multiply_add_fusion, s32[512]{0:T(512)S(1)} %copy-done), kind=kOutput, calls=%fused_computation.6 | convolution fusion | flops 537133056 | bytes 2101248 | tf_op jit(solution)/shard_map/gkias,gar->kisr/dot_general | solution.py:306
  111.1 0.1 copy.56
  111.2 0.1 collective-permute-start.1
  111.3 0.6 collective-permute-done.2
  111.9 2.8 %pad_maximum_fusion.1 = bf16[32,64,512]{2,1,0:T(8,128)(2,1)} fusion(bf16[32,32,512]{2,1,0:T(8,128)(2,1)} %collective-permute-done.2, bf16[32,32,512]{2,1,0:T(8,128)(2,1)S(1)} %bitcast.77), kind=kLoop, calls=%fused_computation.13 | loop fusion | flops 4194304 | bytes 4194304 | tf_op jit(solution)/shard_map/concatenate | solution.py:27
  114.7 7.5 %shard_map.48.refs_0_ = bf16[2,64,256,512]{3,2,1,0:T(8,128)(2,1)} custom-call(s32[1]{0:T(128)} %bitcast.block_ref, bf16[16,128,512]{2,1,0:T(8,128)(2,1)} %bitcast.68, bf16[16,128,512]{2,1,0:T(8,128)(2,1)} %bitcast.69), custom_call_target="tpu_custom_call" | custom-call | flops 1073741824 | bytes 11534336 | tf_op jit(solution)/shard_map/pallas_call | solution.py:237
  122.2 6.7 %convolution_convert_fusion = bf16[2048,256]{0,1:T(8,128)(2,1)} fusion(bf16[2048,2048]{1,0:T(8,128)(2,1)} %bitcast.65, bf16[256,2048]{1,0:T(8,128)(2,1)S(1)} %copy-done.2), kind=kOutput, calls=%fused_computation.8 | convolution fusion | flops 2148007936 | bytes 10485760 | tf_op jit(solution)/shard_map/kj,nj->kn/dot_general | solution.py:300
  129.0 6.0 %all-to-all-start.3 = ((bf16[16,16,2048]{2,1,0:T(8,128)(2,1)}), bf16[16,16,2048]{2,1,0:T(8,128)(2,1)S(1)}, u32[]{:S(2)}, u32[]{:S(2)}) async-start(bf16[16,16,2048]{2,1,0:T(8,128)(2,1)} %bitcast.21), calls=%async_computation.3 | async-start | bytes 2097152 | tf_op jit(solution)/shard_map/all_to_all | solution.py:304
  135.0 2.2 collective-permute-done.1
  137.2 2.8 %pad_maximum_fusion = bf16[32,64,512]{2,1,0:T(8,128)(2,1)} fusion(bf16[32,32,512]{2,1,0:T(8,128)(2,1)} %collective-permute-done.1, bf16[32,32,512]{2,1,0:T(8,128)(2,1)S(1)} %bitcast.81), kind=kLoop, calls=%fused_computation.12 | loop fusion | flops 4194304 | bytes 4194304 | tf_op jit(solution)/shard_map/concatenate | solution.py:27
  140.0 7.5 %shard_map.49.refs_0_ = bf16[2,64,256,512]{3,2,1,0:T(8,128)(2,1)} custom-call(s32[1]{0:T(128)} %bitcast.block_ref, bf16[16,128,512]{2,1,0:T(8,128)(2,1)} %bitcast.72, bf16[16,128,512]{2,1,0:T(8,128)(2,1)} %bitcast.73, bf16[2,64,256,512]{3,2,1,0:T(8,128)(2,1)} %shard_map.48.refs_0_), custom_call_target="tpu_custom_call", output_to_operand_aliasing={{}: (3, {})} | custom-call | flops 1073741824 | bytes 11534336 | tf_op jit(solution)/shard_map/pallas_call | solution.py:237
  147.5 6.8 %convolution_convert_fusion.1 = bf16[2048,256]{0,1:T(8,128)(2,1)} fusion(bf16[2048,2048]{1,0:T(8,128)(2,1)} %bitcast.66, bf16[256,2048]{1,0:T(8,128)(2,1)S(1)} %copy-done.1), kind=kOutput, calls=%fused_computation.9 | convolution fusion | flops 2148007936 | bytes 10485760 | tf_op jit(solution)/shard_map/kj,nj->kn/dot_general | solution.py:300
  154.3 5.4 %all-to-all-done.3 = bf16[16,16,2048]{2,1,0:T(8,128)(2,1)S(1)} async-done(((bf16[16,16,2048]{2,1,0:T(8,128)(2,1)}), bf16[16,16,2048]{2,1,0:T(8,128)(2,1)S(1)}, u32[]{:S(2)}, u32[]{:S(2)}) %all-to-all-start.3) | async-done | bytes 1048608 | tf_op jit(solution)/shard_map/all_to_all | solution.py:304
  159.7 5.1 %all-to-all-start.2 = ((bf16[16,16,2048]{2,1,0:T(8,128)(2,1)}), bf16[16,16,2048]{2,1,0:T(8,128)(2,1)S(1)}, u32[]{:S(2)}, u32[]{:S(2)}) async-start(bf16[16,16,2048]{2,1,0:T(8,128)(2,1)} %bitcast.16), calls=%async_computation.2 | async-start | bytes 2097152 | tf_op jit(solution)/shard_map/all_to_all | solution.py:304
  164.8 4.4 %reshape.93 = bf16[16,16,2,32,32]{4,3,2,1,0:T(8,128)(2,1)} reshape(bf16[16,16,2048]{2,1,0:T(8,128)(2,1)S(1)} %all-to-all-done.3) | data formatting | bytes 2097152 | tf_op jit(solution)/shard_map/reshape | solution.py:305
  169.2 3.6 %fusion = bf16[16,2,32,512,1]{3,2,0,1,4:T(8,128)(2,1)S(1)} fusion(bf16[16,16,2,32,32]{4,3,2,1,0:T(8,128)(2,1)} %reshape.93, s32[16,32]{1,0:T(8,128)S(1)} %multiply_add_fusion, s32[512]{0:T(512)S(1)} %copy-done), kind=kOutput, calls=%fused_computation | convolution fusion | flops 537133056 | bytes 2101248 | tf_op jit(solution)/shard_map/gkias,gar->kisr/dot_general | solution.py:306
  172.8 0.1 copy.53
  172.9 0.5 collective-permute-start.4
  173.4 16.1 %all-to-all-done.2 = bf16[16,16,2048]{2,1,0:T(8,128)(2,1)S(1)} async-done(((bf16[16,16,2048]{2,1,0:T(8,128)(2,1)}), bf16[16,16,2048]{2,1,0:T(8,128)(2,1)S(1)}, u32[]{:S(2)}, u32[]{:S(2)}) %all-to-all-start.2) | async-done | bytes 1048608 | tf_op jit(solution)/shard_map/all_to_all | solution.py:304
  189.5 4.4 %reshape.89 = bf16[16,16,2,32,32]{4,3,2,1,0:T(8,128)(2,1)} reshape(bf16[16,16,2048]{2,1,0:T(8,128)(2,1)S(1)} %all-to-all-done.2) | data formatting | bytes 2097152 | tf_op jit(solution)/shard_map/reshape | solution.py:305
  194.0 3.6 %fusion.2 = bf16[16,2,32,512,1]{3,2,0,1,4:T(8,128)(2,1)S(1)} fusion(bf16[16,16,2,32,32]{4,3,2,1,0:T(8,128)(2,1)} %reshape.89, s32[16,32]{1,0:T(8,128)S(1)} %multiply_add_fusion, s32[512]{0:T(512)S(1)} %copy-done), kind=kOutput, calls=%fused_computation.2 | convolution fusion | flops 537133056 | bytes 2101248 | tf_op jit(solution)/shard_map/gkias,gar->kisr/dot_general | solution.py:306
  197.5 0.1 copy.54
  197.6 0.5 collective-permute-start.3
  198.2 1.5 pad_maximum_fusion.3
  199.7 7.4 %shard_map.50.refs_0_ = bf16[2,64,256,512]{3,2,1,0:T(8,128)(2,1)} custom-call(s32[1]{0:T(128)} %bitcast.block_ref, bf16[16,128,512]{2,1,0:T(8,128)(2,1)} %bitcast.74, bf16[16,128,512]{2,1,0:T(8,128)(2,1)} %bitcast.75, bf16[2,64,256,512]{3,2,1,0:T(8,128)(2,1)} %shard_map.49.refs_0_), custom_call_target="tpu_custom_call", output_to_operand_aliasing={{}: (3, {})} | custom-call | flops 1073741824 | bytes 11534336 | tf_op jit(solution)/shard_map/pallas_call | solution.py:237
  207.1 16.3 %collective-permute-done.3 = bf16[32,32,512]{2,1,0:T(8,128)(2,1)} collective-permute-done((bf16[32,32,512]{2,1,0:T(8,128)(2,1)S(1)}, bf16[32,32,512]{2,1,0:T(8,128)(2,1)}, u32[]{:S(2)}, u32[]{:S(2)}) %collective-permute-start.3) | collective-permute-done | bytes 1048608 | tf_op jit(solution)/shard_map/ppermute | solution.py:26
  223.4 2.8 %pad_maximum_fusion.2 = bf16[32,64,512]{2,1,0:T(8,128)(2,1)} fusion(bf16[32,32,512]{2,1,0:T(8,128)(2,1)} %collective-permute-done.3, bf16[32,32,512]{2,1,0:T(8,128)(2,1)S(1)} %bitcast.83), kind=kLoop, calls=%fused_computation.14 | loop fusion | flops 4194304 | bytes 4194304 | tf_op jit(solution)/shard_map/concatenate | solution.py:27
  226.2 7.4 %shard_map.51 = bf16[2,64,256,512]{3,2,1,0:T(8,128)(2,1)} custom-call(s32[1]{0:T(128)} %bitcast.block_ref, bf16[16,128,512]{2,1,0:T(8,128)(2,1)} %bitcast.70, bf16[16,128,512]{2,1,0:T(8,128)(2,1)} %bitcast.71, bf16[2,64,256,512]{3,2,1,0:T(8,128)(2,1)} %shard_map.50.refs_0_), custom_call_target="tpu_custom_call", output_to_operand_aliasing={{}: (3, {})} | custom-call | flops 1073741824 | bytes 11534336 | tf_op jit(solution)/shard_map/pallas_call | solution.py:237
  (12 shorter events, 0.1 us)
Async XLA Ops:
  4.0 24.0 %collective-permute-start = (bf16[2,32,7,1024]{3,1,2,0:T(8,128)(2,1)S(1)}, bf16[2,32,7,1024]{3,1,2,0:T(8,128)(2,1)S(1)}, u32[]{:S(2)}, u32[]{:S(2)}) collective-permute-start(bf16[2,32,7,1024]{3,1,2,0:T(8,128)(2,1)S(1)} %bitcast.85), channel_id=1, source_target_pairs={{0,1},{2,3},{4,5},{6,7},{8,9},{10,11},{12,13},{14,15},{16,17},{18,... | collective-permute-start | bytes 2752520 | tf_op jit(solution)/shard_map/ppermute | solution.py:18
  29.5 6.1 %copy-start.4 = (bf16[256,2048]{1,0:T(8,128)(2,1)S(1)}, bf16[256,2048]{1,0:T(8,128)(2,1)}, u32[]{:S(2)}) copy-start(bf16[256,2048]{1,0:T(8,128)(2,1)} %constant.12) | copy-start | bytes 3145732
  35.6 13.1 %copy-start.3 = (bf16[256,2048]{1,0:T(8,128)(2,1)S(1)}, bf16[256,2048]{1,0:T(8,128)(2,1)}, u32[]{:S(2)}) copy-start(bf16[256,2048]{1,0:T(8,128)(2,1)} %constant.10) | copy-start | bytes 3145732
  42.4 31.0 %all-to-all-start.1 = ((bf16[16,16,2048]{2,1,0:T(8,128)(2,1)}), bf16[16,16,2048]{2,1,0:T(8,128)(2,1)S(1)}, u32[]{:S(2)}, u32[]{:S(2)}) async-start(bf16[16,16,2048]{2,1,0:T(8,128)(2,1)} %bitcast.10), calls=%async_computation.1 | async-start | bytes 2097152 | tf_op jit(solution)/shard_map/all_to_all | solution.py:304
  55.5 27.4 %copy-start = (s32[512]{0:T(512)S(1)}, s32[512]{0:T(512)}, u32[]{:S(2)}) copy-start(s32[512]{0:T(512)} %param.6) | copy-start | bytes 6148
  73.4 29.8 %all-to-all-start = ((bf16[16,16,2048]{2,1,0:T(8,128)(2,1)}), bf16[16,16,2048]{2,1,0:T(8,128)(2,1)S(1)}, u32[]{:S(2)}, u32[]{:S(2)}) async-start(bf16[16,16,2048]{2,1,0:T(8,128)(2,1)} %bitcast.3), calls=%async_computation | async-start | bytes 2097152 | tf_op jit(solution)/shard_map/all_to_all | solution.py:304
  86.5 25.4 %collective-permute-start.2 = (bf16[32,32,512]{2,1,0:T(8,128)(2,1)S(1)}, bf16[32,32,512]{2,1,0:T(8,128)(2,1)}, u32[]{:S(2)}, u32[]{:S(2)}) collective-permute-start(bf16[32,32,512]{2,1,0:T(8,128)(2,1)S(1)} %bitcast.76), channel_id=1, source_target_pairs={{0,1},{1,0},{2,3},{3,2},{4,5},{5,4},{6,7},{7,6},{8,9},{9,8},{10,11... | collective-permute-start | bytes 3145736 | tf_op jit(solution)/shard_map/ppermute | solution.py:26
  111.2 25.9 %collective-permute-start.1 = (bf16[32,32,512]{2,1,0:T(8,128)(2,1)S(1)}, bf16[32,32,512]{2,1,0:T(8,128)(2,1)}, u32[]{:S(2)}, u32[]{:S(2)}) collective-permute-start(bf16[32,32,512]{2,1,0:T(8,128)(2,1)S(1)} %bitcast.80), channel_id=1, source_target_pairs={{0,1},{1,0},{2,3},{3,2},{4,5},{5,4},{6,7},{7,6},{8,9},{9,8},{10,11... | collective-permute-start | bytes 3145736 | tf_op jit(solution)/shard_map/ppermute | solution.py:26
  114.7 7.5 %copy-start.2 = (bf16[256,2048]{1,0:T(8,128)(2,1)S(1)}, bf16[256,2048]{1,0:T(8,128)(2,1)}, u32[]{:S(2)}) copy-start(bf16[256,2048]{1,0:T(8,128)(2,1)} %constant.16) | copy-start | bytes 3145732
  129.0 30.8 %all-to-all-start.3 = ((bf16[16,16,2048]{2,1,0:T(8,128)(2,1)}), bf16[16,16,2048]{2,1,0:T(8,128)(2,1)S(1)}, u32[]{:S(2)}, u32[]{:S(2)}) async-start(bf16[16,16,2048]{2,1,0:T(8,128)(2,1)} %bitcast.21), calls=%async_computation.3 | async-start | bytes 2097152 | tf_op jit(solution)/shard_map/all_to_all | solution.py:304
  140.0 7.5 %copy-start.1 = (bf16[256,2048]{1,0:T(8,128)(2,1)S(1)}, bf16[256,2048]{1,0:T(8,128)(2,1)}, u32[]{:S(2)}) copy-start(bf16[256,2048]{1,0:T(8,128)(2,1)} %constant.14) | copy-start | bytes 3145732
  159.7 29.8 %all-to-all-start.2 = ((bf16[16,16,2048]{2,1,0:T(8,128)(2,1)}), bf16[16,16,2048]{2,1,0:T(8,128)(2,1)S(1)}, u32[]{:S(2)}, u32[]{:S(2)}) async-start(bf16[16,16,2048]{2,1,0:T(8,128)(2,1)} %bitcast.16), calls=%async_computation.2 | async-start | bytes 2097152 | tf_op jit(solution)/shard_map/all_to_all | solution.py:304
  172.9 25.3 %collective-permute-start.4 = (bf16[32,32,512]{2,1,0:T(8,128)(2,1)S(1)}, bf16[32,32,512]{2,1,0:T(8,128)(2,1)S(1)}, u32[]{:S(2)}, u32[]{:S(2)}) collective-permute-start(bf16[32,32,512]{2,1,0:T(8,128)(2,1)S(1)} %bitcast.78), channel_id=1, source_target_pairs={{0,1},{1,0},{2,3},{3,2},{4,5},{5,4},{6,7},{7,6},{8,9},{9,8},{10,11... | collective-permute-start | bytes 3145736 | tf_op jit(solution)/shard_map/ppermute | solution.py:26
  197.6 25.8 %collective-permute-start.3 = (bf16[32,32,512]{2,1,0:T(8,128)(2,1)S(1)}, bf16[32,32,512]{2,1,0:T(8,128)(2,1)}, u32[]{:S(2)}, u32[]{:S(2)}) collective-permute-start(bf16[32,32,512]{2,1,0:T(8,128)(2,1)S(1)} %bitcast.82), channel_id=1, source_target_pairs={{0,1},{1,0},{2,3},{3,2},{4,5},{5,4},{6,7},{7,6},{8,9},{9,8},{10,11... | collective-permute-start | bytes 3145736 | tf_op jit(solution)/shard_map/ppermute | solution.py:26

commit v10 on v9

--- a/solution.py
+++ b/solution.py
@@ -290,25 +290,37 @@
         right = gathered.reshape(width, -1, stations)
         return correlate_chunk(left, right, result, chunk * width, local_channels)
 
+    def reorder(turned):
+        turned = turned.reshape(groups, width, 2, stations_local, spectra_local)
+        ordered = jnp.einsum(
+            "gkias,gar->kisr", turned, selector, preferred_element_type=jnp.float32
+        ).astype(jnp.bfloat16)
+        return ordered.reshape(width * 2, spectra_local, stations)
+
     result = None
     pending = []
+    finished = 0
+    turned = None
     for chunk in range(chunks):
         source = filtered
-        if chunk >= 2:
-            result = correlate(chunk - 2, pending[chunk - 2], result)
+        if chunk >= 3:
+            result = correlate(finished, pending[finished], result)
+            finished += 1
             source, result = lax.optimization_barrier((filtered, result))
         spectra = jnp.einsum(
             "kj,nj->kn", weights[chunk], source, preferred_element_type=jnp.float32
         ).astype(jnp.bfloat16)
         spectra = spectra.reshape(groups, width, 2 * stations_local * spectra_local)
+        if chunk >= 1:
+            turned, spectra = lax.optimization_barrier((turned, spectra))
+            pending.append(gathered_along(reorder(turned), "blk", 1))
         turned = lax.all_to_all(spectra, "stn", split_axis=0, concat_axis=0, tiled=True)
-        turned = turned.reshape(groups, width, 2, stations_local, spectra_local)
-        ordered = jnp.einsum(
-            "gkias,gar->kisr", turned, selector, preferred_element_type=jnp.float32
-        ).astype(jnp.bfloat16)
-        ordered = ordered.reshape(width * 2, spectra_local, stations)
-        pending.append(gathered_along(ordered, "blk", 1))
-    for chunk in range(max(0, chunks - 2), chunks):
+    if finished + 3 <= chunks:
+        result = correlate(finished, pending[finished], result)
+        finished += 1
+        turned, result = lax.optimization_barrier((turned, result))
+    pending.append(gathered_along(reorder(turned), "blk", 1))
+    for chunk in range(finished, chunks):
         result = correlate(chunk, pending[chunk], result)
     return result
 

time: 235 us -> 246 us (1.047)
  waiting for transfers between devices: 79.1 us -> 87.9 us
    ppermute x4, waiting for transfers between devices: 19.1 us -> 56.4 us  [gathered_along(): parts.append(lax.ppermute(value, axis, pairs))]
    all_to_all x4, waiting for transfers between devices: 56.1 us -> 27.6 us  [per_device(): lax.all_to_all(spectra, 'stn', split_axis=0, concat_axis=0, tiled=True)]
  transfers between devices with their start and end apart: 9 -> 9, of which waited for: 8 -> 7; matrix products, arithmetic and copies ran while one was open for 27% -> 26% of each run, Pallas kernels for 16% -> 15%
where the time goes in v10:
time: 246 us; the launch traced here: 243 us
  waiting for transfers between devices  87.9 us (36%)
  Pallas kernels  50.2 us (20%)
  matrix products  41.6 us (17%)
  starting transfers between devices  26.3 us (11%)
  local copies, waits for them, and re-layouts  24.2 us (10%)
  other arithmetic  12.3 us (5%)
    ppermute x4, waiting for transfers between devices, gathered_along(): parts.append(lax.ppermute(value, axis, pairs))  56.4 us
    pallas_call x4, Pallas kernels, correlate_rows_chunk(): pl.pallas_call(correlate_rows_kernel, grid_spec=grid_spec, out_shape=jax....  29.8 us
    all_to_all x4, waiting for transfers between devices, per_device(): lax.all_to_all(spectra, 'stn', split_axis=0, concat_axis=0, tiled=True)  27.6 us
    dot_general x4, matrix products, per_device(): jnp.einsum('kj,nj->kn', weights[chunk], source, preferred_element_type=jn...  27.3 us
    all_to_all x4, starting transfers between devices, per_device(): lax.all_to_all(spectra, 'stn', split_axis=0, concat_axis=0, tiled=True)  22.4 us
    reshape x4, local copies, waits for them, and re-layouts, reorder(): turned = turned.reshape(groups, width, 2, stations_local, spectra_local)  17.7 us
    dot_general x4, matrix products, reorder(): jnp.einsum('gkias,gar->kisr', turned, selector, preferred_element_type=jn...  14.3 us
    pallas_call x1, Pallas kernels, filter_frames(): pl.pallas_call(fir_kernel, grid=(stations_local // group,), in_specs=[pl....  14.3 us
  transfers between devices with their start and end apart: 9, of which 7 were waited for; matrix products, arithmetic and copies ran while one was open for 26% of the time, Pallas kernels for 15%

profile of v10, /device:TPU:14, one launch (start us, length us, event | category | flops | bytes accessed | tf_op | source)
XLA Modules:
  0.0 242.7 jit_solution(4490122919353119048)
XLA Ops:
  0.0 3.8 %convert.3 = bf16[2,32,32768]{2,1,0:T(8,128)(2,1)S(1)} convert(s32[2,32,32768]{2,1,0:T(8,128)} %param.4) | non-fusion elementwise | flops 2097152 | bytes 12582912 | tf_op jit(solution)/shard_map/convert
  3.8 0.1 slice.21
  3.9 0.1 copy.57
  4.0 1.3 collective-permute-start
  5.3 4.5 %copy.39 = bf16[8,8,32,1024]{3,2,1,0:T(8,128)(2,1)} copy(bf16[8,8,32,1024]{3,1,2,0:T(8,128)(2,1)S(1)} %bitcast.67) | data formatting | bytes 8388608
  9.7 14.3 %shard_map.46.previous_ref = bf16[2,32,32,2048]{3,2,1,0:T(8,128)(2,1)} custom-call(f32[8,1024]{1,0:T(8,128)} %taps_ref.3, bf16[2,32,32,1024]{3,2,1,0:T(8,128)(2,1)} %bitcast.61), custom_call_target="tpu_custom_call" | custom-call | flops 67108864 | bytes 12582912 | tf_op jit(solution)/shard_map/pallas_call | solution.py:110
  24.0 3.9 %collective-permute-done = bf16[2,32,7,1024]{3,1,2,0:T(8,128)(2,1)S(1)} collective-permute-done((bf16[2,32,7,1024]{3,1,2,0:T(8,128)(2,1)S(1)}, bf16[2,32,7,1024]{3,1,2,0:T(8,128)(2,1)S(1)}, u32[]{:S(2)}, u32[]{:S(2)}) %collective-permute-start) | collective-permute-done | bytes 917536 | tf_op jit(solution)/shard_map/ppermute | solution.py:18
  27.9 1.6 copy.20.halo_ref
  29.5 6.1 %shard_map.47 = bf16[2,32,32,2048]{3,2,1,0:T(8,128)(2,1)} custom-call(f32[8,1024]{1,0:T(8,128)} %taps_ref.3, bf16[2,32,7,1024]{3,2,1,0:T(8,128)(2,1)} %copy.20.halo_ref, bf16[2,32,32,1024]{3,2,1,0:T(8,128)(2,1)} %bitcast.62, bf16[2,32,32,2048]{3,2,1,0:T(8,128)(2,1)} %shard_map.46.previous_ref), custom_call_target="tpu_custom_call", output_to_operand_aliasing={{}: (3, {})} | custom-call | flops 16777216 | bytes 4194304 | tf_op jit(solution)/shard_map/pallas_call | solution.py:127
  35.6 6.8 %convolution_convert_fusion.3 = bf16[2048,256]{0,1:T(8,128)(2,1)} fusion(bf16[2048,2048]{1,0:T(8,128)(2,1)} %bitcast.63, bf16[256,2048]{1,0:T(8,128)(2,1)S(1)} %copy-done.4), kind=kOutput, calls=%fused_computation.11 | convolution fusion | flops 2148007936 | bytes 10485760 | tf_op jit(solution)/shard_map/kj,nj->kn/dot_general | solution.py:310
  42.4 6.2 %all-to-all-start = ((bf16[16,16,2048]{2,1,0:T(8,128)(2,1)}), bf16[16,16,2048]{2,1,0:T(8,128)(2,1)S(1)}, u32[]{:S(2)}, u32[]{:S(2)}) async-start(bf16[16,16,2048]{2,1,0:T(8,128)(2,1)} %bitcast.3), calls=%async_computation | async-start | bytes 2097152 | tf_op jit(solution)/shard_map/all_to_all | solution.py:317
  48.7 6.8 %convolution_convert_fusion.2 = bf16[2048,256]{0,1:T(8,128)(2,1)} fusion(bf16[2048,2048]{1,0:T(8,128)(2,1)} %bitcast.64, bf16[256,2048]{1,0:T(8,128)(2,1)S(1)} %copy-done.3), kind=kOutput, calls=%fused_computation.10 | convolution fusion | flops 2148007936 | bytes 10485760 | tf_op jit(solution)/shard_map/kj,nj->kn/dot_general | solution.py:310
  55.5 17.9 %all-to-all-done = bf16[16,16,2048]{2,1,0:T(8,128)(2,1)S(1)} async-done(((bf16[16,16,2048]{2,1,0:T(8,128)(2,1)}), bf16[16,16,2048]{2,1,0:T(8,128)(2,1)S(1)}, u32[]{:S(2)}, u32[]{:S(2)}) %all-to-all-start) | async-done | bytes 1048608 | tf_op jit(solution)/shard_map/all_to_all | solution.py:317
  73.4 5.1 %all-to-all-start.1 = ((bf16[16,16,2048]{2,1,0:T(8,128)(2,1)}), bf16[16,16,2048]{2,1,0:T(8,128)(2,1)S(1)}, u32[]{:S(2)}, u32[]{:S(2)}) async-start(bf16[16,16,2048]{2,1,0:T(8,128)(2,1)} %bitcast.5), calls=%async_computation.1 | async-start | bytes 2097152 | tf_op jit(solution)/shard_map/all_to_all | solution.py:317
  78.5 4.4 %reshape.83 = bf16[16,16,2,32,32]{4,3,2,1,0:T(8,128)(2,1)} reshape(bf16[16,16,2048]{2,1,0:T(8,128)(2,1)S(1)} %all-to-all-done) | data formatting | bytes 2097152 | tf_op jit(solution)/shard_map/reshape | solution.py:294
  82.9 3.6 %fusion.6 = bf16[16,2,32,512,1]{3,2,0,1,4:T(8,128)(2,1)S(1)} fusion(bf16[16,16,2,32,32]{4,3,2,1,0:T(8,128)(2,1)} %reshape.83, s32[16,32]{1,0:T(8,128)S(1)} %multiply_add_fusion, s32[512]{0:T(512)S(1)} %copy-done), kind=kOutput, calls=%fused_computation.6 | convolution fusion | flops 537133056 | bytes 2101248 | tf_op jit(solution)/shard_map/gkias,gar->kisr/dot_general | solution.py:295
  86.5 0.1 copy.56
  86.6 0.1 collective-permute-start.1
  86.7 6.8 %convolution_convert_fusion.1 = bf16[2048,256]{0,1:T(8,128)(2,1)} fusion(bf16[2048,2048]{1,0:T(8,128)(2,1)} %bitcast.65, bf16[256,2048]{1,0:T(8,128)(2,1)S(1)} %copy-done.2), kind=kOutput, calls=%fused_computation.9 | convolution fusion | flops 2148007936 | bytes 10485760 | tf_op jit(solution)/shard_map/kj,nj->kn/dot_general | solution.py:310
  93.6 9.7 %all-to-all-done.1 = bf16[16,16,2048]{2,1,0:T(8,128)(2,1)S(1)} async-done(((bf16[16,16,2048]{2,1,0:T(8,128)(2,1)}), bf16[16,16,2048]{2,1,0:T(8,128)(2,1)S(1)}, u32[]{:S(2)}, u32[]{:S(2)}) %all-to-all-start.1) | async-done | bytes 1048608 | tf_op jit(solution)/shard_map/all_to_all | solution.py:317
  103.2 5.1 %all-to-all-start.2 = ((bf16[16,16,2048]{2,1,0:T(8,128)(2,1)}), bf16[16,16,2048]{2,1,0:T(8,128)(2,1)S(1)}, u32[]{:S(2)}, u32[]{:S(2)}) async-start(bf16[16,16,2048]{2,1,0:T(8,128)(2,1)} %bitcast.85), calls=%async_computation.2 | async-start | bytes 2097152 | tf_op jit(solution)/shard_map/all_to_all | solution.py:317
  108.3 3.7 %collective-permute-done.1 = bf16[32,32,512]{2,1,0:T(8,128)(2,1)} collective-permute-done((bf16[32,32,512]{2,1,0:T(8,128)(2,1)S(1)}, bf16[32,32,512]{2,1,0:T(8,128)(2,1)}, u32[]{:S(2)}, u32[]{:S(2)}) %collective-permute-start.1) | collective-permute-done | bytes 1048608 | tf_op jit(solution)/shard_map/ppermute | solution.py:26
  112.0 2.8 %pad_maximum_fusion = bf16[32,64,512]{2,1,0:T(8,128)(2,1)} fusion(bf16[32,32,512]{2,1,0:T(8,128)(2,1)} %collective-permute-done.1, bf16[32,32,512]{2,1,0:T(8,128)(2,1)S(1)} %bitcast.77), kind=kLoop, calls=%fused_computation.12 | loop fusion | flops 4194304 | bytes 4194304 | tf_op jit(solution)/shard_map/concatenate | solution.py:27
  114.8 7.5 %shard_map.48.refs_0_ = bf16[2,64,256,512]{3,2,1,0:T(8,128)(2,1)} custom-call(s32[1]{0:T(128)} %bitcast.block_ref, bf16[16,128,512]{2,1,0:T(8,128)(2,1)} %bitcast.68, bf16[16,128,512]{2,1,0:T(8,128)(2,1)} %bitcast.69), custom_call_target="tpu_custom_call" | custom-call | flops 1073741824 | bytes 11534336 | tf_op jit(solution)/shard_map/pallas_call | solution.py:237
  122.3 6.8 %convolution_convert_fusion = bf16[2048,256]{0,1:T(8,128)(2,1)} fusion(bf16[2048,2048]{1,0:T(8,128)(2,1)} %bitcast.66, bf16[256,2048]{1,0:T(8,128)(2,1)S(1)} %copy-done.1), kind=kOutput, calls=%fused_computation.8 | convolution fusion | flops 2148007936 | bytes 10485760 | tf_op jit(solution)/shard_map/kj,nj->kn/dot_general | solution.py:310
  129.1 4.4 %reshape.87 = bf16[16,16,2,32,32]{4,3,2,1,0:T(8,128)(2,1)} reshape(bf16[16,16,2048]{2,1,0:T(8,128)(2,1)S(1)} %all-to-all-done.1) | data formatting | bytes 2097152 | tf_op jit(solution)/shard_map/reshape | solution.py:294
  133.5 0.0 all-to-all-done.2
  133.5 6.0 %all-to-all-start.3 = ((bf16[16,16,2048]{2,1,0:T(8,128)(2,1)}), bf16[16,16,2048]{2,1,0:T(8,128)(2,1)S(1)}, u32[]{:S(2)}, u32[]{:S(2)}) async-start(bf16[16,16,2048]{2,1,0:T(8,128)(2,1)} %bitcast.14), calls=%async_computation.3 | async-start | bytes 2097152 | tf_op jit(solution)/shard_map/all_to_all | solution.py:317
  139.6 3.6 %fusion.4 = bf16[16,2,32,512,1]{3,2,0,1,4:T(8,128)(2,1)S(1)} fusion(bf16[16,16,2,32,32]{4,3,2,1,0:T(8,128)(2,1)} %reshape.87, s32[16,32]{1,0:T(8,128)S(1)} %multiply_add_fusion, s32[512]{0:T(512)S(1)} %copy-done), kind=kOutput, calls=%fused_computation.4 | convolution fusion | flops 537133056 | bytes 2101248 | tf_op jit(solution)/shard_map/gkias,gar->kisr/dot_general | solution.py:295
  143.1 0.1 copy.55
  143.2 0.4 collective-permute-start.2
  143.6 24.9 %collective-permute-done.2 = bf16[32,32,512]{2,1,0:T(8,128)(2,1)S(1)} collective-permute-done((bf16[32,32,512]{2,1,0:T(8,128)(2,1)S(1)}, bf16[32,32,512]{2,1,0:T(8,128)(2,1)S(1)}, u32[]{:S(2)}, u32[]{:S(2)}) %collective-permute-start.2) | collective-permute-done | bytes 1048608 | tf_op jit(solution)/shard_map/ppermute | solution.py:26
  168.5 1.5 pad_maximum_fusion.1
  170.0 7.4 %shard_map.49.refs_0_ = bf16[2,64,256,512]{3,2,1,0:T(8,128)(2,1)} custom-call(s32[1]{0:T(128)} %bitcast.block_ref, bf16[16,128,512]{2,1,0:T(8,128)(2,1)} %bitcast.72, bf16[16,128,512]{2,1,0:T(8,128)(2,1)} %bitcast.73, bf16[2,64,256,512]{3,2,1,0:T(8,128)(2,1)} %shard_map.48.refs_0_), custom_call_target="tpu_custom_call", output_to_operand_aliasing={{}: (3, {})} | custom-call | flops 1073741824 | bytes 11534336 | tf_op jit(solution)/shard_map/pallas_call | solution.py:237
  177.4 4.4 %reshape.93 = bf16[16,16,2,32,32]{4,3,2,1,0:T(8,128)(2,1)} reshape(bf16[16,16,2048]{2,1,0:T(8,128)(2,1)S(1)} %all-to-all-done.2) | data formatting | bytes 2097152 | tf_op jit(solution)/shard_map/reshape | solution.py:294
  181.8 3.6 %fusion = bf16[16,2,32,512,1]{3,2,0,1,4:T(8,128)(2,1)S(1)} fusion(bf16[16,16,2,32,32]{4,3,2,1,0:T(8,128)(2,1)} %reshape.93, s32[16,32]{1,0:T(8,128)S(1)} %multiply_add_fusion, s32[512]{0:T(512)S(1)} %copy-done), kind=kOutput, calls=%fused_computation | convolution fusion | flops 537133056 | bytes 2101248 | tf_op jit(solution)/shard_map/gkias,gar->kisr/dot_general | solution.py:295
  185.4 0.1 copy.53
  185.5 0.4 collective-permute-start.4
  185.9 4.4 %reshape.90 = bf16[16,16,2,32,32]{4,3,2,1,0:T(8,128)(2,1)} reshape(bf16[16,16,2048]{2,1,0:T(8,128)(2,1)S(1)} %all-to-all-done.3) | data formatting | bytes 2097152 | tf_op jit(solution)/shard_map/reshape | solution.py:294
  190.3 3.6 %fusion.2 = bf16[16,2,32,512,1]{3,2,0,1,4:T(8,128)(2,1)S(1)} fusion(bf16[16,16,2,32,32]{4,3,2,1,0:T(8,128)(2,1)} %reshape.90, s32[16,32]{1,0:T(8,128)S(1)} %multiply_add_fusion, s32[512]{0:T(512)S(1)} %copy-done), kind=kOutput, calls=%fused_computation.2 | convolution fusion | flops 537133056 | bytes 2101248 | tf_op jit(solution)/shard_map/gkias,gar->kisr/dot_general | solution.py:295
  193.9 0.1 copy.54
  193.9 1.8 collective-permute-start.3
  195.7 15.9 %collective-permute-done.4 = bf16[32,32,512]{2,1,0:T(8,128)(2,1)S(1)} collective-permute-done((bf16[32,32,512]{2,1,0:T(8,128)(2,1)S(1)}, bf16[32,32,512]{2,1,0:T(8,128)(2,1)S(1)}, u32[]{:S(2)}, u32[]{:S(2)}) %collective-permute-start.4) | collective-permute-done | bytes 1048608 | tf_op jit(solution)/shard_map/ppermute | solution.py:26
  211.7 1.5 pad_maximum_fusion.3
  213.2 7.4 %shard_map.50.refs_0_ = bf16[2,64,256,512]{3,2,1,0:T(8,128)(2,1)} custom-call(s32[1]{0:T(128)} %bitcast.block_ref, bf16[16,128,512]{2,1,0:T(8,128)(2,1)} %bitcast.74, bf16[16,128,512]{2,1,0:T(8,128)(2,1)} %bitcast.75, bf16[2,64,256,512]{3,2,1,0:T(8,128)(2,1)} %shard_map.49.refs_0_), custom_call_target="tpu_custom_call", output_to_operand_aliasing={{}: (3, {})} | custom-call | flops 1073741824 | bytes 11534336 | tf_op jit(solution)/shard_map/pallas_call | solution.py:237
  220.6 11.9 %collective-permute-done.3 = bf16[32,32,512]{2,1,0:T(8,128)(2,1)} collective-permute-done((bf16[32,32,512]{2,1,0:T(8,128)(2,1)S(1)}, bf16[32,32,512]{2,1,0:T(8,128)(2,1)}, u32[]{:S(2)}, u32[]{:S(2)}) %collective-permute-start.3) | collective-permute-done | bytes 1048608 | tf_op jit(solution)/shard_map/ppermute | solution.py:26
  232.5 2.8 %pad_maximum_fusion.2 = bf16[32,64,512]{2,1,0:T(8,128)(2,1)} fusion(bf16[32,32,512]{2,1,0:T(8,128)(2,1)} %collective-permute-done.3, bf16[32,32,512]{2,1,0:T(8,128)(2,1)S(1)} %bitcast.81), kind=kLoop, calls=%fused_computation.14 | loop fusion | flops 4194304 | bytes 4194304 | tf_op jit(solution)/shard_map/concatenate | solution.py:27
  235.3 7.4 %shard_map.51 = bf16[2,64,256,512]{3,2,1,0:T(8,128)(2,1)} custom-call(s32[1]{0:T(128)} %bitcast.block_ref, bf16[16,128,512]{2,1,0:T(8,128)(2,1)} %bitcast.70, bf16[16,128,512]{2,1,0:T(8,128)(2,1)} %bitcast.71, bf16[2,64,256,512]{3,2,1,0:T(8,128)(2,1)} %shard_map.50.refs_0_), custom_call_target="tpu_custom_call", output_to_operand_aliasing={{}: (3, {})} | custom-call | flops 1073741824 | bytes 11534336 | tf_op jit(solution)/shard_map/pallas_call | solution.py:237
  (12 shorter events, 0.0 us)
Async XLA Ops:
  4.0 24.0 %collective-permute-start = (bf16[2,32,7,1024]{3,1,2,0:T(8,128)(2,1)S(1)}, bf16[2,32,7,1024]{3,1,2,0:T(8,128)(2,1)S(1)}, u32[]{:S(2)}, u32[]{:S(2)}) collective-permute-start(bf16[2,32,7,1024]{3,1,2,0:T(8,128)(2,1)S(1)} %bitcast.86), channel_id=1, source_target_pairs={{0,1},{2,3},{4,5},{6,7},{8,9},{10,11},{12,13},{14,15},{16,17},{18,... | collective-permute-start | bytes 2752520 | tf_op jit(solution)/shard_map/ppermute | solution.py:18
  29.5 6.1 %copy-start.4 = (bf16[256,2048]{1,0:T(8,128)(2,1)S(1)}, bf16[256,2048]{1,0:T(8,128)(2,1)}, u32[]{:S(2)}) copy-start(bf16[256,2048]{1,0:T(8,128)(2,1)} %constant.10) | copy-start | bytes 3145732
  35.6 13.1 %copy-start.3 = (bf16[256,2048]{1,0:T(8,128)(2,1)S(1)}, bf16[256,2048]{1,0:T(8,128)(2,1)}, u32[]{:S(2)}) copy-start(bf16[256,2048]{1,0:T(8,128)(2,1)} %constant.12) | copy-start | bytes 3145732
  42.4 31.0 %all-to-all-start = ((bf16[16,16,2048]{2,1,0:T(8,128)(2,1)}), bf16[16,16,2048]{2,1,0:T(8,128)(2,1)S(1)}, u32[]{:S(2)}, u32[]{:S(2)}) async-start(bf16[16,16,2048]{2,1,0:T(8,128)(2,1)} %bitcast.3), calls=%async_computation | async-start | bytes 2097152 | tf_op jit(solution)/shard_map/all_to_all | solution.py:317
  55.5 27.4 %copy-start = (s32[512]{0:T(512)S(1)}, s32[512]{0:T(512)}, u32[]{:S(2)}) copy-start(s32[512]{0:T(512)} %param.6) | copy-start | bytes 6148
  73.4 29.8 %all-to-all-start.1 = ((bf16[16,16,2048]{2,1,0:T(8,128)(2,1)}), bf16[16,16,2048]{2,1,0:T(8,128)(2,1)S(1)}, u32[]{:S(2)}, u32[]{:S(2)}) async-start(bf16[16,16,2048]{2,1,0:T(8,128)(2,1)} %bitcast.5), calls=%async_computation.1 | async-start | bytes 2097152 | tf_op jit(solution)/shard_map/all_to_all | solution.py:317
  82.9 3.8 %copy-start.2 = (bf16[256,2048]{1,0:T(8,128)(2,1)S(1)}, bf16[256,2048]{1,0:T(8,128)(2,1)}, u32[]{:S(2)}) copy-start(bf16[256,2048]{1,0:T(8,128)(2,1)} %constant.14) | copy-start | bytes 3145732
  86.6 25.4 %collective-permute-start.1 = (bf16[32,32,512]{2,1,0:T(8,128)(2,1)S(1)}, bf16[32,32,512]{2,1,0:T(8,128)(2,1)}, u32[]{:S(2)}, u32[]{:S(2)}) collective-permute-start(bf16[32,32,512]{2,1,0:T(8,128)(2,1)S(1)} %bitcast.76), channel_id=1, source_target_pairs={{0,1},{1,0},{2,3},{3,2},{4,5},{5,4},{6,7},{7,6},{8,9},{9,8},{10,11... | collective-permute-start | bytes 3145736 | tf_op jit(solution)/shard_map/ppermute | solution.py:26
  103.2 30.3 %all-to-all-start.2 = ((bf16[16,16,2048]{2,1,0:T(8,128)(2,1)}), bf16[16,16,2048]{2,1,0:T(8,128)(2,1)S(1)}, u32[]{:S(2)}, u32[]{:S(2)}) async-start(bf16[16,16,2048]{2,1,0:T(8,128)(2,1)} %bitcast.85), calls=%async_computation.2 | async-start | bytes 2097152 | tf_op jit(solution)/shard_map/all_to_all | solution.py:317
  114.8 7.5 %copy-start.1 = (bf16[256,2048]{1,0:T(8,128)(2,1)S(1)}, bf16[256,2048]{1,0:T(8,128)(2,1)}, u32[]{:S(2)}) copy-start(bf16[256,2048]{1,0:T(8,128)(2,1)} %constant.16) | copy-start | bytes 3145732
  133.5 52.3 %all-to-all-start.3 = ((bf16[16,16,2048]{2,1,0:T(8,128)(2,1)}), bf16[16,16,2048]{2,1,0:T(8,128)(2,1)S(1)}, u32[]{:S(2)}, u32[]{:S(2)}) async-start(bf16[16,16,2048]{2,1,0:T(8,128)(2,1)} %bitcast.14), calls=%async_computation.3 | async-start | bytes 2097152 | tf_op jit(solution)/shard_map/all_to_all | solution.py:317
  143.2 25.3 %collective-permute-start.2 = (bf16[32,32,512]{2,1,0:T(8,128)(2,1)S(1)}, bf16[32,32,512]{2,1,0:T(8,128)(2,1)S(1)}, u32[]{:S(2)}, u32[]{:S(2)}) collective-permute-start(bf16[32,32,512]{2,1,0:T(8,128)(2,1)S(1)} %bitcast.82), channel_id=1, source_target_pairs={{0,1},{1,0},{2,3},{3,2},{4,5},{5,4},{6,7},{7,6},{8,9},{9,8},{10,11... | collective-permute-start | bytes 3145736 | tf_op jit(solution)/shard_map/ppermute | solution.py:26
  185.5 26.2 %collective-permute-start.4 = (bf16[32,32,512]{2,1,0:T(8,128)(2,1)S(1)}, bf16[32,32,512]{2,1,0:T(8,128)(2,1)S(1)}, u32[]{:S(2)}, u32[]{:S(2)}) collective-permute-start(bf16[32,32,512]{2,1,0:T(8,128)(2,1)S(1)} %bitcast.78), channel_id=1, source_target_pairs={{0,1},{1,0},{2,3},{3,2},{4,5},{5,4},{6,7},{7,6},{8,9},{9,8},{10,11... | collective-permute-start | bytes 3145736 | tf_op jit(solution)/shard_map/ppermute | solution.py:26
  193.9 38.6 %collective-permute-start.3 = (bf16[32,32,512]{2,1,0:T(8,128)(2,1)S(1)}, bf16[32,32,512]{2,1,0:T(8,128)(2,1)}, u32[]{:S(2)}, u32[]{:S(2)}) collective-permute-start(bf16[32,32,512]{2,1,0:T(8,128)(2,1)S(1)} %bitcast.80), channel_id=1, source_target_pairs={{0,1},{1,0},{2,3},{3,2},{4,5},{5,4},{6,7},{7,6},{8,9},{9,8},{10,11... | collective-permute-start | bytes 3145736 | tf_op jit(solution)/shard_map/ppermute | solution.py:26

commit v11 on v9

--- a/solution.py
+++ b/solution.py
@@ -64,18 +64,28 @@
     out_ref[1, station, :, channels:] = -filtered[0]
 
 
-def fir_kernel(taps_ref, frames_ref, out_ref):
-    halo = taps_ref.shape[0] - 1
+def fir_kernel(taps_ref, frames_ref, out_ref, scratch_ref):
+    tap_count = taps_ref.shape[0]
     spectra = frames_ref.shape[2]
     channels = frames_ref.shape[3]
+    edge = 8
+    count = spectra - edge
+    start = edge - (tap_count - 1)
 
     def body(station, carry):
         filtered = []
         for part in range(2):
-            frames = frames_ref[part, station].astype(jnp.float32)
-            extended = jnp.concatenate([jnp.zeros((halo, channels), jnp.float32), frames], axis=0)
-            filtered.append(fir_rows(taps_ref, extended, spectra))
-        fir_store(out_ref, station, filtered, channels)
+            scratch_ref[...] = frames_ref[part, station].astype(jnp.float32)
+            total = taps_ref[0:1, :] * scratch_ref[pl.ds(start, count), :]
+            for tap_index in range(1, tap_count):
+                total = total + taps_ref[tap_index : tap_index + 1, :] * scratch_ref[
+                    pl.ds(start + tap_index, count), :
+                ]
+            filtered.append(total.astype(jnp.bfloat16))
+        out_ref[0, station, edge:, 0:channels] = filtered[0]
+        out_ref[0, station, edge:, channels:] = filtered[1]
+        out_ref[1, station, edge:, 0:channels] = filtered[1]
+        out_ref[1, station, edge:, channels:] = -filtered[0]
         return carry
 
     lax.fori_loop(0, frames_ref.shape[1], body, 0)
@@ -116,6 +126,7 @@
         ],
         out_specs=pl.BlockSpec((2, group, spectra, 2 * channels), lambda a: (0, a, 0, 0)),
         out_shape=out_shape,
+        scratch_shapes=[pltpu.VMEM((spectra, channels), jnp.float32)],
         cost_estimate=pl.CostEstimate(
             flops=4 * tap_count * frames.size,
             transcendentals=0,

time: 235 us -> 235 us (level)
  transfers between devices with their start and end apart: 9 -> 9, of which waited for: 8 -> 8; matrix products, arithmetic and copies ran while one was open for 27% -> 27% of each run, Pallas kernels for 16% -> 15%
where the time goes in v11:
time: 235 us; the launch traced here: 234 us
  waiting for transfers between devices  79.8 us (34%)
  Pallas kernels  49.6 us (21%)
  matrix products  41.4 us (18%)
  starting transfers between devices  24.9 us (11%)
  local copies, waits for them, and re-layouts  24.1 us (10%)
  other arithmetic  13.6 us (6%)
    all_to_all x4, waiting for transfers between devices, per_device(): lax.all_to_all(spectra, 'stn', split_axis=0, concat_axis=0, tiled=True)  56.1 us
    pallas_call x4, Pallas kernels, correlate_rows_chunk(): pl.pallas_call(correlate_rows_kernel, grid_spec=grid_spec, out_shape=jax....  29.9 us
    dot_general x4, matrix products, per_device(): jnp.einsum('kj,nj->kn', weights[chunk], source, preferred_element_type=jn...  27.1 us
    all_to_all x4, starting transfers between devices, per_device(): lax.all_to_all(spectra, 'stn', split_axis=0, concat_axis=0, tiled=True)  22.4 us
    ppermute x4, waiting for transfers between devices, gathered_along(): parts.append(lax.ppermute(value, axis, pairs))  19.1 us
    reshape x4, local copies, waits for them, and re-layouts, per_device(): turned = turned.reshape(groups, width, 2, stations_local, spectra_local)  17.6 us
    dot_general x4, matrix products, per_device(): jnp.einsum('gkias,gar->kisr', turned, selector, preferred_element_type=jn...  14.2 us
    pallas_call x1, Pallas kernels, filter_frames(): pl.pallas_call(fir_kernel, grid=(stations_local // group,), in_specs=[pl....  13.6 us
  transfers between devices with their start and end apart: 9, of which 8 were waited for; matrix products, arithmetic and copies ran while one was open for 27% of the time, Pallas kernels for 15%

profile of v11, /device:TPU:14, one launch (start us, length us, event | category | flops | bytes accessed | tf_op | source)
XLA Modules:
  0.0 233.6 jit_solution(3788860448834050773)
XLA Ops:
  0.0 3.8 %convert.3 = bf16[2,32,32768]{2,1,0:T(8,128)(2,1)S(1)} convert(s32[2,32,32768]{2,1,0:T(8,128)} %param.4) | non-fusion elementwise | flops 2097152 | bytes 12582912 | tf_op jit(solution)/shard_map/convert
  3.8 0.1 slice.21
  3.9 0.1 copy.57
  4.0 1.3 collective-permute-start
  5.3 4.5 %copy.39 = bf16[8,8,32,1024]{3,2,1,0:T(8,128)(2,1)} copy(bf16[8,8,32,1024]{3,1,2,0:T(8,128)(2,1)S(1)} %bitcast.67) | data formatting | bytes 8388608
  9.7 13.6 %shard_map.46.previous_ref = bf16[2,32,32,2048]{3,2,1,0:T(8,128)(2,1)} custom-call(f32[8,1024]{1,0:T(8,128)} %taps_ref.3, bf16[2,32,32,1024]{3,2,1,0:T(8,128)(2,1)} %bitcast.61), custom_call_target="tpu_custom_call" | custom-call | flops 67108864 | bytes 12582912 | tf_op jit(solution)/shard_map/pallas_call | solution.py:120
  23.3 4.6 %collective-permute-done = bf16[2,32,7,1024]{3,1,2,0:T(8,128)(2,1)S(1)} collective-permute-done((bf16[2,32,7,1024]{3,1,2,0:T(8,128)(2,1)S(1)}, bf16[2,32,7,1024]{3,1,2,0:T(8,128)(2,1)S(1)}, u32[]{:S(2)}, u32[]{:S(2)}) %collective-permute-start) | collective-permute-done | bytes 917536 | tf_op jit(solution)/shard_map/ppermute | solution.py:18
  27.9 1.6 copy.20.halo_ref
  29.5 6.1 %shard_map.47 = bf16[2,32,32,2048]{3,2,1,0:T(8,128)(2,1)} custom-call(f32[8,1024]{1,0:T(8,128)} %taps_ref.3, bf16[2,32,7,1024]{3,2,1,0:T(8,128)(2,1)} %copy.20.halo_ref, bf16[2,32,32,1024]{3,2,1,0:T(8,128)(2,1)} %bitcast.62, bf16[2,32,32,2048]{3,2,1,0:T(8,128)(2,1)} %shard_map.46.previous_ref), custom_call_target="tpu_custom_call", output_to_operand_aliasing={{}: (3, {})} | custom-call | flops 16777216 | bytes 4194304 | tf_op jit(solution)/shard_map/pallas_call | solution.py:138
  35.6 6.8 %convolution_convert_fusion.2 = bf16[2048,256]{0,1:T(8,128)(2,1)} fusion(bf16[2048,2048]{1,0:T(8,128)(2,1)} %bitcast.63, bf16[256,2048]{1,0:T(8,128)(2,1)S(1)} %copy-done.4), kind=kOutput, calls=%fused_computation.10 | convolution fusion | flops 2148007936 | bytes 10485760 | tf_op jit(solution)/shard_map/kj,nj->kn/dot_general | solution.py:311
  42.4 6.2 %all-to-all-start.1 = ((bf16[16,16,2048]{2,1,0:T(8,128)(2,1)}), bf16[16,16,2048]{2,1,0:T(8,128)(2,1)S(1)}, u32[]{:S(2)}, u32[]{:S(2)}) async-start(bf16[16,16,2048]{2,1,0:T(8,128)(2,1)} %bitcast.10), calls=%async_computation.1 | async-start | bytes 2097152 | tf_op jit(solution)/shard_map/all_to_all | solution.py:315
  48.7 6.8 %convolution_convert_fusion.3 = bf16[2048,256]{0,1:T(8,128)(2,1)} fusion(bf16[2048,2048]{1,0:T(8,128)(2,1)} %bitcast.64, bf16[256,2048]{1,0:T(8,128)(2,1)S(1)} %copy-done.3), kind=kOutput, calls=%fused_computation.11 | convolution fusion | flops 2148007936 | bytes 10485760 | tf_op jit(solution)/shard_map/kj,nj->kn/dot_general | solution.py:311
  55.5 17.9 %all-to-all-done.1 = bf16[16,16,2048]{2,1,0:T(8,128)(2,1)S(1)} async-done(((bf16[16,16,2048]{2,1,0:T(8,128)(2,1)}), bf16[16,16,2048]{2,1,0:T(8,128)(2,1)S(1)}, u32[]{:S(2)}, u32[]{:S(2)}) %all-to-all-start.1) | async-done | bytes 1048608 | tf_op jit(solution)/shard_map/all_to_all | solution.py:315
  73.4 5.1 %all-to-all-start = ((bf16[16,16,2048]{2,1,0:T(8,128)(2,1)}), bf16[16,16,2048]{2,1,0:T(8,128)(2,1)S(1)}, u32[]{:S(2)}, u32[]{:S(2)}) async-start(bf16[16,16,2048]{2,1,0:T(8,128)(2,1)} %bitcast.3), calls=%async_computation | async-start | bytes 2097152 | tf_op jit(solution)/shard_map/all_to_all | solution.py:315
  78.5 4.4 %reshape.85 = bf16[16,16,2,32,32]{4,3,2,1,0:T(8,128)(2,1)} reshape(bf16[16,16,2048]{2,1,0:T(8,128)(2,1)S(1)} %all-to-all-done.1) | data formatting | bytes 2097152 | tf_op jit(solution)/shard_map/reshape | solution.py:316
  82.9 3.6 %fusion.4 = bf16[16,2,32,512,1]{3,2,0,1,4:T(8,128)(2,1)S(1)} fusion(bf16[16,16,2,32,32]{4,3,2,1,0:T(8,128)(2,1)} %reshape.85, s32[16,32]{1,0:T(8,128)S(1)} %multiply_add_fusion, s32[512]{0:T(512)S(1)} %copy-done), kind=kOutput, calls=%fused_computation.4 | convolution fusion | flops 537133056 | bytes 2101248 | tf_op jit(solution)/shard_map/gkias,gar->kisr/dot_general | solution.py:317
  86.4 0.1 copy.55
  86.5 0.1 collective-permute-start.2
  86.6 16.6 %all-to-all-done = bf16[16,16,2048]{2,1,0:T(8,128)(2,1)S(1)} async-done(((bf16[16,16,2048]{2,1,0:T(8,128)(2,1)}), bf16[16,16,2048]{2,1,0:T(8,128)(2,1)S(1)}, u32[]{:S(2)}, u32[]{:S(2)}) %all-to-all-start) | async-done | bytes 1048608 | tf_op jit(solution)/shard_map/all_to_all | solution.py:315
  103.2 4.4 %reshape.81 = bf16[16,16,2,32,32]{4,3,2,1,0:T(8,128)(2,1)} reshape(bf16[16,16,2048]{2,1,0:T(8,128)(2,1)S(1)} %all-to-all-done) | data formatting | bytes 2097152 | tf_op jit(solution)/shard_map/reshape | solution.py:316
  107.6 3.6 %fusion.6 = bf16[16,2,32,512,1]{3,2,0,1,4:T(8,128)(2,1)S(1)} fusion(bf16[16,16,2,32,32]{4,3,2,1,0:T(8,128)(2,1)} %reshape.81, s32[16,32]{1,0:T(8,128)S(1)} %multiply_add_fusion, s32[512]{0:T(512)S(1)} %copy-done), kind=kOutput, calls=%fused_computation.6 | convolution fusion | flops 537133056 | bytes 2101248 | tf_op jit(solution)/shard_map/gkias,gar->kisr/dot_general | solution.py:317
  111.1 0.1 copy.56
  111.2 0.1 collective-permute-start.1
  111.3 0.6 collective-permute-done.2
  111.9 2.8 %pad_maximum_fusion.1 = bf16[32,64,512]{2,1,0:T(8,128)(2,1)} fusion(bf16[32,32,512]{2,1,0:T(8,128)(2,1)} %collective-permute-done.2, bf16[32,32,512]{2,1,0:T(8,128)(2,1)S(1)} %bitcast.77), kind=kLoop, calls=%fused_computation.13 | loop fusion | flops 4194304 | bytes 4194304 | tf_op jit(solution)/shard_map/concatenate | solution.py:27
  114.7 7.5 %shard_map.48.refs_0_ = bf16[2,64,256,512]{3,2,1,0:T(8,128)(2,1)} custom-call(s32[1]{0:T(128)} %bitcast.block_ref, bf16[16,128,512]{2,1,0:T(8,128)(2,1)} %bitcast.68, bf16[16,128,512]{2,1,0:T(8,128)(2,1)} %bitcast.69), custom_call_target="tpu_custom_call" | custom-call | flops 1073741824 | bytes 11534336 | tf_op jit(solution)/shard_map/pallas_call | solution.py:248
  122.2 6.7 %convolution_convert_fusion = bf16[2048,256]{0,1:T(8,128)(2,1)} fusion(bf16[2048,2048]{1,0:T(8,128)(2,1)} %bitcast.65, bf16[256,2048]{1,0:T(8,128)(2,1)S(1)} %copy-done.2), kind=kOutput, calls=%fused_computation.8 | convolution fusion | flops 2148007936 | bytes 10485760 | tf_op jit(solution)/shard_map/kj,nj->kn/dot_general | solution.py:311
  129.0 6.0 %all-to-all-start.3 = ((bf16[16,16,2048]{2,1,0:T(8,128)(2,1)}), bf16[16,16,2048]{2,1,0:T(8,128)(2,1)S(1)}, u32[]{:S(2)}, u32[]{:S(2)}) async-start(bf16[16,16,2048]{2,1,0:T(8,128)(2,1)} %bitcast.21), calls=%async_computation.3 | async-start | bytes 2097152 | tf_op jit(solution)/shard_map/all_to_all | solution.py:315
  135.0 2.2 collective-permute-done.1
  137.2 2.8 %pad_maximum_fusion = bf16[32,64,512]{2,1,0:T(8,128)(2,1)} fusion(bf16[32,32,512]{2,1,0:T(8,128)(2,1)} %collective-permute-done.1, bf16[32,32,512]{2,1,0:T(8,128)(2,1)S(1)} %bitcast.81), kind=kLoop, calls=%fused_computation.12 | loop fusion | flops 4194304 | bytes 4194304 | tf_op jit(solution)/shard_map/concatenate | solution.py:27
  140.0 7.5 %shard_map.49.refs_0_ = bf16[2,64,256,512]{3,2,1,0:T(8,128)(2,1)} custom-call(s32[1]{0:T(128)} %bitcast.block_ref, bf16[16,128,512]{2,1,0:T(8,128)(2,1)} %bitcast.72, bf16[16,128,512]{2,1,0:T(8,128)(2,1)} %bitcast.73, bf16[2,64,256,512]{3,2,1,0:T(8,128)(2,1)} %shard_map.48.refs_0_), custom_call_target="tpu_custom_call", output_to_operand_aliasing={{}: (3, {})} | custom-call | flops 1073741824 | bytes 11534336 | tf_op jit(solution)/shard_map/pallas_call | solution.py:248
  147.5 6.8 %convolution_convert_fusion.1 = bf16[2048,256]{0,1:T(8,128)(2,1)} fusion(bf16[2048,2048]{1,0:T(8,128)(2,1)} %bitcast.66, bf16[256,2048]{1,0:T(8,128)(2,1)S(1)} %copy-done.1), kind=kOutput, calls=%fused_computation.9 | convolution fusion | flops 2148007936 | bytes 10485760 | tf_op jit(solution)/shard_map/kj,nj->kn/dot_general | solution.py:311
  154.3 5.4 %all-to-all-done.3 = bf16[16,16,2048]{2,1,0:T(8,128)(2,1)S(1)} async-done(((bf16[16,16,2048]{2,1,0:T(8,128)(2,1)}), bf16[16,16,2048]{2,1,0:T(8,128)(2,1)S(1)}, u32[]{:S(2)}, u32[]{:S(2)}) %all-to-all-start.3) | async-done | bytes 1048608 | tf_op jit(solution)/shard_map/all_to_all | solution.py:315
  159.7 5.1 %all-to-all-start.2 = ((bf16[16,16,2048]{2,1,0:T(8,128)(2,1)}), bf16[16,16,2048]{2,1,0:T(8,128)(2,1)S(1)}, u32[]{:S(2)}, u32[]{:S(2)}) async-start(bf16[16,16,2048]{2,1,0:T(8,128)(2,1)} %bitcast.16), calls=%async_computation.2 | async-start | bytes 2097152 | tf_op jit(solution)/shard_map/all_to_all | solution.py:315
  164.8 4.4 %reshape.93 = bf16[16,16,2,32,32]{4,3,2,1,0:T(8,128)(2,1)} reshape(bf16[16,16,2048]{2,1,0:T(8,128)(2,1)S(1)} %all-to-all-done.3) | data formatting | bytes 2097152 | tf_op jit(solution)/shard_map/reshape | solution.py:316
  169.2 3.6 %fusion = bf16[16,2,32,512,1]{3,2,0,1,4:T(8,128)(2,1)S(1)} fusion(bf16[16,16,2,32,32]{4,3,2,1,0:T(8,128)(2,1)} %reshape.93, s32[16,32]{1,0:T(8,128)S(1)} %multiply_add_fusion, s32[512]{0:T(512)S(1)} %copy-done), kind=kOutput, calls=%fused_computation | convolution fusion | flops 537133056 | bytes 2101248 | tf_op jit(solution)/shard_map/gkias,gar->kisr/dot_general | solution.py:317
  172.8 0.1 copy.53
  172.9 0.5 collective-permute-start.4
  173.4 16.1 %all-to-all-done.2 = bf16[16,16,2048]{2,1,0:T(8,128)(2,1)S(1)} async-done(((bf16[16,16,2048]{2,1,0:T(8,128)(2,1)}), bf16[16,16,2048]{2,1,0:T(8,128)(2,1)S(1)}, u32[]{:S(2)}, u32[]{:S(2)}) %all-to-all-start.2) | async-done | bytes 1048608 | tf_op jit(solution)/shard_map/all_to_all | solution.py:315
  189.5 4.4 %reshape.89 = bf16[16,16,2,32,32]{4,3,2,1,0:T(8,128)(2,1)} reshape(bf16[16,16,2048]{2,1,0:T(8,128)(2,1)S(1)} %all-to-all-done.2) | data formatting | bytes 2097152 | tf_op jit(solution)/shard_map/reshape | solution.py:316
  194.0 3.6 %fusion.2 = bf16[16,2,32,512,1]{3,2,0,1,4:T(8,128)(2,1)S(1)} fusion(bf16[16,16,2,32,32]{4,3,2,1,0:T(8,128)(2,1)} %reshape.89, s32[16,32]{1,0:T(8,128)S(1)} %multiply_add_fusion, s32[512]{0:T(512)S(1)} %copy-done), kind=kOutput, calls=%fused_computation.2 | convolution fusion | flops 537133056 | bytes 2101248 | tf_op jit(solution)/shard_map/gkias,gar->kisr/dot_general | solution.py:317
  197.5 0.1 copy.54
  197.6 0.5 collective-permute-start.3
  198.2 1.5 pad_maximum_fusion.3
  199.7 7.4 %shard_map.50.refs_0_ = bf16[2,64,256,512]{3,2,1,0:T(8,128)(2,1)} custom-call(s32[1]{0:T(128)} %bitcast.block_ref, bf16[16,128,512]{2,1,0:T(8,128)(2,1)} %bitcast.74, bf16[16,128,512]{2,1,0:T(8,128)(2,1)} %bitcast.75, bf16[2,64,256,512]{3,2,1,0:T(8,128)(2,1)} %shard_map.49.refs_0_), custom_call_target="tpu_custom_call", output_to_operand_aliasing={{}: (3, {})} | custom-call | flops 1073741824 | bytes 11534336 | tf_op jit(solution)/shard_map/pallas_call | solution.py:248
  207.1 16.3 %collective-permute-done.3 = bf16[32,32,512]{2,1,0:T(8,128)(2,1)} collective-permute-done((bf16[32,32,512]{2,1,0:T(8,128)(2,1)S(1)}, bf16[32,32,512]{2,1,0:T(8,128)(2,1)}, u32[]{:S(2)}, u32[]{:S(2)}) %collective-permute-start.3) | collective-permute-done | bytes 1048608 | tf_op jit(solution)/shard_map/ppermute | solution.py:26
  223.4 2.8 %pad_maximum_fusion.2 = bf16[32,64,512]{2,1,0:T(8,128)(2,1)} fusion(bf16[32,32,512]{2,1,0:T(8,128)(2,1)} %collective-permute-done.3, bf16[32,32,512]{2,1,0:T(8,128)(2,1)S(1)} %bitcast.83), kind=kLoop, calls=%fused_computation.14 | loop fusion | flops 4194304 | bytes 4194304 | tf_op jit(solution)/shard_map/concatenate | solution.py:27
  226.2 7.4 %shard_map.51 = bf16[2,64,256,512]{3,2,1,0:T(8,128)(2,1)} custom-call(s32[1]{0:T(128)} %bitcast.block_ref, bf16[16,128,512]{2,1,0:T(8,128)(2,1)} %bitcast.70, bf16[16,128,512]{2,1,0:T(8,128)(2,1)} %bitcast.71, bf16[2,64,256,512]{3,2,1,0:T(8,128)(2,1)} %shard_map.50.refs_0_), custom_call_target="tpu_custom_call", output_to_operand_aliasing={{}: (3, {})} | custom-call | flops 1073741824 | bytes 11534336 | tf_op jit(solution)/shard_map/pallas_call | solution.py:248
  (12 shorter events, 0.1 us)
Async XLA Ops:
  4.0 24.0 %collective-permute-start = (bf16[2,32,7,1024]{3,1,2,0:T(8,128)(2,1)S(1)}, bf16[2,32,7,1024]{3,1,2,0:T(8,128)(2,1)S(1)}, u32[]{:S(2)}, u32[]{:S(2)}) collective-permute-start(bf16[2,32,7,1024]{3,1,2,0:T(8,128)(2,1)S(1)} %bitcast.85), channel_id=1, source_target_pairs={{0,1},{2,3},{4,5},{6,7},{8,9},{10,11},{12,13},{14,15},{16,17},{18,... | collective-permute-start | bytes 2752520 | tf_op jit(solution)/shard_map/ppermute | solution.py:18
  29.5 6.1 %copy-start.4 = (bf16[256,2048]{1,0:T(8,128)(2,1)S(1)}, bf16[256,2048]{1,0:T(8,128)(2,1)}, u32[]{:S(2)}) copy-start(bf16[256,2048]{1,0:T(8,128)(2,1)} %constant.12) | copy-start | bytes 3145732
  35.6 13.1 %copy-start.3 = (bf16[256,2048]{1,0:T(8,128)(2,1)S(1)}, bf16[256,2048]{1,0:T(8,128)(2,1)}, u32[]{:S(2)}) copy-start(bf16[256,2048]{1,0:T(8,128)(2,1)} %constant.10) | copy-start | bytes 3145732
  42.4 31.0 %all-to-all-start.1 = ((bf16[16,16,2048]{2,1,0:T(8,128)(2,1)}), bf16[16,16,2048]{2,1,0:T(8,128)(2,1)S(1)}, u32[]{:S(2)}, u32[]{:S(2)}) async-start(bf16[16,16,2048]{2,1,0:T(8,128)(2,1)} %bitcast.10), calls=%async_computation.1 | async-start | bytes 2097152 | tf_op jit(solution)/shard_map/all_to_all | solution.py:315
  55.5 27.4 %copy-start = (s32[512]{0:T(512)S(1)}, s32[512]{0:T(512)}, u32[]{:S(2)}) copy-start(s32[512]{0:T(512)} %param.6) | copy-start | bytes 6148
  73.4 29.8 %all-to-all-start = ((bf16[16,16,2048]{2,1,0:T(8,128)(2,1)}), bf16[16,16,2048]{2,1,0:T(8,128)(2,1)S(1)}, u32[]{:S(2)}, u32[]{:S(2)}) async-start(bf16[16,16,2048]{2,1,0:T(8,128)(2,1)} %bitcast.3), calls=%async_computation | async-start | bytes 2097152 | tf_op jit(solution)/shard_map/all_to_all | solution.py:315
  86.5 25.4 %collective-permute-start.2 = (bf16[32,32,512]{2,1,0:T(8,128)(2,1)S(1)}, bf16[32,32,512]{2,1,0:T(8,128)(2,1)}, u32[]{:S(2)}, u32[]{:S(2)}) collective-permute-start(bf16[32,32,512]{2,1,0:T(8,128)(2,1)S(1)} %bitcast.76), channel_id=1, source_target_pairs={{0,1},{1,0},{2,3},{3,2},{4,5},{5,4},{6,7},{7,6},{8,9},{9,8},{10,11... | collective-permute-start | bytes 3145736 | tf_op jit(solution)/shard_map/ppermute | solution.py:26
  111.2 25.9 %collective-permute-start.1 = (bf16[32,32,512]{2,1,0:T(8,128)(2,1)S(1)}, bf16[32,32,512]{2,1,0:T(8,128)(2,1)}, u32[]{:S(2)}, u32[]{:S(2)}) collective-permute-start(bf16[32,32,512]{2,1,0:T(8,128)(2,1)S(1)} %bitcast.80), channel_id=1, source_target_pairs={{0,1},{1,0},{2,3},{3,2},{4,5},{5,4},{6,7},{7,6},{8,9},{9,8},{10,11... | collective-permute-start | bytes 3145736 | tf_op jit(solution)/shard_map/ppermute | solution.py:26
  114.7 7.5 %copy-start.2 = (bf16[256,2048]{1,0:T(8,128)(2,1)S(1)}, bf16[256,2048]{1,0:T(8,128)(2,1)}, u32[]{:S(2)}) copy-start(bf16[256,2048]{1,0:T(8,128)(2,1)} %constant.16) | copy-start | bytes 3145732
  129.0 30.8 %all-to-all-start.3 = ((bf16[16,16,2048]{2,1,0:T(8,128)(2,1)}), bf16[16,16,2048]{2,1,0:T(8,128)(2,1)S(1)}, u32[]{:S(2)}, u32[]{:S(2)}) async-start(bf16[16,16,2048]{2,1,0:T(8,128)(2,1)} %bitcast.21), calls=%async_computation.3 | async-start | bytes 2097152 | tf_op jit(solution)/shard_map/all_to_all | solution.py:315
  140.0 7.5 %copy-start.1 = (bf16[256,2048]{1,0:T(8,128)(2,1)S(1)}, bf16[256,2048]{1,0:T(8,128)(2,1)}, u32[]{:S(2)}) copy-start(bf16[256,2048]{1,0:T(8,128)(2,1)} %constant.14) | copy-start | bytes 3145732
  159.7 29.8 %all-to-all-start.2 = ((bf16[16,16,2048]{2,1,0:T(8,128)(2,1)}), bf16[16,16,2048]{2,1,0:T(8,128)(2,1)S(1)}, u32[]{:S(2)}, u32[]{:S(2)}) async-start(bf16[16,16,2048]{2,1,0:T(8,128)(2,1)} %bitcast.16), calls=%async_computation.2 | async-start | bytes 2097152 | tf_op jit(solution)/shard_map/all_to_all | solution.py:315
  172.9 25.3 %collective-permute-start.4 = (bf16[32,32,512]{2,1,0:T(8,128)(2,1)S(1)}, bf16[32,32,512]{2,1,0:T(8,128)(2,1)S(1)}, u32[]{:S(2)}, u32[]{:S(2)}) collective-permute-start(bf16[32,32,512]{2,1,0:T(8,128)(2,1)S(1)} %bitcast.78), channel_id=1, source_target_pairs={{0,1},{1,0},{2,3},{3,2},{4,5},{5,4},{6,7},{7,6},{8,9},{9,8},{10,11... | collective-permute-start | bytes 3145736 | tf_op jit(solution)/shard_map/ppermute | solution.py:26
  197.6 25.8 %collective-permute-start.3 = (bf16[32,32,512]{2,1,0:T(8,128)(2,1)S(1)}, bf16[32,32,512]{2,1,0:T(8,128)(2,1)}, u32[]{:S(2)}, u32[]{:S(2)}) collective-permute-start(bf16[32,32,512]{2,1,0:T(8,128)(2,1)S(1)} %bitcast.82), channel_id=1, source_target_pairs={{0,1},{1,0},{2,3},{3,2},{4,5},{5,4},{6,7},{7,6},{8,9},{9,8},{10,11... | collective-permute-start | bytes 3145736 | tf_op jit(solution)/shard_map/ppermute | solution.py:26

commit v12 on v11

--- a/solution.py
+++ b/solution.py
@@ -58,10 +58,8 @@
 
 
 def fir_store(out_ref, station, filtered, channels):
-    out_ref[0, station, :, 0:channels] = filtered[0]
-    out_ref[0, station, :, channels:] = filtered[1]
-    out_ref[1, station, :, 0:channels] = filtered[1]
-    out_ref[1, station, :, channels:] = -filtered[0]
+    out_ref[station, :, 0:channels] = filtered[0]
+    out_ref[station, :, channels:] = filtered[1]
 
 
 def fir_kernel(taps_ref, frames_ref, out_ref, scratch_ref):
@@ -82,10 +80,8 @@
                     pl.ds(start + tap_index, count), :
                 ]
             filtered.append(total.astype(jnp.bfloat16))
-        out_ref[0, station, edge:, 0:channels] = filtered[0]
-        out_ref[0, station, edge:, channels:] = filtered[1]
-        out_ref[1, station, edge:, 0:channels] = filtered[1]
-        out_ref[1, station, edge:, channels:] = -filtered[0]
+        out_ref[station, edge:, 0:channels] = filtered[0]
+        out_ref[station, edge:, channels:] = filtered[1]
         return carry
 
     lax.fori_loop(0, frames_ref.shape[1], body, 0)
@@ -115,7 +111,7 @@
 def filter_frames(fir_taps, earlier, frames):
     tap_count, channels = fir_taps.shape
     _, stations_local, spectra, _ = frames.shape
-    out_shape = jax.ShapeDtypeStruct((2, stations_local, spectra, 2 * channels), jnp.bfloat16)
+    out_shape = jax.ShapeDtypeStruct((stations_local, spectra, 2 * channels), jnp.bfloat16)
     group = 4 if stations_local % 4 == 0 else 1
     whole = pl.pallas_call(
         fir_kernel,
@@ -124,13 +120,13 @@
             pl.BlockSpec((tap_count, channels), lambda a: (0, 0)),
             pl.BlockSpec((2, group, spectra, channels), lambda a: (0, a, 0, 0)),
         ],
-        out_specs=pl.BlockSpec((2, group, spectra, 2 * channels), lambda a: (0, a, 0, 0)),
+        out_specs=pl.BlockSpec((group, spectra, 2 * channels), lambda a: (a, 0, 0)),
         out_shape=out_shape,
         scratch_shapes=[pltpu.VMEM((spectra, channels), jnp.float32)],
         cost_estimate=pl.CostEstimate(
             flops=4 * tap_count * frames.size,
             transcendentals=0,
-            bytes_accessed=2 * frames.size + 4 * frames.size,
+            bytes_accessed=2 * frames.size + 2 * frames.size,
         ),
     )(fir_taps, frames)
     edge = 8
@@ -144,13 +140,13 @@
             pl.BlockSpec((2, edge_group, edge, channels), lambda a: (0, a, 0, 0)),
             pl.BlockSpec(memory_space=pl.ANY),
         ],
-        out_specs=pl.BlockSpec((2, edge_group, edge, 2 * channels), lambda a: (0, a, 0, 0)),
+        out_specs=pl.BlockSpec((edge_group, edge, 2 * channels), lambda a: (a, 0, 0)),
         out_shape=out_shape,
         input_output_aliases={3: 0},
         cost_estimate=pl.CostEstimate(
             flops=4 * tap_count * edge * frames.size // spectra,
             transcendentals=0,
-            bytes_accessed=8 * edge * frames.size // spectra,
+            bytes_accessed=6 * edge * frames.size // spectra,
         ),
     )(fir_taps, earlier, frames, whole)
 
@@ -276,9 +272,12 @@
     frames = samples.astype(jnp.bfloat16).reshape(2, stations_local, spectra_local, channels)
     earlier = passed_along(earlier, "blk", 1)
     filtered = filter_frames(fir_taps, earlier, frames)
-    filtered = filtered.reshape(2 * stations_local * spectra_local, 2 * channels)
-
-    weights = dft_weights(channels, groups, chunks)
+    filtered = filtered.reshape(stations_local * spectra_local, 2 * channels)
+
+    table = dft_weights(channels, groups, chunks).reshape(chunks, groups, 1, width, 2 * channels)
+    table = lax.optimization_barrier(table)
+    rotated = jnp.concatenate([-table[..., channels:], table[..., :channels]], axis=-1)
+    weights = jnp.concatenate([table, rotated], axis=2).reshape(chunks, groups * 2 * width, -1)
     selector = (
         station_order[None, :] == jnp.arange(stations, dtype=jnp.int32)[:, None]
     ).astype(jnp.bfloat16)
@@ -311,11 +310,11 @@
         spectra = jnp.einsum(
             "kj,nj->kn", weights[chunk], source, preferred_element_type=jnp.float32
         ).astype(jnp.bfloat16)
-        spectra = spectra.reshape(groups, width, 2 * stations_local * spectra_local)
+        spectra = spectra.reshape(groups, 2 * width, stations_local * spectra_local)
         turned = lax.all_to_all(spectra, "stn", split_axis=0, concat_axis=0, tiled=True)
-        turned = turned.reshape(groups, width, 2, stations_local, spectra_local)
+        turned = turned.reshape(groups, 2, width, stations_local, spectra_local)
         ordered = jnp.einsum(
-            "gkias,gar->kisr", turned, selector, preferred_element_type=jnp.float32
+            "gikas,gar->kisr", turned, selector, preferred_element_type=jnp.float32
         ).astype(jnp.bfloat16)
         ordered = ordered.reshape(width * 2, spectra_local, stations)
         pending.append(gathered_along(ordered, "blk", 1))

time: 235 us -> 259 us (1.10)
  waiting for transfers between devices: 79.8 us -> 91.1 us
  starting transfers between devices: 24.9 us -> 33.7 us
  local copies, waits for them, and re-layouts: 24.1 us -> 30.5 us
  matrix products: 41.4 us -> 37.4 us
    ppermute x4, waiting for transfers between devices: 19.1 us -> 44.7 us  [gathered_along(): parts.append(lax.ppermute(value, axis, pairs))]
    all_to_all x4, waiting for transfers between devices: 56.1 us -> 46.4 us  [per_device(): lax.all_to_all(spectra, 'stn', split_axis=0, concat_axis=0, tiled=True)]
    ppermute x4, starting transfers between devices: 1.21 us -> 9.03 us  [gathered_along(): parts.append(lax.ppermute(value, axis, pairs))]
    slice x0 -> x1, local copies, waits for them, and re-layouts: none -> 5.61 us  [per_device(): weights[chunk]]
    ppermute x1, waiting for transfers between devices: 4.62 us -> 0.01 us  [passed_along(): lax.ppermute(value, axis, [(source, source + steps) for source in range(i...]
    dot_general x4, matrix products: 27.1 us -> 22.8 us  [per_device(): jnp.einsum('kj,nj->kn', weights[chunk], source, preferred_element_type=jn...]
    concatenate x0 -> x1, other arithmetic: none -> 3.67 us  [per_device(): jnp.concatenate([table, rotated], axis=2)]
    concatenate x4, other arithmetic: 9.85 us -> 7.23 us  [gathered_along(): return jnp.concatenate(parts, axis=dimension)]
  transfers between devices with their start and end apart: 9 -> 9, of which waited for: 8 -> 6; matrix products, arithmetic and copies ran while one was open for 27% -> 24% of each run, Pallas kernels for 15% -> 11%
where the time goes in v12:
time: 259 us; the launch traced here: 256 us
  waiting for transfers between devices  91.1 us (35%)
  Pallas kernels  48.5 us (19%)
  matrix products  37.4 us (14%)
  starting transfers between devices  33.7 us (13%)
  local copies, waits for them, and re-layouts  30.5 us (12%)
  other arithmetic  15.1 us (6%)
    all_to_all x4, waiting for transfers between devices, per_device(): lax.all_to_all(spectra, 'stn', split_axis=0, concat_axis=0, tiled=True)  46.4 us
    ppermute x4, waiting for transfers between devices, gathered_along(): parts.append(lax.ppermute(value, axis, pairs))  44.7 us
    pallas_call x4, Pallas kernels, correlate_rows_chunk(): pl.pallas_call(correlate_rows_kernel, grid_spec=grid_spec, out_shape=jax....  30.1 us
    all_to_all x4, starting transfers between devices, per_device(): lax.all_to_all(spectra, 'stn', split_axis=0, concat_axis=0, tiled=True)  23.3 us
    dot_general x4, matrix products, per_device(): jnp.einsum('kj,nj->kn', weights[chunk], source, preferred_element_type=jn...  22.8 us
    reshape x4, local copies, waits for them, and re-layouts, per_device(): turned = turned.reshape(groups, 2, width, stations_local, spectra_local)  17.3 us
    dot_general x4, matrix products, per_device(): jnp.einsum('gikas,gar->kisr', turned, selector, preferred_element_type=jn...  14.5 us
    pallas_call x1, Pallas kernels, filter_frames(): pl.pallas_call(fir_kernel, grid=(stations_local // group,), in_specs=[pl....  12.6 us
  transfers between devices with their start and end apart: 9, of which 6 were waited for; matrix products, arithmetic and copies ran while one was open for 24% of the time, Pallas kernels for 11%

profile of v12, /device:TPU:14, one launch (start us, length us, event | category | flops | bytes accessed | tf_op | source)
XLA Modules:
  0.0 256.4 jit_solution(13454516333453776615)
XLA Ops:
  0.0 3.9 %convert.3 = bf16[2,32,32768]{2,1,0:T(8,128)(2,1)S(1)} convert(s32[2,32,32768]{2,1,0:T(8,128)} %param.4) | non-fusion elementwise | flops 2097152 | bytes 12582912 | tf_op jit(solution)/shard_map/convert
  4.0 0.1 copy.43
  4.1 1.3 collective-permute-start
  5.4 0.3 slice_negate_fusion
  5.7 3.7 %maximum_maximum_fusion = bf16[4,16,2,16,2048]{4,3,2,1,0:T(8,128)(2,1)} fusion(bf16[4,16,1,16,1024]{4,3,2,1,0:T(8,128)(2,1)S(1)} %get-tuple-element.18, bf16[4,16,1,16,1024]{4,3,2,1,0:T(8,128)(2,1)S(1)} %get-tuple-element.17, bf16[4,16,1,16,2048]{4,3,2,1,0:T(8,128)(2,1)S(1)} %copy-done), kind=kLoop, calls=%fused_computation | loop fusion | flops 25165824 | bytes 16777216 | tf_op jit(solution)/shard_map/concatenate | solution.py:280
  9.4 4.4 %copy.41 = bf16[8,8,32,1024]{3,2,1,0:T(8,128)(2,1)} copy(bf16[8,8,32,1024]{3,1,2,0:T(8,128)(2,1)S(1)} %bitcast.92) | data formatting | bytes 8388608
  13.8 12.6 %shard_map.46.previous_ref = bf16[32,32,2048]{2,1,0:T(8,128)(2,1)} custom-call(f32[8,1024]{1,0:T(8,128)} %taps_ref.3, bf16[2,32,32,1024]{3,2,1,0:T(8,128)(2,1)} %bitcast.90), custom_call_target="tpu_custom_call" | custom-call | flops 67108864 | bytes 8388608 | tf_op jit(solution)/shard_map/pallas_call | solution.py:116
  26.4 5.6 %fusion.20 = (bf16[1,16,2,16,2048]{4,3,2,1,0:T(8,128)(2,1)}, bf16[1,16,2,16,2048]{4,3,2,1,0:T(8,128)(2,1)S(1)}, bf16[1,16,2,16,2048]{4,3,2,1,0:T(8,128)(2,1)}, bf16[1,16,2,16,2048]{4,3,2,1,0:T(8,128)(2,1)}) fusion(bf16[4,16,2,16,2048]{4,3,2,1,0:T(8,128)(2,1)} %maximum_maximum_fusion), kind=kLoop, calls=%fused_computation.36 | loop fusion | bytes 16777216 | tf_op jit(solution)/shard_map/slice | solution.py:311
  32.1 2.7 %copy.18.halo_ref = bf16[2,32,7,1024]{3,2,1,0:T(8,128)(2,1)} copy(bf16[2,32,7,1024]{3,1,2,0:T(8,128)(2,1)} %collective-permute-done) | data formatting | bytes 1835008 | tf_op jit(solution)/shard_map/ppermute | solution.py:18
  34.7 5.8 %shard_map.47 = bf16[32,32,2048]{2,1,0:T(8,128)(2,1)} custom-call(f32[8,1024]{1,0:T(8,128)} %taps_ref.3, bf16[2,32,7,1024]{3,2,1,0:T(8,128)(2,1)} %copy.18.halo_ref, bf16[2,32,32,1024]{3,2,1,0:T(8,128)(2,1)} %bitcast.91, bf16[32,32,2048]{2,1,0:T(8,128)(2,1)} %shard_map.46.previous_ref), custom_call_target="tpu_custom_call", output_to_operand_aliasing={{}: (3, {})} | custom-call | flops 16777216 | bytes 3145728 | tf_op jit(solution)/shard_map/pallas_call | solution.py:134
  40.5 5.5 %convolution_convert_fusion.2 = bf16[512,1024]{1,0:T(8,128)(2,1)} fusion(bf16[512,2048]{1,0:T(8,128)(2,1)S(1)} %bitcast.117, bf16[1024,2048]{1,0:T(8,128)(2,1)} %bitcast.101), kind=kOutput, calls=%fused_computation.12 | convolution fusion | flops 2148007936 | bytes 7340032 | tf_op jit(solution)/shard_map/kj,nj->kn/dot_general | solution.py:310
  46.0 6.2 %all-to-all-start.1 = ((bf16[16,32,1024]{2,1,0:T(8,128)(2,1)}), bf16[16,32,1024]{2,1,0:T(8,128)(2,1)S(1)}, u32[]{:S(2)}, u32[]{:S(2)}) async-start(bf16[16,32,1024]{2,1,0:T(8,128)(2,1)} %bitcast.14), calls=%async_computation.1 | async-start | bytes 2097152 | tf_op jit(solution)/shard_map/all_to_all | solution.py:314
  52.3 6.2 %convolution_convert_fusion.3 = bf16[512,1024]{1,0:T(8,128)(2,1)} fusion(bf16[512,2048]{1,0:T(8,128)(2,1)} %bitcast.116, bf16[1024,2048]{1,0:T(8,128)(2,1)} %bitcast.102), kind=kOutput, calls=%fused_computation.13 | convolution fusion | flops 2148007936 | bytes 7340032 | tf_op jit(solution)/shard_map/kj,nj->kn/dot_general | solution.py:310
  58.5 18.6 %all-to-all-done.1 = bf16[16,32,1024]{2,1,0:T(8,128)(2,1)S(1)} async-done(((bf16[16,32,1024]{2,1,0:T(8,128)(2,1)}), bf16[16,32,1024]{2,1,0:T(8,128)(2,1)S(1)}, u32[]{:S(2)}, u32[]{:S(2)}) %all-to-all-start.1) | async-done | bytes 1048608 | tf_op jit(solution)/shard_map/all_to_all | solution.py:314
  77.0 5.1 %all-to-all-start = ((bf16[16,32,1024]{2,1,0:T(8,128)(2,1)}), bf16[16,32,1024]{2,1,0:T(8,128)(2,1)S(1)}, u32[]{:S(2)}, u32[]{:S(2)}) async-start(bf16[16,32,1024]{2,1,0:T(8,128)(2,1)} %bitcast.7), calls=%async_computation | async-start | bytes 2097152 | tf_op jit(solution)/shard_map/all_to_all | solution.py:314
  82.1 4.3 %reshape.98 = bf16[16,2,16,32,32]{4,3,2,1,0:T(8,128)(2,1)} reshape(bf16[16,32,1024]{2,1,0:T(8,128)(2,1)S(1)} %all-to-all-done.1) | data formatting | bytes 2097152 | tf_op jit(solution)/shard_map/reshape | solution.py:315
  86.4 3.6 %fusion.1 = bf16[16,2,32,512]{3,2,0,1:T(8,128)(2,1)S(1)} fusion(bf16[16,2,16,32,32]{4,3,2,1,0:T(8,128)(2,1)} %reshape.98, s32[16,32]{1,0:T(8,128)S(1)} %multiply_add_fusion, s32[512]{0:T(512)S(1)} %copy-done.3), kind=kOutput, calls=%fused_computation.15 | convolution fusion | flops 537657344 | bytes 2101248 | tf_op jit(solution)/shard_map/gikas,gar->kisr/dot_general | solution.py:316
  90.0 0.1 copy.22
  90.2 3.6 %collective-permute-start.2 = (bf16[32,32,512]{2,1,0:T(8,128)(2,1)S(1)}, bf16[32,32,512]{2,1,0:T(8,128)(2,1)S(1)}, u32[]{:S(2)}, u32[]{:S(2)}) collective-permute-start(bf16[32,32,512]{2,1,0:T(8,128)(2,1)S(1)} %bitcast.107), channel_id=1, source_target_pairs={{0,1},{1,0},{2,3},{3,2},{4,5},{5,4},{6,7},{7,6},{8,9},{9,8},{10,11... | collective-permute-start | bytes 3145736 | tf_op jit(solution)/shard_map/ppermute | solution.py:26
  93.8 13.0 %all-to-all-done = bf16[16,32,1024]{2,1,0:T(8,128)(2,1)S(1)} async-done(((bf16[16,32,1024]{2,1,0:T(8,128)(2,1)}), bf16[16,32,1024]{2,1,0:T(8,128)(2,1)S(1)}, u32[]{:S(2)}, u32[]{:S(2)}) %all-to-all-start) | async-done | bytes 1048608 | tf_op jit(solution)/shard_map/all_to_all | solution.py:314
  106.8 4.3 %reshape.94 = bf16[16,2,16,32,32]{4,3,2,1,0:T(8,128)(2,1)} reshape(bf16[16,32,1024]{2,1,0:T(8,128)(2,1)S(1)} %all-to-all-done) | data formatting | bytes 2097152 | tf_op jit(solution)/shard_map/reshape | solution.py:315
  111.2 6.1 %collective-permute-done.2 = bf16[32,32,512]{2,1,0:T(8,128)(2,1)S(1)} collective-permute-done((bf16[32,32,512]{2,1,0:T(8,128)(2,1)S(1)}, bf16[32,32,512]{2,1,0:T(8,128)(2,1)S(1)}, u32[]{:S(2)}, u32[]{:S(2)}) %collective-permute-start.2) | collective-permute-done | bytes 1048608 | tf_op jit(solution)/shard_map/ppermute | solution.py:26
  117.3 1.5 pad_maximum_fusion.1
  118.8 7.6 %shard_map.48.refs_0_ = bf16[2,64,256,512]{3,2,1,0:T(8,128)(2,1)} custom-call(s32[1]{0:T(128)} %bitcast.block_ref, bf16[16,128,512]{2,1,0:T(8,128)(2,1)} %bitcast.93, bf16[16,128,512]{2,1,0:T(8,128)(2,1)} %bitcast.94), custom_call_target="tpu_custom_call" | custom-call | flops 1073741824 | bytes 11534336 | tf_op jit(solution)/shard_map/pallas_call | solution.py:244
  126.4 5.5 %convolution_convert_fusion = bf16[512,1024]{1,0:T(8,128)(2,1)} fusion(bf16[512,2048]{1,0:T(8,128)(2,1)S(1)} %bitcast.115, bf16[1024,2048]{1,0:T(8,128)(2,1)} %bitcast.103), kind=kOutput, calls=%fused_computation.10 | convolution fusion | flops 2148007936 | bytes 7340032 | tf_op jit(solution)/shard_map/kj,nj->kn/dot_general | solution.py:310
  131.9 6.0 %all-to-all-start.3 = ((bf16[16,32,1024]{2,1,0:T(8,128)(2,1)}), bf16[16,32,1024]{2,1,0:T(8,128)(2,1)S(1)}, u32[]{:S(2)}, u32[]{:S(2)}) async-start(bf16[16,32,1024]{2,1,0:T(8,128)(2,1)} %bitcast.27), calls=%async_computation.3 | async-start | bytes 2097152 | tf_op jit(solution)/shard_map/all_to_all | solution.py:314
  137.9 3.6 %fusion = bf16[16,2,32,512]{3,2,0,1:T(8,128)(2,1)S(1)} fusion(bf16[16,2,16,32,32]{4,3,2,1,0:T(8,128)(2,1)} %reshape.94, s32[16,32]{1,0:T(8,128)S(1)} %multiply_add_fusion, s32[512]{0:T(512)S(1)} %copy-done.3), kind=kOutput, calls=%fused_computation.14 | convolution fusion | flops 537657344 | bytes 2101248 | tf_op jit(solution)/shard_map/gikas,gar->kisr/dot_general | solution.py:316
  141.5 0.1 copy.20
  141.6 1.8 collective-permute-start.1
  143.4 23.5 %collective-permute-done.1 = bf16[32,32,512]{2,1,0:T(8,128)(2,1)S(1)} collective-permute-done((bf16[32,32,512]{2,1,0:T(8,128)(2,1)S(1)}, bf16[32,32,512]{2,1,0:T(8,128)(2,1)S(1)}, u32[]{:S(2)}, u32[]{:S(2)}) %collective-permute-start.1) | collective-permute-done | bytes 1048608 | tf_op jit(solution)/shard_map/ppermute | solution.py:26
  166.9 1.5 pad_maximum_fusion
  168.4 7.6 %shard_map.49.refs_0_ = bf16[2,64,256,512]{3,2,1,0:T(8,128)(2,1)} custom-call(s32[1]{0:T(128)} %bitcast.block_ref, bf16[16,128,512]{2,1,0:T(8,128)(2,1)} %bitcast.97, bf16[16,128,512]{2,1,0:T(8,128)(2,1)} %bitcast.98, bf16[2,64,256,512]{3,2,1,0:T(8,128)(2,1)} %shard_map.48.refs_0_), custom_call_target="tpu_custom_call", output_to_operand_aliasing={{}: (3, {})} | custom-call | flops 1073741824 | bytes 11534336 | tf_op jit(solution)/shard_map/pallas_call | solution.py:244
  176.0 5.6 %convolution_convert_fusion.1 = bf16[512,1024]{1,0:T(8,128)(2,1)} fusion(bf16[512,2048]{1,0:T(8,128)(2,1)S(1)} %bitcast.114, bf16[1024,2048]{1,0:T(8,128)(2,1)} %bitcast.104), kind=kOutput, calls=%fused_computation.11 | convolution fusion | flops 2148007936 | bytes 7340032 | tf_op jit(solution)/shard_map/kj,nj->kn/dot_general | solution.py:310
  181.6 6.0 %all-to-all-start.2 = ((bf16[16,32,1024]{2,1,0:T(8,128)(2,1)}), bf16[16,32,1024]{2,1,0:T(8,128)(2,1)S(1)}, u32[]{:S(2)}, u32[]{:S(2)}) async-start(bf16[16,32,1024]{2,1,0:T(8,128)(2,1)} %bitcast.118), calls=%async_computation.2 | async-start | bytes 2097152 | tf_op jit(solution)/shard_map/all_to_all | solution.py:314
  187.6 4.3 %reshape.106 = bf16[16,2,16,32,32]{4,3,2,1,0:T(8,128)(2,1)} reshape(bf16[16,32,1024]{2,1,0:T(8,128)(2,1)S(1)} %all-to-all-done.3) | data formatting | bytes 2097152 | tf_op jit(solution)/shard_map/reshape | solution.py:315
  191.9 3.6 %fusion.3 = bf16[16,2,32,512]{3,2,0,1:T(8,128)(2,1)S(1)} fusion(bf16[16,2,16,32,32]{4,3,2,1,0:T(8,128)(2,1)} %reshape.106, s32[16,32]{1,0:T(8,128)S(1)} %multiply_add_fusion, s32[512]{0:T(512)S(1)} %copy-done.3), kind=kOutput, calls=%fused_computation.17 | convolution fusion | flops 537657344 | bytes 2101248 | tf_op jit(solution)/shard_map/gikas,gar->kisr/dot_general | solution.py:316
  195.6 0.1 copy.26
  195.7 1.8 collective-permute-start.4
  197.5 14.8 %all-to-all-done.2 = bf16[16,32,1024]{2,1,0:T(8,128)(2,1)S(1)} async-done(((bf16[16,32,1024]{2,1,0:T(8,128)(2,1)}), bf16[16,32,1024]{2,1,0:T(8,128)(2,1)S(1)}, u32[]{:S(2)}, u32[]{:S(2)}) %all-to-all-start.2) | async-done | bytes 1048608 | tf_op jit(solution)/shard_map/all_to_all | solution.py:314
  212.3 4.3 %reshape.102 = bf16[16,2,16,32,32]{4,3,2,1,0:T(8,128)(2,1)} reshape(bf16[16,32,1024]{2,1,0:T(8,128)(2,1)S(1)} %all-to-all-done.2) | data formatting | bytes 2097152 | tf_op jit(solution)/shard_map/reshape | solution.py:315
  216.7 3.6 %fusion.2 = bf16[16,2,32,512]{3,2,0,1:T(8,128)(2,1)S(1)} fusion(bf16[16,2,16,32,32]{4,3,2,1,0:T(8,128)(2,1)} %reshape.102, s32[16,32]{1,0:T(8,128)S(1)} %multiply_add_fusion, s32[512]{0:T(512)S(1)} %copy-done.3), kind=kOutput, calls=%fused_computation.16 | convolution fusion | flops 537657344 | bytes 2101248 | tf_op jit(solution)/shard_map/gikas,gar->kisr/dot_general | solution.py:316
  220.3 0.1 copy.24
  220.4 1.8 collective-permute-start.3
  222.2 1.5 pad_maximum_fusion.3
  223.7 7.4 %shard_map.50.refs_0_ = bf16[2,64,256,512]{3,2,1,0:T(8,128)(2,1)} custom-call(s32[1]{0:T(128)} %bitcast.block_ref, bf16[16,128,512]{2,1,0:T(8,128)(2,1)} %bitcast.99, bf16[16,128,512]{2,1,0:T(8,128)(2,1)} %bitcast.100, bf16[2,64,256,512]{3,2,1,0:T(8,128)(2,1)} %shard_map.49.refs_0_), custom_call_target="tpu_custom_call", output_to_operand_aliasing={{}: (3, {})} | custom-call | flops 1073741824 | bytes 11534336 | tf_op jit(solution)/shard_map/pallas_call | solution.py:244
  231.1 15.1 %collective-permute-done.3 = bf16[32,32,512]{2,1,0:T(8,128)(2,1)} collective-permute-done((bf16[32,32,512]{2,1,0:T(8,128)(2,1)S(1)}, bf16[32,32,512]{2,1,0:T(8,128)(2,1)}, u32[]{:S(2)}, u32[]{:S(2)}) %collective-permute-start.3) | collective-permute-done | bytes 1048608 | tf_op jit(solution)/shard_map/ppermute | solution.py:26
  246.2 2.7 %pad_maximum_fusion.2 = bf16[32,64,512]{2,1,0:T(8,128)(2,1)} fusion(bf16[32,32,512]{2,1,0:T(8,128)(2,1)} %collective-permute-done.3, bf16[32,32,512]{2,1,0:T(8,128)(2,1)S(1)} %bitcast.110), kind=kLoop, calls=%fused_computation.8 | loop fusion | flops 4194304 | bytes 4194304 | tf_op jit(solution)/shard_map/concatenate | solution.py:27
  249.0 7.4 %shard_map.51 = bf16[2,64,256,512]{3,2,1,0:T(8,128)(2,1)} custom-call(s32[1]{0:T(128)} %bitcast.block_ref, bf16[16,128,512]{2,1,0:T(8,128)(2,1)} %bitcast.95, bf16[16,128,512]{2,1,0:T(8,128)(2,1)} %bitcast.96, bf16[2,64,256,512]{3,2,1,0:T(8,128)(2,1)} %shard_map.50.refs_0_), custom_call_target="tpu_custom_call", output_to_operand_aliasing={{}: (3, {})} | custom-call | flops 1073741824 | bytes 11534336 | tf_op jit(solution)/shard_map/pallas_call | solution.py:244
  (13 shorter events, 0.1 us)
Async XLA Ops:
  0.0 5.4 %copy-start = (bf16[4,16,1,16,2048]{4,3,2,1,0:T(8,128)(2,1)S(1)}, bf16[4,16,1,16,2048]{4,3,2,1,0:T(8,128)(2,1)}, u32[]{:S(2)}) copy-start(bf16[4,16,1,16,2048]{4,3,2,1,0:T(8,128)(2,1)} %constant.9) | copy-start | bytes 12582916
  4.1 28.0 %collective-permute-start = (bf16[2,32,7,1024]{3,1,2,0:T(8,128)(2,1)S(1)}, bf16[2,32,7,1024]{3,1,2,0:T(8,128)(2,1)}, u32[]{:S(2)}, u32[]{:S(2)}) collective-permute-start(bf16[2,32,7,1024]{3,1,2,0:T(8,128)(2,1)S(1)} %bitcast.119), channel_id=1, source_target_pairs={{0,1},{2,3},{4,5},{6,7},{8,9},{10,11},{12,13},{14,15},{16,17},{18,... | collective-permute-start | bytes 2752520 | tf_op jit(solution)/shard_map/ppermute | solution.py:18
  46.0 31.0 %all-to-all-start.1 = ((bf16[16,32,1024]{2,1,0:T(8,128)(2,1)}), bf16[16,32,1024]{2,1,0:T(8,128)(2,1)S(1)}, u32[]{:S(2)}, u32[]{:S(2)}) async-start(bf16[16,32,1024]{2,1,0:T(8,128)(2,1)} %bitcast.14), calls=%async_computation.1 | async-start | bytes 2097152 | tf_op jit(solution)/shard_map/all_to_all | solution.py:314
  58.5 27.9 %copy-start.3 = (s32[512]{0:T(512)S(1)}, s32[512]{0:T(512)}, u32[]{:S(2)}) copy-start(s32[512]{0:T(512)} %param.6) | copy-start | bytes 6148
  77.0 29.8 %all-to-all-start = ((bf16[16,32,1024]{2,1,0:T(8,128)(2,1)}), bf16[16,32,1024]{2,1,0:T(8,128)(2,1)S(1)}, u32[]{:S(2)}, u32[]{:S(2)}) async-start(bf16[16,32,1024]{2,1,0:T(8,128)(2,1)} %bitcast.7), calls=%async_computation | async-start | bytes 2097152 | tf_op jit(solution)/shard_map/all_to_all | solution.py:314
  90.2 27.1 %collective-permute-start.2 = (bf16[32,32,512]{2,1,0:T(8,128)(2,1)S(1)}, bf16[32,32,512]{2,1,0:T(8,128)(2,1)S(1)}, u32[]{:S(2)}, u32[]{:S(2)}) collective-permute-start(bf16[32,32,512]{2,1,0:T(8,128)(2,1)S(1)} %bitcast.107), channel_id=1, source_target_pairs={{0,1},{1,0},{2,3},{3,2},{4,5},{5,4},{6,7},{7,6},{8,9},{9,8},{10,11... | collective-permute-start | bytes 3145736 | tf_op jit(solution)/shard_map/ppermute | solution.py:26
  118.8 7.6 %copy-start.2 = (bf16[1,16,2,16,2048]{4,3,2,1,0:T(8,128)(2,1)S(1)}, bf16[1,16,2,16,2048]{4,3,2,1,0:T(8,128)(2,1)}, u32[]{:S(2)}) copy-start(bf16[1,16,2,16,2048]{4,3,2,1,0:T(8,128)(2,1)} %get-tuple-element.13) | copy-start | bytes 6291460
  131.9 49.7 %all-to-all-start.3 = ((bf16[16,32,1024]{2,1,0:T(8,128)(2,1)}), bf16[16,32,1024]{2,1,0:T(8,128)(2,1)S(1)}, u32[]{:S(2)}, u32[]{:S(2)}) async-start(bf16[16,32,1024]{2,1,0:T(8,128)(2,1)} %bitcast.27), calls=%async_computation.3 | async-start | bytes 2097152 | tf_op jit(solution)/shard_map/all_to_all | solution.py:314
  141.6 25.3 %collective-permute-start.1 = (bf16[32,32,512]{2,1,0:T(8,128)(2,1)S(1)}, bf16[32,32,512]{2,1,0:T(8,128)(2,1)S(1)}, u32[]{:S(2)}, u32[]{:S(2)}) collective-permute-start(bf16[32,32,512]{2,1,0:T(8,128)(2,1)S(1)} %bitcast.111), channel_id=1, source_target_pairs={{0,1},{1,0},{2,3},{3,2},{4,5},{5,4},{6,7},{7,6},{8,9},{9,8},{10,11... | collective-permute-start | bytes 3145736 | tf_op jit(solution)/shard_map/ppermute | solution.py:26
  168.4 7.6 %copy-start.1 = (bf16[1,16,2,16,2048]{4,3,2,1,0:T(8,128)(2,1)S(1)}, bf16[1,16,2,16,2048]{4,3,2,1,0:T(8,128)(2,1)}, u32[]{:S(2)}) copy-start(bf16[1,16,2,16,2048]{4,3,2,1,0:T(8,128)(2,1)} %get-tuple-element.16) | copy-start | bytes 6291460
  181.6 30.7 %all-to-all-start.2 = ((bf16[16,32,1024]{2,1,0:T(8,128)(2,1)}), bf16[16,32,1024]{2,1,0:T(8,128)(2,1)S(1)}, u32[]{:S(2)}, u32[]{:S(2)}) async-start(bf16[16,32,1024]{2,1,0:T(8,128)(2,1)} %bitcast.118), calls=%async_computation.2 | async-start | bytes 2097152 | tf_op jit(solution)/shard_map/all_to_all | solution.py:314
  195.7 26.5 %collective-permute-start.4 = (bf16[32,32,512]{2,1,0:T(8,128)(2,1)S(1)}, bf16[32,32,512]{2,1,0:T(8,128)(2,1)S(1)}, u32[]{:S(2)}, u32[]{:S(2)}) collective-permute-start(bf16[32,32,512]{2,1,0:T(8,128)(2,1)S(1)} %bitcast.105), channel_id=1, source_target_pairs={{0,1},{1,0},{2,3},{3,2},{4,5},{5,4},{6,7},{7,6},{8,9},{9,8},{10,11... | collective-permute-start | bytes 3145736 | tf_op jit(solution)/shard_map/ppermute | solution.py:26
  220.4 25.8 %collective-permute-start.3 = (bf16[32,32,512]{2,1,0:T(8,128)(2,1)S(1)}, bf16[32,32,512]{2,1,0:T(8,128)(2,1)}, u32[]{:S(2)}, u32[]{:S(2)}) collective-permute-start(bf16[32,32,512]{2,1,0:T(8,128)(2,1)S(1)} %bitcast.109), channel_id=1, source_target_pairs={{0,1},{1,0},{2,3},{3,2},{4,5},{5,4},{6,7},{7,6},{8,9},{9,8},{10,11... | collective-permute-start | bytes 3145736 | tf_op jit(solution)/shard_map/ppermute | solution.py:26

commit v13 on v9

--- a/solution.py
+++ b/solution.py
@@ -262,6 +262,7 @@
 
     earlier = samples[:, :, (spectra_local - (tap_count - 1)) * channels :].astype(jnp.bfloat16)
     earlier = earlier.reshape(2, stations_local, tap_count - 1, channels)
+    earlier, samples = lax.optimization_barrier((earlier, samples))
     frames = samples.astype(jnp.bfloat16).reshape(2, stations_local, spectra_local, channels)
     earlier = passed_along(earlier, "blk", 1)
     filtered = filter_frames(fir_taps, earlier, frames)

time: 235 us -> 236 us (level)
  waiting for transfers between devices: 79.1 us -> 70 us
  starting transfers between devices: 24.9 us -> 31.3 us
    ppermute x4, starting transfers between devices: 1.21 us -> 8.54 us  [gathered_along(): parts.append(lax.ppermute(value, axis, pairs))]
    ppermute x1, waiting for transfers between devices: 3.92 us -> 0.11 us  [passed_along(): lax.ppermute(value, axis, [(source, source + steps) for source in range(i...]
    convert_element_type x0 -> x1, other arithmetic: none -> 3.8 us  [per_device(): samples.astype(jnp.bfloat16)]
    all_to_all x4, waiting for transfers between devices: 56.1 us -> 52.6 us  [per_device(): lax.all_to_all(spectra, 'stn', split_axis=0, concat_axis=0, tiled=True)]
  transfers between devices with their start and end apart: 9 -> 9, of which waited for: 8 -> 7; matrix products, arithmetic and copies ran while one was open for 27% -> 29% of each run, Pallas kernels for 16% -> 16%
where the time goes in v13:
time: 236 us; the launch traced here: 234 us
  waiting for transfers between devices  70 us (30%)
  Pallas kernels  50.3 us (21%)
  matrix products  41.4 us (18%)
  starting transfers between devices  31.3 us (13%)
  local copies, waits for them, and re-layouts  25.7 us (11%)
  other arithmetic  15.2 us (6%)
    all_to_all x4, waiting for transfers between devices, per_device(): lax.all_to_all(spectra, 'stn', split_axis=0, concat_axis=0, tiled=True)  52.6 us
    pallas_call x4, Pallas kernels, correlate_rows_chunk(): pl.pallas_call(correlate_rows_kernel, grid_spec=grid_spec, out_shape=jax....  29.9 us
    dot_general x4, matrix products, per_device(): jnp.einsum('kj,nj->kn', weights[chunk], source, preferred_element_type=jn...  27.1 us
    all_to_all x4, starting transfers between devices, per_device(): lax.all_to_all(spectra, 'stn', split_axis=0, concat_axis=0, tiled=True)  21.5 us
    reshape x4, local copies, waits for them, and re-layouts, per_device(): turned = turned.reshape(groups, width, 2, stations_local, spectra_local)  17.6 us
    ppermute x4, waiting for transfers between devices, gathered_along(): parts.append(lax.ppermute(value, axis, pairs))  17.2 us
    pallas_call x1, Pallas kernels, filter_frames(): pl.pallas_call(fir_kernel, grid=(stations_local // group,), in_specs=[pl....  14.3 us
    dot_general x4, matrix products, per_device(): jnp.einsum('gkias,gar->kisr', turned, selector, preferred_element_type=jn...  14.2 us
  transfers between devices with their start and end apart: 9, of which 7 were waited for; matrix products, arithmetic and copies ran while one was open for 29% of the time, Pallas kernels for 16%

profile of v13, /device:TPU:14, one launch (start us, length us, event | category | flops | bytes accessed | tf_op | source)
XLA Modules:
  0.0 234.1 jit_solution(1471408942226292806)
XLA Ops:
  0.0 1.6 slice_convert_fusion
  1.6 1.2 reshape.77
  2.8 0.6 copy.19
  3.3 1.3 collective-permute-start
  4.6 3.8 %convert_element_type.41 = bf16[2,32,32768]{2,1,0:T(8,128)(2,1)S(1)} convert(s32[2,32,32768]{2,1,0:T(8,128)} %param.4) | non-fusion elementwise | flops 2097152 | bytes 12582912 | tf_op jit(solution)/shard_map/convert_element_type | solution.py:266
  8.4 4.5 %copy.38 = bf16[8,8,32,1024]{3,2,1,0:T(8,128)(2,1)} copy(bf16[8,8,32,1024]{3,1,2,0:T(8,128)(2,1)S(1)} %bitcast.71) | data formatting | bytes 8388608
  12.9 14.3 %shard_map.46.previous_ref = bf16[2,32,32,2048]{3,2,1,0:T(8,128)(2,1)} custom-call(f32[8,1024]{1,0:T(8,128)} %taps_ref.3, bf16[2,32,32,1024]{3,2,1,0:T(8,128)(2,1)} %bitcast.57), custom_call_target="tpu_custom_call" | custom-call | flops 67108864 | bytes 12582912 | tf_op jit(solution)/shard_map/pallas_call | solution.py:110
  27.2 0.1 collective-permute-done
  27.3 1.6 copy.20.halo_ref
  28.9 6.1 %shard_map.47 = bf16[2,32,32,2048]{3,2,1,0:T(8,128)(2,1)} custom-call(f32[8,1024]{1,0:T(8,128)} %taps_ref.3, bf16[2,32,7,1024]{3,2,1,0:T(8,128)(2,1)} %copy.20.halo_ref, bf16[2,32,32,1024]{3,2,1,0:T(8,128)(2,1)} %bitcast.58, bf16[2,32,32,2048]{3,2,1,0:T(8,128)(2,1)} %shard_map.46.previous_ref), custom_call_target="tpu_custom_call", output_to_operand_aliasing={{}: (3, {})} | custom-call | flops 16777216 | bytes 4194304 | tf_op jit(solution)/shard_map/pallas_call | solution.py:127
  35.0 6.8 %convolution_convert_fusion.2 = bf16[2048,256]{0,1:T(8,128)(2,1)} fusion(bf16[2048,2048]{1,0:T(8,128)(2,1)} %bitcast.59, bf16[256,2048]{1,0:T(8,128)(2,1)S(1)} %copy-done.4), kind=kOutput, calls=%fused_computation.10 | convolution fusion | flops 2148007936 | bytes 10485760 | tf_op jit(solution)/shard_map/kj,nj->kn/dot_general | solution.py:301
  41.8 6.2 %all-to-all-start.1 = ((bf16[16,16,2048]{2,1,0:T(8,128)(2,1)}), bf16[16,16,2048]{2,1,0:T(8,128)(2,1)S(1)}, u32[]{:S(2)}, u32[]{:S(2)}) async-start(bf16[16,16,2048]{2,1,0:T(8,128)(2,1)} %bitcast.10), calls=%async_computation.1 | async-start | bytes 2097152 | tf_op jit(solution)/shard_map/all_to_all | solution.py:305
  48.1 6.8 %convolution_convert_fusion.3 = bf16[2048,256]{0,1:T(8,128)(2,1)} fusion(bf16[2048,2048]{1,0:T(8,128)(2,1)} %bitcast.60, bf16[256,2048]{1,0:T(8,128)(2,1)S(1)} %copy-done.3), kind=kOutput, calls=%fused_computation.11 | convolution fusion | flops 2148007936 | bytes 10485760 | tf_op jit(solution)/shard_map/kj,nj->kn/dot_general | solution.py:301
  54.9 17.9 %all-to-all-done.1 = bf16[16,16,2048]{2,1,0:T(8,128)(2,1)S(1)} async-done(((bf16[16,16,2048]{2,1,0:T(8,128)(2,1)}), bf16[16,16,2048]{2,1,0:T(8,128)(2,1)S(1)}, u32[]{:S(2)}, u32[]{:S(2)}) %all-to-all-start.1) | async-done | bytes 1048608 | tf_op jit(solution)/shard_map/all_to_all | solution.py:305
  72.8 5.1 %all-to-all-start = ((bf16[16,16,2048]{2,1,0:T(8,128)(2,1)}), bf16[16,16,2048]{2,1,0:T(8,128)(2,1)S(1)}, u32[]{:S(2)}, u32[]{:S(2)}) async-start(bf16[16,16,2048]{2,1,0:T(8,128)(2,1)} %bitcast.3), calls=%async_computation | async-start | bytes 2097152 | tf_op jit(solution)/shard_map/all_to_all | solution.py:305
  77.9 4.4 %reshape.85 = bf16[16,16,2,32,32]{4,3,2,1,0:T(8,128)(2,1)} reshape(bf16[16,16,2048]{2,1,0:T(8,128)(2,1)S(1)} %all-to-all-done.1) | data formatting | bytes 2097152 | tf_op jit(solution)/shard_map/reshape | solution.py:306
  82.3 3.6 %fusion.4 = bf16[16,2,32,512,1]{3,2,0,1,4:T(8,128)(2,1)S(1)} fusion(bf16[16,16,2,32,32]{4,3,2,1,0:T(8,128)(2,1)} %reshape.85, s32[16,32]{1,0:T(8,128)S(1)} %multiply_add_fusion, s32[512]{0:T(512)S(1)} %copy-done), kind=kOutput, calls=%fused_computation.4 | convolution fusion | flops 537133056 | bytes 2101248 | tf_op jit(solution)/shard_map/gkias,gar->kisr/dot_general | solution.py:307
  85.8 0.1 copy.53
  85.9 2.7 %collective-permute-start.2 = (bf16[32,32,512]{2,1,0:T(8,128)(2,1)S(1)}, bf16[32,32,512]{2,1,0:T(8,128)(2,1)}, u32[]{:S(2)}, u32[]{:S(2)}) collective-permute-start(bf16[32,32,512]{2,1,0:T(8,128)(2,1)S(1)} %bitcast.72), channel_id=1, source_target_pairs={{0,1},{1,0},{2,3},{3,2},{4,5},{5,4},{6,7},{7,6},{8,9},{9,8},{10,11... | collective-permute-start | bytes 3145736 | tf_op jit(solution)/shard_map/ppermute | solution.py:26
  88.6 14.0 %all-to-all-done = bf16[16,16,2048]{2,1,0:T(8,128)(2,1)S(1)} async-done(((bf16[16,16,2048]{2,1,0:T(8,128)(2,1)}), bf16[16,16,2048]{2,1,0:T(8,128)(2,1)S(1)}, u32[]{:S(2)}, u32[]{:S(2)}) %all-to-all-start) | async-done | bytes 1048608 | tf_op jit(solution)/shard_map/all_to_all | solution.py:305
  102.6 4.4 %reshape.81 = bf16[16,16,2,32,32]{4,3,2,1,0:T(8,128)(2,1)} reshape(bf16[16,16,2048]{2,1,0:T(8,128)(2,1)S(1)} %all-to-all-done) | data formatting | bytes 2097152 | tf_op jit(solution)/shard_map/reshape | solution.py:306
  107.0 3.6 %fusion.6 = bf16[16,2,32,512,1]{3,2,0,1,4:T(8,128)(2,1)S(1)} fusion(bf16[16,16,2,32,32]{4,3,2,1,0:T(8,128)(2,1)} %reshape.81, s32[16,32]{1,0:T(8,128)S(1)} %multiply_add_fusion, s32[512]{0:T(512)S(1)} %copy-done), kind=kOutput, calls=%fused_computation.6 | convolution fusion | flops 537133056 | bytes 2101248 | tf_op jit(solution)/shard_map/gkias,gar->kisr/dot_general | solution.py:307
  110.5 0.1 copy.54
  110.6 2.7 %collective-permute-start.1 = (bf16[32,32,512]{2,1,0:T(8,128)(2,1)S(1)}, bf16[32,32,512]{2,1,0:T(8,128)(2,1)}, u32[]{:S(2)}, u32[]{:S(2)}) collective-permute-start(bf16[32,32,512]{2,1,0:T(8,128)(2,1)S(1)} %bitcast.76), channel_id=1, source_target_pairs={{0,1},{1,0},{2,3},{3,2},{4,5},{5,4},{6,7},{7,6},{8,9},{9,8},{10,11... | collective-permute-start | bytes 3145736 | tf_op jit(solution)/shard_map/ppermute | solution.py:26
  113.3 2.8 %pad_maximum_fusion.1 = bf16[32,64,512]{2,1,0:T(8,128)(2,1)} fusion(bf16[32,32,512]{2,1,0:T(8,128)(2,1)} %collective-permute-done.2, bf16[32,32,512]{2,1,0:T(8,128)(2,1)S(1)} %bitcast.73), kind=kLoop, calls=%fused_computation.13 | loop fusion | flops 4194304 | bytes 4194304 | tf_op jit(solution)/shard_map/concatenate | solution.py:27
  116.1 7.5 %shard_map.48.refs_0_ = bf16[2,64,256,512]{3,2,1,0:T(8,128)(2,1)} custom-call(s32[1]{0:T(128)} %bitcast.block_ref, bf16[16,128,512]{2,1,0:T(8,128)(2,1)} %bitcast.63, bf16[16,128,512]{2,1,0:T(8,128)(2,1)} %bitcast.64), custom_call_target="tpu_custom_call" | custom-call | flops 1073741824 | bytes 11534336 | tf_op jit(solution)/shard_map/pallas_call | solution.py:237
  123.6 6.7 %convolution_convert_fusion = bf16[2048,256]{0,1:T(8,128)(2,1)} fusion(bf16[2048,2048]{1,0:T(8,128)(2,1)} %bitcast.61, bf16[256,2048]{1,0:T(8,128)(2,1)S(1)} %copy-done.2), kind=kOutput, calls=%fused_computation.8 | convolution fusion | flops 2148007936 | bytes 10485760 | tf_op jit(solution)/shard_map/kj,nj->kn/dot_general | solution.py:301
  130.3 5.1 %all-to-all-start.3 = ((bf16[16,16,2048]{2,1,0:T(8,128)(2,1)}), bf16[16,16,2048]{2,1,0:T(8,128)(2,1)S(1)}, u32[]{:S(2)}, u32[]{:S(2)}) async-start(bf16[16,16,2048]{2,1,0:T(8,128)(2,1)} %bitcast.21), calls=%async_computation.3 | async-start | bytes 2097152 | tf_op jit(solution)/shard_map/all_to_all | solution.py:305
  135.4 2.0 collective-permute-done.1
  137.4 2.8 %pad_maximum_fusion = bf16[32,64,512]{2,1,0:T(8,128)(2,1)} fusion(bf16[32,32,512]{2,1,0:T(8,128)(2,1)} %collective-permute-done.1, bf16[32,32,512]{2,1,0:T(8,128)(2,1)S(1)} %bitcast.77), kind=kLoop, calls=%fused_computation.12 | loop fusion | flops 4194304 | bytes 4194304 | tf_op jit(solution)/shard_map/concatenate | solution.py:27
  140.2 7.5 %shard_map.49.refs_0_ = bf16[2,64,256,512]{3,2,1,0:T(8,128)(2,1)} custom-call(s32[1]{0:T(128)} %bitcast.block_ref, bf16[16,128,512]{2,1,0:T(8,128)(2,1)} %bitcast.67, bf16[16,128,512]{2,1,0:T(8,128)(2,1)} %bitcast.68, bf16[2,64,256,512]{3,2,1,0:T(8,128)(2,1)} %shard_map.48.refs_0_), custom_call_target="tpu_custom_call", output_to_operand_aliasing={{}: (3, {})} | custom-call | flops 1073741824 | bytes 11534336 | tf_op jit(solution)/shard_map/pallas_call | solution.py:237
  147.7 6.8 %convolution_convert_fusion.1 = bf16[2048,256]{0,1:T(8,128)(2,1)} fusion(bf16[2048,2048]{1,0:T(8,128)(2,1)} %bitcast.62, bf16[256,2048]{1,0:T(8,128)(2,1)S(1)} %copy-done.1), kind=kOutput, calls=%fused_computation.9 | convolution fusion | flops 2148007936 | bytes 10485760 | tf_op jit(solution)/shard_map/kj,nj->kn/dot_general | solution.py:301
  154.5 5.6 %all-to-all-done.3 = bf16[16,16,2048]{2,1,0:T(8,128)(2,1)S(1)} async-done(((bf16[16,16,2048]{2,1,0:T(8,128)(2,1)}), bf16[16,16,2048]{2,1,0:T(8,128)(2,1)S(1)}, u32[]{:S(2)}, u32[]{:S(2)}) %all-to-all-start.3) | async-done | bytes 1048608 | tf_op jit(solution)/shard_map/all_to_all | solution.py:305
  160.1 5.1 %all-to-all-start.2 = ((bf16[16,16,2048]{2,1,0:T(8,128)(2,1)}), bf16[16,16,2048]{2,1,0:T(8,128)(2,1)S(1)}, u32[]{:S(2)}, u32[]{:S(2)}) async-start(bf16[16,16,2048]{2,1,0:T(8,128)(2,1)} %bitcast.16), calls=%async_computation.2 | async-start | bytes 2097152 | tf_op jit(solution)/shard_map/all_to_all | solution.py:305
  165.2 4.4 %reshape.93 = bf16[16,16,2,32,32]{4,3,2,1,0:T(8,128)(2,1)} reshape(bf16[16,16,2048]{2,1,0:T(8,128)(2,1)S(1)} %all-to-all-done.3) | data formatting | bytes 2097152 | tf_op jit(solution)/shard_map/reshape | solution.py:306
  169.7 3.6 %fusion = bf16[16,2,32,512,1]{3,2,0,1,4:T(8,128)(2,1)S(1)} fusion(bf16[16,16,2,32,32]{4,3,2,1,0:T(8,128)(2,1)} %reshape.93, s32[16,32]{1,0:T(8,128)S(1)} %multiply_add_fusion, s32[512]{0:T(512)S(1)} %copy-done), kind=kOutput, calls=%fused_computation | convolution fusion | flops 537133056 | bytes 2101248 | tf_op jit(solution)/shard_map/gkias,gar->kisr/dot_general | solution.py:307
  173.2 0.1 copy.51
  173.3 1.6 collective-permute-start.4
  174.9 15.0 %all-to-all-done.2 = bf16[16,16,2048]{2,1,0:T(8,128)(2,1)S(1)} async-done(((bf16[16,16,2048]{2,1,0:T(8,128)(2,1)}), bf16[16,16,2048]{2,1,0:T(8,128)(2,1)S(1)}, u32[]{:S(2)}, u32[]{:S(2)}) %all-to-all-start.2) | async-done | bytes 1048608 | tf_op jit(solution)/shard_map/all_to_all | solution.py:305
  190.0 4.4 %reshape.89 = bf16[16,16,2,32,32]{4,3,2,1,0:T(8,128)(2,1)} reshape(bf16[16,16,2048]{2,1,0:T(8,128)(2,1)S(1)} %all-to-all-done.2) | data formatting | bytes 2097152 | tf_op jit(solution)/shard_map/reshape | solution.py:306
  194.4 3.6 %fusion.2 = bf16[16,2,32,512,1]{3,2,0,1,4:T(8,128)(2,1)S(1)} fusion(bf16[16,16,2,32,32]{4,3,2,1,0:T(8,128)(2,1)} %reshape.89, s32[16,32]{1,0:T(8,128)S(1)} %multiply_add_fusion, s32[512]{0:T(512)S(1)} %copy-done), kind=kOutput, calls=%fused_computation.2 | convolution fusion | flops 537133056 | bytes 2101248 | tf_op jit(solution)/shard_map/gkias,gar->kisr/dot_general | solution.py:307
  197.9 0.1 copy.52
  198.0 1.6 collective-permute-start.3
  199.6 1.5 pad_maximum_fusion.3
  201.2 7.4 %shard_map.50.refs_0_ = bf16[2,64,256,512]{3,2,1,0:T(8,128)(2,1)} custom-call(s32[1]{0:T(128)} %bitcast.block_ref, bf16[16,128,512]{2,1,0:T(8,128)(2,1)} %bitcast.69, bf16[16,128,512]{2,1,0:T(8,128)(2,1)} %bitcast.70, bf16[2,64,256,512]{3,2,1,0:T(8,128)(2,1)} %shard_map.49.refs_0_), custom_call_target="tpu_custom_call", output_to_operand_aliasing={{}: (3, {})} | custom-call | flops 1073741824 | bytes 11534336 | tf_op jit(solution)/shard_map/pallas_call | solution.py:237
  208.6 15.3 %collective-permute-done.3 = bf16[32,32,512]{2,1,0:T(8,128)(2,1)} collective-permute-done((bf16[32,32,512]{2,1,0:T(8,128)(2,1)S(1)}, bf16[32,32,512]{2,1,0:T(8,128)(2,1)}, u32[]{:S(2)}, u32[]{:S(2)}) %collective-permute-start.3) | collective-permute-done | bytes 1048608 | tf_op jit(solution)/shard_map/ppermute | solution.py:26
  223.9 2.8 %pad_maximum_fusion.2 = bf16[32,64,512]{2,1,0:T(8,128)(2,1)} fusion(bf16[32,32,512]{2,1,0:T(8,128)(2,1)} %collective-permute-done.3, bf16[32,32,512]{2,1,0:T(8,128)(2,1)S(1)} %bitcast.79), kind=kLoop, calls=%fused_computation.14 | loop fusion | flops 4194304 | bytes 4194304 | tf_op jit(solution)/shard_map/concatenate | solution.py:27
  226.6 7.4 %shard_map.51 = bf16[2,64,256,512]{3,2,1,0:T(8,128)(2,1)} custom-call(s32[1]{0:T(128)} %bitcast.block_ref, bf16[16,128,512]{2,1,0:T(8,128)(2,1)} %bitcast.65, bf16[16,128,512]{2,1,0:T(8,128)(2,1)} %bitcast.66, bf16[2,64,256,512]{3,2,1,0:T(8,128)(2,1)} %shard_map.50.refs_0_), custom_call_target="tpu_custom_call", output_to_operand_aliasing={{}: (3, {})} | custom-call | flops 1073741824 | bytes 11534336 | tf_op jit(solution)/shard_map/pallas_call | solution.py:237
  (13 shorter events, 0.0 us)
Async XLA Ops:
  3.3 24.0 %collective-permute-start = (bf16[2,32,7,1024]{3,1,2,0:T(8,128)(2,1)S(1)}, bf16[2,32,7,1024]{3,1,2,0:T(8,128)(2,1)S(1)}, u32[]{:S(2)}, u32[]{:S(2)}) collective-permute-start(bf16[2,32,7,1024]{3,1,2,0:T(8,128)(2,1)S(1)} %copy.19), channel_id=1, source_target_pairs={{0,1},{2,3},{4,5},{6,7},{8,9},{10,11},{12,13},{14,15},{16,17},{18,... | collective-permute-start | bytes 2752520 | tf_op jit(solution)/shard_map/ppermute | solution.py:18
  28.9 6.1 %copy-start.4 = (bf16[256,2048]{1,0:T(8,128)(2,1)S(1)}, bf16[256,2048]{1,0:T(8,128)(2,1)}, u32[]{:S(2)}) copy-start(bf16[256,2048]{1,0:T(8,128)(2,1)} %constant.12) | copy-start | bytes 3145732
  35.0 13.0 %copy-start.3 = (bf16[256,2048]{1,0:T(8,128)(2,1)S(1)}, bf16[256,2048]{1,0:T(8,128)(2,1)}, u32[]{:S(2)}) copy-start(bf16[256,2048]{1,0:T(8,128)(2,1)} %constant.10) | copy-start | bytes 3145732
  41.8 31.0 %all-to-all-start.1 = ((bf16[16,16,2048]{2,1,0:T(8,128)(2,1)}), bf16[16,16,2048]{2,1,0:T(8,128)(2,1)S(1)}, u32[]{:S(2)}, u32[]{:S(2)}) async-start(bf16[16,16,2048]{2,1,0:T(8,128)(2,1)} %bitcast.10), calls=%async_computation.1 | async-start | bytes 2097152 | tf_op jit(solution)/shard_map/all_to_all | solution.py:305
  54.9 27.4 %copy-start = (s32[512]{0:T(512)S(1)}, s32[512]{0:T(512)}, u32[]{:S(2)}) copy-start(s32[512]{0:T(512)} %param.6) | copy-start | bytes 6148
  72.8 29.8 %all-to-all-start = ((bf16[16,16,2048]{2,1,0:T(8,128)(2,1)}), bf16[16,16,2048]{2,1,0:T(8,128)(2,1)S(1)}, u32[]{:S(2)}, u32[]{:S(2)}) async-start(bf16[16,16,2048]{2,1,0:T(8,128)(2,1)} %bitcast.3), calls=%async_computation | async-start | bytes 2097152 | tf_op jit(solution)/shard_map/all_to_all | solution.py:305
  85.9 27.4 %collective-permute-start.2 = (bf16[32,32,512]{2,1,0:T(8,128)(2,1)S(1)}, bf16[32,32,512]{2,1,0:T(8,128)(2,1)}, u32[]{:S(2)}, u32[]{:S(2)}) collective-permute-start(bf16[32,32,512]{2,1,0:T(8,128)(2,1)S(1)} %bitcast.72), channel_id=1, source_target_pairs={{0,1},{1,0},{2,3},{3,2},{4,5},{5,4},{6,7},{7,6},{8,9},{9,8},{10,11... | collective-permute-start | bytes 3145736 | tf_op jit(solution)/shard_map/ppermute | solution.py:26
  110.6 26.8 %collective-permute-start.1 = (bf16[32,32,512]{2,1,0:T(8,128)(2,1)S(1)}, bf16[32,32,512]{2,1,0:T(8,128)(2,1)}, u32[]{:S(2)}, u32[]{:S(2)}) collective-permute-start(bf16[32,32,512]{2,1,0:T(8,128)(2,1)S(1)} %bitcast.76), channel_id=1, source_target_pairs={{0,1},{1,0},{2,3},{3,2},{4,5},{5,4},{6,7},{7,6},{8,9},{9,8},{10,11... | collective-permute-start | bytes 3145736 | tf_op jit(solution)/shard_map/ppermute | solution.py:26
  116.1 7.5 %copy-start.2 = (bf16[256,2048]{1,0:T(8,128)(2,1)S(1)}, bf16[256,2048]{1,0:T(8,128)(2,1)}, u32[]{:S(2)}) copy-start(bf16[256,2048]{1,0:T(8,128)(2,1)} %constant.16) | copy-start | bytes 3145732
  130.3 29.8 %all-to-all-start.3 = ((bf16[16,16,2048]{2,1,0:T(8,128)(2,1)}), bf16[16,16,2048]{2,1,0:T(8,128)(2,1)S(1)}, u32[]{:S(2)}, u32[]{:S(2)}) async-start(bf16[16,16,2048]{2,1,0:T(8,128)(2,1)} %bitcast.21), calls=%async_computation.3 | async-start | bytes 2097152 | tf_op jit(solution)/shard_map/all_to_all | solution.py:305
  140.2 7.5 %copy-start.1 = (bf16[256,2048]{1,0:T(8,128)(2,1)S(1)}, bf16[256,2048]{1,0:T(8,128)(2,1)}, u32[]{:S(2)}) copy-start(bf16[256,2048]{1,0:T(8,128)(2,1)} %constant.14) | copy-start | bytes 3145732
  160.1 29.8 %all-to-all-start.2 = ((bf16[16,16,2048]{2,1,0:T(8,128)(2,1)}), bf16[16,16,2048]{2,1,0:T(8,128)(2,1)S(1)}, u32[]{:S(2)}, u32[]{:S(2)}) async-start(bf16[16,16,2048]{2,1,0:T(8,128)(2,1)} %bitcast.16), calls=%async_computation.2 | async-start | bytes 2097152 | tf_op jit(solution)/shard_map/all_to_all | solution.py:305
  173.3 26.3 %collective-permute-start.4 = (bf16[32,32,512]{2,1,0:T(8,128)(2,1)S(1)}, bf16[32,32,512]{2,1,0:T(8,128)(2,1)S(1)}, u32[]{:S(2)}, u32[]{:S(2)}) collective-permute-start(bf16[32,32,512]{2,1,0:T(8,128)(2,1)S(1)} %bitcast.74), channel_id=1, source_target_pairs={{0,1},{1,0},{2,3},{3,2},{4,5},{5,4},{6,7},{7,6},{8,9},{9,8},{10,11... | collective-permute-start | bytes 3145736 | tf_op jit(solution)/shard_map/ppermute | solution.py:26
  198.0 25.8 %collective-permute-start.3 = (bf16[32,32,512]{2,1,0:T(8,128)(2,1)S(1)}, bf16[32,32,512]{2,1,0:T(8,128)(2,1)}, u32[]{:S(2)}, u32[]{:S(2)}) collective-permute-start(bf16[32,32,512]{2,1,0:T(8,128)(2,1)S(1)} %bitcast.78), channel_id=1, source_target_pairs={{0,1},{1,0},{2,3},{3,2},{4,5},{5,4},{6,7},{7,6},{8,9},{9,8},{10,11... | collective-permute-start | bytes 3145736 | tf_op jit(solution)/shard_map/ppermute | solution.py:26

commit v14 on v9

--- a/solution.py
+++ b/solution.py
@@ -215,7 +215,7 @@
 
 def correlate_rows_chunk(right, block, row_count, previous, offset, local_channels):
     width, depth, stations = right.shape
-    step = 4 if width % 4 == 0 and offset % 4 == 0 else 1
+    step = 8 if width % 8 == 0 and offset % 8 == 0 else 1
     in_specs = [
         pl.BlockSpec((step, depth, row_count), lambda k, b: (k, 0, b[0])),
         pl.BlockSpec((step, depth, stations), lambda k, b: (k, 0, 0)),

time: 235 us -> 234 us (level)
  transfers between devices with their start and end apart: 9 -> 9, of which waited for: 8 -> 8; matrix products, arithmetic and copies ran while one was open for 27% -> 27% of each run, Pallas kernels for 16% -> 15%
where the time goes in v14:
time: 234 us; the launch traced here: 233 us
  waiting for transfers between devices  79.8 us (34%)
  Pallas kernels  49 us (21%)
  matrix products  41.4 us (18%)
  starting transfers between devices  25 us (11%)
  local copies, waits for them, and re-layouts  24.1 us (10%)
  other arithmetic  13.6 us (6%)
    all_to_all x4, waiting for transfers between devices, per_device(): lax.all_to_all(spectra, 'stn', split_axis=0, concat_axis=0, tiled=True)  56 us
    pallas_call x4, Pallas kernels, correlate_rows_chunk(): pl.pallas_call(correlate_rows_kernel, grid_spec=grid_spec, out_shape=jax....  28.6 us
    dot_general x4, matrix products, per_device(): jnp.einsum('kj,nj->kn', weights[chunk], source, preferred_element_type=jn...  27.1 us
    all_to_all x4, starting transfers between devices, per_device(): lax.all_to_all(spectra, 'stn', split_axis=0, concat_axis=0, tiled=True)  22.4 us
    ppermute x4, waiting for transfers between devices, gathered_along(): parts.append(lax.ppermute(value, axis, pairs))  19.8 us
    reshape x4, local copies, waits for them, and re-layouts, per_device(): turned = turned.reshape(groups, width, 2, stations_local, spectra_local)  17.6 us
    pallas_call x1, Pallas kernels, filter_frames(): pl.pallas_call(fir_kernel, grid=(stations_local // group,), in_specs=[pl....  14.3 us
    dot_general x4, matrix products, per_device(): jnp.einsum('gkias,gar->kisr', turned, selector, preferred_element_type=jn...  14.2 us
  transfers between devices with their start and end apart: 9, of which 8 were waited for; matrix products, arithmetic and copies ran while one was open for 27% of the time, Pallas kernels for 15%

profile of v14, /device:TPU:14, one launch (start us, length us, event | category | flops | bytes accessed | tf_op | source)
XLA Modules:
  0.0 232.9 jit_solution(101220241356771841)
XLA Ops:
  0.0 3.8 %convert.3 = bf16[2,32,32768]{2,1,0:T(8,128)(2,1)S(1)} convert(s32[2,32,32768]{2,1,0:T(8,128)} %param.4) | non-fusion elementwise | flops 2097152 | bytes 12582912 | tf_op jit(solution)/shard_map/convert
  3.8 0.1 slice.21
  3.9 0.1 copy.57
  4.0 1.3 collective-permute-start
  5.3 4.5 %copy.39 = bf16[8,8,32,1024]{3,2,1,0:T(8,128)(2,1)} copy(bf16[8,8,32,1024]{3,1,2,0:T(8,128)(2,1)S(1)} %bitcast.67) | data formatting | bytes 8388608
  9.7 14.3 %shard_map.46.previous_ref = bf16[2,32,32,2048]{3,2,1,0:T(8,128)(2,1)} custom-call(f32[8,1024]{1,0:T(8,128)} %taps_ref.3, bf16[2,32,32,1024]{3,2,1,0:T(8,128)(2,1)} %bitcast.61), custom_call_target="tpu_custom_call" | custom-call | flops 67108864 | bytes 12582912 | tf_op jit(solution)/shard_map/pallas_call | solution.py:110
  24.0 3.9 %collective-permute-done = bf16[2,32,7,1024]{3,1,2,0:T(8,128)(2,1)S(1)} collective-permute-done((bf16[2,32,7,1024]{3,1,2,0:T(8,128)(2,1)S(1)}, bf16[2,32,7,1024]{3,1,2,0:T(8,128)(2,1)S(1)}, u32[]{:S(2)}, u32[]{:S(2)}) %collective-permute-start) | collective-permute-done | bytes 917536 | tf_op jit(solution)/shard_map/ppermute | solution.py:18
  27.9 1.6 copy.20.halo_ref
  29.5 6.1 %shard_map.47 = bf16[2,32,32,2048]{3,2,1,0:T(8,128)(2,1)} custom-call(f32[8,1024]{1,0:T(8,128)} %taps_ref.3, bf16[2,32,7,1024]{3,2,1,0:T(8,128)(2,1)} %copy.20.halo_ref, bf16[2,32,32,1024]{3,2,1,0:T(8,128)(2,1)} %bitcast.62, bf16[2,32,32,2048]{3,2,1,0:T(8,128)(2,1)} %shard_map.46.previous_ref), custom_call_target="tpu_custom_call", output_to_operand_aliasing={{}: (3, {})} | custom-call | flops 16777216 | bytes 4194304 | tf_op jit(solution)/shard_map/pallas_call | solution.py:127
  35.6 6.8 %convolution_convert_fusion.2 = bf16[2048,256]{0,1:T(8,128)(2,1)} fusion(bf16[2048,2048]{1,0:T(8,128)(2,1)} %bitcast.63, bf16[256,2048]{1,0:T(8,128)(2,1)S(1)} %copy-done.4), kind=kOutput, calls=%fused_computation.10 | convolution fusion | flops 2148007936 | bytes 10485760 | tf_op jit(solution)/shard_map/kj,nj->kn/dot_general | solution.py:300
  42.4 6.2 %all-to-all-start.1 = ((bf16[16,16,2048]{2,1,0:T(8,128)(2,1)}), bf16[16,16,2048]{2,1,0:T(8,128)(2,1)S(1)}, u32[]{:S(2)}, u32[]{:S(2)}) async-start(bf16[16,16,2048]{2,1,0:T(8,128)(2,1)} %bitcast.10), calls=%async_computation.1 | async-start | bytes 2097152 | tf_op jit(solution)/shard_map/all_to_all | solution.py:304
  48.7 6.8 %convolution_convert_fusion.3 = bf16[2048,256]{0,1:T(8,128)(2,1)} fusion(bf16[2048,2048]{1,0:T(8,128)(2,1)} %bitcast.64, bf16[256,2048]{1,0:T(8,128)(2,1)S(1)} %copy-done.3), kind=kOutput, calls=%fused_computation.11 | convolution fusion | flops 2148007936 | bytes 10485760 | tf_op jit(solution)/shard_map/kj,nj->kn/dot_general | solution.py:300
  55.5 17.9 %all-to-all-done.1 = bf16[16,16,2048]{2,1,0:T(8,128)(2,1)S(1)} async-done(((bf16[16,16,2048]{2,1,0:T(8,128)(2,1)}), bf16[16,16,2048]{2,1,0:T(8,128)(2,1)S(1)}, u32[]{:S(2)}, u32[]{:S(2)}) %all-to-all-start.1) | async-done | bytes 1048608 | tf_op jit(solution)/shard_map/all_to_all | solution.py:304
  73.4 5.1 %all-to-all-start = ((bf16[16,16,2048]{2,1,0:T(8,128)(2,1)}), bf16[16,16,2048]{2,1,0:T(8,128)(2,1)S(1)}, u32[]{:S(2)}, u32[]{:S(2)}) async-start(bf16[16,16,2048]{2,1,0:T(8,128)(2,1)} %bitcast.3), calls=%async_computation | async-start | bytes 2097152 | tf_op jit(solution)/shard_map/all_to_all | solution.py:304
  78.5 4.4 %reshape.85 = bf16[16,16,2,32,32]{4,3,2,1,0:T(8,128)(2,1)} reshape(bf16[16,16,2048]{2,1,0:T(8,128)(2,1)S(1)} %all-to-all-done.1) | data formatting | bytes 2097152 | tf_op jit(solution)/shard_map/reshape | solution.py:305
  82.9 3.6 %fusion.4 = bf16[16,2,32,512,1]{3,2,0,1,4:T(8,128)(2,1)S(1)} fusion(bf16[16,16,2,32,32]{4,3,2,1,0:T(8,128)(2,1)} %reshape.85, s32[16,32]{1,0:T(8,128)S(1)} %multiply_add_fusion, s32[512]{0:T(512)S(1)} %copy-done), kind=kOutput, calls=%fused_computation.4 | convolution fusion | flops 537133056 | bytes 2101248 | tf_op jit(solution)/shard_map/gkias,gar->kisr/dot_general | solution.py:306
  86.4 0.1 copy.55
  86.5 0.1 collective-permute-start.2
  86.6 16.6 %all-to-all-done = bf16[16,16,2048]{2,1,0:T(8,128)(2,1)S(1)} async-done(((bf16[16,16,2048]{2,1,0:T(8,128)(2,1)}), bf16[16,16,2048]{2,1,0:T(8,128)(2,1)S(1)}, u32[]{:S(2)}, u32[]{:S(2)}) %all-to-all-start) | async-done | bytes 1048608 | tf_op jit(solution)/shard_map/all_to_all | solution.py:304
  103.2 4.4 %reshape.81 = bf16[16,16,2,32,32]{4,3,2,1,0:T(8,128)(2,1)} reshape(bf16[16,16,2048]{2,1,0:T(8,128)(2,1)S(1)} %all-to-all-done) | data formatting | bytes 2097152 | tf_op jit(solution)/shard_map/reshape | solution.py:305
  107.6 3.6 %fusion.6 = bf16[16,2,32,512,1]{3,2,0,1,4:T(8,128)(2,1)S(1)} fusion(bf16[16,16,2,32,32]{4,3,2,1,0:T(8,128)(2,1)} %reshape.81, s32[16,32]{1,0:T(8,128)S(1)} %multiply_add_fusion, s32[512]{0:T(512)S(1)} %copy-done), kind=kOutput, calls=%fused_computation.6 | convolution fusion | flops 537133056 | bytes 2101248 | tf_op jit(solution)/shard_map/gkias,gar->kisr/dot_general | solution.py:306
  111.1 0.1 copy.56
  111.2 0.1 collective-permute-start.1
  111.3 0.6 collective-permute-done.2
  111.9 2.8 %pad_maximum_fusion.1 = bf16[32,64,512]{2,1,0:T(8,128)(2,1)} fusion(bf16[32,32,512]{2,1,0:T(8,128)(2,1)} %collective-permute-done.2, bf16[32,32,512]{2,1,0:T(8,128)(2,1)S(1)} %bitcast.77), kind=kLoop, calls=%fused_computation.13 | loop fusion | flops 4194304 | bytes 4194304 | tf_op jit(solution)/shard_map/concatenate | solution.py:27
  114.7 7.2 %shard_map.48.refs_0_ = bf16[2,64,256,512]{3,2,1,0:T(8,128)(2,1)} custom-call(s32[1]{0:T(128)} %bitcast.block_ref, bf16[16,128,512]{2,1,0:T(8,128)(2,1)} %bitcast.68, bf16[16,128,512]{2,1,0:T(8,128)(2,1)} %bitcast.69), custom_call_target="tpu_custom_call" | custom-call | flops 1073741824 | bytes 11534336 | tf_op jit(solution)/shard_map/pallas_call | solution.py:237
  121.9 6.7 %convolution_convert_fusion = bf16[2048,256]{0,1:T(8,128)(2,1)} fusion(bf16[2048,2048]{1,0:T(8,128)(2,1)} %bitcast.65, bf16[256,2048]{1,0:T(8,128)(2,1)S(1)} %copy-done.2), kind=kOutput, calls=%fused_computation.8 | convolution fusion | flops 2148007936 | bytes 10485760 | tf_op jit(solution)/shard_map/kj,nj->kn/dot_general | solution.py:300
  128.6 6.0 %all-to-all-start.3 = ((bf16[16,16,2048]{2,1,0:T(8,128)(2,1)}), bf16[16,16,2048]{2,1,0:T(8,128)(2,1)S(1)}, u32[]{:S(2)}, u32[]{:S(2)}) async-start(bf16[16,16,2048]{2,1,0:T(8,128)(2,1)} %bitcast.21), calls=%async_computation.3 | async-start | bytes 2097152 | tf_op jit(solution)/shard_map/all_to_all | solution.py:304
  134.6 2.5 %collective-permute-done.1 = bf16[32,32,512]{2,1,0:T(8,128)(2,1)} collective-permute-done((bf16[32,32,512]{2,1,0:T(8,128)(2,1)S(1)}, bf16[32,32,512]{2,1,0:T(8,128)(2,1)}, u32[]{:S(2)}, u32[]{:S(2)}) %collective-permute-start.1) | collective-permute-done | bytes 1048608 | tf_op jit(solution)/shard_map/ppermute | solution.py:26
  137.2 2.8 %pad_maximum_fusion = bf16[32,64,512]{2,1,0:T(8,128)(2,1)} fusion(bf16[32,32,512]{2,1,0:T(8,128)(2,1)} %collective-permute-done.1, bf16[32,32,512]{2,1,0:T(8,128)(2,1)S(1)} %bitcast.81), kind=kLoop, calls=%fused_computation.12 | loop fusion | flops 4194304 | bytes 4194304 | tf_op jit(solution)/shard_map/concatenate | solution.py:27
  140.0 7.2 %shard_map.49.refs_0_ = bf16[2,64,256,512]{3,2,1,0:T(8,128)(2,1)} custom-call(s32[1]{0:T(128)} %bitcast.block_ref, bf16[16,128,512]{2,1,0:T(8,128)(2,1)} %bitcast.72, bf16[16,128,512]{2,1,0:T(8,128)(2,1)} %bitcast.73, bf16[2,64,256,512]{3,2,1,0:T(8,128)(2,1)} %shard_map.48.refs_0_), custom_call_target="tpu_custom_call", output_to_operand_aliasing={{}: (3, {})} | custom-call | flops 1073741824 | bytes 11534336 | tf_op jit(solution)/shard_map/pallas_call | solution.py:237
  147.1 6.8 %convolution_convert_fusion.1 = bf16[2048,256]{0,1:T(8,128)(2,1)} fusion(bf16[2048,2048]{1,0:T(8,128)(2,1)} %bitcast.66, bf16[256,2048]{1,0:T(8,128)(2,1)S(1)} %copy-done.1), kind=kOutput, calls=%fused_computation.9 | convolution fusion | flops 2148007936 | bytes 10485760 | tf_op jit(solution)/shard_map/kj,nj->kn/dot_general | solution.py:300
  153.9 5.4 %all-to-all-done.3 = bf16[16,16,2048]{2,1,0:T(8,128)(2,1)S(1)} async-done(((bf16[16,16,2048]{2,1,0:T(8,128)(2,1)}), bf16[16,16,2048]{2,1,0:T(8,128)(2,1)S(1)}, u32[]{:S(2)}, u32[]{:S(2)}) %all-to-all-start.3) | async-done | bytes 1048608 | tf_op jit(solution)/shard_map/all_to_all | solution.py:304
  159.4 5.1 %all-to-all-start.2 = ((bf16[16,16,2048]{2,1,0:T(8,128)(2,1)}), bf16[16,16,2048]{2,1,0:T(8,128)(2,1)S(1)}, u32[]{:S(2)}, u32[]{:S(2)}) async-start(bf16[16,16,2048]{2,1,0:T(8,128)(2,1)} %bitcast.16), calls=%async_computation.2 | async-start | bytes 2097152 | tf_op jit(solution)/shard_map/all_to_all | solution.py:304
  164.5 4.4 %reshape.93 = bf16[16,16,2,32,32]{4,3,2,1,0:T(8,128)(2,1)} reshape(bf16[16,16,2048]{2,1,0:T(8,128)(2,1)S(1)} %all-to-all-done.3) | data formatting | bytes 2097152 | tf_op jit(solution)/shard_map/reshape | solution.py:305
  168.9 3.6 %fusion = bf16[16,2,32,512,1]{3,2,0,1,4:T(8,128)(2,1)S(1)} fusion(bf16[16,16,2,32,32]{4,3,2,1,0:T(8,128)(2,1)} %reshape.93, s32[16,32]{1,0:T(8,128)S(1)} %multiply_add_fusion, s32[512]{0:T(512)S(1)} %copy-done), kind=kOutput, calls=%fused_computation | convolution fusion | flops 537133056 | bytes 2101248 | tf_op jit(solution)/shard_map/gkias,gar->kisr/dot_general | solution.py:306
  172.5 0.1 copy.53
  172.5 0.5 collective-permute-start.4
  173.1 16.1 %all-to-all-done.2 = bf16[16,16,2048]{2,1,0:T(8,128)(2,1)S(1)} async-done(((bf16[16,16,2048]{2,1,0:T(8,128)(2,1)}), bf16[16,16,2048]{2,1,0:T(8,128)(2,1)S(1)}, u32[]{:S(2)}, u32[]{:S(2)}) %all-to-all-start.2) | async-done | bytes 1048608 | tf_op jit(solution)/shard_map/all_to_all | solution.py:304
  189.2 4.4 %reshape.89 = bf16[16,16,2,32,32]{4,3,2,1,0:T(8,128)(2,1)} reshape(bf16[16,16,2048]{2,1,0:T(8,128)(2,1)S(1)} %all-to-all-done.2) | data formatting | bytes 2097152 | tf_op jit(solution)/shard_map/reshape | solution.py:305
  193.6 3.6 %fusion.2 = bf16[16,2,32,512,1]{3,2,0,1,4:T(8,128)(2,1)S(1)} fusion(bf16[16,16,2,32,32]{4,3,2,1,0:T(8,128)(2,1)} %reshape.89, s32[16,32]{1,0:T(8,128)S(1)} %multiply_add_fusion, s32[512]{0:T(512)S(1)} %copy-done), kind=kOutput, calls=%fused_computation.2 | convolution fusion | flops 537133056 | bytes 2101248 | tf_op jit(solution)/shard_map/gkias,gar->kisr/dot_general | solution.py:306
  197.2 0.1 copy.54
  197.3 0.5 collective-permute-start.3
  197.8 1.5 pad_maximum_fusion.3
  199.3 7.1 %shard_map.50.refs_0_ = bf16[2,64,256,512]{3,2,1,0:T(8,128)(2,1)} custom-call(s32[1]{0:T(128)} %bitcast.block_ref, bf16[16,128,512]{2,1,0:T(8,128)(2,1)} %bitcast.74, bf16[16,128,512]{2,1,0:T(8,128)(2,1)} %bitcast.75, bf16[2,64,256,512]{3,2,1,0:T(8,128)(2,1)} %shard_map.49.refs_0_), custom_call_target="tpu_custom_call", output_to_operand_aliasing={{}: (3, {})} | custom-call | flops 1073741824 | bytes 11534336 | tf_op jit(solution)/shard_map/pallas_call | solution.py:237
  206.4 16.7 %collective-permute-done.3 = bf16[32,32,512]{2,1,0:T(8,128)(2,1)} collective-permute-done((bf16[32,32,512]{2,1,0:T(8,128)(2,1)S(1)}, bf16[32,32,512]{2,1,0:T(8,128)(2,1)}, u32[]{:S(2)}, u32[]{:S(2)}) %collective-permute-start.3) | collective-permute-done | bytes 1048608 | tf_op jit(solution)/shard_map/ppermute | solution.py:26
  223.1 2.8 %pad_maximum_fusion.2 = bf16[32,64,512]{2,1,0:T(8,128)(2,1)} fusion(bf16[32,32,512]{2,1,0:T(8,128)(2,1)} %collective-permute-done.3, bf16[32,32,512]{2,1,0:T(8,128)(2,1)S(1)} %bitcast.83), kind=kLoop, calls=%fused_computation.14 | loop fusion | flops 4194304 | bytes 4194304 | tf_op jit(solution)/shard_map/concatenate | solution.py:27
  225.8 7.1 %shard_map.51 = bf16[2,64,256,512]{3,2,1,0:T(8,128)(2,1)} custom-call(s32[1]{0:T(128)} %bitcast.block_ref, bf16[16,128,512]{2,1,0:T(8,128)(2,1)} %bitcast.70, bf16[16,128,512]{2,1,0:T(8,128)(2,1)} %bitcast.71, bf16[2,64,256,512]{3,2,1,0:T(8,128)(2,1)} %shard_map.50.refs_0_), custom_call_target="tpu_custom_call", output_to_operand_aliasing={{}: (3, {})} | custom-call | flops 1073741824 | bytes 11534336 | tf_op jit(solution)/shard_map/pallas_call | solution.py:237
  (12 shorter events, 0.0 us)
Async XLA Ops:
  4.0 24.0 %collective-permute-start = (bf16[2,32,7,1024]{3,1,2,0:T(8,128)(2,1)S(1)}, bf16[2,32,7,1024]{3,1,2,0:T(8,128)(2,1)S(1)}, u32[]{:S(2)}, u32[]{:S(2)}) collective-permute-start(bf16[2,32,7,1024]{3,1,2,0:T(8,128)(2,1)S(1)} %bitcast.85), channel_id=1, source_target_pairs={{0,1},{2,3},{4,5},{6,7},{8,9},{10,11},{12,13},{14,15},{16,17},{18,... | collective-permute-start | bytes 2752520 | tf_op jit(solution)/shard_map/ppermute | solution.py:18
  29.5 6.1 %copy-start.4 = (bf16[256,2048]{1,0:T(8,128)(2,1)S(1)}, bf16[256,2048]{1,0:T(8,128)(2,1)}, u32[]{:S(2)}) copy-start(bf16[256,2048]{1,0:T(8,128)(2,1)} %constant.12) | copy-start | bytes 3145732
  35.6 13.1 %copy-start.3 = (bf16[256,2048]{1,0:T(8,128)(2,1)S(1)}, bf16[256,2048]{1,0:T(8,128)(2,1)}, u32[]{:S(2)}) copy-start(bf16[256,2048]{1,0:T(8,128)(2,1)} %constant.10) | copy-start | bytes 3145732
  42.4 31.0 %all-to-all-start.1 = ((bf16[16,16,2048]{2,1,0:T(8,128)(2,1)}), bf16[16,16,2048]{2,1,0:T(8,128)(2,1)S(1)}, u32[]{:S(2)}, u32[]{:S(2)}) async-start(bf16[16,16,2048]{2,1,0:T(8,128)(2,1)} %bitcast.10), calls=%async_computation.1 | async-start | bytes 2097152 | tf_op jit(solution)/shard_map/all_to_all | solution.py:304
  55.5 27.4 %copy-start = (s32[512]{0:T(512)S(1)}, s32[512]{0:T(512)}, u32[]{:S(2)}) copy-start(s32[512]{0:T(512)} %param.6) | copy-start | bytes 6148
  73.4 29.8 %all-to-all-start = ((bf16[16,16,2048]{2,1,0:T(8,128)(2,1)}), bf16[16,16,2048]{2,1,0:T(8,128)(2,1)S(1)}, u32[]{:S(2)}, u32[]{:S(2)}) async-start(bf16[16,16,2048]{2,1,0:T(8,128)(2,1)} %bitcast.3), calls=%async_computation | async-start | bytes 2097152 | tf_op jit(solution)/shard_map/all_to_all | solution.py:304
  86.5 25.4 %collective-permute-start.2 = (bf16[32,32,512]{2,1,0:T(8,128)(2,1)S(1)}, bf16[32,32,512]{2,1,0:T(8,128)(2,1)}, u32[]{:S(2)}, u32[]{:S(2)}) collective-permute-start(bf16[32,32,512]{2,1,0:T(8,128)(2,1)S(1)} %bitcast.76), channel_id=1, source_target_pairs={{0,1},{1,0},{2,3},{3,2},{4,5},{5,4},{6,7},{7,6},{8,9},{9,8},{10,11... | collective-permute-start | bytes 3145736 | tf_op jit(solution)/shard_map/ppermute | solution.py:26
  111.2 25.9 %collective-permute-start.1 = (bf16[32,32,512]{2,1,0:T(8,128)(2,1)S(1)}, bf16[32,32,512]{2,1,0:T(8,128)(2,1)}, u32[]{:S(2)}, u32[]{:S(2)}) collective-permute-start(bf16[32,32,512]{2,1,0:T(8,128)(2,1)S(1)} %bitcast.80), channel_id=1, source_target_pairs={{0,1},{1,0},{2,3},{3,2},{4,5},{5,4},{6,7},{7,6},{8,9},{9,8},{10,11... | collective-permute-start | bytes 3145736 | tf_op jit(solution)/shard_map/ppermute | solution.py:26
  114.7 7.2 %copy-start.2 = (bf16[256,2048]{1,0:T(8,128)(2,1)S(1)}, bf16[256,2048]{1,0:T(8,128)(2,1)}, u32[]{:S(2)}) copy-start(bf16[256,2048]{1,0:T(8,128)(2,1)} %constant.16) | copy-start | bytes 3145732
  128.6 30.7 %all-to-all-start.3 = ((bf16[16,16,2048]{2,1,0:T(8,128)(2,1)}), bf16[16,16,2048]{2,1,0:T(8,128)(2,1)S(1)}, u32[]{:S(2)}, u32[]{:S(2)}) async-start(bf16[16,16,2048]{2,1,0:T(8,128)(2,1)} %bitcast.21), calls=%async_computation.3 | async-start | bytes 2097152 | tf_op jit(solution)/shard_map/all_to_all | solution.py:304
  140.0 7.2 %copy-start.1 = (bf16[256,2048]{1,0:T(8,128)(2,1)S(1)}, bf16[256,2048]{1,0:T(8,128)(2,1)}, u32[]{:S(2)}) copy-start(bf16[256,2048]{1,0:T(8,128)(2,1)} %constant.14) | copy-start | bytes 3145732
  159.4 29.8 %all-to-all-start.2 = ((bf16[16,16,2048]{2,1,0:T(8,128)(2,1)}), bf16[16,16,2048]{2,1,0:T(8,128)(2,1)S(1)}, u32[]{:S(2)}, u32[]{:S(2)}) async-start(bf16[16,16,2048]{2,1,0:T(8,128)(2,1)} %bitcast.16), calls=%async_computation.2 | async-start | bytes 2097152 | tf_op jit(solution)/shard_map/all_to_all | solution.py:304
  172.5 25.3 %collective-permute-start.4 = (bf16[32,32,512]{2,1,0:T(8,128)(2,1)S(1)}, bf16[32,32,512]{2,1,0:T(8,128)(2,1)S(1)}, u32[]{:S(2)}, u32[]{:S(2)}) collective-permute-start(bf16[32,32,512]{2,1,0:T(8,128)(2,1)S(1)} %bitcast.78), channel_id=1, source_target_pairs={{0,1},{1,0},{2,3},{3,2},{4,5},{5,4},{6,7},{7,6},{8,9},{9,8},{10,11... | collective-permute-start | bytes 3145736 | tf_op jit(solution)/shard_map/ppermute | solution.py:26
  197.3 25.8 %collective-permute-start.3 = (bf16[32,32,512]{2,1,0:T(8,128)(2,1)S(1)}, bf16[32,32,512]{2,1,0:T(8,128)(2,1)}, u32[]{:S(2)}, u32[]{:S(2)}) collective-permute-start(bf16[32,32,512]{2,1,0:T(8,128)(2,1)S(1)} %bitcast.82), channel_id=1, source_target_pairs={{0,1},{1,0},{2,3},{3,2},{4,5},{5,4},{6,7},{7,6},{8,9},{9,8},{10,11... | collective-permute-start | bytes 3145736 | tf_op jit(solution)/shard_map/ppermute | solution.py:26

commit v15 on v14

--- a/solution.py
+++ b/solution.py
@@ -24,6 +24,8 @@
     for shift in range(1, count):
         pairs = [(source, (source + shift) % count) for source in range(count)]
         parts.append(lax.ppermute(value, axis, pairs))
+    if dimension is None:
+        return parts
     return jnp.concatenate(parts, axis=dimension)
 
 
@@ -247,6 +249,68 @@
     )(*operands)
 
 
+def correlate_pieces_kernel(block_ref, *refs):
+    out_ref = refs[-1]
+    pieces = (len(refs) - 1) // 2
+    rows_refs = refs[0:pieces]
+    cols_refs = refs[pieces : 2 * pieces]
+    contract_first = (((0,), (0,)), ((), ()))
+    for index in range(out_ref.shape[1]):
+        rows = jnp.concatenate(
+            [ref[index, part] for part in range(2) for ref in rows_refs], axis=0
+        )
+        right = jnp.concatenate(
+            [ref[index, part] for part in range(2) for ref in cols_refs], axis=0
+        )
+        half = rows.shape[0] // 2
+        swapped = jnp.concatenate([rows[half:], -rows[:half]], axis=0)
+        real_vis = lax.dot_general(rows, right, contract_first, preferred_element_type=jnp.float32)
+        imag_vis = lax.dot_general(swapped, right, contract_first, preferred_element_type=jnp.float32)
+        right = right.astype(jnp.float32)
+        rows = rows.astype(jnp.float32)
+        column_power = jnp.sum(right * right, axis=0, keepdims=True)
+        row_power = jnp.sum(jnp.transpose(rows * rows), axis=1, keepdims=True)
+        scale_row = lax.rsqrt(row_power + epsilon)
+        scale_column = lax.rsqrt(column_power + epsilon)
+        out_ref[0, index] = (real_vis * scale_row * scale_column).astype(out_ref.dtype)
+        out_ref[1, index] = (imag_vis * scale_row * scale_column).astype(out_ref.dtype)
+
+
+def correlate_pieces_chunk(parts, block, row_count, previous, offset, local_channels):
+    width, _, spectra, stations = parts[0].shape
+    step = 4 if width % 4 == 0 and offset % 4 == 0 else 1
+    rows_spec = pl.BlockSpec((step, 2, spectra, row_count), lambda k, b: (k, 0, 0, b[0]))
+    cols_spec = pl.BlockSpec((step, 2, spectra, stations), lambda k, b: (k, 0, 0, 0))
+    in_specs = [rows_spec] * len(parts) + [cols_spec] * len(parts)
+    operands = [block] + list(parts) + list(parts)
+    aliases = {}
+    if previous is not None:
+        in_specs.append(pl.BlockSpec(memory_space=pl.ANY))
+        operands.append(previous)
+        aliases = {len(operands) - 1: 0}
+    grid_spec = pltpu.PrefetchScalarGridSpec(
+        num_scalar_prefetch=1,
+        grid=(width // step,),
+        in_specs=in_specs,
+        out_specs=pl.BlockSpec(
+            (2, step, row_count, stations), lambda k, b: (0, offset // step + k, 0, 0)
+        ),
+    )
+    depth = 2 * spectra * len(parts)
+    return pl.pallas_call(
+        correlate_pieces_kernel,
+        grid_spec=grid_spec,
+        out_shape=jax.ShapeDtypeStruct((2, local_channels, row_count, stations), jnp.bfloat16),
+        input_output_aliases=aliases,
+        cost_estimate=pl.CostEstimate(
+            flops=4 * width * row_count * depth * stations,
+            transcendentals=width * (row_count + stations),
+            bytes_accessed=2 * width * depth * (stations + row_count)
+            + 4 * width * row_count * stations,
+        ),
+    )(*operands)
+
+
 def per_device(samples, fir_taps, station_order):
     tap_count = fir_taps.shape[0]
     channels = fir_taps.shape[1]
@@ -277,6 +341,13 @@
     block_index = jnp.reshape(lax.axis_index("blk"), (1,)).astype(jnp.int32)
 
     def correlate(chunk, gathered, result):
+        if isinstance(gathered, list):
+            if row_count % 128 == 0:
+                parts = [part.reshape(width, 2, spectra_local, stations) for part in gathered]
+                return correlate_pieces_chunk(
+                    parts, block_index, row_count, result, chunk * width, local_channels
+                )
+            gathered = jnp.concatenate(gathered, axis=1)
         if row_count % 128 == 0:
             right = gathered.reshape(width, -1, stations)
             return correlate_rows_chunk(
@@ -307,7 +378,8 @@
             "gkias,gar->kisr", turned, selector, preferred_element_type=jnp.float32
         ).astype(jnp.bfloat16)
         ordered = ordered.reshape(width * 2, spectra_local, stations)
-        pending.append(gathered_along(ordered, "blk", 1))
+        last = chunk == chunks - 1
+        pending.append(gathered_along(ordered, "blk", None if last else 1))
     for chunk in range(max(0, chunks - 2), chunks):
         result = correlate(chunk, pending[chunk], result)
     return result

time: 234 us -> 232 us (level)
    pallas_call x0 -> x1, Pallas kernels: none -> 7.32 us  [correlate_pieces_chunk(): pl.pallas_call(correlate_pieces_kernel, grid_spec=grid_spec, out_shape=ja...]
    pallas_call x4 -> x3, Pallas kernels: 28.6 us -> 21.5 us  [correlate_rows_chunk(): pl.pallas_call(correlate_rows_kernel, grid_spec=grid_spec, out_shape=jax....]
    concatenate x4 -> x3, other arithmetic: 9.85 us -> 8.36 us  [gathered_along(): return jnp.concatenate(parts, axis=dimension)]
    unnamed x11 -> x15, local copies, waits for them, and re-layouts: 4.5 us -> 5.49 us
  transfers between devices with their start and end apart: 9 -> 9, of which waited for: 8 -> 9; matrix products, arithmetic and copies ran while one was open for 27% -> 28% of each run, Pallas kernels for 15% -> 15%
where the time goes in v15:
time: 232 us; the launch traced here: 231 us
  waiting for transfers between devices  78.5 us (34%)
  Pallas kernels  49.2 us (21%)
  matrix products  41.4 us (18%)
  local copies, waits for them, and re-layouts  25 us (11%)
  starting transfers between devices  25 us (11%)
  other arithmetic  12.2 us (5%)
    all_to_all x4, waiting for transfers between devices, per_device(): lax.all_to_all(spectra, 'stn', split_axis=0, concat_axis=0, tiled=True)  56 us
    dot_general x4, matrix products, per_device(): jnp.einsum('kj,nj->kn', weights[chunk], source, preferred_element_type=jn...  27.1 us
    all_to_all x4, starting transfers between devices, per_device(): lax.all_to_all(spectra, 'stn', split_axis=0, concat_axis=0, tiled=True)  22.4 us
    pallas_call x3, Pallas kernels, correlate_rows_chunk(): pl.pallas_call(correlate_rows_kernel, grid_spec=grid_spec, out_shape=jax....  21.5 us
    ppermute x4, waiting for transfers between devices, gathered_along(): parts.append(lax.ppermute(value, axis, pairs))  18.5 us
    reshape x4, local copies, waits for them, and re-layouts, per_device(): turned = turned.reshape(groups, width, 2, stations_local, spectra_local)  17.5 us
    pallas_call x1, Pallas kernels, filter_frames(): pl.pallas_call(fir_kernel, grid=(stations_local // group,), in_specs=[pl....  14.3 us
    dot_general x4, matrix products, per_device(): jnp.einsum('gkias,gar->kisr', turned, selector, preferred_element_type=jn...  14.2 us
  transfers between devices with their start and end apart: 9, of which 9 were waited for; matrix products, arithmetic and copies ran while one was open for 28% of the time, Pallas kernels for 15%

profile of v15, /device:TPU:14, one launch (start us, length us, event | category | flops | bytes accessed | tf_op | source)
XLA Modules:
  0.0 231.3 jit_solution(13955161694174887078)
XLA Ops:
  0.0 3.8 %convert.3 = bf16[2,32,32768]{2,1,0:T(8,128)(2,1)S(1)} convert(s32[2,32,32768]{2,1,0:T(8,128)} %param.4) | non-fusion elementwise | flops 2097152 | bytes 12582912 | tf_op jit(solution)/shard_map/convert
  3.9 0.1 copy.58
  4.0 1.3 collective-permute-start
  5.3 4.5 %copy.40 = bf16[8,8,32,1024]{3,2,1,0:T(8,128)(2,1)} copy(bf16[8,8,32,1024]{3,1,2,0:T(8,128)(2,1)S(1)} %bitcast.67) | data formatting | bytes 8388608
  9.7 14.3 %shard_map.46.previous_ref = bf16[2,32,32,2048]{3,2,1,0:T(8,128)(2,1)} custom-call(f32[8,1024]{1,0:T(8,128)} %taps_ref.3, bf16[2,32,32,1024]{3,2,1,0:T(8,128)(2,1)} %bitcast.61), custom_call_target="tpu_custom_call" | custom-call | flops 67108864 | bytes 12582912 | tf_op jit(solution)/shard_map/pallas_call | solution.py:112
  24.0 3.9 %collective-permute-done = bf16[2,32,7,1024]{3,1,2,0:T(8,128)(2,1)S(1)} collective-permute-done((bf16[2,32,7,1024]{3,1,2,0:T(8,128)(2,1)S(1)}, bf16[2,32,7,1024]{3,1,2,0:T(8,128)(2,1)S(1)}, u32[]{:S(2)}, u32[]{:S(2)}) %collective-permute-start) | collective-permute-done | bytes 917536 | tf_op jit(solution)/shard_map/ppermute | solution.py:18
  27.9 1.6 copy.21.halo_ref
  29.5 6.1 %shard_map.47 = bf16[2,32,32,2048]{3,2,1,0:T(8,128)(2,1)} custom-call(f32[8,1024]{1,0:T(8,128)} %taps_ref.3, bf16[2,32,7,1024]{3,2,1,0:T(8,128)(2,1)} %copy.21.halo_ref, bf16[2,32,32,1024]{3,2,1,0:T(8,128)(2,1)} %bitcast.62, bf16[2,32,32,2048]{3,2,1,0:T(8,128)(2,1)} %shard_map.46.previous_ref), custom_call_target="tpu_custom_call", output_to_operand_aliasing={{}: (3, {})} | custom-call | flops 16777216 | bytes 4194304 | tf_op jit(solution)/shard_map/pallas_call | solution.py:129
  35.6 6.8 %convolution_convert_fusion.2 = bf16[2048,256]{0,1:T(8,128)(2,1)} fusion(bf16[2048,2048]{1,0:T(8,128)(2,1)} %bitcast.63, bf16[256,2048]{1,0:T(8,128)(2,1)S(1)} %copy-done.6), kind=kOutput, calls=%fused_computation.10 | convolution fusion | flops 2148007936 | bytes 10485760 | tf_op jit(solution)/shard_map/kj,nj->kn/dot_general | solution.py:371
  42.4 6.2 %all-to-all-start.1 = ((bf16[16,16,2048]{2,1,0:T(8,128)(2,1)}), bf16[16,16,2048]{2,1,0:T(8,128)(2,1)S(1)}, u32[]{:S(2)}, u32[]{:S(2)}) async-start(bf16[16,16,2048]{2,1,0:T(8,128)(2,1)} %bitcast.10), calls=%async_computation.1 | async-start | bytes 2097152 | tf_op jit(solution)/shard_map/all_to_all | solution.py:375
  48.7 6.8 %convolution_convert_fusion.3 = bf16[2048,256]{0,1:T(8,128)(2,1)} fusion(bf16[2048,2048]{1,0:T(8,128)(2,1)} %bitcast.64, bf16[256,2048]{1,0:T(8,128)(2,1)S(1)} %copy-done.5), kind=kOutput, calls=%fused_computation.11 | convolution fusion | flops 2148007936 | bytes 10485760 | tf_op jit(solution)/shard_map/kj,nj->kn/dot_general | solution.py:371
  55.5 17.9 %all-to-all-done.1 = bf16[16,16,2048]{2,1,0:T(8,128)(2,1)S(1)} async-done(((bf16[16,16,2048]{2,1,0:T(8,128)(2,1)}), bf16[16,16,2048]{2,1,0:T(8,128)(2,1)S(1)}, u32[]{:S(2)}, u32[]{:S(2)}) %all-to-all-start.1) | async-done | bytes 1048608 | tf_op jit(solution)/shard_map/all_to_all | solution.py:375
  73.4 5.1 %all-to-all-start = ((bf16[16,16,2048]{2,1,0:T(8,128)(2,1)}), bf16[16,16,2048]{2,1,0:T(8,128)(2,1)S(1)}, u32[]{:S(2)}, u32[]{:S(2)}) async-start(bf16[16,16,2048]{2,1,0:T(8,128)(2,1)} %bitcast.3), calls=%async_computation | async-start | bytes 2097152 | tf_op jit(solution)/shard_map/all_to_all | solution.py:375
  78.5 4.4 %reshape.85 = bf16[16,16,2,32,32]{4,3,2,1,0:T(8,128)(2,1)} reshape(bf16[16,16,2048]{2,1,0:T(8,128)(2,1)S(1)} %all-to-all-done.1) | data formatting | bytes 2097152 | tf_op jit(solution)/shard_map/reshape | solution.py:376
  82.9 3.6 %fusion.4 = bf16[16,2,32,512,1]{3,2,0,1,4:T(8,128)(2,1)S(1)} fusion(bf16[16,16,2,32,32]{4,3,2,1,0:T(8,128)(2,1)} %reshape.85, s32[16,32]{1,0:T(8,128)S(1)} %multiply_add_fusion, s32[512]{0:T(512)S(1)} %copy-done.2), kind=kOutput, calls=%fused_computation.4 | convolution fusion | flops 537133056 | bytes 2101248 | tf_op jit(solution)/shard_map/gkias,gar->kisr/dot_general | solution.py:377
  86.4 0.1 copy.56
  86.5 0.1 collective-permute-start.2
  86.6 16.6 %all-to-all-done = bf16[16,16,2048]{2,1,0:T(8,128)(2,1)S(1)} async-done(((bf16[16,16,2048]{2,1,0:T(8,128)(2,1)}), bf16[16,16,2048]{2,1,0:T(8,128)(2,1)S(1)}, u32[]{:S(2)}, u32[]{:S(2)}) %all-to-all-start) | async-done | bytes 1048608 | tf_op jit(solution)/shard_map/all_to_all | solution.py:375
  103.2 4.4 %reshape.81 = bf16[16,16,2,32,32]{4,3,2,1,0:T(8,128)(2,1)} reshape(bf16[16,16,2048]{2,1,0:T(8,128)(2,1)S(1)} %all-to-all-done) | data formatting | bytes 2097152 | tf_op jit(solution)/shard_map/reshape | solution.py:376
  107.6 3.6 %fusion.6 = bf16[16,2,32,512,1]{3,2,0,1,4:T(8,128)(2,1)S(1)} fusion(bf16[16,16,2,32,32]{4,3,2,1,0:T(8,128)(2,1)} %reshape.81, s32[16,32]{1,0:T(8,128)S(1)} %multiply_add_fusion, s32[512]{0:T(512)S(1)} %copy-done.2), kind=kOutput, calls=%fused_computation.6 | convolution fusion | flops 537133056 | bytes 2101248 | tf_op jit(solution)/shard_map/gkias,gar->kisr/dot_general | solution.py:377
  111.1 0.1 copy.57
  111.2 0.1 collective-permute-start.1
  111.3 0.6 collective-permute-done.2
  111.9 2.8 %pad_maximum_fusion.1 = bf16[32,64,512]{2,1,0:T(8,128)(2,1)} fusion(bf16[32,32,512]{2,1,0:T(8,128)(2,1)} %collective-permute-done.2, bf16[32,32,512]{2,1,0:T(8,128)(2,1)S(1)} %bitcast.80), kind=kLoop, calls=%fused_computation.13 | loop fusion | flops 4194304 | bytes 4194304 | tf_op jit(solution)/shard_map/concatenate | solution.py:29
  114.7 7.2 %shard_map.48.refs_0_ = bf16[2,64,256,512]{3,2,1,0:T(8,128)(2,1)} custom-call(s32[1]{0:T(128)} %bitcast.block_ref, bf16[16,128,512]{2,1,0:T(8,128)(2,1)} %bitcast.68, bf16[16,128,512]{2,1,0:T(8,128)(2,1)} %bitcast.69), custom_call_target="tpu_custom_call" | custom-call | flops 1073741824 | bytes 11534336 | tf_op jit(solution)/shard_map/pallas_call | solution.py:239
  121.9 6.7 %convolution_convert_fusion = bf16[2048,256]{0,1:T(8,128)(2,1)} fusion(bf16[2048,2048]{1,0:T(8,128)(2,1)} %bitcast.65, bf16[256,2048]{1,0:T(8,128)(2,1)S(1)} %copy-done.4), kind=kOutput, calls=%fused_computation.8 | convolution fusion | flops 2148007936 | bytes 10485760 | tf_op jit(solution)/shard_map/kj,nj->kn/dot_general | solution.py:371
  128.6 6.0 %all-to-all-start.3 = ((bf16[16,16,2048]{2,1,0:T(8,128)(2,1)}), bf16[16,16,2048]{2,1,0:T(8,128)(2,1)S(1)}, u32[]{:S(2)}, u32[]{:S(2)}) async-start(bf16[16,16,2048]{2,1,0:T(8,128)(2,1)} %bitcast.21), calls=%async_computation.3 | async-start | bytes 2097152 | tf_op jit(solution)/shard_map/all_to_all | solution.py:375
  134.6 2.5 %collective-permute-done.1 = bf16[32,32,512]{2,1,0:T(8,128)(2,1)} collective-permute-done((bf16[32,32,512]{2,1,0:T(8,128)(2,1)S(1)}, bf16[32,32,512]{2,1,0:T(8,128)(2,1)}, u32[]{:S(2)}, u32[]{:S(2)}) %collective-permute-start.1) | collective-permute-done | bytes 1048608 | tf_op jit(solution)/shard_map/ppermute | solution.py:26
  137.1 2.8 %pad_maximum_fusion = bf16[32,64,512]{2,1,0:T(8,128)(2,1)} fusion(bf16[32,32,512]{2,1,0:T(8,128)(2,1)} %collective-permute-done.1, bf16[32,32,512]{2,1,0:T(8,128)(2,1)S(1)} %bitcast.84), kind=kLoop, calls=%fused_computation.12 | loop fusion | flops 4194304 | bytes 4194304 | tf_op jit(solution)/shard_map/concatenate | solution.py:29
  139.9 7.2 %shard_map.49.refs_0_ = bf16[2,64,256,512]{3,2,1,0:T(8,128)(2,1)} custom-call(s32[1]{0:T(128)} %bitcast.block_ref, bf16[16,128,512]{2,1,0:T(8,128)(2,1)} %bitcast.70, bf16[16,128,512]{2,1,0:T(8,128)(2,1)} %bitcast.71, bf16[2,64,256,512]{3,2,1,0:T(8,128)(2,1)} %shard_map.48.refs_0_), custom_call_target="tpu_custom_call", output_to_operand_aliasing={{}: (3, {})} | custom-call | flops 1073741824 | bytes 11534336 | tf_op jit(solution)/shard_map/pallas_call | solution.py:239
  147.1 6.8 %convolution_convert_fusion.1 = bf16[2048,256]{0,1:T(8,128)(2,1)} fusion(bf16[2048,2048]{1,0:T(8,128)(2,1)} %bitcast.66, bf16[256,2048]{1,0:T(8,128)(2,1)S(1)} %copy-done.3), kind=kOutput, calls=%fused_computation.9 | convolution fusion | flops 2148007936 | bytes 10485760 | tf_op jit(solution)/shard_map/kj,nj->kn/dot_general | solution.py:371
  153.9 5.4 %all-to-all-done.3 = bf16[16,16,2048]{2,1,0:T(8,128)(2,1)S(1)} async-done(((bf16[16,16,2048]{2,1,0:T(8,128)(2,1)}), bf16[16,16,2048]{2,1,0:T(8,128)(2,1)S(1)}, u32[]{:S(2)}, u32[]{:S(2)}) %all-to-all-start.3) | async-done | bytes 1048608 | tf_op jit(solution)/shard_map/all_to_all | solution.py:375
  159.3 5.1 %all-to-all-start.2 = ((bf16[16,16,2048]{2,1,0:T(8,128)(2,1)}), bf16[16,16,2048]{2,1,0:T(8,128)(2,1)S(1)}, u32[]{:S(2)}, u32[]{:S(2)}) async-start(bf16[16,16,2048]{2,1,0:T(8,128)(2,1)} %bitcast.16), calls=%async_computation.2 | async-start | bytes 2097152 | tf_op jit(solution)/shard_map/all_to_all | solution.py:375
  164.4 4.4 %reshape.93 = bf16[16,16,2,32,32]{4,3,2,1,0:T(8,128)(2,1)} reshape(bf16[16,16,2048]{2,1,0:T(8,128)(2,1)S(1)} %all-to-all-done.3) | data formatting | bytes 2097152 | tf_op jit(solution)/shard_map/reshape | solution.py:376
  168.8 3.6 %fusion = bf16[16,2,32,512,1]{3,2,0,1,4:T(8,128)(2,1)S(1)} fusion(bf16[16,16,2,32,32]{4,3,2,1,0:T(8,128)(2,1)} %reshape.93, s32[16,32]{1,0:T(8,128)S(1)} %multiply_add_fusion, s32[512]{0:T(512)S(1)} %copy-done.2), kind=kOutput, calls=%fused_computation | convolution fusion | flops 537133056 | bytes 2101248 | tf_op jit(solution)/shard_map/gkias,gar->kisr/dot_general | solution.py:377
  172.4 0.1 copy.54
  172.5 0.6 collective-permute-start.4
  173.0 16.1 %all-to-all-done.2 = bf16[16,16,2048]{2,1,0:T(8,128)(2,1)S(1)} async-done(((bf16[16,16,2048]{2,1,0:T(8,128)(2,1)}), bf16[16,16,2048]{2,1,0:T(8,128)(2,1)S(1)}, u32[]{:S(2)}, u32[]{:S(2)}) %all-to-all-start.2) | async-done | bytes 1048608 | tf_op jit(solution)/shard_map/all_to_all | solution.py:375
  189.2 4.4 %reshape.89 = bf16[16,16,2,32,32]{4,3,2,1,0:T(8,128)(2,1)} reshape(bf16[16,16,2048]{2,1,0:T(8,128)(2,1)S(1)} %all-to-all-done.2) | data formatting | bytes 2097152 | tf_op jit(solution)/shard_map/reshape | solution.py:376
  193.6 3.6 %fusion.2 = bf16[16,2,32,512,1]{3,2,0,1,4:T(8,128)(2,1)S(1)} fusion(bf16[16,16,2,32,32]{4,3,2,1,0:T(8,128)(2,1)} %reshape.89, s32[16,32]{1,0:T(8,128)S(1)} %multiply_add_fusion, s32[512]{0:T(512)S(1)} %copy-done.2), kind=kOutput, calls=%fused_computation.2 | convolution fusion | flops 537133056 | bytes 2101248 | tf_op jit(solution)/shard_map/gkias,gar->kisr/dot_general | solution.py:377
  197.1 0.1 copy.55
  197.2 0.6 collective-permute-start.3
  197.8 0.1 collective-permute-done.4
  197.9 2.8 %pad_maximum_fusion.2 = bf16[32,64,512]{2,1,0:T(8,128)(2,1)} fusion(bf16[32,32,512]{2,1,0:T(8,128)(2,1)} %collective-permute-done.4, bf16[32,32,512]{2,1,0:T(8,128)(2,1)S(1)} %bitcast.82), kind=kLoop, calls=%fused_computation.14 | loop fusion | flops 4194304 | bytes 4194304 | tf_op jit(solution)/shard_map/concatenate | solution.py:29
  200.6 7.1 %shard_map.50.refs_4_ = bf16[2,64,256,512]{3,2,1,0:T(8,128)(2,1)} custom-call(s32[1]{0:T(128)} %bitcast.block_ref, bf16[16,128,512]{2,1,0:T(8,128)(2,1)} %bitcast.72, bf16[16,128,512]{2,1,0:T(8,128)(2,1)} %bitcast.73, bf16[2,64,256,512]{3,2,1,0:T(8,128)(2,1)} %shard_map.49.refs_0_), custom_call_target="tpu_custom_call", output_to_operand_aliasing={{}: (3, {})} | custom-call | flops 1073741824 | bytes 11534336 | tf_op jit(solution)/shard_map/pallas_call | solution.py:239
  207.7 15.3 %collective-permute-done.3 = bf16[32,32,512]{2,1,0:T(8,128)(2,1)S(1)} collective-permute-done((bf16[32,32,512]{2,1,0:T(8,128)(2,1)S(1)}, bf16[32,32,512]{2,1,0:T(8,128)(2,1)S(1)}, u32[]{:S(2)}, u32[]{:S(2)}) %collective-permute-start.3) | collective-permute-done | bytes 1048608 | tf_op jit(solution)/shard_map/ppermute | solution.py:26
  223.0 1.0 copy-done.1
  224.0 7.3 %shard_map.51 = bf16[2,64,256,512]{3,2,1,0:T(8,128)(2,1)} custom-call(s32[1]{0:T(128)} %bitcast.block_ref, bf16[16,2,32,512]{3,2,1,0:T(8,128)(2,1)} %bitcast.75, bf16[16,2,32,512]{3,2,1,0:T(8,128)(2,1)} %bitcast.77, bf16[16,2,32,512]{3,2,1,0:T(8,128)(2,1)} %bitcast.76, bf16[16,2,32,512]{3,2,1,0:T(8,128)(2,1)} %bitcast.78, ...), custom_call_target="tpu_custom_call", output_to_operand_aliasing={{}: (5, {})} | custom-call | flops 1073741824 | bytes 11534336 | tf_op jit(solution)/shard_map/pallas_call | solution.py:300
  (15 shorter events, 0.1 us)
Async XLA Ops:
  4.0 24.0 %collective-permute-start = (bf16[2,32,7,1024]{3,1,2,0:T(8,128)(2,1)S(1)}, bf16[2,32,7,1024]{3,1,2,0:T(8,128)(2,1)S(1)}, u32[]{:S(2)}, u32[]{:S(2)}) collective-permute-start(bf16[2,32,7,1024]{3,1,2,0:T(8,128)(2,1)S(1)} %bitcast.86), channel_id=1, source_target_pairs={{0,1},{2,3},{4,5},{6,7},{8,9},{10,11},{12,13},{14,15},{16,17},{18,... | collective-permute-start | bytes 2752520 | tf_op jit(solution)/shard_map/ppermute | solution.py:18
  29.5 6.1 %copy-start.6 = (bf16[256,2048]{1,0:T(8,128)(2,1)S(1)}, bf16[256,2048]{1,0:T(8,128)(2,1)}, u32[]{:S(2)}) copy-start(bf16[256,2048]{1,0:T(8,128)(2,1)} %constant.12) | copy-start | bytes 3145732
  35.6 13.1 %copy-start.5 = (bf16[256,2048]{1,0:T(8,128)(2,1)S(1)}, bf16[256,2048]{1,0:T(8,128)(2,1)}, u32[]{:S(2)}) copy-start(bf16[256,2048]{1,0:T(8,128)(2,1)} %constant.10) | copy-start | bytes 3145732
  42.4 31.0 %all-to-all-start.1 = ((bf16[16,16,2048]{2,1,0:T(8,128)(2,1)}), bf16[16,16,2048]{2,1,0:T(8,128)(2,1)S(1)}, u32[]{:S(2)}, u32[]{:S(2)}) async-start(bf16[16,16,2048]{2,1,0:T(8,128)(2,1)} %bitcast.10), calls=%async_computation.1 | async-start | bytes 2097152 | tf_op jit(solution)/shard_map/all_to_all | solution.py:375
  55.5 27.4 %copy-start.2 = (s32[512]{0:T(512)S(1)}, s32[512]{0:T(512)}, u32[]{:S(2)}) copy-start(s32[512]{0:T(512)} %param.6) | copy-start | bytes 6148
  73.4 29.8 %all-to-all-start = ((bf16[16,16,2048]{2,1,0:T(8,128)(2,1)}), bf16[16,16,2048]{2,1,0:T(8,128)(2,1)S(1)}, u32[]{:S(2)}, u32[]{:S(2)}) async-start(bf16[16,16,2048]{2,1,0:T(8,128)(2,1)} %bitcast.3), calls=%async_computation | async-start | bytes 2097152 | tf_op jit(solution)/shard_map/all_to_all | solution.py:375
  86.5 25.4 %collective-permute-start.2 = (bf16[32,32,512]{2,1,0:T(8,128)(2,1)S(1)}, bf16[32,32,512]{2,1,0:T(8,128)(2,1)}, u32[]{:S(2)}, u32[]{:S(2)}) collective-permute-start(bf16[32,32,512]{2,1,0:T(8,128)(2,1)S(1)} %bitcast.79), channel_id=1, source_target_pairs={{0,1},{1,0},{2,3},{3,2},{4,5},{5,4},{6,7},{7,6},{8,9},{9,8},{10,11... | collective-permute-start | bytes 3145736 | tf_op jit(solution)/shard_map/ppermute | solution.py:26
  111.2 25.9 %collective-permute-start.1 = (bf16[32,32,512]{2,1,0:T(8,128)(2,1)S(1)}, bf16[32,32,512]{2,1,0:T(8,128)(2,1)}, u32[]{:S(2)}, u32[]{:S(2)}) collective-permute-start(bf16[32,32,512]{2,1,0:T(8,128)(2,1)S(1)} %bitcast.83), channel_id=1, source_target_pairs={{0,1},{1,0},{2,3},{3,2},{4,5},{5,4},{6,7},{7,6},{8,9},{9,8},{10,11... | collective-permute-start | bytes 3145736 | tf_op jit(solution)/shard_map/ppermute | solution.py:26
  114.7 7.2 %copy-start.4 = (bf16[256,2048]{1,0:T(8,128)(2,1)S(1)}, bf16[256,2048]{1,0:T(8,128)(2,1)}, u32[]{:S(2)}) copy-start(bf16[256,2048]{1,0:T(8,128)(2,1)} %constant.16) | copy-start | bytes 3145732
  128.6 30.7 %all-to-all-start.3 = ((bf16[16,16,2048]{2,1,0:T(8,128)(2,1)}), bf16[16,16,2048]{2,1,0:T(8,128)(2,1)S(1)}, u32[]{:S(2)}, u32[]{:S(2)}) async-start(bf16[16,16,2048]{2,1,0:T(8,128)(2,1)} %bitcast.21), calls=%async_computation.3 | async-start | bytes 2097152 | tf_op jit(solution)/shard_map/all_to_all | solution.py:375
  139.9 7.2 %copy-start.3 = (bf16[256,2048]{1,0:T(8,128)(2,1)S(1)}, bf16[256,2048]{1,0:T(8,128)(2,1)}, u32[]{:S(2)}) copy-start(bf16[256,2048]{1,0:T(8,128)(2,1)} %constant.14) | copy-start | bytes 3145732
  159.3 29.8 %all-to-all-start.2 = ((bf16[16,16,2048]{2,1,0:T(8,128)(2,1)}), bf16[16,16,2048]{2,1,0:T(8,128)(2,1)S(1)}, u32[]{:S(2)}, u32[]{:S(2)}) async-start(bf16[16,16,2048]{2,1,0:T(8,128)(2,1)} %bitcast.16), calls=%async_computation.2 | async-start | bytes 2097152 | tf_op jit(solution)/shard_map/all_to_all | solution.py:375
  172.5 25.4 %collective-permute-start.4 = (bf16[32,32,512]{2,1,0:T(8,128)(2,1)S(1)}, bf16[32,32,512]{2,1,0:T(8,128)(2,1)}, u32[]{:S(2)}, u32[]{:S(2)}) collective-permute-start(bf16[32,32,512]{2,1,0:T(8,128)(2,1)S(1)} %bitcast.81), channel_id=1, source_target_pairs={{0,1},{1,0},{2,3},{3,2},{4,5},{5,4},{6,7},{7,6},{8,9},{9,8},{10,11... | collective-permute-start | bytes 3145736 | tf_op jit(solution)/shard_map/ppermute | solution.py:26
  197.2 10.5 %copy-start = (bf16[16,2,32,512,1]{3,2,1,0,4:T(8,128)(2,1)}, bf16[16,2,32,512,1]{3,2,1,0,4:T(8,128)(2,1)S(1)}, u32[]{:S(2)}) copy-start(bf16[16,2,32,512,1]{3,2,1,0,4:T(8,128)(2,1)S(1)} %copy.55) | copy-start | bytes 3145732
  197.2 25.8 %collective-permute-start.3 = (bf16[32,32,512]{2,1,0:T(8,128)(2,1)S(1)}, bf16[32,32,512]{2,1,0:T(8,128)(2,1)S(1)}, u32[]{:S(2)}, u32[]{:S(2)}) collective-permute-start(bf16[32,32,512]{2,1,0:T(8,128)(2,1)S(1)} %bitcast.74), channel_id=1, source_target_pairs={{0,1},{1,0},{2,3},{3,2},{4,5},{5,4},{6,7},{7,6},{8,9},{9,8},{10,11... | collective-permute-start | bytes 3145736 | tf_op jit(solution)/shard_map/ppermute | solution.py:26
  223.0 1.0 copy-start.1

commit v16 on v15

--- a/solution.py
+++ b/solution.py
@@ -278,7 +278,7 @@
 
 def correlate_pieces_chunk(parts, block, row_count, previous, offset, local_channels):
     width, _, spectra, stations = parts[0].shape
-    step = 4 if width % 4 == 0 and offset % 4 == 0 else 1
+    step = 8 if width % 8 == 0 and offset % 8 == 0 else 1
     rows_spec = pl.BlockSpec((step, 2, spectra, row_count), lambda k, b: (k, 0, 0, b[0]))
     cols_spec = pl.BlockSpec((step, 2, spectra, stations), lambda k, b: (k, 0, 0, 0))
     in_specs = [rows_spec] * len(parts) + [cols_spec] * len(parts)

time: 232 us -> 232 us (level)
  no operation moved by 1% of the time
where the time goes in v16:
time: 232 us; the launch traced here: 231 us
  waiting for transfers between devices  78.5 us (34%)
  Pallas kernels  48.8 us (21%)
  matrix products  41.4 us (18%)
  local copies, waits for them, and re-layouts  25 us (11%)
  starting transfers between devices  25 us (11%)
  other arithmetic  12.2 us (5%)
    all_to_all x4, waiting for transfers between devices, per_device(): lax.all_to_all(spectra, 'stn', split_axis=0, concat_axis=0, tiled=True)  56 us
    dot_general x4, matrix products, per_device(): jnp.einsum('kj,nj->kn', weights[chunk], source, preferred_element_type=jn...  27.1 us
    all_to_all x4, starting transfers between devices, per_device(): lax.all_to_all(spectra, 'stn', split_axis=0, concat_axis=0, tiled=True)  22.4 us
    pallas_call x3, Pallas kernels, correlate_rows_chunk(): pl.pallas_call(correlate_rows_kernel, grid_spec=grid_spec, out_shape=jax....  21.5 us
    ppermute x4, waiting for transfers between devices, gathered_along(): parts.append(lax.ppermute(value, axis, pairs))  18.5 us
    reshape x4, local copies, waits for them, and re-layouts, per_device(): turned = turned.reshape(groups, width, 2, stations_local, spectra_local)  17.5 us
    pallas_call x1, Pallas kernels, filter_frames(): pl.pallas_call(fir_kernel, grid=(stations_local // group,), in_specs=[pl....  14.3 us
    dot_general x4, matrix products, per_device(): jnp.einsum('gkias,gar->kisr', turned, selector, preferred_element_type=jn...  14.2 us
  transfers between devices with their start and end apart: 9, of which 9 were waited for; matrix products, arithmetic and copies ran while one was open for 28% of the time, Pallas kernels for 15%

profile of v16, /device:TPU:14, one launch (start us, length us, event | category | flops | bytes accessed | tf_op | source)
XLA Modules:
  0.0 230.9 jit_solution(7451686200983638306)
XLA Ops:
  0.0 3.8 %convert.3 = bf16[2,32,32768]{2,1,0:T(8,128)(2,1)S(1)} convert(s32[2,32,32768]{2,1,0:T(8,128)} %param.4) | non-fusion elementwise | flops 2097152 | bytes 12582912 | tf_op jit(solution)/shard_map/convert
  3.9 0.1 copy.58
  4.0 1.3 collective-permute-start
  5.3 4.5 %copy.40 = bf16[8,8,32,1024]{3,2,1,0:T(8,128)(2,1)} copy(bf16[8,8,32,1024]{3,1,2,0:T(8,128)(2,1)S(1)} %bitcast.67) | data formatting | bytes 8388608
  9.7 14.3 %shard_map.46.previous_ref = bf16[2,32,32,2048]{3,2,1,0:T(8,128)(2,1)} custom-call(f32[8,1024]{1,0:T(8,128)} %taps_ref.3, bf16[2,32,32,1024]{3,2,1,0:T(8,128)(2,1)} %bitcast.61), custom_call_target="tpu_custom_call" | custom-call | flops 67108864 | bytes 12582912 | tf_op jit(solution)/shard_map/pallas_call | solution.py:112
  24.0 3.9 %collective-permute-done = bf16[2,32,7,1024]{3,1,2,0:T(8,128)(2,1)S(1)} collective-permute-done((bf16[2,32,7,1024]{3,1,2,0:T(8,128)(2,1)S(1)}, bf16[2,32,7,1024]{3,1,2,0:T(8,128)(2,1)S(1)}, u32[]{:S(2)}, u32[]{:S(2)}) %collective-permute-start) | collective-permute-done | bytes 917536 | tf_op jit(solution)/shard_map/ppermute | solution.py:18
  27.9 1.6 copy.21.halo_ref
  29.5 6.1 %shard_map.47 = bf16[2,32,32,2048]{3,2,1,0:T(8,128)(2,1)} custom-call(f32[8,1024]{1,0:T(8,128)} %taps_ref.3, bf16[2,32,7,1024]{3,2,1,0:T(8,128)(2,1)} %copy.21.halo_ref, bf16[2,32,32,1024]{3,2,1,0:T(8,128)(2,1)} %bitcast.62, bf16[2,32,32,2048]{3,2,1,0:T(8,128)(2,1)} %shard_map.46.previous_ref), custom_call_target="tpu_custom_call", output_to_operand_aliasing={{}: (3, {})} | custom-call | flops 16777216 | bytes 4194304 | tf_op jit(solution)/shard_map/pallas_call | solution.py:129
  35.6 6.8 %convolution_convert_fusion.2 = bf16[2048,256]{0,1:T(8,128)(2,1)} fusion(bf16[2048,2048]{1,0:T(8,128)(2,1)} %bitcast.63, bf16[256,2048]{1,0:T(8,128)(2,1)S(1)} %copy-done.6), kind=kOutput, calls=%fused_computation.10 | convolution fusion | flops 2148007936 | bytes 10485760 | tf_op jit(solution)/shard_map/kj,nj->kn/dot_general | solution.py:371
  42.4 6.2 %all-to-all-start.1 = ((bf16[16,16,2048]{2,1,0:T(8,128)(2,1)}), bf16[16,16,2048]{2,1,0:T(8,128)(2,1)S(1)}, u32[]{:S(2)}, u32[]{:S(2)}) async-start(bf16[16,16,2048]{2,1,0:T(8,128)(2,1)} %bitcast.10), calls=%async_computation.1 | async-start | bytes 2097152 | tf_op jit(solution)/shard_map/all_to_all | solution.py:375
  48.7 6.8 %convolution_convert_fusion.3 = bf16[2048,256]{0,1:T(8,128)(2,1)} fusion(bf16[2048,2048]{1,0:T(8,128)(2,1)} %bitcast.64, bf16[256,2048]{1,0:T(8,128)(2,1)S(1)} %copy-done.5), kind=kOutput, calls=%fused_computation.11 | convolution fusion | flops 2148007936 | bytes 10485760 | tf_op jit(solution)/shard_map/kj,nj->kn/dot_general | solution.py:371
  55.5 17.9 %all-to-all-done.1 = bf16[16,16,2048]{2,1,0:T(8,128)(2,1)S(1)} async-done(((bf16[16,16,2048]{2,1,0:T(8,128)(2,1)}), bf16[16,16,2048]{2,1,0:T(8,128)(2,1)S(1)}, u32[]{:S(2)}, u32[]{:S(2)}) %all-to-all-start.1) | async-done | bytes 1048608 | tf_op jit(solution)/shard_map/all_to_all | solution.py:375
  73.4 5.1 %all-to-all-start = ((bf16[16,16,2048]{2,1,0:T(8,128)(2,1)}), bf16[16,16,2048]{2,1,0:T(8,128)(2,1)S(1)}, u32[]{:S(2)}, u32[]{:S(2)}) async-start(bf16[16,16,2048]{2,1,0:T(8,128)(2,1)} %bitcast.3), calls=%async_computation | async-start | bytes 2097152 | tf_op jit(solution)/shard_map/all_to_all | solution.py:375
  78.5 4.4 %reshape.85 = bf16[16,16,2,32,32]{4,3,2,1,0:T(8,128)(2,1)} reshape(bf16[16,16,2048]{2,1,0:T(8,128)(2,1)S(1)} %all-to-all-done.1) | data formatting | bytes 2097152 | tf_op jit(solution)/shard_map/reshape | solution.py:376
  82.9 3.6 %fusion.4 = bf16[16,2,32,512,1]{3,2,0,1,4:T(8,128)(2,1)S(1)} fusion(bf16[16,16,2,32,32]{4,3,2,1,0:T(8,128)(2,1)} %reshape.85, s32[16,32]{1,0:T(8,128)S(1)} %multiply_add_fusion, s32[512]{0:T(512)S(1)} %copy-done.2), kind=kOutput, calls=%fused_computation.4 | convolution fusion | flops 537133056 | bytes 2101248 | tf_op jit(solution)/shard_map/gkias,gar->kisr/dot_general | solution.py:377
  86.4 0.1 copy.56
  86.5 0.1 collective-permute-start.2
  86.6 16.6 %all-to-all-done = bf16[16,16,2048]{2,1,0:T(8,128)(2,1)S(1)} async-done(((bf16[16,16,2048]{2,1,0:T(8,128)(2,1)}), bf16[16,16,2048]{2,1,0:T(8,128)(2,1)S(1)}, u32[]{:S(2)}, u32[]{:S(2)}) %all-to-all-start) | async-done | bytes 1048608 | tf_op jit(solution)/shard_map/all_to_all | solution.py:375
  103.2 4.4 %reshape.81 = bf16[16,16,2,32,32]{4,3,2,1,0:T(8,128)(2,1)} reshape(bf16[16,16,2048]{2,1,0:T(8,128)(2,1)S(1)} %all-to-all-done) | data formatting | bytes 2097152 | tf_op jit(solution)/shard_map/reshape | solution.py:376
  107.6 3.6 %fusion.6 = bf16[16,2,32,512,1]{3,2,0,1,4:T(8,128)(2,1)S(1)} fusion(bf16[16,16,2,32,32]{4,3,2,1,0:T(8,128)(2,1)} %reshape.81, s32[16,32]{1,0:T(8,128)S(1)} %multiply_add_fusion, s32[512]{0:T(512)S(1)} %copy-done.2), kind=kOutput, calls=%fused_computation.6 | convolution fusion | flops 537133056 | bytes 2101248 | tf_op jit(solution)/shard_map/gkias,gar->kisr/dot_general | solution.py:377
  111.1 0.1 copy.57
  111.2 0.1 collective-permute-start.1
  111.3 0.6 collective-permute-done.2
  111.9 2.8 %pad_maximum_fusion.1 = bf16[32,64,512]{2,1,0:T(8,128)(2,1)} fusion(bf16[32,32,512]{2,1,0:T(8,128)(2,1)} %collective-permute-done.2, bf16[32,32,512]{2,1,0:T(8,128)(2,1)S(1)} %bitcast.80), kind=kLoop, calls=%fused_computation.13 | loop fusion | flops 4194304 | bytes 4194304 | tf_op jit(solution)/shard_map/concatenate | solution.py:29
  114.7 7.2 %shard_map.48.refs_0_ = bf16[2,64,256,512]{3,2,1,0:T(8,128)(2,1)} custom-call(s32[1]{0:T(128)} %bitcast.block_ref, bf16[16,128,512]{2,1,0:T(8,128)(2,1)} %bitcast.68, bf16[16,128,512]{2,1,0:T(8,128)(2,1)} %bitcast.69), custom_call_target="tpu_custom_call" | custom-call | flops 1073741824 | bytes 11534336 | tf_op jit(solution)/shard_map/pallas_call | solution.py:239
  121.9 6.7 %convolution_convert_fusion = bf16[2048,256]{0,1:T(8,128)(2,1)} fusion(bf16[2048,2048]{1,0:T(8,128)(2,1)} %bitcast.65, bf16[256,2048]{1,0:T(8,128)(2,1)S(1)} %copy-done.4), kind=kOutput, calls=%fused_computation.8 | convolution fusion | flops 2148007936 | bytes 10485760 | tf_op jit(solution)/shard_map/kj,nj->kn/dot_general | solution.py:371
  128.6 6.0 %all-to-all-start.3 = ((bf16[16,16,2048]{2,1,0:T(8,128)(2,1)}), bf16[16,16,2048]{2,1,0:T(8,128)(2,1)S(1)}, u32[]{:S(2)}, u32[]{:S(2)}) async-start(bf16[16,16,2048]{2,1,0:T(8,128)(2,1)} %bitcast.21), calls=%async_computation.3 | async-start | bytes 2097152 | tf_op jit(solution)/shard_map/all_to_all | solution.py:375
  134.6 2.5 %collective-permute-done.1 = bf16[32,32,512]{2,1,0:T(8,128)(2,1)} collective-permute-done((bf16[32,32,512]{2,1,0:T(8,128)(2,1)S(1)}, bf16[32,32,512]{2,1,0:T(8,128)(2,1)}, u32[]{:S(2)}, u32[]{:S(2)}) %collective-permute-start.1) | collective-permute-done | bytes 1048608 | tf_op jit(solution)/shard_map/ppermute | solution.py:26
  137.1 2.8 %pad_maximum_fusion = bf16[32,64,512]{2,1,0:T(8,128)(2,1)} fusion(bf16[32,32,512]{2,1,0:T(8,128)(2,1)} %collective-permute-done.1, bf16[32,32,512]{2,1,0:T(8,128)(2,1)S(1)} %bitcast.84), kind=kLoop, calls=%fused_computation.12 | loop fusion | flops 4194304 | bytes 4194304 | tf_op jit(solution)/shard_map/concatenate | solution.py:29
  139.9 7.2 %shard_map.49.refs_0_ = bf16[2,64,256,512]{3,2,1,0:T(8,128)(2,1)} custom-call(s32[1]{0:T(128)} %bitcast.block_ref, bf16[16,128,512]{2,1,0:T(8,128)(2,1)} %bitcast.70, bf16[16,128,512]{2,1,0:T(8,128)(2,1)} %bitcast.71, bf16[2,64,256,512]{3,2,1,0:T(8,128)(2,1)} %shard_map.48.refs_0_), custom_call_target="tpu_custom_call", output_to_operand_aliasing={{}: (3, {})} | custom-call | flops 1073741824 | bytes 11534336 | tf_op jit(solution)/shard_map/pallas_call | solution.py:239
  147.1 6.8 %convolution_convert_fusion.1 = bf16[2048,256]{0,1:T(8,128)(2,1)} fusion(bf16[2048,2048]{1,0:T(8,128)(2,1)} %bitcast.66, bf16[256,2048]{1,0:T(8,128)(2,1)S(1)} %copy-done.3), kind=kOutput, calls=%fused_computation.9 | convolution fusion | flops 2148007936 | bytes 10485760 | tf_op jit(solution)/shard_map/kj,nj->kn/dot_general | solution.py:371
  153.9 5.4 %all-to-all-done.3 = bf16[16,16,2048]{2,1,0:T(8,128)(2,1)S(1)} async-done(((bf16[16,16,2048]{2,1,0:T(8,128)(2,1)}), bf16[16,16,2048]{2,1,0:T(8,128)(2,1)S(1)}, u32[]{:S(2)}, u32[]{:S(2)}) %all-to-all-start.3) | async-done | bytes 1048608 | tf_op jit(solution)/shard_map/all_to_all | solution.py:375
  159.3 5.1 %all-to-all-start.2 = ((bf16[16,16,2048]{2,1,0:T(8,128)(2,1)}), bf16[16,16,2048]{2,1,0:T(8,128)(2,1)S(1)}, u32[]{:S(2)}, u32[]{:S(2)}) async-start(bf16[16,16,2048]{2,1,0:T(8,128)(2,1)} %bitcast.16), calls=%async_computation.2 | async-start | bytes 2097152 | tf_op jit(solution)/shard_map/all_to_all | solution.py:375
  164.4 4.4 %reshape.93 = bf16[16,16,2,32,32]{4,3,2,1,0:T(8,128)(2,1)} reshape(bf16[16,16,2048]{2,1,0:T(8,128)(2,1)S(1)} %all-to-all-done.3) | data formatting | bytes 2097152 | tf_op jit(solution)/shard_map/reshape | solution.py:376
  168.8 3.6 %fusion = bf16[16,2,32,512,1]{3,2,0,1,4:T(8,128)(2,1)S(1)} fusion(bf16[16,16,2,32,32]{4,3,2,1,0:T(8,128)(2,1)} %reshape.93, s32[16,32]{1,0:T(8,128)S(1)} %multiply_add_fusion, s32[512]{0:T(512)S(1)} %copy-done.2), kind=kOutput, calls=%fused_computation | convolution fusion | flops 537133056 | bytes 2101248 | tf_op jit(solution)/shard_map/gkias,gar->kisr/dot_general | solution.py:377
  172.4 0.1 copy.54
  172.5 0.6 collective-permute-start.4
  173.0 16.1 %all-to-all-done.2 = bf16[16,16,2048]{2,1,0:T(8,128)(2,1)S(1)} async-done(((bf16[16,16,2048]{2,1,0:T(8,128)(2,1)}), bf16[16,16,2048]{2,1,0:T(8,128)(2,1)S(1)}, u32[]{:S(2)}, u32[]{:S(2)}) %all-to-all-start.2) | async-done | bytes 1048608 | tf_op jit(solution)/shard_map/all_to_all | solution.py:375
  189.2 4.4 %reshape.89 = bf16[16,16,2,32,32]{4,3,2,1,0:T(8,128)(2,1)} reshape(bf16[16,16,2048]{2,1,0:T(8,128)(2,1)S(1)} %all-to-all-done.2) | data formatting | bytes 2097152 | tf_op jit(solution)/shard_map/reshape | solution.py:376
  193.6 3.6 %fusion.2 = bf16[16,2,32,512,1]{3,2,0,1,4:T(8,128)(2,1)S(1)} fusion(bf16[16,16,2,32,32]{4,3,2,1,0:T(8,128)(2,1)} %reshape.89, s32[16,32]{1,0:T(8,128)S(1)} %multiply_add_fusion, s32[512]{0:T(512)S(1)} %copy-done.2), kind=kOutput, calls=%fused_computation.2 | convolution fusion | flops 537133056 | bytes 2101248 | tf_op jit(solution)/shard_map/gkias,gar->kisr/dot_general | solution.py:377
  197.1 0.1 copy.55
  197.2 0.6 collective-permute-start.3
  197.8 0.1 collective-permute-done.4
  197.9 2.8 %pad_maximum_fusion.2 = bf16[32,64,512]{2,1,0:T(8,128)(2,1)} fusion(bf16[32,32,512]{2,1,0:T(8,128)(2,1)} %collective-permute-done.4, bf16[32,32,512]{2,1,0:T(8,128)(2,1)S(1)} %bitcast.82), kind=kLoop, calls=%fused_computation.14 | loop fusion | flops 4194304 | bytes 4194304 | tf_op jit(solution)/shard_map/concatenate | solution.py:29
  200.6 7.1 %shard_map.50.refs_4_ = bf16[2,64,256,512]{3,2,1,0:T(8,128)(2,1)} custom-call(s32[1]{0:T(128)} %bitcast.block_ref, bf16[16,128,512]{2,1,0:T(8,128)(2,1)} %bitcast.72, bf16[16,128,512]{2,1,0:T(8,128)(2,1)} %bitcast.73, bf16[2,64,256,512]{3,2,1,0:T(8,128)(2,1)} %shard_map.49.refs_0_), custom_call_target="tpu_custom_call", output_to_operand_aliasing={{}: (3, {})} | custom-call | flops 1073741824 | bytes 11534336 | tf_op jit(solution)/shard_map/pallas_call | solution.py:239
  207.7 15.3 %collective-permute-done.3 = bf16[32,32,512]{2,1,0:T(8,128)(2,1)S(1)} collective-permute-done((bf16[32,32,512]{2,1,0:T(8,128)(2,1)S(1)}, bf16[32,32,512]{2,1,0:T(8,128)(2,1)S(1)}, u32[]{:S(2)}, u32[]{:S(2)}) %collective-permute-start.3) | collective-permute-done | bytes 1048608 | tf_op jit(solution)/shard_map/ppermute | solution.py:26
  223.0 1.0 copy-done.1
  224.0 6.9 %shard_map.51 = bf16[2,64,256,512]{3,2,1,0:T(8,128)(2,1)} custom-call(s32[1]{0:T(128)} %bitcast.block_ref, bf16[16,2,32,512]{3,2,1,0:T(8,128)(2,1)} %bitcast.75, bf16[16,2,32,512]{3,2,1,0:T(8,128)(2,1)} %bitcast.77, bf16[16,2,32,512]{3,2,1,0:T(8,128)(2,1)} %bitcast.76, bf16[16,2,32,512]{3,2,1,0:T(8,128)(2,1)} %bitcast.78, ...), custom_call_target="tpu_custom_call", output_to_operand_aliasing={{}: (5, {})} | custom-call | flops 1073741824 | bytes 11534336 | tf_op jit(solution)/shard_map/pallas_call | solution.py:300
  (15 shorter events, 0.1 us)
Async XLA Ops:
  4.0 24.0 %collective-permute-start = (bf16[2,32,7,1024]{3,1,2,0:T(8,128)(2,1)S(1)}, bf16[2,32,7,1024]{3,1,2,0:T(8,128)(2,1)S(1)}, u32[]{:S(2)}, u32[]{:S(2)}) collective-permute-start(bf16[2,32,7,1024]{3,1,2,0:T(8,128)(2,1)S(1)} %bitcast.86), channel_id=1, source_target_pairs={{0,1},{2,3},{4,5},{6,7},{8,9},{10,11},{12,13},{14,15},{16,17},{18,... | collective-permute-start | bytes 2752520 | tf_op jit(solution)/shard_map/ppermute | solution.py:18
  29.5 6.1 %copy-start.6 = (bf16[256,2048]{1,0:T(8,128)(2,1)S(1)}, bf16[256,2048]{1,0:T(8,128)(2,1)}, u32[]{:S(2)}) copy-start(bf16[256,2048]{1,0:T(8,128)(2,1)} %constant.12) | copy-start | bytes 3145732
  35.6 13.1 %copy-start.5 = (bf16[256,2048]{1,0:T(8,128)(2,1)S(1)}, bf16[256,2048]{1,0:T(8,128)(2,1)}, u32[]{:S(2)}) copy-start(bf16[256,2048]{1,0:T(8,128)(2,1)} %constant.10) | copy-start | bytes 3145732
  42.4 31.0 %all-to-all-start.1 = ((bf16[16,16,2048]{2,1,0:T(8,128)(2,1)}), bf16[16,16,2048]{2,1,0:T(8,128)(2,1)S(1)}, u32[]{:S(2)}, u32[]{:S(2)}) async-start(bf16[16,16,2048]{2,1,0:T(8,128)(2,1)} %bitcast.10), calls=%async_computation.1 | async-start | bytes 2097152 | tf_op jit(solution)/shard_map/all_to_all | solution.py:375
  55.5 27.4 %copy-start.2 = (s32[512]{0:T(512)S(1)}, s32[512]{0:T(512)}, u32[]{:S(2)}) copy-start(s32[512]{0:T(512)} %param.6) | copy-start | bytes 6148
  73.4 29.8 %all-to-all-start = ((bf16[16,16,2048]{2,1,0:T(8,128)(2,1)}), bf16[16,16,2048]{2,1,0:T(8,128)(2,1)S(1)}, u32[]{:S(2)}, u32[]{:S(2)}) async-start(bf16[16,16,2048]{2,1,0:T(8,128)(2,1)} %bitcast.3), calls=%async_computation | async-start | bytes 2097152 | tf_op jit(solution)/shard_map/all_to_all | solution.py:375
  86.5 25.4 %collective-permute-start.2 = (bf16[32,32,512]{2,1,0:T(8,128)(2,1)S(1)}, bf16[32,32,512]{2,1,0:T(8,128)(2,1)}, u32[]{:S(2)}, u32[]{:S(2)}) collective-permute-start(bf16[32,32,512]{2,1,0:T(8,128)(2,1)S(1)} %bitcast.79), channel_id=1, source_target_pairs={{0,1},{1,0},{2,3},{3,2},{4,5},{5,4},{6,7},{7,6},{8,9},{9,8},{10,11... | collective-permute-start | bytes 3145736 | tf_op jit(solution)/shard_map/ppermute | solution.py:26
  111.2 25.9 %collective-permute-start.1 = (bf16[32,32,512]{2,1,0:T(8,128)(2,1)S(1)}, bf16[32,32,512]{2,1,0:T(8,128)(2,1)}, u32[]{:S(2)}, u32[]{:S(2)}) collective-permute-start(bf16[32,32,512]{2,1,0:T(8,128)(2,1)S(1)} %bitcast.83), channel_id=1, source_target_pairs={{0,1},{1,0},{2,3},{3,2},{4,5},{5,4},{6,7},{7,6},{8,9},{9,8},{10,11... | collective-permute-start | bytes 3145736 | tf_op jit(solution)/shard_map/ppermute | solution.py:26
  114.7 7.2 %copy-start.4 = (bf16[256,2048]{1,0:T(8,128)(2,1)S(1)}, bf16[256,2048]{1,0:T(8,128)(2,1)}, u32[]{:S(2)}) copy-start(bf16[256,2048]{1,0:T(8,128)(2,1)} %constant.16) | copy-start | bytes 3145732
  128.6 30.7 %all-to-all-start.3 = ((bf16[16,16,2048]{2,1,0:T(8,128)(2,1)}), bf16[16,16,2048]{2,1,0:T(8,128)(2,1)S(1)}, u32[]{:S(2)}, u32[]{:S(2)}) async-start(bf16[16,16,2048]{2,1,0:T(8,128)(2,1)} %bitcast.21), calls=%async_computation.3 | async-start | bytes 2097152 | tf_op jit(solution)/shard_map/all_to_all | solution.py:375
  139.9 7.2 %copy-start.3 = (bf16[256,2048]{1,0:T(8,128)(2,1)S(1)}, bf16[256,2048]{1,0:T(8,128)(2,1)}, u32[]{:S(2)}) copy-start(bf16[256,2048]{1,0:T(8,128)(2,1)} %constant.14) | copy-start | bytes 3145732
  159.3 29.8 %all-to-all-start.2 = ((bf16[16,16,2048]{2,1,0:T(8,128)(2,1)}), bf16[16,16,2048]{2,1,0:T(8,128)(2,1)S(1)}, u32[]{:S(2)}, u32[]{:S(2)}) async-start(bf16[16,16,2048]{2,1,0:T(8,128)(2,1)} %bitcast.16), calls=%async_computation.2 | async-start | bytes 2097152 | tf_op jit(solution)/shard_map/all_to_all | solution.py:375
  172.5 25.4 %collective-permute-start.4 = (bf16[32,32,512]{2,1,0:T(8,128)(2,1)S(1)}, bf16[32,32,512]{2,1,0:T(8,128)(2,1)}, u32[]{:S(2)}, u32[]{:S(2)}) collective-permute-start(bf16[32,32,512]{2,1,0:T(8,128)(2,1)S(1)} %bitcast.81), channel_id=1, source_target_pairs={{0,1},{1,0},{2,3},{3,2},{4,5},{5,4},{6,7},{7,6},{8,9},{9,8},{10,11... | collective-permute-start | bytes 3145736 | tf_op jit(solution)/shard_map/ppermute | solution.py:26
  197.2 10.5 %copy-start = (bf16[16,2,32,512,1]{3,2,1,0,4:T(8,128)(2,1)}, bf16[16,2,32,512,1]{3,2,1,0,4:T(8,128)(2,1)S(1)}, u32[]{:S(2)}) copy-start(bf16[16,2,32,512,1]{3,2,1,0,4:T(8,128)(2,1)S(1)} %copy.55) | copy-start | bytes 3145732
  197.2 25.8 %collective-permute-start.3 = (bf16[32,32,512]{2,1,0:T(8,128)(2,1)S(1)}, bf16[32,32,512]{2,1,0:T(8,128)(2,1)S(1)}, u32[]{:S(2)}, u32[]{:S(2)}) collective-permute-start(bf16[32,32,512]{2,1,0:T(8,128)(2,1)S(1)} %bitcast.74), channel_id=1, source_target_pairs={{0,1},{1,0},{2,3},{3,2},{4,5},{5,4},{6,7},{7,6},{8,9},{9,8},{10,11... | collective-permute-start | bytes 3145736 | tf_op jit(solution)/shard_map/ppermute | solution.py:26
  223.0 1.0 copy-start.1
